TPU v7x, 32 devices: a whole 2x2x4 slice. The times are simulated.
32 devices in a mesh: node: 4 (over z), local: 8 (over y, x, core).
Axes of the slice: x: 2, y: 2, z: 4, core: 2. Of those that a mesh axis runs over, the one named last changes fastest.
Arguments:
- hidden_in: bfloat16 [4096, 3584], P(('node', 'local')), may hold values from -6 to 6
- out_grad: bfloat16 [4096, 3584], P(('node', 'local')), may hold values from -6 to 6
- expert_ids: int32 [4, 1024, 8], P(None, 'local'), may hold values from 0 to 31, as said below
- gate_int: int32 [4, 1024, 8], P(None, 'local'), may hold values from 1 to 256
- gate_saved: bfloat16 [32768, 1024], P(('node', 'local')), may hold values from -6 to 6
- w_in: bfloat16 [32, 3584, 2048], P(('node', 'local')), may hold values from -0.09375 to 0.09375
- w_out: bfloat16 [32, 1024, 3584], P(('node', 'local')), may hold values from -0.1875 to 0.1875
Outputs:
- grad_in: bfloat16 [4096, 3584], P(('node', 'local'))
Inputs may be any that keep to these rules, and one draw needn't show every extreme that they name: `expert_ids`: each token names 8 different experts, two on each of 4 different nodes. Among the 128 tokens of one device (one n, one value of j // 128) every expert is named exactly 32 times.
All inputs are finite; a program needn't handle non-finite values.
Results may differ from a plain program's by a relative error of at most 0.0085.
Values may be sent and summed in bfloat16 or wider, within the bound.
No kernel may reach another device: no remote copies, remote signals or barrier semaphores. Data moves between devices by JAX's collectives and lax.ppermute only.
A program may use at most 128 MiB of HBM per device.

v0:
```python
import jax
import jax.numpy as jnp
from jax import lax
from jax.sharding import PartitionSpec as P

FF = 1024
TOK_DEV = 128
TOPK = 8


def slot_ranks(flat_ids, columns):
    onehot = (flat_ids[..., None] == jnp.arange(columns, dtype=jnp.int32)).astype(jnp.int32)
    counts = jnp.cumsum(onehot, axis=-2)
    return jnp.sum(counts * onehot, axis=-1) - 1


def expert_backward(rows_x, rows_dy, rows_gate, saved, weight_in, weight_out):
    up_pre = jnp.dot(rows_x, weight_in[:, FF:], preferred_element_type=jnp.float32)
    grad_hidden = lax.dot_general(
        rows_dy, weight_out, (((1,), (1,)), ((), ())), preferred_element_type=jnp.float32
    )
    grad_hidden = grad_hidden * rows_gate.astype(jnp.float32)[:, None]
    gate_pre = saved.astype(jnp.float32)
    sigmoid_gate = jax.nn.sigmoid(gate_pre)
    grad_gate = grad_hidden * up_pre * sigmoid_gate * (1.0 + gate_pre * (1.0 - sigmoid_gate))
    grad_up = grad_hidden * gate_pre * sigmoid_gate
    grad_pre = jnp.concatenate([grad_gate, grad_up], axis=1).astype(jnp.bfloat16)
    contrib = lax.dot_general(
        grad_pre, weight_in, (((1,), (1,)), ((), ())), preferred_element_type=jnp.float32
    )
    return contrib.astype(jnp.bfloat16)


def pair_sums(contribs, node_of):
    slot_order = jnp.argsort(node_of, axis=1, stable=True)
    ordered = jnp.take_along_axis(contribs, slot_order[:, :, None], axis=1)
    paired = ordered.reshape(ordered.shape[0], TOPK // 2, 2, ordered.shape[2])
    return (paired[:, :, 0].astype(jnp.float32) + paired[:, :, 1].astype(jnp.float32)).astype(
        jnp.bfloat16
    )


def on_device(hidden_in, out_grad, expert_ids, gate_int, gate_saved, w_in, w_out):
    n_node = lax.axis_size("node")
    n_local = lax.axis_size("local")
    experts = n_node * n_local
    capacity = TOK_DEV * TOPK // experts
    row_count = experts * capacity
    model_width = hidden_in.shape[1]
    node_here = lax.axis_index("node")
    weight_in = w_in[0]
    weight_out = w_out[0]
    own_ids = lax.dynamic_index_in_dim(expert_ids, node_here, 0, keepdims=False)
    own_gate = lax.dynamic_index_in_dim(gate_int, node_here, 0, keepdims=False)
    flat_ids = own_ids.reshape(-1)
    flat_range = jnp.arange(TOK_DEV * TOPK, dtype=jnp.int32)
    row_rank = slot_ranks(flat_ids, experts)
    position = flat_ids * capacity + row_rank
    source_row = jnp.zeros((row_count,), jnp.int32).at[position].set(flat_range)
    token_row = source_row // TOPK
    send_x = hidden_in[token_row].reshape(experts, capacity, model_width)
    send_dy = out_grad[token_row].reshape(experts, capacity, model_width)
    send_gate = (
        (own_gate.reshape(-1)[source_row].astype(jnp.float32) / 1024.0)
        .astype(jnp.bfloat16)
        .reshape(experts, capacity)
    )
    recv_x, recv_dy, recv_gate = (
        lax.all_to_all(send_x, ("node", "local"), split_axis=0, concat_axis=0, tiled=True),
        lax.all_to_all(send_dy, ("node", "local"), split_axis=0, concat_axis=0, tiled=True),
        lax.all_to_all(send_gate, ("node", "local"), split_axis=0, concat_axis=0, tiled=True),
    )
    contrib = expert_backward(
        recv_x.reshape(row_count, model_width),
        recv_dy.reshape(row_count, model_width),
        recv_gate.reshape(row_count),
        gate_saved,
        weight_in,
        weight_out,
    )
    returned = lax.all_to_all(
        contrib.reshape(experts, capacity, model_width),
        ("node", "local"),
        split_axis=0,
        concat_axis=0,
        tiled=True,
    )
    gathered = returned.reshape(row_count, model_width)[position].reshape(
        TOK_DEV, TOPK, model_width
    )
    node_sum = pair_sums(gathered, own_ids // n_local)
    return jnp.sum(node_sum.astype(jnp.float32), axis=1).astype(jnp.bfloat16)


def solution(mesh):
    in_specs = (
        P(("node", "local"), None),
        P(("node", "local"), None),
        P(None, "local", None),
        P(None, "local", None),
        P(("node", "local"), None),
        P(("node", "local"), None, None),
        P(("node", "local"), None, None),
    )
    out_specs = P(("node", "local"), None)
    return jax.shard_map(
        on_device, mesh=mesh, in_specs=in_specs, out_specs=out_specs, check_vma=False
    )
```

profile of v0, /device:TPU:0, one launch (start us, length us, event | category | flops | bytes accessed | tf_op | source)
XLA Modules:
  0.0 650.3 jit_solution(8397261017630189863)
XLA Ops:
  0.0 0.0 copy-start
  0.0 0.8 add_select_fusion.2
  0.8 0.1 copy.39
  0.9 0.1 eq.29
  1.0 0.1 eq.25
  1.1 0.7 constant_dynamic-slice_fusion
  1.8 0.1 copy.43
  1.9 0.1 reshape.130
  2.0 0.1 copy.38
  2.1 0.1 mul.47
  2.2 9.0 %reduce-window.6 = s32[32,8,128]{2,1,0:T(8,128)S(1)} reduce-window(s32[32,8,128]{2,1,0:T(8,128)S(1)} %fusion.20, s32[]{:T(128)} %constant.57.clone.1), window={size=1x1x128 pad=0_0x0_0x127_0}, to_apply=%region_1.2 | reduce-window | flops 4161536 | bytes 262148 | tf_op jit(solution)/shard_map/reduce-window
  11.2 0.1 slice.30
  11.3 0.1 copy.41
  11.5 0.1 copy.42
  11.5 0.1 broadcast_add_fusion
  11.7 4.3 scatter_custom_fusion
  16.1 4.5 gather_fusion.1
  20.6 0.7 convert_element_type.74
  21.3 7.3 %all-to-all-start.1 = ((bf16[32,1,32]{2,1,0:T(2,128)(2,1)}), bf16[32,1,32]{2,1,0:T(2,128)(2,1)S(1)}, u32[]{:S(2)}, u32[]{:S(2)}) async-start(bf16[32,1,32]{2,1,0:T(2,128)(2,1)} %convert_element_type.74), calls=%async_computation.1 | async-start | bytes 32768 | tf_op jit(solution)/shard_map/all_to_all | solution.py:71
  28.6 0.0 copy-done
  28.6 7.3 %gather_fusion = bf16[1024,3584]{1,0:T(8,128)(2,1)} fusion(bf16[128,3584]{1,0:T(8,128)(2,1)S(1)} %copy-done, s32[1024]{0:T(1024)S(1)} %get-tuple-element.10), kind=kCustom, calls=%fused_computation | custom fusion | bytes 14684160 | tf_op jit(solution)/shard_map/gather | solution.py:62
  35.9 0.0 all-to-all-done.1
  35.9 0.0 copy-start.2
  35.9 5.9 all-to-all-start
  41.9 0.0 copy-done.2
  41.9 7.3 %gather_fusion.2 = bf16[1024,3584]{1,0:T(8,128)(2,1)} fusion(bf16[128,3584]{1,0:T(8,128)(2,1)S(1)} %copy-done.2, s32[1024]{0:T(1024)S(1)} %get-tuple-element.10), kind=kCustom, calls=%fused_computation.2 | custom fusion | bytes 14684160 | tf_op jit(solution)/shard_map/gather | solution.py:61
  49.2 155.8 %all-to-all-done = bf16[32,32,3584]{2,1,0:T(8,128)(2,1)} async-done(((bf16[32,32,3584]{2,1,0:T(8,128)(2,1)}), bf16[32,32,3584]{2,1,0:T(8,128)(2,1)}, u32[]{:S(2)}, u32[]{:S(2)}) %all-to-all-start) | async-done | bytes 7340064 | tf_op jit(solution)/shard_map/all_to_all | solution.py:70
  205.0 0.0 copy-start.3
  205.0 3.8 all-to-all-start.2
  208.8 0.0 copy-done.3
  208.8 2.6 copy.45
  211.4 0.1 convert_reduce_fusion
  211.5 0.1 reshape.136
  211.5 0.0 copy-start.4
  211.5 14.7 %fusion.11 = (bf16[1024,1024]{0,1:T(8,128)(2,1)}, f32[1024,1024]{0,1:T(8,128)}) fusion(bf16[1024,1024]{0,1:T(8,128)(2,1)} %copy.45, f32[1024]{0:T(1024)S(1)} %reshape.136, bf16[1024,3584]{1,0:T(8,128)(2,1)} %bitcast.6, bf16[1,1024,3584]{2,1,0:T(8,128)(2,1)} %param.13), kind=kOutput, calls=%fused_computation.23 | convolution fusion | flops 7524581376 | bytes 23072768 | tf_op jit(solution)/shard_map/dot_general | solution.py:19
  226.2 145.6 %all-to-all-done.2 = bf16[32,32,3584]{2,1,0:T(8,128)(2,1)} async-done(((bf16[32,32,3584]{2,1,0:T(8,128)(2,1)}), bf16[32,32,3584]{2,1,0:T(8,128)(2,1)}, u32[]{:S(2)}, u32[]{:S(2)}) %all-to-all-start.2) | async-done | bytes 7340064 | tf_op jit(solution)/shard_map/all_to_all | solution.py:69
  371.9 0.0 copy-done.4
  371.9 15.2 %fusion.9 = bf16[1024,1024]{0,1:T(8,128)(2,1)} fusion(bf16[1024,1024]{0,1:T(8,128)(2,1)S(1)} %copy-done.4, f32[1024,1024]{0,1:T(8,128)} %get-tuple-element.12, bf16[1024,3584]{1,0:T(8,128)(2,1)} %bitcast.9, bf16[3584,2048]{1,0:T(8,128)(2,1)} %bitcast.64, f32[1024]{0:T(1024)S(1)} %reshape.136), kind=kOutput, calls=%fused_computation.21 | convolution fusion | flops 7528775680 | bytes 23072768 | tf_op jit(solution)/shard_map/dot_general | solution.py:18
  387.1 21.8 %convolution_convert_fusion = bf16[1024,3584]{1,0:T(8,128)(2,1)} fusion(bf16[1024,1024]{0,1:T(8,128)(2,1)} %get-tuple-element.11, bf16[1024,1024]{0,1:T(8,128)(2,1)} %fusion.9, bf16[1,3584,2048]{2,1,0:T(8,128)(2,1)} %param.12), kind=kOutput, calls=%fused_computation.6 | convolution fusion | flops 15044444160 | bytes 26214400 | tf_op jit(solution)/shard_map/dot_general | solution.py:28
  408.9 3.9 all-to-all-start.3
  412.7 0.7 sort.17
  413.4 0.1 copy.46
  413.5 0.1 reshape.169
  413.6 162.2 %all-to-all-done.3 = bf16[32,32,3584]{2,1,0:T(8,128)(2,1)} async-done(((bf16[32,32,3584]{2,1,0:T(8,128)(2,1)}), bf16[32,32,3584]{2,1,0:T(8,128)(2,1)}, u32[]{:S(2)}, u32[]{:S(2)}) %all-to-all-start.3) | async-done | bytes 7340064 | tf_op jit(solution)/shard_map/all_to_all | solution.py:81
  575.8 17.8 %gather_fusion.3 = bf16[1024,3584]{1,0:T(8,128)(2,1)} fusion(bf16[1024,3584]{1,0:T(8,128)(2,1)} %bitcast.12, s32[1024]{0:T(1024)S(1)} %broadcast_clamp_fusion), kind=kCustom, calls=%fused_computation.3 | custom fusion | bytes 14684160 | tf_op jit(solution)/shard_map/gather | solution.py:88
  593.6 31.8 %gather_fusion.4 = bf16[1024,3584]{1,0:T(8,128)(2,1)} fusion(bf16[128,8,3584]{2,1,0:T(8,128)(2,1)} %bitcast.55, s32[1024]{0:T(1024)S(1)} %reshape.169), kind=kCustom, calls=%fused_computation.4 | custom fusion | bytes 14688256 | tf_op jit(solution)/shard_map/jit(take_along_axis)/gather | solution.py:36
  625.4 14.9 %gather.23 = bf16[128,4,2,3584]{3,2,1,0:T(2,128)(2,1)} reshape(bf16[1024,3584]{1,0:T(8,128)(2,1)} %gather_fusion.4) | data formatting | bytes 14680064 | tf_op jit(solution)/shard_map/jit(take_along_axis)/gather | solution.py:36
  640.3 0.0 copy-start.1
  640.3 7.9 %copy_select_fusion = bf16[128,4,2,3584]{3,0,2,1:T(8,128)(2,1)S(1)} fusion(bf16[128,4,2,3584]{3,2,1,0:T(2,128)(2,1)} %gather.23, pred[128,4,2]{0,2,1:T(4,128)(4,1)S(1)} %broadcast_in_dim.22), kind=kLoop, calls=%fused_computation.11 | loop fusion | flops 3670016 | bytes 14681088 | tf_op jit(solution)/shard_map/jit(take_along_axis)/select_n | solution.py:36
  648.2 2.1 fusion.15
  650.3 0.0 copy-done.1
  (15 shorter events, 0.2 us)
Async XLA Ops:
  0.0 28.6 %copy-start = (bf16[128,3584]{1,0:T(8,128)(2,1)S(1)}, bf16[128,3584]{1,0:T(8,128)(2,1)}, u32[]{:S(2)}) copy-start(bf16[128,3584]{1,0:T(8,128)(2,1)} %param.8) | copy-start | bytes 2752516
  21.3 14.6 %all-to-all-start.1 = ((bf16[32,1,32]{2,1,0:T(2,128)(2,1)}), bf16[32,1,32]{2,1,0:T(2,128)(2,1)S(1)}, u32[]{:S(2)}, u32[]{:S(2)}) async-start(bf16[32,1,32]{2,1,0:T(2,128)(2,1)} %convert_element_type.74), calls=%async_computation.1 | async-start | bytes 32768 | tf_op jit(solution)/shard_map/all_to_all | solution.py:71
  35.9 6.0 copy-start.2
  35.9 169.1 %all-to-all-start = ((bf16[32,32,3584]{2,1,0:T(8,128)(2,1)}), bf16[32,32,3584]{2,1,0:T(8,128)(2,1)}, u32[]{:S(2)}, u32[]{:S(2)}) async-start(bf16[32,32,3584]{2,1,0:T(8,128)(2,1)} %bitcast.57), calls=%async_computation | async-start | bytes 14680064 | tf_op jit(solution)/shard_map/all_to_all | solution.py:70
  205.0 3.8 copy-start.3
  205.0 166.9 %all-to-all-start.2 = ((bf16[32,32,3584]{2,1,0:T(8,128)(2,1)}), bf16[32,32,3584]{2,1,0:T(8,128)(2,1)}, u32[]{:S(2)}, u32[]{:S(2)}) async-start(bf16[32,32,3584]{2,1,0:T(8,128)(2,1)} %bitcast.56), calls=%async_computation.2 | async-start | bytes 14680064 | tf_op jit(solution)/shard_map/all_to_all | solution.py:69
  211.5 160.4 %copy-start.4 = (bf16[1024,1024]{0,1:T(8,128)(2,1)S(1)}, bf16[1024,1024]{0,1:T(8,128)(2,1)}, u32[]{:S(2)}) copy-start(bf16[1024,1024]{0,1:T(8,128)(2,1)} %copy.45) | copy-start | bytes 6291460
  408.9 166.9 %all-to-all-start.3 = ((bf16[32,32,3584]{2,1,0:T(8,128)(2,1)}), bf16[32,32,3584]{2,1,0:T(8,128)(2,1)}, u32[]{:S(2)}, u32[]{:S(2)}) async-start(bf16[32,32,3584]{2,1,0:T(8,128)(2,1)} %bitcast.58), calls=%async_computation.3 | async-start | bytes 14680064 | tf_op jit(solution)/shard_map/all_to_all | solution.py:81
  640.3 10.0 %copy-start.1 = (bf16[128,3584]{1,0:T(8,128)(2,1)S(1)}, bf16[128,3584]{1,0:T(8,128)(2,1)}, u32[]{:S(2)}) copy-start(bf16[128,3584]{1,0:T(8,128)(2,1)} %param.8) | copy-start | bytes 2752516
where the time goes:
time: 652 us; the launch traced here: 650 us
  waiting for transfers between devices  464 us (71%)
  local copies, waits for them, and re-layouts  93.2 us (14%)
  matrix products  51.7 us (8%)
  starting transfers between devices  20.9 us (3%)
  other arithmetic  20.8 us (3%)
    all_to_all x1, waiting for transfers between devices, on_device(): lax.all_to_all(contrib.reshape(experts, capacity, model_width), ('node',...  162 us
    all_to_all x1, waiting for transfers between devices, on_device(): lax.all_to_all(send_dy, ('node', 'local'), split_axis=0, concat_axis=0, t...  156 us
    all_to_all x1, waiting for transfers between devices, on_device(): lax.all_to_all(send_x, ('node', 'local'), split_axis=0, concat_axis=0, ti...  146 us
    gather x4, local copies, waits for them, and re-layouts, pair_sums(): ordered = jnp.take_along_axis(contribs, slot_order[:, :, None], axis=1)  46.9 us
    dot_general x1, matrix products, expert_backward(): lax.dot_general(grad_pre, weight_in, (((1,), (1,)), ((), ())), preferred_...  21.8 us
    gather x1, local copies, waits for them, and re-layouts, on_device(): returned.reshape(row_count, model_width)[position]  17.8 us
    dot_general x1, matrix products, expert_backward(): jnp.dot(rows_x, weight_in[:, FF:], preferred_element_type=jnp.float32)  15.2 us
    dot_general x1, matrix products, expert_backward(): lax.dot_general(rows_dy, weight_out, (((1,), (1,)), ((), ())), preferred_...  14.7 us
  transfers between devices with their start and end apart: 4, of which 3 were waited for; matrix products, arithmetic and copies ran while one was open for 5% of the time, Pallas kernels for 0%

commit v1 on v0

v1 whole, which is shorter than its diff:
```python
import jax
import jax.numpy as jnp
from jax import lax
from jax.sharding import PartitionSpec as P

FF = 1024
TOK_DEV = 128
TOPK = 8


def slot_ranks(flat_ids, columns):
    onehot = (flat_ids[..., None] == jnp.arange(columns, dtype=jnp.int32)).astype(jnp.int32)
    counts = jnp.cumsum(onehot, axis=-2)
    return jnp.sum(counts * onehot, axis=-1) - 1


def expert_backward(rows_x, rows_dy, rows_gate, saved, weight_in, weight_out):
    up_pre = jnp.dot(rows_x, weight_in[:, FF:], preferred_element_type=jnp.float32)
    grad_hidden = lax.dot_general(
        rows_dy, weight_out, (((1,), (1,)), ((), ())), preferred_element_type=jnp.float32
    )
    grad_hidden = grad_hidden * rows_gate.astype(jnp.float32)[:, None]
    gate_pre = saved.astype(jnp.float32)
    sigmoid_gate = jax.nn.sigmoid(gate_pre)
    grad_gate = grad_hidden * up_pre * sigmoid_gate * (1.0 + gate_pre * (1.0 - sigmoid_gate))
    grad_up = grad_hidden * gate_pre * sigmoid_gate
    grad_pre = jnp.concatenate([grad_gate, grad_up], axis=1).astype(jnp.bfloat16)
    contrib = lax.dot_general(
        grad_pre, weight_in, (((1,), (1,)), ((), ())), preferred_element_type=jnp.float32
    )
    return contrib.astype(jnp.bfloat16)


def on_device(hidden_in, out_grad, expert_ids, gate_int, gate_saved, w_in, w_out):
    n_node = lax.axis_size("node")
    n_local = lax.axis_size("local")
    experts = n_node * n_local
    tok = hidden_in.shape[0]
    capacity = tok * TOPK // experts
    per_dest = n_node * capacity
    row_count = n_local * per_dest
    model_width = hidden_in.shape[1]
    node_here = lax.axis_index("node")

    gathered_x = lax.all_gather(hidden_in, "node", tiled=True)
    gathered_dy = lax.all_gather(out_grad, "node", tiled=True)

    ids = expert_ids.reshape(n_node, tok * TOPK)
    ranks = slot_ranks(ids, experts)
    on_here = (ids // n_local) == node_here
    node_range = jnp.arange(n_node, dtype=jnp.int32)[:, None]
    position = (ids % n_local) * per_dest + node_range * capacity + ranks
    position = jnp.where(on_here, position, row_count)
    flat_slot = jnp.arange(n_node * tok * TOPK, dtype=jnp.int32)
    slot_of_row = (
        jnp.zeros((row_count,), jnp.int32).at[position.reshape(-1)].set(flat_slot, mode="drop")
    )
    token_row = slot_of_row // TOPK
    send_x = gathered_x[token_row]
    send_dy = gathered_dy[token_row]
    weight = (gate_int.reshape(-1).astype(jnp.float32) / 1024.0).astype(jnp.bfloat16)
    send_gate = weight[slot_of_row]

    recv_x = lax.all_to_all(
        send_x.reshape(n_local, per_dest, model_width), "local", 0, 0, tiled=True
    )
    recv_dy = lax.all_to_all(
        send_dy.reshape(n_local, per_dest, model_width), "local", 0, 0, tiled=True
    )
    recv_gate = lax.all_to_all(send_gate.reshape(n_local, per_dest), "local", 0, 0, tiled=True)

    saved = (
        gate_saved.reshape(n_node, n_local, capacity, FF)
        .transpose(1, 0, 2, 3)
        .reshape(row_count, FF)
    )
    contrib = expert_backward(
        recv_x.reshape(row_count, model_width),
        recv_dy.reshape(row_count, model_width),
        recv_gate.reshape(row_count),
        saved,
        w_in[0],
        w_out[0],
    )
    returned = lax.all_to_all(
        contrib.reshape(n_local, per_dest, model_width), "local", 0, 0, tiled=True
    ).reshape(row_count, model_width)

    token_pos = position.reshape(n_node * tok, TOPK)
    first = jnp.min(token_pos, axis=1)
    second = jnp.max(jnp.where(token_pos < row_count, token_pos, -1), axis=1)
    has_pair = first < row_count
    first = jnp.where(has_pair, first, 0)
    second = jnp.where(has_pair, second, 0)
    pair = returned[first].astype(jnp.float32) + returned[second].astype(jnp.float32)
    node_sum = jnp.where(has_pair[:, None], pair, 0.0).astype(jnp.bfloat16)

    back = lax.all_to_all(
        node_sum.reshape(n_node, tok, model_width), "node", 0, 0, tiled=True
    )
    return jnp.sum(back.astype(jnp.float32), axis=0).astype(jnp.bfloat16)


def solution(mesh):
    in_specs = (
        P(("node", "local"), None),
        P(("node", "local"), None),
        P(None, "local", None),
        P(None, "local", None),
        P(("node", "local"), None),
        P(("node", "local"), None, None),
        P(("node", "local"), None, None),
    )
    out_specs = P(("node", "local"), None)
    return jax.shard_map(
        on_device, mesh=mesh, in_specs=in_specs, out_specs=out_specs, check_vma=False
    )
```

time: 652 us -> 539 us (0.83)
  waiting for transfers between devices: 464 us -> 225 us
  blocking collectives: 0 us -> 82.7 us
  other arithmetic: 20.8 us -> 47.3 us
  between operations: 0.2 us -> 14.1 us
    all_to_all x4, waiting for transfers between devices: 464 us -> 142 us  [the longest x1 82.2 us: on_device(): lax.all_to_all(contrib.reshape(n_local, per_dest, model_width), 'local',...]
    all_to_all x0 -> x1, blocking collectives: none -> 82.7 us  [on_device(): lax.all_to_all(node_sum.reshape(n_node, tok, model_width), 'node', 0, 0,...]
    all_gather x0 -> x2, waiting for transfers between devices: none -> 81.5 us  [the longest x1 72.9 us: on_device(): gathered_x = lax.all_gather(hidden_in, 'node', tiled=True)]
    another operation x3, other arithmetic: 9.15 us -> 36.2 us
    gather x8 -> x5, local copies, waits for them, and re-layouts: 83.8 us -> 63.2 us  [the longest x1 16.3 us: on_device(): send_dy = gathered_dy[token_row]]
    scatter x1, local copies, waits for them, and re-layouts: 4.31 us -> 15.5 us  [on_device(): jnp.zeros((row_count,), jnp.int32).at[position.reshape(-1)]]
    select_n x3 -> x2, other arithmetic: 8.69 us -> 0.16 us  [the longest x1 0.15 us: on_device(): jnp.zeros((row_count,), jnp.int32).at[position.reshape(-1)]]
    convert_element_type x2 -> x4, local copies, waits for them, and re-layouts: 0.76 us -> 8.15 us  [the longest x2 7.82 us: expert_backward(): gate_pre = saved.astype(jnp.float32)]
  transfers between devices with their start and end apart: 4 -> 6, of which waited for: 3 -> 4; matrix products, arithmetic and copies ran while one was open for 5% -> 22% of each run, Pallas kernels for 0% -> 0%
where the time goes in v1:
time: 539 us; the launch traced here: 531 us
  waiting for transfers between devices  225 us (42%)
  local copies, waits for them, and re-layouts  89.7 us (17%)
  blocking collectives  82.7 us (15%)
  matrix products  52 us (10%)
  other arithmetic  47.3 us (9%)
  starting transfers between devices  20.3 us (4%)
  between operations  14.1 us (3%)
    all_to_all x1, blocking collectives, on_device(): lax.all_to_all(node_sum.reshape(n_node, tok, model_width), 'node', 0, 0,...  82.7 us
    all_to_all x1, waiting for transfers between devices, on_device(): lax.all_to_all(contrib.reshape(n_local, per_dest, model_width), 'local',...  82.2 us
    all_gather x1, waiting for transfers between devices, on_device(): gathered_x = lax.all_gather(hidden_in, 'node', tiled=True)  72.9 us
    all_to_all x1, waiting for transfers between devices, on_device(): lax.all_to_all(send_x.reshape(n_local, per_dest, model_width), 'local', 0...  60 us
    another operation x3, other arithmetic  36.2 us
    dot_general x1, matrix products, expert_backward(): lax.dot_general(grad_pre, weight_in, (((1,), (1,)), ((), ())), preferred_...  21.4 us
    gather x1, local copies, waits for them, and re-layouts, on_device(): send_dy = gathered_dy[token_row]  16.3 us
    gather x1, local copies, waits for them, and re-layouts, on_device(): send_x = gathered_x[token_row]  16.3 us
  transfers between devices with their start and end apart: 6, of which 4 were waited for; matrix products, arithmetic and copies ran while one was open for 22% of the time, Pallas kernels for 0%

profile of v1, /device:TPU:0, one launch (start us, length us, event | category | flops | bytes accessed | tf_op | source)
XLA Modules:
  0.0 531.3 jit_solution(3235618719405851506)
XLA Ops:
  6.5 0.0 all-gather.3.cloned.1.call-start
  6.5 0.7 all-gather.3.cloned.1.call-update
  7.3 0.8 copy.36
  8.1 0.2 eq.50
  8.3 0.2 reshape.293
  8.4 0.1 eq.54
  8.6 0.1 broadcast_bitcast_fusion
  8.7 0.7 multiply_convert_fusion.2
  9.4 0.2 copy.45
  9.6 0.2 convert_element_type.60
  9.8 36.0 %reduce-window.6 = s32[4,32,8,128]{3,2,1,0:T(8,128)S(1)} reduce-window(s32[4,32,8,128]{3,2,1,0:T(8,128)S(1)} %fusion.10, s32[]{:T(128)} %constant.64.clone.1), window={size=1x1x1x128 pad=0_0x0_0x0_0x127_0}, to_apply=%region_0.0 | reduce-window | flops 16646144 | bytes 1048580 | tf_op jit(solution)/shard_map/reduce-window
  45.8 0.2 slice.22
  46.0 0.3 copy.42
  46.3 0.1 copy.43
  46.4 0.2 broadcast_add_fusion
  46.6 0.1 reduce_window_sum.16
  46.7 0.1 fusion.9
  46.9 0.2 compare_select_fusion.1
  47.0 15.5 %scatter_custom_fusion = s32[1024]{0:T(1024)S(1)} fusion(s32[4096]{0:T(1024)S(1)} %bitcast.57, s32[4096]{0:T(1024)S(1)} %iota.16, s32[]{:T(128)} %constant.64.clone.1), kind=kCustom, calls=%fused_computation.71 | custom fusion | bytes 4100 | tf_op jit(solution)/shard_map/scatter | solution.py:56
  62.6 6.8 %gather_fusion.1 = bf16[1024]{0:T(1024)(128)(2,1)S(1)} fusion(bf16[4096]{0:T(1024)(128)(2,1)S(1)} %convert_element_type.60, s32[1024]{0:T(1024)S(1)} %get-tuple-element.9), kind=kCustom, calls=%fused_computation.1 | custom fusion | bytes 8192 | tf_op jit(solution)/shard_map/gather | solution.py:62
  69.4 0.6 copy.46
  70.0 5.2 all-to-all-start.1
  75.1 8.6 %all-gather.3.cloned.1.call-done = bf16[512,3584]{1,0:T(8,128)(2,1)} async-done(((bf16[128,3584]{1,0:T(8,128)(2,1)}), bf16[512,3584]{1,0:T(8,128)(2,1)}) %all-gather.3.cloned.1.call-update) | async-done | bytes 3670032 | tf_op jit(solution)/shard_map/all_gather | solution.py:46
  83.8 16.3 %gather_fusion = bf16[1024,3584]{1,0:T(8,128)(2,1)} fusion(bf16[512,3584]{1,0:T(8,128)(2,1)} %all-gather.3.cloned.1.call-done, s32[1024]{0:T(1024)S(1)} %get-tuple-element.10), kind=kCustom, calls=%fused_computation | custom fusion | bytes 14684160 | tf_op jit(solution)/shard_map/gather | solution.py:60
  100.1 0.0 all-to-all-done.1
  100.1 4.8 all-to-all-start
  104.9 0.0 all-gather.5.cloned.1.call-start
  105.0 0.7 all-gather.5.cloned.1.call-update
  105.7 72.9 %all-gather.5.cloned.1.call-done = bf16[512,3584]{1,0:T(8,128)(2,1)} async-done(((bf16[128,3584]{1,0:T(8,128)(2,1)}), bf16[512,3584]{1,0:T(8,128)(2,1)}) %all-gather.5.cloned.1.call-update) | async-done | bytes 3670032 | tf_op jit(solution)/shard_map/all_gather | solution.py:45
  178.6 16.3 %gather_fusion.2 = bf16[1024,3584]{1,0:T(8,128)(2,1)} fusion(bf16[512,3584]{1,0:T(8,128)(2,1)} %all-gather.5.cloned.1.call-done, s32[1024]{0:T(1024)S(1)} %get-tuple-element.10), kind=kCustom, calls=%fused_computation.2 | custom fusion | bytes 14684160 | tf_op jit(solution)/shard_map/gather | solution.py:59
  194.8 0.0 all-to-all-done
  194.8 0.0 copy-start
  194.8 5.1 all-to-all-start.2
  200.0 0.0 copy-done
  200.0 0.5 convert_bitcast_fusion
  200.5 2.4 copy.47
  202.9 5.4 %copy.48 = f32[1024,1024]{0,1:T(8,128)} copy(f32[1024,1024]{1,0:T(8,128)} %bitcast.49) | data formatting | bytes 8388608 | tf_op jit(solution)/shard_map/convert_element_type | solution.py:23
  208.3 14.5 %multiply_convert_fusion = (bf16[1024,1024]{0,1:T(8,128)(2,1)S(1)}, f32[1024,1024]{0,1:T(8,128)}) fusion(f32[1024,1024]{0,1:T(8,128)} %copy.48, f32[1024]{0:T(1024)S(1)} %bitcast.62, bf16[1024,3584]{1,0:T(8,128)(2,1)} %bitcast.4, bf16[1,1024,3584]{2,1,0:T(8,128)(2,1)} %param.13), kind=kOutput, calls=%fused_computation.17 | convolution fusion | flops 7523532800 | bytes 25169920 | tf_op jit(solution)/shard_map/dot_general | solution.py:19
  222.8 60.0 %all-to-all-done.2 = bf16[8,128,3584]{2,1,0:T(8,128)(2,1)} async-done(((bf16[8,128,3584]{2,1,0:T(8,128)(2,1)}), bf16[8,128,3584]{2,1,0:T(8,128)(2,1)}, u32[]{:S(2)}, u32[]{:S(2)}) %all-to-all-start.2) | async-done | bytes 7340064 | tf_op jit(solution)/shard_map/all_to_all | solution.py:64
  282.8 16.0 %multiply_convert_fusion.1 = bf16[1024,1024]{0,1:T(8,128)(2,1)} fusion(f32[1024,1024]{0,1:T(8,128)} %copy.48, f32[1024,1024]{0,1:T(8,128)} %get-tuple-element.14, bf16[1024,3584]{1,0:T(8,128)(2,1)} %bitcast.9, bf16[3584,2048]{1,0:T(8,128)(2,1)} %bitcast.64, f32[1024]{0:T(1024)S(1)} %bitcast.63), kind=kOutput, calls=%fused_computation.18 | convolution fusion | flops 7527727104 | bytes 25169920 | tf_op jit(solution)/shard_map/dot_general | solution.py:18
  298.8 21.4 %convolution_convert_fusion = bf16[1024,3584]{1,0:T(8,128)(2,1)} fusion(bf16[1024,1024]{0,1:T(8,128)(2,1)S(1)} %get-tuple-element.13, bf16[1024,1024]{0,1:T(8,128)(2,1)} %multiply_convert_fusion.1, bf16[1,3584,2048]{2,1,0:T(8,128)(2,1)} %param.12), kind=kOutput, calls=%fused_computation.6 | convolution fusion | flops 15044444160 | bytes 26214400 | tf_op jit(solution)/shard_map/dot_general | solution.py:28
  320.3 5.1 all-to-all-start.3
  325.4 0.2 sub.27
  325.6 0.4 fusion.31
  326.1 82.2 %all-to-all-done.3 = bf16[8,128,3584]{2,1,0:T(8,128)(2,1)} async-done(((bf16[8,128,3584]{2,1,0:T(8,128)(2,1)}), bf16[8,128,3584]{2,1,0:T(8,128)(2,1)}, u32[]{:S(2)}, u32[]{:S(2)}) %all-to-all-start.3) | async-done | bytes 7340064 | tf_op jit(solution)/shard_map/all_to_all | solution.py:85
  408.2 11.9 %gather_fusion.4 = bf16[512,3584]{1,0:T(8,128)(2,1)} fusion(bf16[1024,3584]{1,0:T(8,128)(2,1)} %bitcast.15, s32[1024]{0:T(1024)S(1)} %pad_clamp_fusion), kind=kCustom, calls=%fused_computation.4 | custom fusion | bytes 7342080 | tf_op jit(solution)/shard_map/gather | solution.py:95
  420.2 11.9 %gather_fusion.3 = bf16[512,3584]{1,0:T(8,128)(2,1)} fusion(bf16[1024,3584]{1,0:T(8,128)(2,1)} %bitcast.15, s32[1024]{0:T(1024)S(1)} %pad_clamp_fusion.1), kind=kCustom, calls=%fused_computation.3 | custom fusion | bytes 7342080 | tf_op jit(solution)/shard_map/gather | solution.py:95
  432.1 4.0 convert_add_fusion
  436.2 1.3 select_convert_fusion
  437.5 82.7 %all_to_all.29 = bf16[4,128,3584]{2,1,0:T(8,128)(2,1)} all-to-all(bf16[4,128,3584]{2,1,0:T(8,128)(2,1)S(1)} %select_convert_fusion), channel_id=1, replica_groups=mesh['node'=4,'local'=8] {'node'}, dimensions={0} | all-to-all | bytes 7340032 | tf_op jit(solution)/shard_map/all_to_all | solution.py:98
  520.2 3.8 reduce_sum.22
  (14 shorter events, 0.2 us)
Async XLA Ops:
  6.5 77.2 %all-gather.3.cloned.1.call-start = ((), (), s32[]{:S(2)}) async-start(), calls=%async_computation.5 | async-start | bytes 4587520 | tf_op jit(solution)/shard_map/all_gather | solution.py:46
  70.0 30.1 %all-to-all-start.1 = ((bf16[8,1,128]{2,1,0:T(2,128)(2,1)}), bf16[8,1,128]{2,1,0:T(2,128)(2,1)S(1)}, u32[]{:S(2)}, u32[]{:S(2)}) async-start(bf16[8,1,128]{2,1,0:T(2,128)(2,1)} %copy.46), calls=%async_computation.1 | async-start | bytes 8192 | tf_op jit(solution)/shard_map/all_to_all | solution.py:70
  100.1 94.8 %all-to-all-start = ((bf16[8,128,3584]{2,1,0:T(8,128)(2,1)}), bf16[8,128,3584]{2,1,0:T(8,128)(2,1)}, u32[]{:S(2)}, u32[]{:S(2)}) async-start(bf16[8,128,3584]{2,1,0:T(8,128)(2,1)} %bitcast.47), calls=%async_computation | async-start | bytes 14680064 | tf_op jit(solution)/shard_map/all_to_all | solution.py:67
  104.9 73.6 %all-gather.5.cloned.1.call-start = ((), (), s32[]{:S(2)}) async-start(), calls=%async_computation.6 | async-start | bytes 4587520 | tf_op jit(solution)/shard_map/all_gather | solution.py:45
  194.8 5.2 copy-start
  194.8 88.0 %all-to-all-start.2 = ((bf16[8,128,3584]{2,1,0:T(8,128)(2,1)}), bf16[8,128,3584]{2,1,0:T(8,128)(2,1)}, u32[]{:S(2)}, u32[]{:S(2)}) async-start(bf16[8,128,3584]{2,1,0:T(8,128)(2,1)} %bitcast.48), calls=%async_computation.2 | async-start | bytes 14680064 | tf_op jit(solution)/shard_map/all_to_all | solution.py:64
  320.3 87.9 %all-to-all-start.3 = ((bf16[8,128,3584]{2,1,0:T(8,128)(2,1)}), bf16[8,128,3584]{2,1,0:T(8,128)(2,1)}, u32[]{:S(2)}, u32[]{:S(2)}) async-start(bf16[8,128,3584]{2,1,0:T(8,128)(2,1)} %bitcast.51), calls=%async_computation.3 | async-start | bytes 14680064 | tf_op jit(solution)/shard_map/all_to_all | solution.py:85
Sparse Core Ops, SparseCore 0:
  8.9 74.8 all-gather.2
  107.3 71.1 all-gather.4

commit v2 on v1

--- a/solution.py
+++ b/solution.py
@@ -8,10 +8,35 @@
 TOPK = 8
 
 
-def slot_ranks(flat_ids, columns):
-    onehot = (flat_ids[..., None] == jnp.arange(columns, dtype=jnp.int32)).astype(jnp.int32)
-    counts = jnp.cumsum(onehot, axis=-2)
-    return jnp.sum(counts * onehot, axis=-1) - 1
+def slot_ranks(ids, columns):
+    slots = ids.shape[-1]
+    onehot = (ids[..., None] == jnp.arange(columns, dtype=jnp.int32)).astype(jnp.bfloat16)
+    order = jnp.arange(slots, dtype=jnp.int32)
+    earlier = (order[:, None] > order[None, :]).astype(jnp.bfloat16)
+    before = jnp.einsum("st,nte->nse", earlier, onehot, preferred_element_type=jnp.float32)
+    return jnp.sum(before * onehot.astype(jnp.float32), axis=-1).astype(jnp.int32)
+
+
+def line_gather(block, n_node, node_here):
+    gathered = jnp.zeros((n_node,) + block.shape, block.dtype)
+    gathered = lax.dynamic_update_slice_in_dim(gathered, block[None], node_here, 0)
+    from_low = block
+    from_high = block
+    for hop in range(1, n_node):
+        up = [(i, i + 1) for i in range(hop - 1, n_node - 1)]
+        down = [(i, i - 1) for i in range(1, n_node - hop + 1)]
+        from_low = lax.ppermute(from_low, "node", up)
+        from_high = lax.ppermute(from_high, "node", down)
+        for held, source, valid in (
+            (from_low, node_here - hop, node_here >= hop),
+            (from_high, node_here + hop, node_here + hop < n_node),
+        ):
+            index = jnp.clip(source, 0, n_node - 1)
+            current = lax.dynamic_index_in_dim(gathered, index, 0, keepdims=True)
+            gathered = lax.dynamic_update_slice_in_dim(
+                gathered, jnp.where(valid, held[None], current), index, 0
+            )
+    return gathered.reshape((n_node * block.shape[0],) + block.shape[1:])
 
 
 def expert_backward(rows_x, rows_dy, rows_gate, saved, weight_in, weight_out):
@@ -31,6 +56,13 @@
     return contrib.astype(jnp.bfloat16)
 
 
+def select_rows(onehot, rows):
+    picked = lax.dot_general(
+        onehot, rows, (((0,), (0,)), ((), ())), preferred_element_type=jnp.float32
+    )
+    return picked.astype(jnp.bfloat16)
+
+
 def on_device(hidden_in, out_grad, expert_ids, gate_int, gate_saved, w_in, w_out):
     n_node = lax.axis_size("node")
     n_local = lax.axis_size("local")
@@ -42,8 +74,8 @@
     model_width = hidden_in.shape[1]
     node_here = lax.axis_index("node")
 
-    gathered_x = lax.all_gather(hidden_in, "node", tiled=True)
-    gathered_dy = lax.all_gather(out_grad, "node", tiled=True)
+    gathered_x = line_gather(hidden_in, n_node, node_here)
+    gathered_dy = line_gather(out_grad, n_node, node_here)
 
     ids = expert_ids.reshape(n_node, tok * TOPK)
     ranks = slot_ranks(ids, experts)
@@ -51,19 +83,23 @@
     node_range = jnp.arange(n_node, dtype=jnp.int32)[:, None]
     position = (ids % n_local) * per_dest + node_range * capacity + ranks
     position = jnp.where(on_here, position, row_count)
-    flat_slot = jnp.arange(n_node * tok * TOPK, dtype=jnp.int32)
-    slot_of_row = (
-        jnp.zeros((row_count,), jnp.int32).at[position.reshape(-1)].set(flat_slot, mode="drop")
+    slot_hits = (
+        position.reshape(n_node * tok, TOPK)[:, :, None]
+        == jnp.arange(row_count, dtype=jnp.int32)[None, None, :]
+    ).astype(jnp.bfloat16)
+    dispatch = jnp.sum(slot_hits, axis=1)
+    weight = (gate_int.reshape(n_node * tok, TOPK).astype(jnp.float32) / 1024.0).astype(
+        jnp.bfloat16
     )
-    token_row = slot_of_row // TOPK
-    send_x = gathered_x[token_row]
-    send_dy = gathered_dy[token_row]
-    weight = (gate_int.reshape(-1).astype(jnp.float32) / 1024.0).astype(jnp.bfloat16)
-    send_gate = weight[slot_of_row]
+    send_gate = jnp.einsum(
+        "tk,tkr->r", weight, slot_hits, preferred_element_type=jnp.float32
+    ).astype(jnp.bfloat16)
 
+    send_x = select_rows(dispatch, gathered_x)
     recv_x = lax.all_to_all(
         send_x.reshape(n_local, per_dest, model_width), "local", 0, 0, tiled=True
     )
+    send_dy = select_rows(dispatch, gathered_dy)
     recv_dy = lax.all_to_all(
         send_dy.reshape(n_local, per_dest, model_width), "local", 0, 0, tiled=True
     )
@@ -86,14 +122,9 @@
         contrib.reshape(n_local, per_dest, model_width), "local", 0, 0, tiled=True
     ).reshape(row_count, model_width)
 
-    token_pos = position.reshape(n_node * tok, TOPK)
-    first = jnp.min(token_pos, axis=1)
-    second = jnp.max(jnp.where(token_pos < row_count, token_pos, -1), axis=1)
-    has_pair = first < row_count
-    first = jnp.where(has_pair, first, 0)
-    second = jnp.where(has_pair, second, 0)
-    pair = returned[first].astype(jnp.float32) + returned[second].astype(jnp.float32)
-    node_sum = jnp.where(has_pair[:, None], pair, 0.0).astype(jnp.bfloat16)
+    node_sum = jnp.dot(dispatch, returned, preferred_element_type=jnp.float32).astype(
+        jnp.bfloat16
+    )
 
     back = lax.all_to_all(
         node_sum.reshape(n_node, tok, model_width), "node", 0, 0, tiled=True

time: 539 us -> 531 us (0.985); the launches traced: 531 us -> 530 us
  blocking collectives: 82.7 us -> 176 us
  local copies, waits for them, and re-layouts: 89.7 us -> 13.2 us
  other arithmetic: 47.3 us -> 19.4 us
  matrix products: 52 us -> 76.1 us
  waiting for transfers between devices: 225 us -> 208 us
  starting transfers between devices: 20.3 us -> 37 us
  between operations: 14.1 us -> 0.36 us
    all_to_all x0 -> x1, blocking collectives: none -> 86.5 us  [on_device(): lax.all_to_all(contrib.reshape(n_local, per_dest, model_width), 'local',...]
    all_to_all x1 -> x0, waiting for transfers between devices: 82.2 us -> none  [on_device(): lax.all_to_all(contrib.reshape(n_local, per_dest, model_width), 'local',...]
    all_gather x2 -> x0, waiting for transfers between devices: 81.5 us -> none  [the longest x1 72.9 us: on_device(): gathered_x = lax.all_gather(hidden_in, 'node', tiled=True)]
    all_to_all x1, waiting for transfers between devices: 0.01 us -> 74.7 us  [on_device(): lax.all_to_all(send_dy.reshape(n_local, per_dest, model_width), 'local',...]
    ppermute x0 -> x12, waiting for transfers between devices: none -> 73.7 us  [the longest x6 73.6 us: line_gather(): from_high = lax.ppermute(from_high, 'node', down)]
    gather x5 -> x0, local copies, waits for them, and re-layouts: 63.2 us -> none  [the longest x1 16.3 us: on_device(): send_dy = gathered_dy[token_row]]
    another operation x3 -> x0, other arithmetic: 36.2 us -> none
    dot_general x0 -> x5, matrix products: none -> 23.4 us  [the longest x2 14.3 us: select_rows(): lax.dot_general(onehot, rows, (((0,), (0,)), ((), ())), preferred_element...]
  transfers between devices with their start and end apart: 6 -> 15, of which waited for: 4 -> 7; matrix products, arithmetic and copies ran while one was open for 22% -> 11% of each run, Pallas kernels for 0% -> 0%
where the time goes in v2:
time: 531 us; the launch traced here: 530 us
  waiting for transfers between devices  208 us (39%)
  blocking collectives  176 us (33%)
  matrix products  76.1 us (14%)
  starting transfers between devices  37 us (7%)
  other arithmetic  19.4 us (4%)
  local copies, waits for them, and re-layouts  13.2 us (2%)
    all_to_all x1, blocking collectives, on_device(): lax.all_to_all(node_sum.reshape(n_node, tok, model_width), 'node', 0, 0,...  89.7 us
    all_to_all x1, blocking collectives, on_device(): lax.all_to_all(contrib.reshape(n_local, per_dest, model_width), 'local',...  86.5 us
    all_to_all x1, waiting for transfers between devices, on_device(): lax.all_to_all(send_dy.reshape(n_local, per_dest, model_width), 'local',...  74.7 us
    ppermute x6, waiting for transfers between devices, line_gather(): from_high = lax.ppermute(from_high, 'node', down)  73.6 us
    all_to_all x1, waiting for transfers between devices, on_device(): lax.all_to_all(send_x.reshape(n_local, per_dest, model_width), 'local', 0...  59.4 us
    dot_general x1, matrix products, expert_backward(): lax.dot_general(grad_pre, weight_in, (((1,), (1,)), ((), ())), preferred_...  21.8 us
    dot_general x1, matrix products, expert_backward(): jnp.dot(rows_x, weight_in[:, FF:], preferred_element_type=jnp.float32)  16 us
    ppermute x6, starting transfers between devices, line_gather(): from_low = lax.ppermute(from_low, 'node', up)  15 us
  transfers between devices with their start and end apart: 15, of which 7 were waited for; matrix products, arithmetic and copies ran while one was open for 11% of the time, Pallas kernels for 0%

profile of v2, /device:TPU:0, one launch (start us, length us, event | category | flops | bytes accessed | tf_op | source)
XLA Modules:
  0.0 530.0 jit_solution(14693322215926438752)
XLA Ops:
  0.0 1.3 collective-permute-start.7
  1.3 6.5 %collective-permute-start.6 = (bf16[128,3584]{1,0:T(8,128)(2,1)}, bf16[128,3584]{1,0:T(8,128)(2,1)}, u32[]{:S(2)}, u32[]{:S(2)}) collective-permute-start(bf16[128,3584]{1,0:T(8,128)(2,1)} %param.7), channel_id=1, source_target_pairs={{0,8},{8,16},{16,24},{1,9},{9,17},{17,25},{2,10},{10,18},{18,26},{... | collective-permute-start | bytes 2752520 | tf_op jit(solution)/shard_map/ppermute | solution.py:28
  7.8 1.3 collective-permute-start.1
  9.1 5.5 %collective-permute-start = (bf16[128,3584]{1,0:T(8,128)(2,1)}, bf16[128,3584]{1,0:T(8,128)(2,1)}, u32[]{:S(2)}, u32[]{:S(2)}) collective-permute-start(bf16[128,3584]{1,0:T(8,128)(2,1)} %param.8), channel_id=1, source_target_pairs={{0,8},{8,16},{16,24},{1,9},{9,17},{17,25},{2,10},{10,18},{18,26},{... | collective-permute-start | bytes 2752520 | tf_op jit(solution)/shard_map/ppermute | solution.py:28
  14.6 0.1 broadcast_bitcast_fusion
  14.6 0.7 fusion.47
  15.4 0.2 copy.38
  15.5 0.8 copy.30
  16.4 0.2 eq.42
  16.5 0.6 fusion.22
  17.2 0.2 convert_element_type.75
  17.4 0.1 copy.31
  17.5 0.8 fusion.43
  18.2 0.1 copy.32
  18.4 4.3 fusion
  22.6 0.6 copy.33
  23.3 4.2 all-to-all-start.1
  27.4 5.4 %fusion.2 = bf16[512,1024]{1,0:T(8,128)(2,1)S(1)} fusion(s32[512,8]{1,0:T(8,128)S(1)} %copy.32), kind=kLoop, calls=%fused_computation.3 | loop fusion | flops 12058624 | bytes 1064960 | tf_op jit(solution)/shard_map/reduce_sum | solution.py:90
  32.8 0.3 broadcast.98.clone
  33.1 0.1 bitcast_dynamic-update-slice_fusion
  33.2 0.3 broadcast.98.clone.1
  33.5 0.5 copy-done.3
  34.0 0.1 bitcast_dynamic-update-slice_fusion.1
  34.1 1.3 collective-permute-start.9
  35.4 0.7 collective-permute-start.8
  36.1 9.9 %collective-permute-done.1 = bf16[128,3584]{1,0:T(8,128)(2,1)} collective-permute-done((bf16[128,3584]{1,0:T(8,128)(2,1)}, bf16[128,3584]{1,0:T(8,128)(2,1)}, u32[]{:S(2)}, u32[]{:S(2)}) %collective-permute-start.1) | collective-permute-done | bytes 917536 | tf_op jit(solution)/shard_map/ppermute | solution.py:29
  46.1 1.3 collective-permute-start.3
  47.4 0.7 collective-permute-start.2
  48.1 1.5 fusion.30
  49.6 1.5 fusion.36
  51.0 1.5 fusion.29
  52.5 1.5 fusion.35
  53.9 11.7 %collective-permute-done.9 = bf16[128,3584]{1,0:T(8,128)(2,1)S(1)} collective-permute-done((bf16[128,3584]{1,0:T(8,128)(2,1)}, bf16[128,3584]{1,0:T(8,128)(2,1)S(1)}, u32[]{:S(2)}, u32[]{:S(2)}) %collective-permute-start.9) | collective-permute-done | bytes 917536 | tf_op jit(solution)/shard_map/ppermute | solution.py:29
  65.6 1.3 collective-permute-start.11
  66.9 0.7 collective-permute-start.10
  67.7 17.6 %collective-permute-done.3 = bf16[128,3584]{1,0:T(8,128)(2,1)S(1)} collective-permute-done((bf16[128,3584]{1,0:T(8,128)(2,1)}, bf16[128,3584]{1,0:T(8,128)(2,1)S(1)}, u32[]{:S(2)}, u32[]{:S(2)}) %collective-permute-start.3) | collective-permute-done | bytes 917536 | tf_op jit(solution)/shard_map/ppermute | solution.py:29
  85.3 1.3 collective-permute-start.5
  86.6 0.9 collective-permute-start.4
  87.5 0.3 fusion.28
  87.8 0.3 fusion.34
  88.1 0.3 fusion.27
  88.4 0.3 fusion.33
  88.8 0.3 fusion.26
  89.1 0.3 fusion.32
  89.4 15.6 %collective-permute-done.11 = bf16[128,3584]{1,0:T(8,128)(2,1)S(1)} collective-permute-done((bf16[128,3584]{1,0:T(8,128)(2,1)S(1)}, bf16[128,3584]{1,0:T(8,128)(2,1)S(1)}, u32[]{:S(2)}, u32[]{:S(2)}) %collective-permute-start.11) | collective-permute-done | bytes 917536 | tf_op jit(solution)/shard_map/ppermute | solution.py:29
  105.0 18.8 %collective-permute-done.5 = bf16[128,3584]{1,0:T(8,128)(2,1)S(1)} collective-permute-done((bf16[128,3584]{1,0:T(8,128)(2,1)S(1)}, bf16[128,3584]{1,0:T(8,128)(2,1)S(1)}, u32[]{:S(2)}, u32[]{:S(2)}) %collective-permute-start.5) | collective-permute-done | bytes 917536 | tf_op jit(solution)/shard_map/ppermute | solution.py:29
  123.8 0.6 fusion.25
  124.4 1.9 copy-done
  126.3 6.1 %convolution_convert_fusion.2 = bf16[1024,3584]{1,0:T(8,128)(2,1)} fusion(bf16[512,1024]{1,0:T(8,128)(2,1)S(1)} %fusion.2, bf16[512,3584]{1,0:T(8,128)(2,1)S(1)} %bitcast.126), kind=kOutput, calls=%fused_computation.7 | convolution fusion | flops 3761766400 | bytes 12058624 | tf_op jit(solution)/shard_map/dot_general | solution.py:60
  132.4 4.8 all-to-all-start
  137.3 8.2 %convolution_convert_fusion.1 = bf16[1024,3584]{1,0:T(8,128)(2,1)} fusion(bf16[512,1024]{1,0:T(8,128)(2,1)S(1)} %fusion.2, bf16[512,3584]{1,0:T(8,128)(2,1)} %bitcast.127), kind=kOutput, calls=%fused_computation.6 | convolution fusion | flops 3761766400 | bytes 12058624 | tf_op jit(solution)/shard_map/dot_general | solution.py:60
  145.4 74.7 %all-to-all-done = bf16[8,128,3584]{2,1,0:T(8,128)(2,1)} async-done(((bf16[8,128,3584]{2,1,0:T(8,128)(2,1)}), bf16[8,128,3584]{2,1,0:T(8,128)(2,1)}, u32[]{:S(2)}, u32[]{:S(2)}) %all-to-all-start) | async-done | bytes 7340064 | tf_op jit(solution)/shard_map/all_to_all | solution.py:103
  220.1 5.2 all-to-all-start.2
  225.3 0.5 convert_bitcast_fusion
  225.8 2.4 copy.34
  228.2 5.4 %copy.35 = f32[1024,1024]{0,1:T(8,128)} copy(f32[1024,1024]{1,0:T(8,128)} %bitcast.128) | data formatting | bytes 8388608 | tf_op jit(solution)/shard_map/convert_element_type | solution.py:48
  233.7 14.8 %multiply_convert_fusion = (bf16[1024,1024]{0,1:T(8,128)(2,1)}, f32[1024,1024]{0,1:T(8,128)}) fusion(f32[1024,1024]{0,1:T(8,128)} %copy.35, f32[1024]{0:T(1024)S(1)} %bitcast.136, bf16[1024,3584]{1,0:T(8,128)(2,1)} %bitcast.13, bf16[1,1024,3584]{2,1,0:T(8,128)(2,1)} %param.13), kind=kOutput, calls=%fused_computation.17 | convolution fusion | flops 7523532800 | bytes 25169920 | tf_op jit(solution)/shard_map/dot_general | solution.py:44
  248.5 59.4 %all-to-all-done.2 = bf16[8,128,3584]{2,1,0:T(8,128)(2,1)} async-done(((bf16[8,128,3584]{2,1,0:T(8,128)(2,1)}), bf16[8,128,3584]{2,1,0:T(8,128)(2,1)}, u32[]{:S(2)}, u32[]{:S(2)}) %all-to-all-start.2) | async-done | bytes 7340064 | tf_op jit(solution)/shard_map/all_to_all | solution.py:99
  307.9 16.0 %multiply_convert_fusion.1 = bf16[1024,1024]{0,1:T(8,128)(2,1)} fusion(f32[1024,1024]{0,1:T(8,128)} %copy.35, f32[1024,1024]{0,1:T(8,128)} %get-tuple-element.6, bf16[1024,3584]{1,0:T(8,128)(2,1)} %bitcast.29, bf16[3584,2048]{1,0:T(8,128)(2,1)} %bitcast.138, f32[1024]{0:T(1024)S(1)} %bitcast.137), kind=kOutput, calls=%fused_computation.18 | convolution fusion | flops 7527727104 | bytes 25169920 | tf_op jit(solution)/shard_map/dot_general | solution.py:43
  324.0 21.8 %convolution_convert_fusion = bf16[1024,3584]{1,0:T(8,128)(2,1)} fusion(bf16[1024,1024]{0,1:T(8,128)(2,1)} %get-tuple-element.5, bf16[1024,1024]{0,1:T(8,128)(2,1)} %multiply_convert_fusion.1, bf16[1,3584,2048]{2,1,0:T(8,128)(2,1)} %param.12), kind=kOutput, calls=%fused_computation.5 | convolution fusion | flops 15044444160 | bytes 26214400 | tf_op jit(solution)/shard_map/dot_general | solution.py:53
  345.8 86.5 %all_to_all.29 = bf16[8,128,3584]{2,1,0:T(8,128)(2,1)S(1)} all-to-all(bf16[8,128,3584]{2,1,0:T(8,128)(2,1)} %bitcast.131), channel_id=1, replica_groups=mesh['node'=4,'local'=8] {'local'}, dimensions={0} | all-to-all | bytes 14680064 | tf_op jit(solution)/shard_map/all_to_all | solution.py:121
  432.3 4.2 convolution_convert_fusion.3
  436.5 89.7 %all_to_all.30 = bf16[4,128,3584]{2,1,0:T(8,128)(2,1)} all-to-all(bf16[4,128,3584]{2,1,0:T(8,128)(2,1)S(1)} %bitcast.133), channel_id=1, replica_groups=mesh['node'=4,'local'=8] {'node'}, dimensions={0} | all-to-all | bytes 7340032 | tf_op jit(solution)/shard_map/all_to_all | solution.py:129
  526.2 3.8 reduce_sum.35
  (18 shorter events, 0.1 us)
Async XLA Ops:
  0.0 34.1 %collective-permute-start.7 = (bf16[128,3584]{1,0:T(8,128)(2,1)}, bf16[128,3584]{1,0:T(8,128)(2,1)}, u32[]{:S(2)}, u32[]{:S(2)}) collective-permute-start(bf16[128,3584]{1,0:T(8,128)(2,1)} %param.7), channel_id=1, source_target_pairs={{8,0},{16,8},{24,16},{9,1},{17,9},{25,17},{10,2},{18,10},{26,18},{... | collective-permute-start | bytes 2752520 | tf_op jit(solution)/shard_map/ppermute | solution.py:29
  1.3 34.1 %collective-permute-start.6 = (bf16[128,3584]{1,0:T(8,128)(2,1)}, bf16[128,3584]{1,0:T(8,128)(2,1)}, u32[]{:S(2)}, u32[]{:S(2)}) collective-permute-start(bf16[128,3584]{1,0:T(8,128)(2,1)} %param.7), channel_id=1, source_target_pairs={{0,8},{8,16},{16,24},{1,9},{9,17},{17,25},{2,10},{10,18},{18,26},{... | collective-permute-start | bytes 2752520 | tf_op jit(solution)/shard_map/ppermute | solution.py:28
  7.8 38.3 %collective-permute-start.1 = (bf16[128,3584]{1,0:T(8,128)(2,1)}, bf16[128,3584]{1,0:T(8,128)(2,1)}, u32[]{:S(2)}, u32[]{:S(2)}) collective-permute-start(bf16[128,3584]{1,0:T(8,128)(2,1)} %param.8), channel_id=1, source_target_pairs={{8,0},{16,8},{24,16},{9,1},{17,9},{25,17},{10,2},{18,10},{26,18},{... | collective-permute-start | bytes 2752520 | tf_op jit(solution)/shard_map/ppermute | solution.py:29
  9.1 38.3 %collective-permute-start = (bf16[128,3584]{1,0:T(8,128)(2,1)}, bf16[128,3584]{1,0:T(8,128)(2,1)}, u32[]{:S(2)}, u32[]{:S(2)}) collective-permute-start(bf16[128,3584]{1,0:T(8,128)(2,1)} %param.8), channel_id=1, source_target_pairs={{0,8},{8,16},{16,24},{1,9},{9,17},{17,25},{2,10},{10,18},{18,26},{... | collective-permute-start | bytes 2752520 | tf_op jit(solution)/shard_map/ppermute | solution.py:28
  22.6 10.5 %copy-start.2 = (bf16[128,3584]{1,0:T(8,128)(2,1)S(1)}, bf16[128,3584]{1,0:T(8,128)(2,1)}, u32[]{:S(2)}) copy-start(bf16[128,3584]{1,0:T(8,128)(2,1)} %param.7) | copy-start | bytes 2752516
  23.3 109.2 %all-to-all-start.1 = ((bf16[8,1,128]{2,1,0:T(2,128)(2,1)}), bf16[8,1,128]{2,1,0:T(2,128)(2,1)S(1)}, u32[]{:S(2)}, u32[]{:S(2)}) async-start(bf16[8,1,128]{2,1,0:T(2,128)(2,1)} %copy.33), calls=%async_computation.1 | async-start | bytes 8192 | tf_op jit(solution)/shard_map/all_to_all | solution.py:106
  32.8 1.2 copy-start.3
  34.1 31.5 %collective-permute-start.9 = (bf16[128,3584]{1,0:T(8,128)(2,1)}, bf16[128,3584]{1,0:T(8,128)(2,1)S(1)}, u32[]{:S(2)}, u32[]{:S(2)}) collective-permute-start(bf16[128,3584]{1,0:T(8,128)(2,1)} %collective-permute-done.7), channel_id=1, source_target_pairs={{8,0},{16,8},{9,1},{17,9},{10,2},{18,10},{11,3},{19,11},{12,4},{20... | collective-permute-start | bytes 2752520 | tf_op jit(solution)/shard_map/ppermute | solution.py:29
  35.4 31.5 %collective-permute-start.8 = (bf16[128,3584]{1,0:T(8,128)(2,1)}, bf16[128,3584]{1,0:T(8,128)(2,1)S(1)}, u32[]{:S(2)}, u32[]{:S(2)}) collective-permute-start(bf16[128,3584]{1,0:T(8,128)(2,1)} %collective-permute-done.6), channel_id=1, source_target_pairs={{8,16},{16,24},{9,17},{17,25},{10,18},{18,26},{11,19},{19,27},{12,... | collective-permute-start | bytes 2752520 | tf_op jit(solution)/shard_map/ppermute | solution.py:28
  46.1 39.2 %collective-permute-start.3 = (bf16[128,3584]{1,0:T(8,128)(2,1)}, bf16[128,3584]{1,0:T(8,128)(2,1)S(1)}, u32[]{:S(2)}, u32[]{:S(2)}) collective-permute-start(bf16[128,3584]{1,0:T(8,128)(2,1)} %collective-permute-done.1), channel_id=1, source_target_pairs={{8,0},{16,8},{9,1},{17,9},{10,2},{18,10},{11,3},{19,11},{12,4},{20... | collective-permute-start | bytes 2752520 | tf_op jit(solution)/shard_map/ppermute | solution.py:29
  47.4 39.2 %collective-permute-start.2 = (bf16[128,3584]{1,0:T(8,128)(2,1)}, bf16[128,3584]{1,0:T(8,128)(2,1)S(1)}, u32[]{:S(2)}, u32[]{:S(2)}) collective-permute-start(bf16[128,3584]{1,0:T(8,128)(2,1)} %collective-permute-done), channel_id=1, source_target_pairs={{8,16},{16,24},{9,17},{17,25},{10,18},{18,26},{11,19},{19,27},{12,... | collective-permute-start | bytes 2752520 | tf_op jit(solution)/shard_map/ppermute | solution.py:28
  65.6 39.3 %collective-permute-start.11 = (bf16[128,3584]{1,0:T(8,128)(2,1)S(1)}, bf16[128,3584]{1,0:T(8,128)(2,1)S(1)}, u32[]{:S(2)}, u32[]{:S(2)}) collective-permute-start(bf16[128,3584]{1,0:T(8,128)(2,1)S(1)} %collective-permute-done.9), channel_id=1, source_target_pairs={{8,0},{9,1},{10,2},{11,3},{12,4},{13,5},{14,6},{15,7}} | collective-permute-start | bytes 2752520 | tf_op jit(solution)/shard_map/ppermute | solution.py:29
  66.9 21.8 %collective-permute-start.10 = (bf16[128,3584]{1,0:T(8,128)(2,1)S(1)}, bf16[128,3584]{1,0:T(8,128)(2,1)S(1)}, u32[]{:S(2)}, u32[]{:S(2)}) collective-permute-start(bf16[128,3584]{1,0:T(8,128)(2,1)S(1)} %collective-permute-done.8), channel_id=1, source_target_pairs={{16,24},{17,25},{18,26},{19,27},{20,28},{21,29},{22,30},{23,31}} | collective-permute-start | bytes 2752520 | tf_op jit(solution)/shard_map/ppermute | solution.py:28
  85.3 38.5 %collective-permute-start.5 = (bf16[128,3584]{1,0:T(8,128)(2,1)S(1)}, bf16[128,3584]{1,0:T(8,128)(2,1)S(1)}, u32[]{:S(2)}, u32[]{:S(2)}) collective-permute-start(bf16[128,3584]{1,0:T(8,128)(2,1)S(1)} %collective-permute-done.3), channel_id=1, source_target_pairs={{8,0},{9,1},{10,2},{11,3},{12,4},{13,5},{14,6},{15,7}} | collective-permute-start | bytes 2752520 | tf_op jit(solution)/shard_map/ppermute | solution.py:29
  86.6 2.5 collective-permute-start.4
  124.4 1.9 copy-start
  132.4 87.7 %all-to-all-start = ((bf16[8,128,3584]{2,1,0:T(8,128)(2,1)}), bf16[8,128,3584]{2,1,0:T(8,128)(2,1)}, u32[]{:S(2)}, u32[]{:S(2)}) async-start(bf16[8,128,3584]{2,1,0:T(8,128)(2,1)} %bitcast.130), calls=%async_computation | async-start | bytes 14680064 | tf_op jit(solution)/shard_map/all_to_all | solution.py:103
  220.1 5.2 copy-start.1
  220.1 87.8 %all-to-all-start.2 = ((bf16[8,128,3584]{2,1,0:T(8,128)(2,1)}), bf16[8,128,3584]{2,1,0:T(8,128)(2,1)}, u32[]{:S(2)}, u32[]{:S(2)}) async-start(bf16[8,128,3584]{2,1,0:T(8,128)(2,1)} %bitcast.129), calls=%async_computation.2 | async-start | bytes 14680064 | tf_op jit(solution)/shard_map/all_to_all | solution.py:99

commit v3 on v0

v3 whole, which is shorter than its diff:
```python
import jax
import jax.numpy as jnp
from jax import lax
from jax.sharding import PartitionSpec as P

FF = 1024
TOK_DEV = 128
TOPK = 8


def slot_ranks(ids, columns):
    slots = ids.shape[-1]
    onehot = (ids[..., None] == jnp.arange(columns, dtype=jnp.int32)).astype(jnp.bfloat16)
    order = jnp.arange(slots, dtype=jnp.int32)
    earlier = (order[:, None] > order[None, :]).astype(jnp.bfloat16)
    before = jnp.einsum("st,nte->nse", earlier, onehot, preferred_element_type=jnp.float32)
    return jnp.sum(before * onehot.astype(jnp.float32), axis=-1).astype(jnp.int32)


def expert_backward(rows_x, rows_dy, rows_gate, saved, weight_in, weight_out):
    up_pre = jnp.dot(rows_x, weight_in[:, FF:], preferred_element_type=jnp.float32)
    grad_hidden = lax.dot_general(
        rows_dy, weight_out, (((1,), (1,)), ((), ())), preferred_element_type=jnp.float32
    )
    grad_hidden = grad_hidden * rows_gate.astype(jnp.float32)[:, None]
    gate_pre = saved.astype(jnp.float32)
    sigmoid_gate = jax.nn.sigmoid(gate_pre)
    grad_gate = grad_hidden * up_pre * sigmoid_gate * (1.0 + gate_pre * (1.0 - sigmoid_gate))
    grad_up = grad_hidden * gate_pre * sigmoid_gate
    grad_pre = jnp.concatenate([grad_gate, grad_up], axis=1).astype(jnp.bfloat16)
    contrib = lax.dot_general(
        grad_pre, weight_in, (((1,), (1,)), ((), ())), preferred_element_type=jnp.float32
    )
    return contrib.astype(jnp.bfloat16)


def select_rows(onehot, rows):
    picked = lax.dot_general(
        onehot, rows, (((0,), (0,)), ((), ())), preferred_element_type=jnp.float32
    )
    return picked.astype(jnp.bfloat16)


def shift(value, n_node, step):
    if step % n_node == 0:
        return value
    return lax.ppermute(value, "node", [(i, (i + step) % n_node) for i in range(n_node)])


def on_device(hidden_in, out_grad, expert_ids, gate_int, gate_saved, w_in, w_out):
    n_node = lax.axis_size("node")
    n_local = lax.axis_size("local")
    experts = n_node * n_local
    tok = hidden_in.shape[0]
    capacity = tok * TOPK // experts
    chunk_rows = n_local * capacity
    model_width = hidden_in.shape[1]
    node_here = lax.axis_index("node")
    weight_in = w_in[0]
    weight_out = w_out[0]

    ids = expert_ids.reshape(n_node, tok * TOPK)
    ranks = slot_ranks(ids, experts)
    on_here = (ids // n_local) == node_here
    position = jnp.where(on_here, (ids % n_local) * capacity + ranks, chunk_rows)
    weight = (gate_int.reshape(n_node, tok, TOPK).astype(jnp.float32) / 1024.0).astype(
        jnp.bfloat16
    )
    row_range = jnp.arange(chunk_rows, dtype=jnp.int32)

    total = None
    for step in range(n_node):
        source = (node_here - step) % n_node
        chunk_x = shift(hidden_in, n_node, step)
        chunk_dy = shift(out_grad, n_node, step)
        chunk_pos = lax.dynamic_index_in_dim(position, source, 0, keepdims=False)
        hits = (
            chunk_pos.reshape(tok, TOPK)[:, :, None] == row_range[None, None, :]
        ).astype(jnp.bfloat16)
        dispatch = jnp.sum(hits, axis=1)
        chunk_weight = lax.dynamic_index_in_dim(weight, source, 0, keepdims=False)
        send_gate = jnp.einsum(
            "tk,tkr->r", chunk_weight, hits, preferred_element_type=jnp.float32
        ).astype(jnp.bfloat16)

        recv_x = lax.all_to_all(
            select_rows(dispatch, chunk_x).reshape(n_local, capacity, model_width),
            "local", 0, 0, tiled=True,
        )
        recv_dy = lax.all_to_all(
            select_rows(dispatch, chunk_dy).reshape(n_local, capacity, model_width),
            "local", 0, 0, tiled=True,
        )
        recv_gate = lax.all_to_all(
            send_gate.reshape(n_local, capacity), "local", 0, 0, tiled=True
        )
        saved = lax.dynamic_slice_in_dim(gate_saved, source * chunk_rows, chunk_rows, 0)
        contrib = expert_backward(
            recv_x.reshape(chunk_rows, model_width),
            recv_dy.reshape(chunk_rows, model_width),
            recv_gate.reshape(chunk_rows),
            saved,
            weight_in,
            weight_out,
        )
        returned = lax.all_to_all(
            contrib.reshape(n_local, capacity, model_width), "local", 0, 0, tiled=True
        ).reshape(chunk_rows, model_width)
        node_sum = jnp.dot(dispatch, returned, preferred_element_type=jnp.float32).astype(
            jnp.bfloat16
        )
        home = shift(node_sum, n_node, -step).astype(jnp.float32)
        total = home if total is None else total + home
    return total.astype(jnp.bfloat16)


def solution(mesh):
    in_specs = (
        P(("node", "local"), None),
        P(("node", "local"), None),
        P(None, "local", None),
        P(None, "local", None),
        P(("node", "local"), None),
        P(("node", "local"), None, None),
        P(("node", "local"), None, None),
    )
    out_specs = P(("node", "local"), None)
    return jax.shard_map(
        on_device, mesh=mesh, in_specs=in_specs, out_specs=out_specs, check_vma=False
    )
```

time: 652 us -> 533 us (0.82); the launches traced: 650 us -> 523 us
  waiting for transfers between devices: 464 us -> 274 us
  matrix products: 51.7 us -> 143 us
  local copies, waits for them, and re-layouts: 93.2 us -> 9.86 us
  starting transfers between devices: 20.9 us -> 94.4 us
  other arithmetic: 20.8 us -> 1.74 us
    all_to_all x4 -> x16, waiting for transfers between devices: 464 us -> 59 us  [the longest x4 21.3 us: on_device(): lax.all_to_all(select_rows(dispatch, chunk_x).reshape(n_local, capacity,...]
    ppermute x0 -> x9, waiting for transfers between devices: none -> 215 us  [shift(): lax.ppermute(value, 'node', [(i, (i + step) % n_node) for i in range(n_no...]
    gather x8 -> x0, local copies, waits for them, and re-layouts: 83.8 us -> none  [the longest x4 46.9 us: pair_sums(): ordered = jnp.take_along_axis(contribs, slot_order[:, :, None], axis=1)]
    all_to_all x4 -> x16, starting transfers between devices: 20.9 us -> 64.8 us  [the longest x4 17.1 us: on_device(): lax.all_to_all(contrib.reshape(n_local, capacity, model_width), 'local',...]
    dot_general x1 -> x4, matrix products: 21.8 us -> 64.7 us  [expert_backward(): lax.dot_general(grad_pre, weight_in, (((1,), (1,)), ((), ())), preferred_...]
    dot_general x0 -> x17, matrix products: none -> 30.5 us  [the longest x8 20 us: select_rows(): lax.dot_general(onehot, rows, (((0,), (0,)), ((), ())), preferred_element...]
    ppermute x0 -> x9, starting transfers between devices: none -> 29.6 us  [shift(): lax.ppermute(value, 'node', [(i, (i + step) % n_node) for i in range(n_no...]
    another operation x3 -> x0, other arithmetic: 9.15 us -> none
  transfers between devices with their start and end apart: 4 -> 25, of which waited for: 3 -> 19; matrix products, arithmetic and copies ran while one was open for 5% -> 27% of each run, Pallas kernels for 0% -> 0%
where the time goes in v3:
time: 533 us; the launch traced here: 523 us
  waiting for transfers between devices  274 us (51%)
  matrix products  143 us (27%)
  starting transfers between devices  94.4 us (18%)
  local copies, waits for them, and re-layouts  9.86 us (2%)
    ppermute x9, waiting for transfers between devices, shift(): lax.ppermute(value, 'node', [(i, (i + step) % n_node) for i in range(n_no...  215 us
    dot_general x4, matrix products, expert_backward(): lax.dot_general(grad_pre, weight_in, (((1,), (1,)), ((), ())), preferred_...  64.7 us
    ppermute x9, starting transfers between devices, shift(): lax.ppermute(value, 'node', [(i, (i + step) % n_node) for i in range(n_no...  29.6 us
    dot_general x4, matrix products, expert_backward(): jnp.dot(rows_x, weight_in[:, FF:], preferred_element_type=jnp.float32)  23.8 us
    dot_general x4, matrix products, expert_backward(): lax.dot_general(rows_dy, weight_out, (((1,), (1,)), ((), ())), preferred_...  23.7 us
    all_to_all x4, waiting for transfers between devices, on_device(): lax.all_to_all(select_rows(dispatch, chunk_x).reshape(n_local, capacity,...  21.3 us
    all_to_all x4, waiting for transfers between devices, on_device(): lax.all_to_all(select_rows(dispatch, chunk_dy).reshape(n_local, capacity,...  20.7 us
    dot_general x8, matrix products, select_rows(): lax.dot_general(onehot, rows, (((0,), (0,)), ((), ())), preferred_element...  20 us
  transfers between devices with their start and end apart: 25, of which 19 were waited for; matrix products, arithmetic and copies ran while one was open for 27% of the time, Pallas kernels for 0%

profile of v3, /device:TPU:0, one launch (start us, length us, event | category | flops | bytes accessed | tf_op | source)
XLA Modules:
  0.0 523.3 jit_solution(3360593193309753298)
XLA Ops:
  3.2 5.2 all-to-all-start.9
  10.5 2.4 all-to-all-done.9
  12.9 3.3 all-to-all-start.13
  17.4 3.5 all-to-all-done.13
  20.9 3.3 all-to-all-start.1
  25.3 3.4 all-to-all-done.1
  28.7 3.3 all-to-all-start.5
  32.0 1.9 convolution_convert_fusion.11
  33.9 2.7 all-to-all-done.5
  36.6 3.6 all-to-all-start
  40.2 3.1 convolution_convert_fusion.10
  43.3 20.7 %all-to-all-done = bf16[8,32,3584]{2,1,0:T(8,128)(2,1)S(1)} async-done(((bf16[8,32,3584]{2,1,0:T(8,128)(2,1)}), bf16[8,32,3584]{2,1,0:T(8,128)(2,1)S(1)}, u32[]{:S(2)}, u32[]{:S(2)}) %all-to-all-start) | async-done | bytes 1835040 | tf_op jit(solution)/shard_map/all_to_all | solution.py:90
  64.0 1.3 copy-done.1
  65.3 3.6 all-to-all-start.2
  68.9 2.7 collective-permute-start.3
  72.0 40.2 %collective-permute-done.3 = bf16[128,3584]{1,0:T(8,128)(2,1)S(1)} collective-permute-done((bf16[128,3584]{1,0:T(8,128)(2,1)S(1)}, bf16[128,3584]{1,0:T(8,128)(2,1)S(1)}, u32[]{:S(2)}, u32[]{:S(2)}) %collective-permute-start.3) | collective-permute-done | bytes 917536 | tf_op jit(solution)/shard_map/ppermute | solution.py:47
  112.1 1.9 convolution_convert_fusion.5
  115.2 4.3 all-to-all-start.8
  119.6 3.5 collective-permute-start.6
  123.5 19.7 %collective-permute-done.6 = bf16[128,3584]{1,0:T(8,128)(2,1)S(1)} collective-permute-done((bf16[128,3584]{1,0:T(8,128)(2,1)S(1)}, bf16[128,3584]{1,0:T(8,128)(2,1)S(1)}, u32[]{:S(2)}, u32[]{:S(2)}) %collective-permute-start.6) | collective-permute-done | bytes 917536 | tf_op jit(solution)/shard_map/ppermute | solution.py:47
  143.2 1.9 convolution_convert_fusion.2
  145.1 3.9 all-to-all-start.12
  149.4 24.9 %collective-permute-done = bf16[128,3584]{1,0:T(8,128)(2,1)S(1)} collective-permute-done((bf16[128,3584]{1,0:T(8,128)(2,1)S(1)}, bf16[128,3584]{1,0:T(8,128)(2,1)S(1)}, u32[]{:S(2)}, u32[]{:S(2)}) %collective-permute-start) | collective-permute-done | bytes 917536 | tf_op jit(solution)/shard_map/ppermute | solution.py:47
  174.3 1.9 convolution_convert_fusion.8
  176.2 4.5 all-to-all-start.4
  180.7 2.3 collective-permute-start.4
  183.0 1.5 collective-permute-start.7
  185.0 21.0 %collective-permute-done.1 = bf16[128,3584]{1,0:T(8,128)(2,1)} collective-permute-done((bf16[128,3584]{1,0:T(8,128)(2,1)S(1)}, bf16[128,3584]{1,0:T(8,128)(2,1)}, u32[]{:S(2)}, u32[]{:S(2)}) %collective-permute-start.1) | collective-permute-done | bytes 917536 | tf_op jit(solution)/shard_map/ppermute | solution.py:47
  206.0 3.1 convolution_convert_fusion.7
  209.0 35.3 %collective-permute-done.4 = bf16[128,3584]{1,0:T(8,128)(2,1)} collective-permute-done((bf16[128,3584]{1,0:T(8,128)(2,1)S(1)}, bf16[128,3584]{1,0:T(8,128)(2,1)}, u32[]{:S(2)}, u32[]{:S(2)}) %collective-permute-start.4) | collective-permute-done | bytes 917536 | tf_op jit(solution)/shard_map/ppermute | solution.py:47
  244.4 3.0 convolution_convert_fusion.4
  247.4 4.5 all-to-all-start.6
  252.0 3.3 convolution_convert_fusion.1
  255.2 6.3 %fusion.20 = f32[256,1024]{1,0:T(8,128)} fusion(bf16[256,3584]{1,0:T(8,128)(2,1)S(1)} %bitcast.121, bf16[1,1024,3584]{2,1,0:T(8,128)(2,1)} %param.13, f32[256]{0:T(256)S(1)} %reshape.161), kind=kOutput, calls=%fused_computation.49 | convolution fusion | flops 1879310336 | bytes 10224640 | tf_op jit(solution)/shard_map/dot_general | solution.py:22
  261.6 4.6 fusion.26
  266.1 9.7 %all-to-all-done.6 = bf16[8,32,3584]{2,1,0:T(8,128)(2,1)} async-done(((bf16[8,32,3584]{2,1,0:T(8,128)(2,1)}), bf16[8,32,3584]{2,1,0:T(8,128)(2,1)}, u32[]{:S(2)}, u32[]{:S(2)}) %all-to-all-start.6) | async-done | bytes 1835040 | tf_op jit(solution)/shard_map/all_to_all | solution.py:86
  275.8 4.3 all-to-all-start.10
  280.1 5.3 %fusion.29 = f32[256,1024]{1,0:T(8,128)S(1)} fusion(bf16[256,3584]{1,0:T(8,128)(2,1)S(1)} %bitcast.122, bf16[1,1024,3584]{2,1,0:T(8,128)(2,1)} %param.13, f32[256]{0:T(256)S(1)} %reshape.164), kind=kOutput, calls=%fused_computation.52 | convolution fusion | flops 1879310336 | bytes 10224640 | tf_op jit(solution)/shard_map/dot_general | solution.py:22
  286.5 7.5 %fusion.100 = (bf16[256,1024]{1,0:T(8,128)(2,1)}, bf16[256,1024]{1,0:T(8,128)(2,1)}, bf16[256,1024]{1,0:T(8,128)(2,1)}, bf16[256,1024]{1,0:T(8,128)(2,1)}, f32[256,1024]{1,0:T(8,128)}) fusion(bf16[1024,1024]{1,0:T(8,128)(2,1)S(1)} %copy-done.7, s32[]{:T(128)S(6)} %select_n.72, f32[256,1024]{1,0:T(8,128)S(1)} %copy-done.8, s32[]{:T(128)S(6)} %select_n.69, ...), kind=kOutput, calls=%fused_computation.83 | convolution fusion | flops 1886650368 | bytes 17564688 | tf_op jit(solution)/shard_map/dot_general | solution.py:22
  293.9 10.0 %all-to-all-done.10 = bf16[8,32,3584]{2,1,0:T(8,128)(2,1)} async-done(((bf16[8,32,3584]{2,1,0:T(8,128)(2,1)}), bf16[8,32,3584]{2,1,0:T(8,128)(2,1)}, u32[]{:S(2)}, u32[]{:S(2)}) %all-to-all-start.10) | async-done | bytes 1835040 | tf_op jit(solution)/shard_map/all_to_all | solution.py:86
  304.0 3.9 all-to-all-start.14
  307.9 6.0 %fusion.71 = bf16[256,1024]{1,0:T(8,128)(2,1)S(1)} fusion(f32[256,1024]{1,0:T(8,128)S(1)} %copy-done.14, bf16[256,3584]{1,0:T(8,128)(2,1)} %bitcast.19, bf16[3584,2048]{1,0:T(8,128)(2,1)} %bitcast.128, bf16[1024,1024]{1,0:T(8,128)(2,1)} %param.11, s32[]{:T(128)S(6)} %select_n.72), kind=kOutput, calls=%fused_computation.66 | convolution fusion | flops 1881931776 | bytes 11272196 | tf_op jit(solution)/shard_map/dot_general | solution.py:21
  313.9 16.2 %convolution_convert_fusion.6 = bf16[256,3584]{1,0:T(8,128)(2,1)} fusion(bf16[256,1024]{1,0:T(8,128)(2,1)S(1)} %copy-done.18, bf16[256,1024]{1,0:T(8,128)(2,1)S(1)} %fusion.71, bf16[1,3584,2048]{2,1,0:T(8,128)(2,1)} %param.12), kind=kOutput, calls=%fused_computation.14 | convolution fusion | flops 3761111040 | bytes 17563648 | tf_op jit(solution)/shard_map/dot_general | solution.py:31
  330.1 1.6 all-to-all-done.14
  331.7 1.3 copy-done.3
  333.0 3.6 all-to-all-start.7
  336.6 6.0 %fusion.74 = bf16[256,1024]{1,0:T(8,128)(2,1)S(1)} fusion(f32[256,1024]{1,0:T(8,128)S(1)} %copy-done.13, bf16[256,3584]{1,0:T(8,128)(2,1)} %bitcast.28, bf16[3584,2048]{1,0:T(8,128)(2,1)} %bitcast.129, bf16[1024,1024]{1,0:T(8,128)(2,1)} %param.11, s32[]{:T(128)S(6)} %select_n.75), kind=kOutput, calls=%fused_computation.67 | convolution fusion | flops 1881931776 | bytes 11272196 | tf_op jit(solution)/shard_map/dot_general | solution.py:21
  342.6 16.1 %convolution_convert_fusion.3 = bf16[256,3584]{1,0:T(8,128)(2,1)} fusion(bf16[256,1024]{1,0:T(8,128)(2,1)S(1)} %copy-done.17, bf16[256,1024]{1,0:T(8,128)(2,1)S(1)} %fusion.74, bf16[1,3584,2048]{2,1,0:T(8,128)(2,1)} %param.12), kind=kOutput, calls=%fused_computation.11 | convolution fusion | flops 3761111040 | bytes 17563648 | tf_op jit(solution)/shard_map/dot_general | solution.py:31
  358.7 1.6 all-to-all-done.7
  360.4 4.7 all-to-all-start.11
  365.1 6.0 %fusion.77 = bf16[256,1024]{1,0:T(8,128)(2,1)S(1)} fusion(f32[256,1024]{1,0:T(8,128)S(1)} %copy-done.11, bf16[256,3584]{1,0:T(8,128)(2,1)} %bitcast.123, bf16[3584,2048]{1,0:T(8,128)(2,1)} %bitcast.130, bf16[1024,1024]{1,0:T(8,128)(2,1)} %param.11, s32[]{:T(128)S(6)} %select_n.78), kind=kOutput, calls=%fused_computation.68 | convolution fusion | flops 1881931776 | bytes 11272196 | tf_op jit(solution)/shard_map/dot_general | solution.py:21
  371.1 16.2 %convolution_convert_fusion = bf16[256,3584]{1,0:T(8,128)(2,1)} fusion(bf16[256,1024]{1,0:T(8,128)(2,1)S(1)} %copy-done.16, bf16[256,1024]{1,0:T(8,128)(2,1)S(1)} %fusion.77, bf16[1,3584,2048]{2,1,0:T(8,128)(2,1)} %param.12), kind=kOutput, calls=%fused_computation.8 | convolution fusion | flops 3761111040 | bytes 17563648 | tf_op jit(solution)/shard_map/dot_general | solution.py:31
  387.3 1.6 all-to-all-done.11
  388.9 4.5 all-to-all-start.15
  393.4 6.0 %fusion.68 = bf16[256,1024]{1,0:T(8,128)(2,1)S(1)} fusion(f32[256,1024]{1,0:T(8,128)S(1)} %copy-done.9, bf16[256,3584]{1,0:T(8,128)(2,1)} %bitcast.120, bf16[3584,2048]{1,0:T(8,128)(2,1)} %bitcast.131, bf16[1024,1024]{1,0:T(8,128)(2,1)} %param.11, s32[]{:T(128)S(6)} %select_n.69), kind=kOutput, calls=%fused_computation.65 | convolution fusion | flops 1881931776 | bytes 11272196 | tf_op jit(solution)/shard_map/dot_general | solution.py:21
  399.4 16.2 %convolution_convert_fusion.9 = bf16[256,3584]{1,0:T(8,128)(2,1)} fusion(bf16[256,1024]{1,0:T(8,128)(2,1)S(1)} %copy-done.15, bf16[256,1024]{1,0:T(8,128)(2,1)S(1)} %fusion.68, bf16[1,3584,2048]{2,1,0:T(8,128)(2,1)} %param.12), kind=kOutput, calls=%fused_computation.17 | convolution fusion | flops 3761111040 | bytes 17563648 | tf_op jit(solution)/shard_map/dot_general | solution.py:31
  415.6 1.7 all-to-all-done.15
  417.2 4.3 all-to-all-start.3
  422.0 18.8 %collective-permute-start.2 = (bf16[128,3584]{1,0:T(8,128)(2,1)S(1)}, bf16[128,3584]{1,0:T(8,128)(2,1)}, u32[]{:S(2)}, u32[]{:S(2)}) collective-permute-start(bf16[128,3584]{1,0:T(8,128)(2,1)S(1)} %convolution_convert_fusion.14), channel_id=1, source_target_pairs={{0,24},{8,0},{16,8},{24,16},{1,25},{9,1},{17,9},{25,17},{2,26},{10... | collective-permute-start | bytes 2752520 | tf_op jit(solution)/shard_map/ppermute | solution.py:47
  440.8 1.9 convolution_convert_fusion.13
  442.8 1.9 convolution_convert_fusion.12
  445.4 16.2 %collective-permute-done.2 = bf16[128,3584]{1,0:T(8,128)(2,1)} collective-permute-done((bf16[128,3584]{1,0:T(8,128)(2,1)S(1)}, bf16[128,3584]{1,0:T(8,128)(2,1)}, u32[]{:S(2)}, u32[]{:S(2)}) %collective-permute-start.2) | collective-permute-done | bytes 917536 | tf_op jit(solution)/shard_map/ppermute | solution.py:47
  461.6 57.5 %collective-permute-done.5 = bf16[128,3584]{1,0:T(8,128)(2,1)} collective-permute-done((bf16[128,3584]{1,0:T(8,128)(2,1)S(1)}, bf16[128,3584]{1,0:T(8,128)(2,1)}, u32[]{:S(2)}, u32[]{:S(2)}) %collective-permute-start.5) | collective-permute-done | bytes 917536 | tf_op jit(solution)/shard_map/ppermute | solution.py:47
  519.1 3.8 add_convert_fusion
  (92 shorter events, 12.6 us)
Async XLA Ops:
  0.0 1.9 copy-start.6
  2.5 29.5 %copy-start.4 = (bf16[128,3584]{1,0:T(8,128)(2,1)S(1)}, bf16[128,3584]{1,0:T(8,128)(2,1)}, u32[]{:S(2)}) copy-start(bf16[128,3584]{1,0:T(8,128)(2,1)} %param.8) | copy-start | bytes 2752516
  3.2 9.8 %all-to-all-start.9 = ((bf16[8,1,32]{2,1,0:T(2,128)(2,1)}), bf16[8,1,32]{2,1,0:T(2,128)(2,1)S(1)}, u32[]{:S(2)}, u32[]{:S(2)}) async-start(bf16[8,1,32]{2,1,0:T(2,128)(2,1)} %all_to_all.82), calls=%async_computation.9 | async-start | bytes 8192 | tf_op jit(solution)/shard_map/all_to_all | solution.py:94
  12.9 7.9 %all-to-all-start.13 = ((bf16[8,1,32]{2,1,0:T(2,128)(2,1)}), bf16[8,1,32]{2,1,0:T(2,128)(2,1)S(1)}, u32[]{:S(2)}, u32[]{:S(2)}) async-start(bf16[8,1,32]{2,1,0:T(2,128)(2,1)} %all_to_all.83), calls=%async_computation.13 | async-start | bytes 8192 | tf_op jit(solution)/shard_map/all_to_all | solution.py:94
  20.9 7.8 %all-to-all-start.1 = ((bf16[8,1,32]{2,1,0:T(2,128)(2,1)}), bf16[8,1,32]{2,1,0:T(2,128)(2,1)S(1)}, u32[]{:S(2)}, u32[]{:S(2)}) async-start(bf16[8,1,32]{2,1,0:T(2,128)(2,1)} %all_to_all.80), calls=%async_computation.1 | async-start | bytes 8192 | tf_op jit(solution)/shard_map/all_to_all | solution.py:94
  28.7 7.9 %all-to-all-start.5 = ((bf16[8,1,32]{2,1,0:T(2,128)(2,1)}), bf16[8,1,32]{2,1,0:T(2,128)(2,1)S(1)}, u32[]{:S(2)}, u32[]{:S(2)}) async-start(bf16[8,1,32]{2,1,0:T(2,128)(2,1)} %all_to_all.81), calls=%async_computation.5 | async-start | bytes 8192 | tf_op jit(solution)/shard_map/all_to_all | solution.py:94
  36.6 27.4 %all-to-all-start = ((bf16[8,32,3584]{2,1,0:T(8,128)(2,1)}), bf16[8,32,3584]{2,1,0:T(8,128)(2,1)S(1)}, u32[]{:S(2)}, u32[]{:S(2)}) async-start(bf16[8,32,3584]{2,1,0:T(8,128)(2,1)} %bitcast.2), calls=%async_computation | async-start | bytes 3670016 | tf_op jit(solution)/shard_map/all_to_all | solution.py:90
  64.0 1.3 copy-start.1
  65.3 48.7 %all-to-all-start.2 = ((bf16[8,32,3584]{2,1,0:T(8,128)(2,1)}), bf16[8,32,3584]{2,1,0:T(8,128)(2,1)S(1)}, u32[]{:S(2)}, u32[]{:S(2)}) async-start(bf16[8,32,3584]{2,1,0:T(8,128)(2,1)} %bitcast.8), calls=%async_computation.2 | async-start | bytes 3670016 | tf_op jit(solution)/shard_map/all_to_all | solution.py:86
  68.9 43.2 %collective-permute-start.3 = (bf16[128,3584]{1,0:T(8,128)(2,1)S(1)}, bf16[128,3584]{1,0:T(8,128)(2,1)S(1)}, u32[]{:S(2)}, u32[]{:S(2)}) collective-permute-start(bf16[128,3584]{1,0:T(8,128)(2,1)S(1)} %copy-done.4), channel_id=1, source_target_pairs={{0,16},{8,24},{16,0},{24,8},{1,17},{9,25},{17,1},{25,9},{2,18},{10... | collective-permute-start | bytes 2752520 | tf_op jit(solution)/shard_map/ppermute | solution.py:47
  114.0 1.3 copy-start
  115.2 29.8 %all-to-all-start.8 = ((bf16[8,32,3584]{2,1,0:T(8,128)(2,1)}), bf16[8,32,3584]{2,1,0:T(8,128)(2,1)}, u32[]{:S(2)}, u32[]{:S(2)}) async-start(bf16[8,32,3584]{2,1,0:T(8,128)(2,1)} %bitcast.22), calls=%async_computation.8 | async-start | bytes 3670016 | tf_op jit(solution)/shard_map/all_to_all | solution.py:90
  119.6 23.6 %collective-permute-start.6 = (bf16[128,3584]{1,0:T(8,128)(2,1)S(1)}, bf16[128,3584]{1,0:T(8,128)(2,1)S(1)}, u32[]{:S(2)}, u32[]{:S(2)}) collective-permute-start(bf16[128,3584]{1,0:T(8,128)(2,1)S(1)} %copy-done.4), channel_id=1, source_target_pairs={{0,24},{8,0},{16,8},{24,16},{1,25},{9,1},{17,9},{25,17},{2,26},{10... | collective-permute-start | bytes 2752520 | tf_op jit(solution)/shard_map/ppermute | solution.py:47
  145.1 31.1 %all-to-all-start.12 = ((bf16[8,32,3584]{2,1,0:T(8,128)(2,1)}), bf16[8,32,3584]{2,1,0:T(8,128)(2,1)S(1)}, u32[]{:S(2)}, u32[]{:S(2)}) async-start(bf16[8,32,3584]{2,1,0:T(8,128)(2,1)} %bitcast.31), calls=%async_computation.12 | async-start | bytes 3670016 | tf_op jit(solution)/shard_map/all_to_all | solution.py:90
  149.0 25.3 %collective-permute-start = (bf16[128,3584]{1,0:T(8,128)(2,1)S(1)}, bf16[128,3584]{1,0:T(8,128)(2,1)S(1)}, u32[]{:S(2)}, u32[]{:S(2)}) collective-permute-start(bf16[128,3584]{1,0:T(8,128)(2,1)S(1)} %copy-done.4), channel_id=1, source_target_pairs={{0,8},{8,16},{16,24},{24,0},{1,9},{9,17},{17,25},{25,1},{2,10},{10... | collective-permute-start | bytes 2752520 | tf_op jit(solution)/shard_map/ppermute | solution.py:47
  176.2 4.5 copy-start.5
  176.2 71.2 %all-to-all-start.4 = ((bf16[8,32,3584]{2,1,0:T(8,128)(2,1)}), bf16[8,32,3584]{2,1,0:T(8,128)(2,1)}, u32[]{:S(2)}, u32[]{:S(2)}) async-start(bf16[8,32,3584]{2,1,0:T(8,128)(2,1)} %bitcast.13), calls=%async_computation.4 | async-start | bytes 3670016 | tf_op jit(solution)/shard_map/all_to_all | solution.py:90
  180.7 25.3 %collective-permute-start.1 = (bf16[128,3584]{1,0:T(8,128)(2,1)S(1)}, bf16[128,3584]{1,0:T(8,128)(2,1)}, u32[]{:S(2)}, u32[]{:S(2)}) collective-permute-start(bf16[128,3584]{1,0:T(8,128)(2,1)S(1)} %copy-done.5), channel_id=1, source_target_pairs={{0,8},{8,16},{16,24},{24,0},{1,9},{9,17},{17,25},{25,1},{2,10},{10... | collective-permute-start | bytes 2752520 | tf_op jit(solution)/shard_map/ppermute | solution.py:47
  180.7 63.6 %collective-permute-start.4 = (bf16[128,3584]{1,0:T(8,128)(2,1)S(1)}, bf16[128,3584]{1,0:T(8,128)(2,1)}, u32[]{:S(2)}, u32[]{:S(2)}) collective-permute-start(bf16[128,3584]{1,0:T(8,128)(2,1)S(1)} %copy-done.5), channel_id=1, source_target_pairs={{0,16},{8,24},{16,0},{24,8},{1,17},{9,25},{17,1},{25,9},{2,18},{10... | collective-permute-start | bytes 2752520 | tf_op jit(solution)/shard_map/ppermute | solution.py:47
  183.0 68.9 %collective-permute-start.7 = (bf16[128,3584]{1,0:T(8,128)(2,1)S(1)}, bf16[128,3584]{1,0:T(8,128)(2,1)}, u32[]{:S(2)}, u32[]{:S(2)}) collective-permute-start(bf16[128,3584]{1,0:T(8,128)(2,1)S(1)} %copy-done.5), channel_id=1, source_target_pairs={{0,24},{8,0},{16,8},{24,16},{1,25},{9,1},{17,9},{25,17},{2,26},{10... | collective-permute-start | bytes 2752520 | tf_op jit(solution)/shard_map/ppermute | solution.py:47
  247.4 28.4 %all-to-all-start.6 = ((bf16[8,32,3584]{2,1,0:T(8,128)(2,1)}), bf16[8,32,3584]{2,1,0:T(8,128)(2,1)}, u32[]{:S(2)}, u32[]{:S(2)}) async-start(bf16[8,32,3584]{2,1,0:T(8,128)(2,1)} %bitcast.18), calls=%async_computation.6 | async-start | bytes 3670016 | tf_op jit(solution)/shard_map/all_to_all | solution.py:86
  251.9 3.3 copy-start.2
  251.9 9.6 %slice-start = ((s8[7340032]{0:T(1024)(128)(4,1)}), s8[4194304]{0:T(1024)(128)(4,1)S(1)}, s32[]{:S(2)}) async-start(s8[7340032]{0:T(1024)(128)(4,1)} %bitcast.132), calls=%async_computation.16 | async-start | bytes 8388608
  255.2 6.3 %slice-start.1 = ((s8[7340032]{0:T(1024)(128)(4,1)}), s8[3145728]{0:T(1024)(128)(4,1)S(1)}, s32[]{:S(2)}) async-start(s8[7340032]{0:T(1024)(128)(4,1)} %bitcast.132), calls=%async_computation.17 | async-start | bytes 6291456
  275.8 28.2 %all-to-all-start.10 = ((bf16[8,32,3584]{2,1,0:T(8,128)(2,1)}), bf16[8,32,3584]{2,1,0:T(8,128)(2,1)}, u32[]{:S(2)}, u32[]{:S(2)}) async-start(bf16[8,32,3584]{2,1,0:T(8,128)(2,1)} %bitcast.27), calls=%async_computation.10 | async-start | bytes 3670016 | tf_op jit(solution)/shard_map/all_to_all | solution.py:86
  280.1 6.3 %copy-start.7 = (bf16[1024,1024]{1,0:T(8,128)(2,1)S(1)}, bf16[1024,1024]{1,0:T(8,128)(2,1)}, u32[]{:S(2)}) copy-start(bf16[1024,1024]{1,0:T(8,128)(2,1)} %param.11) | copy-start | bytes 6291460
  280.1 6.3 %copy-start.8 = (f32[256,1024]{1,0:T(8,128)S(1)}, f32[256,1024]{1,0:T(8,128)}, u32[]{:S(2)}) copy-start(f32[256,1024]{1,0:T(8,128)} %fusion.20) | copy-start | bytes 3145732
  280.1 6.3 %copy-start.12 = (f32[256,1024]{1,0:T(8,128)S(1)}, f32[256,1024]{1,0:T(8,128)}, u32[]{:S(2)}) copy-start(f32[256,1024]{1,0:T(8,128)} %fusion.26) | copy-start | bytes 3145732
  285.5 1.0 copy-start.10
  304.0 3.9 copy-start.14
  304.0 27.7 %all-to-all-start.14 = ((bf16[8,32,3584]{2,1,0:T(8,128)(2,1)}), bf16[8,32,3584]{2,1,0:T(8,128)(2,1)S(1)}, u32[]{:S(2)}, u32[]{:S(2)}) async-start(bf16[8,32,3584]{2,1,0:T(8,128)(2,1)} %bitcast.36), calls=%async_computation.14 | async-start | bytes 3670016 | tf_op jit(solution)/shard_map/all_to_all | solution.py:86
  307.9 6.0 %copy-start.18 = (bf16[256,1024]{1,0:T(8,128)(2,1)S(1)}, bf16[256,1024]{1,0:T(8,128)(2,1)}, u32[]{:S(2)}) copy-start(bf16[256,1024]{1,0:T(8,128)(2,1)} %get-tuple-element.9) | copy-start | bytes 1572868
  331.7 1.3 copy-start.3
  331.7 4.9 copy-start.13
  333.0 27.4 %all-to-all-start.7 = ((bf16[8,32,3584]{2,1,0:T(8,128)(2,1)}), bf16[8,32,3584]{2,1,0:T(8,128)(2,1)S(1)}, u32[]{:S(2)}, u32[]{:S(2)}) async-start(bf16[8,32,3584]{2,1,0:T(8,128)(2,1)} %bitcast.126), calls=%async_computation.7 | async-start | bytes 3670016 | tf_op jit(solution)/shard_map/all_to_all | solution.py:106
  336.6 6.0 %copy-start.17 = (bf16[256,1024]{1,0:T(8,128)(2,1)S(1)}, bf16[256,1024]{1,0:T(8,128)(2,1)}, u32[]{:S(2)}) copy-start(bf16[256,1024]{1,0:T(8,128)(2,1)} %get-tuple-element.11) | copy-start | bytes 1572868
  360.4 4.7 copy-start.11
  360.4 28.6 %all-to-all-start.11 = ((bf16[8,32,3584]{2,1,0:T(8,128)(2,1)}), bf16[8,32,3584]{2,1,0:T(8,128)(2,1)}, u32[]{:S(2)}, u32[]{:S(2)}) async-start(bf16[8,32,3584]{2,1,0:T(8,128)(2,1)} %bitcast.127), calls=%async_computation.11 | async-start | bytes 3670016 | tf_op jit(solution)/shard_map/all_to_all | solution.py:106
  365.1 6.0 %copy-start.16 = (bf16[256,1024]{1,0:T(8,128)(2,1)S(1)}, bf16[256,1024]{1,0:T(8,128)(2,1)}, u32[]{:S(2)}) copy-start(bf16[256,1024]{1,0:T(8,128)(2,1)} %get-tuple-element.12) | copy-start | bytes 1572868
  388.9 4.5 copy-start.9
  388.9 28.3 %all-to-all-start.15 = ((bf16[8,32,3584]{2,1,0:T(8,128)(2,1)}), bf16[8,32,3584]{2,1,0:T(8,128)(2,1)}, u32[]{:S(2)}, u32[]{:S(2)}) async-start(bf16[8,32,3584]{2,1,0:T(8,128)(2,1)} %bitcast.125), calls=%async_computation.15 | async-start | bytes 3670016 | tf_op jit(solution)/shard_map/all_to_all | solution.py:106
  393.4 6.0 %copy-start.15 = (bf16[256,1024]{1,0:T(8,128)(2,1)S(1)}, bf16[256,1024]{1,0:T(8,128)(2,1)}, u32[]{:S(2)}) copy-start(bf16[256,1024]{1,0:T(8,128)(2,1)} %get-tuple-element.10) | copy-start | bytes 1572868
  417.2 28.2 %all-to-all-start.3 = ((bf16[8,32,3584]{2,1,0:T(8,128)(2,1)}), bf16[8,32,3584]{2,1,0:T(8,128)(2,1)}, u32[]{:S(2)}, u32[]{:S(2)}) async-start(bf16[8,32,3584]{2,1,0:T(8,128)(2,1)} %bitcast.124), calls=%async_computation.3 | async-start | bytes 3670016 | tf_op jit(solution)/shard_map/all_to_all | solution.py:106
  422.0 39.6 %collective-permute-start.2 = (bf16[128,3584]{1,0:T(8,128)(2,1)S(1)}, bf16[128,3584]{1,0:T(8,128)(2,1)}, u32[]{:S(2)}, u32[]{:S(2)}) collective-permute-start(bf16[128,3584]{1,0:T(8,128)(2,1)S(1)} %convolution_convert_fusion.14), channel_id=1, source_target_pairs={{0,24},{8,0},{16,8},{24,16},{1,25},{9,1},{17,9},{25,17},{2,26},{10... | collective-permute-start | bytes 2752520 | tf_op jit(solution)/shard_map/ppermute | solution.py:47
  442.7 76.3 %collective-permute-start.5 = (bf16[128,3584]{1,0:T(8,128)(2,1)S(1)}, bf16[128,3584]{1,0:T(8,128)(2,1)}, u32[]{:S(2)}, u32[]{:S(2)}) collective-permute-start(bf16[128,3584]{1,0:T(8,128)(2,1)S(1)} %convolution_convert_fusion.13), channel_id=1, source_target_pairs={{0,16},{8,24},{16,0},{24,8},{1,17},{9,25},{17,1},{25,9},{2,18},{10... | collective-permute-start | bytes 2752520 | tf_op jit(solution)/shard_map/ppermute | solution.py:47
  444.7 74.3 %collective-permute-start.8 = (bf16[128,3584]{1,0:T(8,128)(2,1)S(1)}, bf16[128,3584]{1,0:T(8,128)(2,1)}, u32[]{:S(2)}, u32[]{:S(2)}) collective-permute-start(bf16[128,3584]{1,0:T(8,128)(2,1)S(1)} %convolution_convert_fusion.12), channel_id=1, source_target_pairs={{0,8},{8,16},{16,24},{24,0},{1,9},{9,17},{17,25},{25,1},{2,10},{10... | collective-permute-start | bytes 2752520 | tf_op jit(solution)/shard_map/ppermute | solution.py:47

commit v4 on v3

--- a/solution.py
+++ b/solution.py
@@ -68,49 +68,83 @@
     )
     row_range = jnp.arange(chunk_rows, dtype=jnp.int32)
 
-    total = None
+    sources = [(node_here - step) % n_node for step in range(n_node)]
+    dispatch = []
+    send_gate = []
     for step in range(n_node):
-        source = (node_here - step) % n_node
-        chunk_x = shift(hidden_in, n_node, step)
-        chunk_dy = shift(out_grad, n_node, step)
-        chunk_pos = lax.dynamic_index_in_dim(position, source, 0, keepdims=False)
+        chunk_pos = lax.dynamic_index_in_dim(position, sources[step], 0, keepdims=False)
         hits = (
             chunk_pos.reshape(tok, TOPK)[:, :, None] == row_range[None, None, :]
         ).astype(jnp.bfloat16)
-        dispatch = jnp.sum(hits, axis=1)
-        chunk_weight = lax.dynamic_index_in_dim(weight, source, 0, keepdims=False)
-        send_gate = jnp.einsum(
-            "tk,tkr->r", chunk_weight, hits, preferred_element_type=jnp.float32
-        ).astype(jnp.bfloat16)
+        dispatch.append(jnp.sum(hits, axis=1))
+        chunk_weight = lax.dynamic_index_in_dim(weight, sources[step], 0, keepdims=False)
+        send_gate.append(
+            jnp.einsum("tk,tkr->r", chunk_weight, hits, preferred_element_type=jnp.float32)
+            .astype(jnp.bfloat16)
+            .reshape(n_local, capacity)
+        )
 
-        recv_x = lax.all_to_all(
-            select_rows(dispatch, chunk_x).reshape(n_local, capacity, model_width),
-            "local", 0, 0, tiled=True,
+    def spread(rows):
+        return lax.all_to_all(
+            rows.reshape(n_local, capacity, model_width), "local", 0, 0, tiled=True
         )
-        recv_dy = lax.all_to_all(
-            select_rows(dispatch, chunk_dy).reshape(n_local, capacity, model_width),
-            "local", 0, 0, tiled=True,
+
+    def fetch(step, previous):
+        return shift(previous[0], n_node, 1), shift(previous[1], n_node, 1)
+
+    def send(step, chunk):
+        return (
+            spread(select_rows(dispatch[step], chunk[0])),
+            spread(select_rows(dispatch[step], chunk[1])),
+            lax.all_to_all(send_gate[step], "local", 0, 0, tiled=True),
         )
-        recv_gate = lax.all_to_all(
-            send_gate.reshape(n_local, capacity), "local", 0, 0, tiled=True
-        )
-        saved = lax.dynamic_slice_in_dim(gate_saved, source * chunk_rows, chunk_rows, 0)
-        contrib = expert_backward(
-            recv_x.reshape(chunk_rows, model_width),
-            recv_dy.reshape(chunk_rows, model_width),
-            recv_gate.reshape(chunk_rows),
+
+    def compute(step, received):
+        saved = lax.dynamic_slice_in_dim(gate_saved, sources[step] * chunk_rows, chunk_rows, 0)
+        return expert_backward(
+            received[0].reshape(chunk_rows, model_width),
+            received[1].reshape(chunk_rows, model_width),
+            received[2].reshape(chunk_rows),
             saved,
             weight_in,
             weight_out,
         )
-        returned = lax.all_to_all(
-            contrib.reshape(n_local, capacity, model_width), "local", 0, 0, tiled=True
-        ).reshape(chunk_rows, model_width)
-        node_sum = jnp.dot(dispatch, returned, preferred_element_type=jnp.float32).astype(
+
+    def gather_back(step, contrib):
+        returned = spread(contrib).reshape(chunk_rows, model_width)
+        return jnp.dot(dispatch[step], returned, preferred_element_type=jnp.float32).astype(
             jnp.bfloat16
         )
-        home = shift(node_sum, n_node, -step).astype(jnp.float32)
-        total = home if total is None else total + home
+
+    def send_home(step, node_sum):
+        return shift(node_sum, n_node, -step)
+
+    chunks = {0: (hidden_in, out_grad)}
+    received = {}
+    contribs = {}
+    sums = {}
+    homes = {}
+    for slot in range(-1, n_node + 2):
+        produced = {}
+        if 0 < slot + 2 < n_node:
+            produced["chunk", slot + 2] = fetch(slot + 2, chunks[slot + 1])
+        if 0 <= slot + 1 < n_node:
+            produced["received", slot + 1] = send(slot + 1, chunks[slot + 1])
+        if 0 <= slot < n_node:
+            produced["contrib", slot] = compute(slot, received[slot])
+        if 0 <= slot - 1 < n_node:
+            produced["sum", slot - 1] = gather_back(slot - 1, contribs[slot - 1])
+        if 0 <= slot - 2 < n_node:
+            produced["home", slot - 2] = send_home(slot - 2, sums[slot - 2])
+        keys = list(produced)
+        values = lax.optimization_barrier([produced[key] for key in keys])
+        for (kind, step), value in zip(keys, values):
+            {"chunk": chunks, "received": received, "contrib": contribs, "sum": sums,
+             "home": homes}[kind][step] = value
+
+    total = homes[0].astype(jnp.float32)
+    for step in range(1, n_node):
+        total = total + homes[step].astype(jnp.float32)
     return total.astype(jnp.bfloat16)
 
 

time: 533 us -> 465 us (0.87)
  waiting for transfers between devices: 274 us -> 228 us
  starting transfers between devices: 94.4 us -> 73.3 us
    ppermute x9, waiting for transfers between devices: 215 us -> 60.2 us  [shift(): lax.ppermute(value, 'node', [(i, (i + step) % n_node) for i in range(n_no...]
    all_to_all x16, waiting for transfers between devices: 59 us -> 168 us  [the longest x12 162 us: spread(): lax.all_to_all(rows.reshape(n_local, capacity, model_width), 'local', 0,...]
    ppermute x9, starting transfers between devices: 29.6 us -> 7.79 us  [shift(): lax.ppermute(value, 'node', [(i, (i + step) % n_node) for i in range(n_no...]
  transfers between devices with their start and end apart: 25 -> 25, of which waited for: 19 -> 16; matrix products, arithmetic and copies ran while one was open for 27% -> 31% of each run, Pallas kernels for 0% -> 0%
where the time goes in v4:
time: 465 us; the launch traced here: 456 us
  waiting for transfers between devices  228 us (49%)
  matrix products  141 us (30%)
  starting transfers between devices  73.3 us (16%)
  local copies, waits for them, and re-layouts  7.46 us (2%)
  other arithmetic  5.29 us (1%)
    all_to_all x12, waiting for transfers between devices, spread(): lax.all_to_all(rows.reshape(n_local, capacity, model_width), 'local', 0,...  162 us
    dot_general x4, matrix products, expert_backward(): lax.dot_general(grad_pre, weight_in, (((1,), (1,)), ((), ())), preferred_...  64.5 us
    ppermute x9, waiting for transfers between devices, shift(): lax.ppermute(value, 'node', [(i, (i + step) % n_node) for i in range(n_no...  60.2 us
    all_to_all x12, starting transfers between devices, spread(): lax.all_to_all(rows.reshape(n_local, capacity, model_width), 'local', 0,...  49.9 us
    dot_general x4, matrix products, expert_backward(): lax.dot_general(rows_dy, weight_out, (((1,), (1,)), ((), ())), preferred_...  25.1 us
    dot_general x4, matrix products, expert_backward(): jnp.dot(rows_x, weight_in[:, FF:], preferred_element_type=jnp.float32)  24.4 us
    dot_general x8, matrix products, select_rows(): lax.dot_general(onehot, rows, (((0,), (0,)), ((), ())), preferred_element...  21.4 us
    all_to_all x4, starting transfers between devices, send(): lax.all_to_all(send_gate[step], 'local', 0, 0, tiled=True)  15.6 us
  transfers between devices with their start and end apart: 25, of which 16 were waited for; matrix products, arithmetic and copies ran while one was open for 31% of the time, Pallas kernels for 0%

profile of v4, /device:TPU:0, one launch (start us, length us, event | category | flops | bytes accessed | tf_op | source)
XLA Modules:
  0.0 456.4 jit_solution(3131892255789235519)
XLA Ops:
  0.0 0.7 multiply_convert_fusion
  0.9 0.8 copy.14
  3.2 0.7 all_to_all.92
  3.8 5.2 %all-to-all-start.2 = ((bf16[8,1,32]{2,1,0:T(2,128)(2,1)}), bf16[8,1,32]{2,1,0:T(2,128)(2,1)S(1)}, u32[]{:S(2)}, u32[]{:S(2)}) async-start(bf16[8,1,32]{2,1,0:T(2,128)(2,1)} %all_to_all.92), calls=%async_computation.2 | async-start | bytes 8192 | tf_op jit(solution)/shard_map/all_to_all | solution.py:99
  9.4 1.9 convolution_convert_fusion.10
  11.3 2.2 all-to-all-done.2
  13.6 3.7 all-to-all-start.1
  17.3 1.9 convolution_convert_fusion.11
  19.2 21.9 %all-to-all-done.1 = bf16[8,32,3584]{2,1,0:T(8,128)(2,1)S(1)} async-done(((bf16[8,32,3584]{2,1,0:T(8,128)(2,1)}), bf16[8,32,3584]{2,1,0:T(8,128)(2,1)S(1)}, u32[]{:S(2)}, u32[]{:S(2)}) %all-to-all-start.1) | async-done | bytes 1835040 | tf_op jit(solution)/shard_map/all_to_all | solution.py:88
  41.1 1.2 copy-done.1
  42.3 4.3 all-to-all-start
  46.7 1.6 collective-permute-start
  48.3 1.6 collective-permute-start.1
  51.6 18.9 %all-to-all-done = bf16[8,32,3584]{2,1,0:T(8,128)(2,1)} async-done(((bf16[8,32,3584]{2,1,0:T(8,128)(2,1)}), bf16[8,32,3584]{2,1,0:T(8,128)(2,1)}, u32[]{:S(2)}, u32[]{:S(2)}) %all-to-all-start) | async-done | bytes 1835040 | tf_op jit(solution)/shard_map/all_to_all | solution.py:88
  70.5 3.3 all-to-all-start.5
  73.9 17.0 %collective-permute-done.1 = bf16[128,3584]{1,0:T(8,128)(2,1)S(1)} collective-permute-done((bf16[128,3584]{1,0:T(8,128)(2,1)}, bf16[128,3584]{1,0:T(8,128)(2,1)S(1)}, u32[]{:S(2)}, u32[]{:S(2)}) %collective-permute-start.1) | collective-permute-done | bytes 917536 | tf_op jit(solution)/shard_map/ppermute | solution.py:47
  90.8 1.9 convolution_convert_fusion.9
  92.7 3.9 all-to-all-start.3
  98.0 1.3 collective-permute-start.3
  99.3 3.2 convolution_convert_fusion.8
  102.5 17.9 %all-to-all-done.3 = bf16[8,32,3584]{2,1,0:T(8,128)(2,1)S(1)} async-done(((bf16[8,32,3584]{2,1,0:T(8,128)(2,1)}), bf16[8,32,3584]{2,1,0:T(8,128)(2,1)S(1)}, u32[]{:S(2)}, u32[]{:S(2)}) %all-to-all-start.3) | async-done | bytes 1835040 | tf_op jit(solution)/shard_map/all_to_all | solution.py:88
  120.5 1.2 copy-done
  121.7 4.3 all-to-all-start.4
  126.0 5.8 %fusion.93 = (bf16[256,1024]{1,0:T(8,128)(2,1)S(1)}, f32[256,1024]{1,0:T(8,128)S(1)}) fusion(bf16[1024,1024]{1,0:T(8,128)(2,1)} %param.11, s32[]{:T(128)S(6)} %select_n.73, f32[256]{0:T(256)S(1)} %reshape.157, bf16[256,3584]{1,0:T(8,128)(2,1)} %bitcast.146, bf16[1,1024,3584]{2,1,0:T(8,128)(2,1)} %param.13), kind=kOutput, calls=%fused_computation.76 | convolution fusion | flops 1881145344 | bytes 11273220 | tf_op jit(solution)/shard_map/dot_general | solution.py:22
  131.8 5.9 %fusion.67 = bf16[256,1024]{1,0:T(8,128)(2,1)S(1)} fusion(f32[256,1024]{1,0:T(8,128)S(1)} %get-tuple-element.72, bf16[256,3584]{1,0:T(8,128)(2,1)} %bitcast.14, bf16[3584,2048]{1,0:T(8,128)(2,1)} %bitcast.155, bf16[1024,1024]{1,0:T(8,128)(2,1)} %param.11, s32[]{:T(128)S(6)} %select_n.73), kind=kOutput, calls=%fused_computation.64 | convolution fusion | flops 1881931776 | bytes 11272196 | tf_op jit(solution)/shard_map/dot_general | solution.py:21
  137.8 12.1 %all-to-all-done.4 = bf16[8,32,3584]{2,1,0:T(8,128)(2,1)} async-done(((bf16[8,32,3584]{2,1,0:T(8,128)(2,1)}), bf16[8,32,3584]{2,1,0:T(8,128)(2,1)}, u32[]{:S(2)}, u32[]{:S(2)}) %all-to-all-start.4) | async-done | bytes 1835040 | tf_op jit(solution)/shard_map/all_to_all | solution.py:88
  149.8 3.8 all-to-all-start.8
  153.7 16.1 %convolution_convert_fusion.7 = bf16[256,3584]{1,0:T(8,128)(2,1)} fusion(bf16[256,1024]{1,0:T(8,128)(2,1)S(1)} %get-tuple-element.71, bf16[256,1024]{1,0:T(8,128)(2,1)S(1)} %fusion.67, bf16[1,3584,2048]{2,1,0:T(8,128)(2,1)} %param.12), kind=kOutput, calls=%fused_computation.15 | convolution fusion | flops 3761111040 | bytes 17563648 | tf_op jit(solution)/shard_map/dot_general | solution.py:31
  169.8 4.2 all-to-all-start.9
  174.4 3.2 convolution_convert_fusion.6
  177.5 20.3 %all-to-all-done.9 = bf16[8,32,3584]{2,1,0:T(8,128)(2,1)S(1)} async-done(((bf16[8,32,3584]{2,1,0:T(8,128)(2,1)}), bf16[8,32,3584]{2,1,0:T(8,128)(2,1)S(1)}, u32[]{:S(2)}, u32[]{:S(2)}) %all-to-all-start.9) | async-done | bytes 1835040 | tf_op jit(solution)/shard_map/all_to_all | solution.py:88
  197.8 4.3 all-to-all-start.6
  203.6 1.3 collective-permute-start.5
  204.9 3.1 convolution_convert_fusion.5
  208.0 6.7 %fusion.99 = (bf16[256,1024]{1,0:T(8,128)(2,1)S(1)}, f32[256,1024]{1,0:T(8,128)}) fusion(bf16[1024,1024]{1,0:T(8,128)(2,1)} %param.11, s32[]{:T(128)S(6)} %select_n.76, f32[256]{0:T(256)S(1)} %reshape.158, bf16[256,3584]{1,0:T(8,128)(2,1)} %bitcast.21, bf16[1,1024,3584]{2,1,0:T(8,128)(2,1)} %param.13), kind=kOutput, calls=%fused_computation.82 | convolution fusion | flops 1881145344 | bytes 11273220 | tf_op jit(solution)/shard_map/dot_general | solution.py:22
  214.7 11.2 %all-to-all-done.6 = bf16[8,32,3584]{2,1,0:T(8,128)(2,1)} async-done(((bf16[8,32,3584]{2,1,0:T(8,128)(2,1)}), bf16[8,32,3584]{2,1,0:T(8,128)(2,1)}, u32[]{:S(2)}, u32[]{:S(2)}) %all-to-all-start.6) | async-done | bytes 1835040 | tf_op jit(solution)/shard_map/all_to_all | solution.py:88
  226.0 4.5 all-to-all-start.7
  230.5 6.3 %fusion.70 = bf16[256,1024]{1,0:T(8,128)(2,1)S(1)} fusion(f32[256,1024]{1,0:T(8,128)} %get-tuple-element.74, bf16[256,3584]{1,0:T(8,128)(2,1)} %bitcast.145, bf16[3584,2048]{1,0:T(8,128)(2,1)} %bitcast.156, bf16[1024,1024]{1,0:T(8,128)(2,1)} %param.11, s32[]{:T(128)S(6)} %select_n.76), kind=kOutput, calls=%fused_computation.65 | convolution fusion | flops 1881931776 | bytes 11272196 | tf_op jit(solution)/shard_map/dot_general | solution.py:21
  236.8 16.1 %convolution_convert_fusion.4 = bf16[256,3584]{1,0:T(8,128)(2,1)} fusion(bf16[256,1024]{1,0:T(8,128)(2,1)S(1)} %get-tuple-element.73, bf16[256,1024]{1,0:T(8,128)(2,1)S(1)} %fusion.70, bf16[1,3584,2048]{2,1,0:T(8,128)(2,1)} %param.12), kind=kOutput, calls=%fused_computation.12 | convolution fusion | flops 3761111040 | bytes 17563648 | tf_op jit(solution)/shard_map/dot_general | solution.py:31
  252.9 1.4 all-to-all-done.7
  254.3 3.3 all-to-all-start.12
  258.1 4.1 all-to-all-done.12
  262.2 3.6 all-to-all-start.13
  266.2 3.2 convolution_convert_fusion.3
  269.3 20.2 %all-to-all-done.13 = bf16[8,32,3584]{2,1,0:T(8,128)(2,1)S(1)} async-done(((bf16[8,32,3584]{2,1,0:T(8,128)(2,1)}), bf16[8,32,3584]{2,1,0:T(8,128)(2,1)S(1)}, u32[]{:S(2)}, u32[]{:S(2)}) %all-to-all-start.13) | async-done | bytes 1835040 | tf_op jit(solution)/shard_map/all_to_all | solution.py:88
  289.5 4.3 all-to-all-start.10
  294.0 3.1 convolution_convert_fusion.2
  297.1 6.7 %fusion.105 = (bf16[256,1024]{1,0:T(8,128)(2,1)S(1)}, f32[256,1024]{1,0:T(8,128)}) fusion(bf16[1024,1024]{1,0:T(8,128)(2,1)} %param.11, s32[]{:T(128)S(6)} %select_n.77, f32[256]{0:T(256)S(1)} %reshape.159, bf16[256,3584]{1,0:T(8,128)(2,1)} %bitcast.30, bf16[1,1024,3584]{2,1,0:T(8,128)(2,1)} %param.13), kind=kOutput, calls=%fused_computation.88 | convolution fusion | flops 1881145344 | bytes 11273220 | tf_op jit(solution)/shard_map/dot_general | solution.py:22
  303.8 13.9 %all-to-all-done.10 = bf16[8,32,3584]{2,1,0:T(8,128)(2,1)} async-done(((bf16[8,32,3584]{2,1,0:T(8,128)(2,1)}), bf16[8,32,3584]{2,1,0:T(8,128)(2,1)}, u32[]{:S(2)}, u32[]{:S(2)}) %all-to-all-start.10) | async-done | bytes 1835040 | tf_op jit(solution)/shard_map/all_to_all | solution.py:88
  317.7 4.5 all-to-all-start.11
  322.2 6.2 %fusion.73 = bf16[256,1024]{1,0:T(8,128)(2,1)S(1)} fusion(f32[256,1024]{1,0:T(8,128)} %get-tuple-element.76, bf16[256,3584]{1,0:T(8,128)(2,1)} %bitcast.31, bf16[3584,2048]{1,0:T(8,128)(2,1)} %bitcast.157, bf16[1024,1024]{1,0:T(8,128)(2,1)} %param.11, s32[]{:T(128)S(6)} %select_n.77), kind=kOutput, calls=%fused_computation.66 | convolution fusion | flops 1881931776 | bytes 11272196 | tf_op jit(solution)/shard_map/dot_general | solution.py:21
  328.4 16.1 %convolution_convert_fusion.1 = bf16[256,3584]{1,0:T(8,128)(2,1)} fusion(bf16[256,1024]{1,0:T(8,128)(2,1)S(1)} %get-tuple-element.75, bf16[256,1024]{1,0:T(8,128)(2,1)S(1)} %fusion.73, bf16[1,3584,2048]{2,1,0:T(8,128)(2,1)} %param.12), kind=kOutput, calls=%fused_computation.9 | convolution fusion | flops 3761111040 | bytes 17563648 | tf_op jit(solution)/shard_map/dot_general | solution.py:31
  344.6 1.4 convolution_convert_fusion.14
  346.2 4.1 all-to-all-start.14
  350.2 2.0 collective-permute-start.6
  352.2 5.8 %fusion.111 = (bf16[256,1024]{1,0:T(8,128)(2,1)S(1)}, f32[256,1024]{1,0:T(8,128)S(1)}) fusion(bf16[1024,1024]{1,0:T(8,128)(2,1)} %param.11, s32[]{:T(128)S(6)} %select_n.78, f32[256]{0:T(256)S(1)} %reshape.160, bf16[256,3584]{1,0:T(8,128)(2,1)} %bitcast.34, bf16[1,1024,3584]{2,1,0:T(8,128)(2,1)} %param.13), kind=kOutput, calls=%fused_computation.94 | convolution fusion | flops 1881145344 | bytes 11273220 | tf_op jit(solution)/shard_map/dot_general | solution.py:22
  358.0 5.9 %fusion.76 = bf16[256,1024]{1,0:T(8,128)(2,1)S(1)} fusion(f32[256,1024]{1,0:T(8,128)S(1)} %get-tuple-element.78, bf16[256,3584]{1,0:T(8,128)(2,1)} %bitcast.35, bf16[3584,2048]{1,0:T(8,128)(2,1)} %bitcast.158, bf16[1024,1024]{1,0:T(8,128)(2,1)} %param.11, s32[]{:T(128)S(6)} %select_n.78), kind=kOutput, calls=%fused_computation.67 | convolution fusion | flops 1881931776 | bytes 11272196 | tf_op jit(solution)/shard_map/dot_general | solution.py:21
  364.0 16.1 %convolution_convert_fusion = bf16[256,3584]{1,0:T(8,128)(2,1)} fusion(bf16[256,1024]{1,0:T(8,128)(2,1)S(1)} %get-tuple-element.77, bf16[256,1024]{1,0:T(8,128)(2,1)S(1)} %fusion.76, bf16[1,3584,2048]{2,1,0:T(8,128)(2,1)} %param.12), kind=kOutput, calls=%fused_computation.8 | convolution fusion | flops 3761111040 | bytes 17563648 | tf_op jit(solution)/shard_map/dot_general | solution.py:31
  380.1 1.3 convolution_convert_fusion.13
  381.5 4.2 all-to-all-start.15
  385.7 23.8 %all-to-all-done.15 = bf16[8,32,3584]{2,1,0:T(8,128)(2,1)S(1)} async-done(((bf16[8,32,3584]{2,1,0:T(8,128)(2,1)}), bf16[8,32,3584]{2,1,0:T(8,128)(2,1)S(1)}, u32[]{:S(2)}, u32[]{:S(2)}) %all-to-all-start.15) | async-done | bytes 1835040 | tf_op jit(solution)/shard_map/all_to_all | solution.py:88
  409.9 19.1 %collective-permute-done.7 = bf16[128,3584]{1,0:T(8,128)(2,1)} collective-permute-done((bf16[128,3584]{1,0:T(8,128)(2,1)}, bf16[128,3584]{1,0:T(8,128)(2,1)}, u32[]{:S(2)}, u32[]{:S(2)}) %collective-permute-start.7) | collective-permute-done | bytes 917536 | tf_op jit(solution)/shard_map/ppermute | solution.py:47
  429.1 24.1 %collective-permute-done.8 = bf16[128,3584]{1,0:T(8,128)(2,1)S(1)} collective-permute-done((bf16[128,3584]{1,0:T(8,128)(2,1)S(1)}, bf16[128,3584]{1,0:T(8,128)(2,1)S(1)}, u32[]{:S(2)}, u32[]{:S(2)}) %collective-permute-start.8) | collective-permute-done | bytes 917536 | tf_op jit(solution)/shard_map/ppermute | solution.py:47
  453.2 2.9 add_convert_fusion
  (62 shorter events, 8.5 us)
Async XLA Ops:
  1.9 7.5 %copy-start.3 = (bf16[128,3584]{1,0:T(8,128)(2,1)S(1)}, bf16[128,3584]{1,0:T(8,128)(2,1)}, u32[]{:S(2)}) copy-start(bf16[128,3584]{1,0:T(8,128)(2,1)} %param.8) | copy-start | bytes 2752516
  3.8 9.8 %all-to-all-start.2 = ((bf16[8,1,32]{2,1,0:T(2,128)(2,1)}), bf16[8,1,32]{2,1,0:T(2,128)(2,1)S(1)}, u32[]{:S(2)}, u32[]{:S(2)}) async-start(bf16[8,1,32]{2,1,0:T(2,128)(2,1)} %all_to_all.92), calls=%async_computation.2 | async-start | bytes 8192 | tf_op jit(solution)/shard_map/all_to_all | solution.py:99
  13.6 3.7 copy-start.2
  13.6 27.5 %all-to-all-start.1 = ((bf16[8,32,3584]{2,1,0:T(8,128)(2,1)}), bf16[8,32,3584]{2,1,0:T(8,128)(2,1)S(1)}, u32[]{:S(2)}, u32[]{:S(2)}) async-start(bf16[8,32,3584]{2,1,0:T(8,128)(2,1)} %bitcast.3), calls=%async_computation.1 | async-start | bytes 3670016 | tf_op jit(solution)/shard_map/all_to_all | solution.py:88
  41.1 1.2 copy-start.1
  42.3 28.2 %all-to-all-start = ((bf16[8,32,3584]{2,1,0:T(8,128)(2,1)}), bf16[8,32,3584]{2,1,0:T(8,128)(2,1)}, u32[]{:S(2)}, u32[]{:S(2)}) async-start(bf16[8,32,3584]{2,1,0:T(8,128)(2,1)} %bitcast.2), calls=%async_computation | async-start | bytes 3670016 | tf_op jit(solution)/shard_map/all_to_all | solution.py:88
  46.7 27.2 %collective-permute-start = (bf16[128,3584]{1,0:T(8,128)(2,1)S(1)}, bf16[128,3584]{1,0:T(8,128)(2,1)S(1)}, u32[]{:S(2)}, u32[]{:S(2)}) collective-permute-start(bf16[128,3584]{1,0:T(8,128)(2,1)S(1)} %copy-done.2), channel_id=1, source_target_pairs={{0,8},{8,16},{16,24},{24,0},{1,9},{9,17},{17,25},{25,1},{2,10},{10... | collective-permute-start | bytes 2752520 | tf_op jit(solution)/shard_map/ppermute | solution.py:47
  48.3 42.5 %collective-permute-start.1 = (bf16[128,3584]{1,0:T(8,128)(2,1)}, bf16[128,3584]{1,0:T(8,128)(2,1)S(1)}, u32[]{:S(2)}, u32[]{:S(2)}) collective-permute-start(bf16[128,3584]{1,0:T(8,128)(2,1)} %param.8), channel_id=1, source_target_pairs={{0,8},{8,16},{16,24},{24,0},{1,9},{9,17},{17,25},{25,1},{2,10},{10... | collective-permute-start | bytes 2752520 | tf_op jit(solution)/shard_map/ppermute | solution.py:47
  70.5 22.2 %all-to-all-start.5 = ((bf16[8,1,32]{2,1,0:T(2,128)(2,1)}), bf16[8,1,32]{2,1,0:T(2,128)(2,1)S(1)}, u32[]{:S(2)}, u32[]{:S(2)}) async-start(bf16[8,1,32]{2,1,0:T(2,128)(2,1)} %all_to_all.93), calls=%async_computation.5 | async-start | bytes 8192 | tf_op jit(solution)/shard_map/all_to_all | solution.py:99
  73.9 18.9 %copy-start.4 = (bf16[128,3584]{1,0:T(8,128)(2,1)}, bf16[128,3584]{1,0:T(8,128)(2,1)S(1)}, u32[]{:S(2)}) copy-start(bf16[128,3584]{1,0:T(8,128)(2,1)S(1)} %collective-permute-done) | copy-start | bytes 2752516
  90.8 1.9 copy-start.5
  92.7 27.7 %all-to-all-start.3 = ((bf16[8,32,3584]{2,1,0:T(8,128)(2,1)}), bf16[8,32,3584]{2,1,0:T(8,128)(2,1)S(1)}, u32[]{:S(2)}, u32[]{:S(2)}) async-start(bf16[8,32,3584]{2,1,0:T(8,128)(2,1)} %bitcast.7), calls=%async_computation.3 | async-start | bytes 3670016 | tf_op jit(solution)/shard_map/all_to_all | solution.py:88
  98.0 71.8 %collective-permute-start.2 = (bf16[128,3584]{1,0:T(8,128)(2,1)}, bf16[128,3584]{1,0:T(8,128)(2,1)}, u32[]{:S(2)}, u32[]{:S(2)}) collective-permute-start(bf16[128,3584]{1,0:T(8,128)(2,1)} %copy-done.4), channel_id=1, source_target_pairs={{0,8},{8,16},{16,24},{24,0},{1,9},{9,17},{17,25},{25,1},{2,10},{10... | collective-permute-start | bytes 2752520 | tf_op jit(solution)/shard_map/ppermute | solution.py:47
  98.0 71.7 %collective-permute-start.3 = (bf16[128,3584]{1,0:T(8,128)(2,1)}, bf16[128,3584]{1,0:T(8,128)(2,1)}, u32[]{:S(2)}, u32[]{:S(2)}) collective-permute-start(bf16[128,3584]{1,0:T(8,128)(2,1)} %copy-done.5), channel_id=1, source_target_pairs={{0,8},{8,16},{16,24},{24,0},{1,9},{9,17},{17,25},{25,1},{2,10},{10... | collective-permute-start | bytes 2752520 | tf_op jit(solution)/shard_map/ppermute | solution.py:47
  120.5 1.2 copy-start
  121.7 28.2 %all-to-all-start.4 = ((bf16[8,32,3584]{2,1,0:T(8,128)(2,1)}), bf16[8,32,3584]{2,1,0:T(8,128)(2,1)}, u32[]{:S(2)}, u32[]{:S(2)}) async-start(bf16[8,32,3584]{2,1,0:T(8,128)(2,1)} %bitcast.8), calls=%async_computation.4 | async-start | bytes 3670016 | tf_op jit(solution)/shard_map/all_to_all | solution.py:88
  149.8 19.9 %all-to-all-start.8 = ((bf16[8,1,32]{2,1,0:T(2,128)(2,1)}), bf16[8,1,32]{2,1,0:T(2,128)(2,1)S(1)}, u32[]{:S(2)}, u32[]{:S(2)}) async-start(bf16[8,1,32]{2,1,0:T(2,128)(2,1)} %all_to_all.94), calls=%async_computation.8 | async-start | bytes 8192 | tf_op jit(solution)/shard_map/all_to_all | solution.py:99
  169.8 28.0 %all-to-all-start.9 = ((bf16[8,32,3584]{2,1,0:T(8,128)(2,1)}), bf16[8,32,3584]{2,1,0:T(8,128)(2,1)S(1)}, u32[]{:S(2)}, u32[]{:S(2)}) async-start(bf16[8,32,3584]{2,1,0:T(8,128)(2,1)} %bitcast.149), calls=%async_computation.9 | async-start | bytes 3670016 | tf_op jit(solution)/shard_map/all_to_all | solution.py:88
  197.8 28.2 %all-to-all-start.6 = ((bf16[8,32,3584]{2,1,0:T(8,128)(2,1)}), bf16[8,32,3584]{2,1,0:T(8,128)(2,1)}, u32[]{:S(2)}, u32[]{:S(2)}) async-start(bf16[8,32,3584]{2,1,0:T(8,128)(2,1)} %bitcast.139), calls=%async_computation.6 | async-start | bytes 3670016 | tf_op jit(solution)/shard_map/all_to_all | solution.py:88
  203.5 54.6 %collective-permute-start.4 = (bf16[128,3584]{1,0:T(8,128)(2,1)}, bf16[128,3584]{1,0:T(8,128)(2,1)}, u32[]{:S(2)}, u32[]{:S(2)}) collective-permute-start(bf16[128,3584]{1,0:T(8,128)(2,1)} %collective-permute-done.2), channel_id=1, source_target_pairs={{0,8},{8,16},{16,24},{24,0},{1,9},{9,17},{17,25},{25,1},{2,10},{10... | collective-permute-start | bytes 2752520 | tf_op jit(solution)/shard_map/ppermute | solution.py:47
  203.6 54.5 %collective-permute-start.5 = (bf16[128,3584]{1,0:T(8,128)(2,1)}, bf16[128,3584]{1,0:T(8,128)(2,1)}, u32[]{:S(2)}, u32[]{:S(2)}) collective-permute-start(bf16[128,3584]{1,0:T(8,128)(2,1)} %collective-permute-done.3), channel_id=1, source_target_pairs={{0,8},{8,16},{16,24},{24,0},{1,9},{9,17},{17,25},{25,1},{2,10},{10... | collective-permute-start | bytes 2752520 | tf_op jit(solution)/shard_map/ppermute | solution.py:47
  226.0 28.4 %all-to-all-start.7 = ((bf16[8,32,3584]{2,1,0:T(8,128)(2,1)}), bf16[8,32,3584]{2,1,0:T(8,128)(2,1)}, u32[]{:S(2)}, u32[]{:S(2)}) async-start(bf16[8,32,3584]{2,1,0:T(8,128)(2,1)} %bitcast.143), calls=%async_computation.7 | async-start | bytes 3670016 | tf_op jit(solution)/shard_map/all_to_all | solution.py:88
  254.3 7.8 %all-to-all-start.12 = ((bf16[8,1,32]{2,1,0:T(2,128)(2,1)}), bf16[8,1,32]{2,1,0:T(2,128)(2,1)S(1)}, u32[]{:S(2)}, u32[]{:S(2)}) async-start(bf16[8,1,32]{2,1,0:T(2,128)(2,1)} %all_to_all.95), calls=%async_computation.12 | async-start | bytes 8192 | tf_op jit(solution)/shard_map/all_to_all | solution.py:99
  262.2 27.4 %all-to-all-start.13 = ((bf16[8,32,3584]{2,1,0:T(8,128)(2,1)}), bf16[8,32,3584]{2,1,0:T(8,128)(2,1)S(1)}, u32[]{:S(2)}, u32[]{:S(2)}) async-start(bf16[8,32,3584]{2,1,0:T(8,128)(2,1)} %bitcast.147), calls=%async_computation.13 | async-start | bytes 3670016 | tf_op jit(solution)/shard_map/all_to_all | solution.py:88
  289.5 28.2 %all-to-all-start.10 = ((bf16[8,32,3584]{2,1,0:T(8,128)(2,1)}), bf16[8,32,3584]{2,1,0:T(8,128)(2,1)}, u32[]{:S(2)}, u32[]{:S(2)}) async-start(bf16[8,32,3584]{2,1,0:T(8,128)(2,1)} %bitcast.140), calls=%async_computation.10 | async-start | bytes 3670016 | tf_op jit(solution)/shard_map/all_to_all | solution.py:88
  317.7 28.4 %all-to-all-start.11 = ((bf16[8,32,3584]{2,1,0:T(8,128)(2,1)}), bf16[8,32,3584]{2,1,0:T(8,128)(2,1)}, u32[]{:S(2)}, u32[]{:S(2)}) async-start(bf16[8,32,3584]{2,1,0:T(8,128)(2,1)} %bitcast.142), calls=%async_computation.11 | async-start | bytes 3670016 | tf_op jit(solution)/shard_map/all_to_all | solution.py:88
  346.2 33.9 %all-to-all-start.14 = ((bf16[8,32,3584]{2,1,0:T(8,128)(2,1)}), bf16[8,32,3584]{2,1,0:T(8,128)(2,1)S(1)}, u32[]{:S(2)}, u32[]{:S(2)}) async-start(bf16[8,32,3584]{2,1,0:T(8,128)(2,1)} %bitcast.148), calls=%async_computation.14 | async-start | bytes 3670016 | tf_op jit(solution)/shard_map/all_to_all | solution.py:88
  350.2 31.2 %collective-permute-start.6 = (bf16[128,3584]{1,0:T(8,128)(2,1)}, bf16[128,3584]{1,0:T(8,128)(2,1)}, u32[]{:S(2)}, u32[]{:S(2)}) collective-permute-start(bf16[128,3584]{1,0:T(8,128)(2,1)} %convolution_convert_fusion.14), channel_id=1, source_target_pairs={{0,24},{8,0},{16,8},{24,16},{1,25},{9,1},{17,9},{25,17},{2,26},{10... | collective-permute-start | bytes 2752520 | tf_op jit(solution)/shard_map/ppermute | solution.py:47
  381.5 28.0 %all-to-all-start.15 = ((bf16[8,32,3584]{2,1,0:T(8,128)(2,1)}), bf16[8,32,3584]{2,1,0:T(8,128)(2,1)S(1)}, u32[]{:S(2)}, u32[]{:S(2)}) async-start(bf16[8,32,3584]{2,1,0:T(8,128)(2,1)} %bitcast.150), calls=%async_computation.15 | async-start | bytes 3670016 | tf_op jit(solution)/shard_map/all_to_all | solution.py:88
  385.7 43.4 %collective-permute-start.7 = (bf16[128,3584]{1,0:T(8,128)(2,1)}, bf16[128,3584]{1,0:T(8,128)(2,1)}, u32[]{:S(2)}, u32[]{:S(2)}) collective-permute-start(bf16[128,3584]{1,0:T(8,128)(2,1)} %convolution_convert_fusion.13), channel_id=1, source_target_pairs={{0,16},{8,24},{16,0},{24,8},{1,17},{9,25},{17,1},{25,9},{2,18},{10... | collective-permute-start | bytes 2752520 | tf_op jit(solution)/shard_map/ppermute | solution.py:47
  429.1 24.1 %collective-permute-start.8 = (bf16[128,3584]{1,0:T(8,128)(2,1)S(1)}, bf16[128,3584]{1,0:T(8,128)(2,1)S(1)}, u32[]{:S(2)}, u32[]{:S(2)}) collective-permute-start(bf16[128,3584]{1,0:T(8,128)(2,1)S(1)} %convolution_convert_fusion.12), channel_id=1, source_target_pairs={{0,8},{8,16},{16,24},{24,0},{1,9},{9,17},{17,25},{25,1},{2,10},{10... | collective-permute-start | bytes 2752520 | tf_op jit(solution)/shard_map/ppermute | solution.py:47

commit v5 on v4

--- a/solution.py
+++ b/solution.py
@@ -83,28 +83,26 @@
             .astype(jnp.bfloat16)
             .reshape(n_local, capacity)
         )
+    gates = lax.all_to_all(jnp.stack(send_gate, axis=1), "local", 0, 0, tiled=True)
 
     def spread(rows):
         return lax.all_to_all(
-            rows.reshape(n_local, capacity, model_width), "local", 0, 0, tiled=True
+            rows.reshape(n_local, capacity, rows.shape[-1]), "local", 0, 0, tiled=True
         )
 
     def fetch(step, previous):
-        return shift(previous[0], n_node, 1), shift(previous[1], n_node, 1)
+        return shift(previous, n_node, 1)
 
     def send(step, chunk):
-        return (
-            spread(select_rows(dispatch[step], chunk[0])),
-            spread(select_rows(dispatch[step], chunk[1])),
-            lax.all_to_all(send_gate[step], "local", 0, 0, tiled=True),
-        )
+        return spread(select_rows(dispatch[step], chunk))
 
     def compute(step, received):
         saved = lax.dynamic_slice_in_dim(gate_saved, sources[step] * chunk_rows, chunk_rows, 0)
+        rows = received.reshape(chunk_rows, 2 * model_width)
         return expert_backward(
-            received[0].reshape(chunk_rows, model_width),
-            received[1].reshape(chunk_rows, model_width),
-            received[2].reshape(chunk_rows),
+            rows[:, :model_width],
+            rows[:, model_width:],
+            gates[:, step].reshape(chunk_rows),
             saved,
             weight_in,
             weight_out,
@@ -119,7 +117,7 @@
     def send_home(step, node_sum):
         return shift(node_sum, n_node, -step)
 
-    chunks = {0: (hidden_in, out_grad)}
+    chunks = {0: jnp.concatenate([hidden_in, out_grad], axis=1)}
     received = {}
     contribs = {}
     sums = {}

time: 465 us -> 381 us (0.82)
  waiting for transfers between devices: 228 us -> 187 us
  starting transfers between devices: 73.3 us -> 43.7 us
  matrix products: 141 us -> 134 us
    all_to_all x16 -> x9, waiting for transfers between devices: 168 us -> 113 us  [the longest x8 113 us: spread(): lax.all_to_all(rows.reshape(n_local, capacity, rows.shape[-1]), 'local',...]
    all_to_all x16 -> x9, starting transfers between devices: 65.6 us -> 37.8 us  [the longest x8 34.5 us: spread(): lax.all_to_all(rows.reshape(n_local, capacity, rows.shape[-1]), 'local',...]
    ppermute x9 -> x6, waiting for transfers between devices: 60.2 us -> 74.1 us  [shift(): lax.ppermute(value, 'node', [(i, (i + step) % n_node) for i in range(n_no...]
    dot_general x8 -> x4, matrix products: 21.4 us -> 16.4 us  [select_rows(): lax.dot_general(onehot, rows, (((0,), (0,)), ((), ())), preferred_element...]
  transfers between devices with their start and end apart: 25 -> 15, of which waited for: 16 -> 10; matrix products, arithmetic and copies ran while one was open for 31% -> 36% of each run, Pallas kernels for 0% -> 0%
where the time goes in v5:
time: 381 us; the launch traced here: 375 us
  waiting for transfers between devices  187 us (49%)
  matrix products  134 us (35%)
  starting transfers between devices  43.7 us (11%)
  other arithmetic  4.64 us (1%)
  local copies, waits for them, and re-layouts  4.61 us (1%)
    all_to_all x8, waiting for transfers between devices, spread(): lax.all_to_all(rows.reshape(n_local, capacity, rows.shape[-1]), 'local',...  113 us
    ppermute x6, waiting for transfers between devices, shift(): lax.ppermute(value, 'node', [(i, (i + step) % n_node) for i in range(n_no...  74.1 us
    dot_general x4, matrix products, expert_backward(): lax.dot_general(grad_pre, weight_in, (((1,), (1,)), ((), ())), preferred_...  64.7 us
    all_to_all x8, starting transfers between devices, spread(): lax.all_to_all(rows.reshape(n_local, capacity, rows.shape[-1]), 'local',...  34.5 us
    dot_general x4, matrix products, expert_backward(): jnp.dot(rows_x, weight_in[:, FF:], preferred_element_type=jnp.float32)  23.7 us
    dot_general x4, matrix products, expert_backward(): lax.dot_general(rows_dy, weight_out, (((1,), (1,)), ((), ())), preferred_...  23.3 us
    dot_general x4, matrix products, select_rows(): lax.dot_general(onehot, rows, (((0,), (0,)), ((), ())), preferred_element...  16.4 us
  transfers between devices with their start and end apart: 15, of which 10 were waited for; matrix products, arithmetic and copies ran while one was open for 36% of the time, Pallas kernels for 0%

profile of v5, /device:TPU:0, one launch (start us, length us, event | category | flops | bytes accessed | tf_op | source)
XLA Modules:
  0.0 374.8 jit_solution(8208489508142383603)
XLA Ops:
  0.0 0.9 copy.11
  0.9 0.2 reshape.88
  1.1 0.6 fusion.133
  2.0 0.4 fusion.181
  2.5 1.3 constant_dynamic-update-slice_fusion
  3.7 2.9 convolution_convert_fusion.3
  6.7 5.3 %all-to-all-start = ((bf16[8,32,7168]{2,1,0:T(8,128)(2,1)}), bf16[8,32,7168]{2,1,0:T(8,128)(2,1)}, u32[]{:S(2)}, u32[]{:S(2)}) async-start(bf16[8,32,7168]{2,1,0:T(8,128)(2,1)} %bitcast.101), calls=%async_computation | async-start | bytes 7340032 | tf_op jit(solution)/shard_map/all_to_all | solution.py:89
  12.0 2.4 collective-permute-start
  14.4 0.1 copy.13
  14.5 0.1 copy.16
  14.7 0.1 copy.15
  14.8 0.1 copy.14
  15.0 0.4 fusion.173
  15.4 0.1 stack_reshape.14
  15.6 0.4 fusion.174
  16.1 0.1 stack_reshape.13
  16.2 0.4 fusion.176
  16.6 0.1 stack_reshape.12
  16.8 0.4 fusion.178
  17.2 0.1 stack_reshape.15
  17.3 0.6 copy.12
  17.9 0.4 fusion.182
  18.3 37.3 %all-to-all-done = bf16[8,32,7168]{2,1,0:T(8,128)(2,1)} async-done(((bf16[8,32,7168]{2,1,0:T(8,128)(2,1)}), bf16[8,32,7168]{2,1,0:T(8,128)(2,1)}, u32[]{:S(2)}, u32[]{:S(2)}) %all-to-all-start) | async-done | bytes 3670048 | tf_op jit(solution)/shard_map/all_to_all | solution.py:89
  55.6 3.3 all-to-all-start.2
  58.9 4.6 %convolution_convert_fusion.2 = bf16[256,7168]{1,0:T(8,128)(2,1)} fusion(bf16[128,256]{1,0:T(8,128)(2,1)S(1)} %fusion.182, bf16[128,7168]{1,0:T(8,128)(2,1)} %collective-permute-done), kind=kOutput, calls=%fused_computation.2 | convolution fusion | flops 471597056 | bytes 5570560 | tf_op jit(solution)/shard_map/dot_general | solution.py:38
  63.6 4.5 %all-to-all-start.1 = ((bf16[8,32,7168]{2,1,0:T(8,128)(2,1)}), bf16[8,32,7168]{2,1,0:T(8,128)(2,1)}, u32[]{:S(2)}, u32[]{:S(2)}) async-start(bf16[8,32,7168]{2,1,0:T(8,128)(2,1)} %bitcast.103), calls=%async_computation.1 | async-start | bytes 7340032 | tf_op jit(solution)/shard_map/all_to_all | solution.py:89
  68.2 2.8 collective-permute-start.1
  71.0 5.8 %fusion.141 = (bf16[256,1024]{1,0:T(8,128)(2,1)S(1)}, f32[256,1024]{1,0:T(8,128)S(1)}) fusion(bf16[1024,1024]{1,0:T(8,128)(2,1)} %param.11, s32[]{:T(128)S(6)} %select_n.75, f32[256]{0:T(256)S(1)} %reshape.105, bf16[1,1024,3584]{2,1,0:T(8,128)(2,1)} %param.13, bf16[256,7168]{1,0:T(8,128)(2,1)} %bitcast.4), kind=kOutput, calls=%fused_computation.80 | convolution fusion | flops 1881145344 | bytes 11273220 | tf_op jit(solution)/shard_map/dot_general | solution.py:22
  76.8 5.9 %fusion.107 = bf16[256,1024]{1,0:T(8,128)(2,1)S(1)} fusion(f32[256,1024]{1,0:T(8,128)S(1)} %get-tuple-element.54, bf16[3584,2048]{1,0:T(8,128)(2,1)} %bitcast.113, bf16[256,7168]{1,0:T(8,128)(2,1)} %bitcast.4, bf16[1024,1024]{1,0:T(8,128)(2,1)} %param.11, s32[]{:T(128)S(6)} %select_n.75), kind=kOutput, calls=%fused_computation.68 | convolution fusion | flops 1881931776 | bytes 11272196 | tf_op jit(solution)/shard_map/dot_general | solution.py:21
  82.7 16.2 %convolution_convert_fusion.7 = bf16[256,3584]{1,0:T(8,128)(2,1)} fusion(bf16[256,1024]{1,0:T(8,128)(2,1)S(1)} %get-tuple-element.53, bf16[256,1024]{1,0:T(8,128)(2,1)S(1)} %fusion.107, bf16[1,3584,2048]{2,1,0:T(8,128)(2,1)} %param.12), kind=kOutput, calls=%fused_computation.15 | convolution fusion | flops 3761111040 | bytes 17563648 | tf_op jit(solution)/shard_map/dot_general | solution.py:31
  99.0 14.9 %collective-permute-done.1 = bf16[128,7168]{1,0:T(8,128)(2,1)} collective-permute-done((bf16[128,7168]{1,0:T(8,128)(2,1)}, bf16[128,7168]{1,0:T(8,128)(2,1)}, u32[]{:S(2)}, u32[]{:S(2)}) %collective-permute-start.1) | collective-permute-done | bytes 1835040 | tf_op jit(solution)/shard_map/ppermute | solution.py:47
  113.9 3.9 %all-to-all-start.4 = ((bf16[8,32,3584]{2,1,0:T(8,128)(2,1)}), bf16[8,32,3584]{2,1,0:T(8,128)(2,1)S(1)}, u32[]{:S(2)}, u32[]{:S(2)}) async-start(bf16[8,32,3584]{2,1,0:T(8,128)(2,1)} %bitcast.112), calls=%async_computation.4 | async-start | bytes 3670016 | tf_op jit(solution)/shard_map/all_to_all | solution.py:89
  117.7 0.4 fusion.183
  118.2 4.4 %convolution_convert_fusion.1 = bf16[256,7168]{1,0:T(8,128)(2,1)} fusion(bf16[128,256]{1,0:T(8,128)(2,1)S(1)} %fusion.183, bf16[128,7168]{1,0:T(8,128)(2,1)} %collective-permute-done.1), kind=kOutput, calls=%fused_computation.1 | convolution fusion | flops 471597056 | bytes 5570560 | tf_op jit(solution)/shard_map/dot_general | solution.py:38
  122.6 19.0 %all-to-all-done.4 = bf16[8,32,3584]{2,1,0:T(8,128)(2,1)S(1)} async-done(((bf16[8,32,3584]{2,1,0:T(8,128)(2,1)}), bf16[8,32,3584]{2,1,0:T(8,128)(2,1)S(1)}, u32[]{:S(2)}, u32[]{:S(2)}) %all-to-all-start.4) | async-done | bytes 1835040 | tf_op jit(solution)/shard_map/all_to_all | solution.py:89
  141.6 4.5 %all-to-all-start.3 = ((bf16[8,32,7168]{2,1,0:T(8,128)(2,1)}), bf16[8,32,7168]{2,1,0:T(8,128)(2,1)}, u32[]{:S(2)}, u32[]{:S(2)}) async-start(bf16[8,32,7168]{2,1,0:T(8,128)(2,1)} %bitcast.104), calls=%async_computation.3 | async-start | bytes 7340032 | tf_op jit(solution)/shard_map/all_to_all | solution.py:89
  146.2 0.2 collective-permute-start.2
  146.4 5.8 %fusion.147 = (bf16[256,1024]{1,0:T(8,128)(2,1)S(1)}, f32[256,1024]{1,0:T(8,128)S(1)}) fusion(bf16[1024,1024]{1,0:T(8,128)(2,1)} %param.11, s32[]{:T(128)S(6)} %select_n.76, f32[256]{0:T(256)S(1)} %reshape.106, bf16[1,1024,3584]{2,1,0:T(8,128)(2,1)} %param.13, bf16[256,7168]{1,0:T(8,128)(2,1)} %bitcast.20), kind=kOutput, calls=%fused_computation.86 | convolution fusion | flops 1881145344 | bytes 11273220 | tf_op jit(solution)/shard_map/dot_general | solution.py:22
  152.2 5.9 %fusion.112 = bf16[256,1024]{1,0:T(8,128)(2,1)S(1)} fusion(f32[256,1024]{1,0:T(8,128)S(1)} %get-tuple-element.56, bf16[3584,2048]{1,0:T(8,128)(2,1)} %bitcast.114, bf16[256,7168]{1,0:T(8,128)(2,1)} %bitcast.20, bf16[1024,1024]{1,0:T(8,128)(2,1)} %param.11, s32[]{:T(128)S(6)} %select_n.76), kind=kOutput, calls=%fused_computation.69 | convolution fusion | flops 1881931776 | bytes 11272196 | tf_op jit(solution)/shard_map/dot_general | solution.py:21
  158.2 16.2 %convolution_convert_fusion.6 = bf16[256,3584]{1,0:T(8,128)(2,1)} fusion(bf16[256,1024]{1,0:T(8,128)(2,1)S(1)} %get-tuple-element.55, bf16[256,1024]{1,0:T(8,128)(2,1)S(1)} %fusion.112, bf16[1,3584,2048]{2,1,0:T(8,128)(2,1)} %param.12), kind=kOutput, calls=%fused_computation.14 | convolution fusion | flops 3761111040 | bytes 17563648 | tf_op jit(solution)/shard_map/dot_general | solution.py:31
  174.3 0.4 convolution_convert_fusion.11
  174.7 16.1 %collective-permute-done.2 = bf16[128,7168]{1,0:T(8,128)(2,1)} collective-permute-done((bf16[128,7168]{1,0:T(8,128)(2,1)}, bf16[128,7168]{1,0:T(8,128)(2,1)}, u32[]{:S(2)}, u32[]{:S(2)}) %collective-permute-start.2) | collective-permute-done | bytes 1835040 | tf_op jit(solution)/shard_map/ppermute | solution.py:47
  190.8 3.9 %all-to-all-start.6 = ((bf16[8,32,3584]{2,1,0:T(8,128)(2,1)}), bf16[8,32,3584]{2,1,0:T(8,128)(2,1)S(1)}, u32[]{:S(2)}, u32[]{:S(2)}) async-start(bf16[8,32,3584]{2,1,0:T(8,128)(2,1)} %bitcast.110), calls=%async_computation.6 | async-start | bytes 3670016 | tf_op jit(solution)/shard_map/all_to_all | solution.py:89
  194.7 0.4 fusion.180
  195.1 4.4 %convolution_convert_fusion = bf16[256,7168]{1,0:T(8,128)(2,1)} fusion(bf16[128,256]{1,0:T(8,128)(2,1)S(1)} %fusion.180, bf16[128,7168]{1,0:T(8,128)(2,1)} %collective-permute-done.2), kind=kOutput, calls=%fused_computation | convolution fusion | flops 471597056 | bytes 5570560 | tf_op jit(solution)/shard_map/dot_general | solution.py:38
  199.5 19.0 %all-to-all-done.6 = bf16[8,32,3584]{2,1,0:T(8,128)(2,1)S(1)} async-done(((bf16[8,32,3584]{2,1,0:T(8,128)(2,1)}), bf16[8,32,3584]{2,1,0:T(8,128)(2,1)S(1)}, u32[]{:S(2)}, u32[]{:S(2)}) %all-to-all-start.6) | async-done | bytes 1835040 | tf_op jit(solution)/shard_map/all_to_all | solution.py:89
  218.5 4.7 %all-to-all-start.5 = ((bf16[8,32,7168]{2,1,0:T(8,128)(2,1)}), bf16[8,32,7168]{2,1,0:T(8,128)(2,1)}, u32[]{:S(2)}, u32[]{:S(2)}) async-start(bf16[8,32,7168]{2,1,0:T(8,128)(2,1)} %bitcast.102), calls=%async_computation.5 | async-start | bytes 7340032 | tf_op jit(solution)/shard_map/all_to_all | solution.py:89
  223.4 5.8 %fusion.153 = (bf16[256,1024]{1,0:T(8,128)(2,1)S(1)}, f32[256,1024]{1,0:T(8,128)S(1)}) fusion(bf16[1024,1024]{1,0:T(8,128)(2,1)} %param.11, s32[]{:T(128)S(6)} %select_n.77, f32[256]{0:T(256)S(1)} %reshape.107, bf16[1,1024,3584]{2,1,0:T(8,128)(2,1)} %param.13, bf16[256,7168]{1,0:T(8,128)(2,1)} %bitcast.24), kind=kOutput, calls=%fused_computation.92 | convolution fusion | flops 1881145344 | bytes 11273220 | tf_op jit(solution)/shard_map/dot_general | solution.py:22
  229.2 5.9 %fusion.117 = bf16[256,1024]{1,0:T(8,128)(2,1)S(1)} fusion(f32[256,1024]{1,0:T(8,128)S(1)} %get-tuple-element.58, bf16[3584,2048]{1,0:T(8,128)(2,1)} %bitcast.115, bf16[256,7168]{1,0:T(8,128)(2,1)} %bitcast.24, bf16[1024,1024]{1,0:T(8,128)(2,1)} %param.11, s32[]{:T(128)S(6)} %select_n.77), kind=kOutput, calls=%fused_computation.70 | convolution fusion | flops 1881931776 | bytes 11272196 | tf_op jit(solution)/shard_map/dot_general | solution.py:21
  235.2 16.2 %convolution_convert_fusion.5 = bf16[256,3584]{1,0:T(8,128)(2,1)} fusion(bf16[256,1024]{1,0:T(8,128)(2,1)S(1)} %get-tuple-element.57, bf16[256,1024]{1,0:T(8,128)(2,1)S(1)} %fusion.117, bf16[1,3584,2048]{2,1,0:T(8,128)(2,1)} %param.12), kind=kOutput, calls=%fused_computation.13 | convolution fusion | flops 3761111040 | bytes 17563648 | tf_op jit(solution)/shard_map/dot_general | solution.py:31
  251.3 1.4 convolution_convert_fusion.10
  252.7 14.1 %all-to-all-done.5 = bf16[8,32,7168]{2,1,0:T(8,128)(2,1)} async-done(((bf16[8,32,7168]{2,1,0:T(8,128)(2,1)}), bf16[8,32,7168]{2,1,0:T(8,128)(2,1)}, u32[]{:S(2)}, u32[]{:S(2)}) %all-to-all-start.5) | async-done | bytes 3670048 | tf_op jit(solution)/shard_map/all_to_all | solution.py:89
  266.7 3.6 all-to-all-start.7
  270.3 0.6 collective-permute-start.3
  270.9 5.8 %fusion.159 = (bf16[256,1024]{1,0:T(8,128)(2,1)S(1)}, f32[256,1024]{1,0:T(8,128)S(1)}) fusion(bf16[1024,1024]{1,0:T(8,128)(2,1)} %param.11, s32[]{:T(128)S(6)} %select_n.78, f32[256]{0:T(256)S(1)} %reshape.108, bf16[1,1024,3584]{2,1,0:T(8,128)(2,1)} %param.13, bf16[256,7168]{1,0:T(8,128)(2,1)} %bitcast.27), kind=kOutput, calls=%fused_computation.98 | convolution fusion | flops 1881145344 | bytes 11273220 | tf_op jit(solution)/shard_map/dot_general | solution.py:22
  276.7 5.9 %fusion.122 = bf16[256,1024]{1,0:T(8,128)(2,1)S(1)} fusion(f32[256,1024]{1,0:T(8,128)S(1)} %get-tuple-element.60, bf16[3584,2048]{1,0:T(8,128)(2,1)} %bitcast.116, bf16[256,7168]{1,0:T(8,128)(2,1)} %bitcast.27, bf16[1024,1024]{1,0:T(8,128)(2,1)} %param.11, s32[]{:T(128)S(6)} %select_n.78), kind=kOutput, calls=%fused_computation.71 | convolution fusion | flops 1881931776 | bytes 11272196 | tf_op jit(solution)/shard_map/dot_general | solution.py:21
  282.7 16.2 %convolution_convert_fusion.4 = bf16[256,3584]{1,0:T(8,128)(2,1)} fusion(bf16[256,1024]{1,0:T(8,128)(2,1)S(1)} %get-tuple-element.59, bf16[256,1024]{1,0:T(8,128)(2,1)S(1)} %fusion.122, bf16[1,3584,2048]{2,1,0:T(8,128)(2,1)} %param.12), kind=kOutput, calls=%fused_computation.12 | convolution fusion | flops 3761111040 | bytes 17563648 | tf_op jit(solution)/shard_map/dot_general | solution.py:31
  298.8 1.3 convolution_convert_fusion.9
  300.2 4.1 %all-to-all-start.8 = ((bf16[8,32,3584]{2,1,0:T(8,128)(2,1)}), bf16[8,32,3584]{2,1,0:T(8,128)(2,1)S(1)}, u32[]{:S(2)}, u32[]{:S(2)}) async-start(bf16[8,32,3584]{2,1,0:T(8,128)(2,1)} %bitcast.111), calls=%async_computation.8 | async-start | bytes 3670016 | tf_op jit(solution)/shard_map/all_to_all | solution.py:89
  304.2 23.8 %all-to-all-done.8 = bf16[8,32,3584]{2,1,0:T(8,128)(2,1)S(1)} async-done(((bf16[8,32,3584]{2,1,0:T(8,128)(2,1)}), bf16[8,32,3584]{2,1,0:T(8,128)(2,1)S(1)}, u32[]{:S(2)}, u32[]{:S(2)}) %all-to-all-start.8) | async-done | bytes 1835040 | tf_op jit(solution)/shard_map/all_to_all | solution.py:89
  328.1 0.4 convolution_convert_fusion.8
  328.5 19.4 %collective-permute-done.4 = bf16[128,3584]{1,0:T(8,128)(2,1)} collective-permute-done((bf16[128,3584]{1,0:T(8,128)(2,1)}, bf16[128,3584]{1,0:T(8,128)(2,1)}, u32[]{:S(2)}, u32[]{:S(2)}) %collective-permute-start.4) | collective-permute-done | bytes 917536 | tf_op jit(solution)/shard_map/ppermute | solution.py:47
  347.9 23.8 %collective-permute-done.5 = bf16[128,3584]{1,0:T(8,128)(2,1)S(1)} collective-permute-done((bf16[128,3584]{1,0:T(8,128)(2,1)S(1)}, bf16[128,3584]{1,0:T(8,128)(2,1)S(1)}, u32[]{:S(2)}, u32[]{:S(2)}) %collective-permute-start.5) | collective-permute-done | bytes 917536 | tf_op jit(solution)/shard_map/ppermute | solution.py:47
  371.6 2.9 add_convert_fusion
  (31 shorter events, 1.0 us)
Async XLA Ops:
  0.0 2.4 copy-start
  6.7 7.7 %copy-start.1 = (s32[4,128,8]{1,2,0:T(8,128)S(1)}, s32[4,128,8]{1,2,0:T(8,128)}, u32[]{:S(2)}) copy-start(s32[4,128,8]{1,2,0:T(8,128)} %param.10) | copy-start | bytes 49156
  6.7 48.9 %all-to-all-start = ((bf16[8,32,7168]{2,1,0:T(8,128)(2,1)}), bf16[8,32,7168]{2,1,0:T(8,128)(2,1)}, u32[]{:S(2)}, u32[]{:S(2)}) async-start(bf16[8,32,7168]{2,1,0:T(8,128)(2,1)} %bitcast.101), calls=%async_computation | async-start | bytes 7340032 | tf_op jit(solution)/shard_map/all_to_all | solution.py:89
  12.0 46.9 %collective-permute-start = (bf16[128,7168]{1,0:T(8,128)(2,1)S(1)}, bf16[128,7168]{1,0:T(8,128)(2,1)}, u32[]{:S(2)}, u32[]{:S(2)}) collective-permute-start(bf16[128,7168]{1,0:T(8,128)(2,1)S(1)} %constant_dynamic-update-slice_fusion), channel_id=1, source_target_pairs={{0,8},{8,16},{16,24},{24,0},{1,9},{9,17},{17,25},{25,1},{2,10},{10... | collective-permute-start | bytes 5505032 | tf_op jit(solution)/shard_map/ppermute | solution.py:47
  55.6 8.0 %all-to-all-start.2 = ((bf16[8,4,32]{2,1,0:T(4,128)(2,1)}), bf16[8,4,32]{2,1,0:T(4,128)(2,1)S(1)}, u32[]{:S(2)}, u32[]{:S(2)}) async-start(bf16[8,4,32]{2,1,0:T(4,128)(2,1)} %copy.12), calls=%async_computation.2 | async-start | bytes 16384 | tf_op jit(solution)/shard_map/all_to_all | solution.py:86
  63.6 50.3 %all-to-all-start.1 = ((bf16[8,32,7168]{2,1,0:T(8,128)(2,1)}), bf16[8,32,7168]{2,1,0:T(8,128)(2,1)}, u32[]{:S(2)}, u32[]{:S(2)}) async-start(bf16[8,32,7168]{2,1,0:T(8,128)(2,1)} %bitcast.103), calls=%async_computation.1 | async-start | bytes 7340032 | tf_op jit(solution)/shard_map/all_to_all | solution.py:89
  68.2 45.6 %collective-permute-start.1 = (bf16[128,7168]{1,0:T(8,128)(2,1)}, bf16[128,7168]{1,0:T(8,128)(2,1)}, u32[]{:S(2)}, u32[]{:S(2)}) collective-permute-start(bf16[128,7168]{1,0:T(8,128)(2,1)} %collective-permute-done), channel_id=1, source_target_pairs={{0,8},{8,16},{16,24},{24,0},{1,9},{9,17},{17,25},{25,1},{2,10},{10... | collective-permute-start | bytes 5505032 | tf_op jit(solution)/shard_map/ppermute | solution.py:47
  113.9 27.7 %all-to-all-start.4 = ((bf16[8,32,3584]{2,1,0:T(8,128)(2,1)}), bf16[8,32,3584]{2,1,0:T(8,128)(2,1)S(1)}, u32[]{:S(2)}, u32[]{:S(2)}) async-start(bf16[8,32,3584]{2,1,0:T(8,128)(2,1)} %bitcast.112), calls=%async_computation.4 | async-start | bytes 3670016 | tf_op jit(solution)/shard_map/all_to_all | solution.py:89
  141.6 49.2 %all-to-all-start.3 = ((bf16[8,32,7168]{2,1,0:T(8,128)(2,1)}), bf16[8,32,7168]{2,1,0:T(8,128)(2,1)}, u32[]{:S(2)}, u32[]{:S(2)}) async-start(bf16[8,32,7168]{2,1,0:T(8,128)(2,1)} %bitcast.104), calls=%async_computation.3 | async-start | bytes 7340032 | tf_op jit(solution)/shard_map/all_to_all | solution.py:89
  146.2 44.6 %collective-permute-start.2 = (bf16[128,7168]{1,0:T(8,128)(2,1)}, bf16[128,7168]{1,0:T(8,128)(2,1)}, u32[]{:S(2)}, u32[]{:S(2)}) collective-permute-start(bf16[128,7168]{1,0:T(8,128)(2,1)} %collective-permute-done.1), channel_id=1, source_target_pairs={{0,8},{8,16},{16,24},{24,0},{1,9},{9,17},{17,25},{25,1},{2,10},{10... | collective-permute-start | bytes 5505032 | tf_op jit(solution)/shard_map/ppermute | solution.py:47
  190.8 27.7 %all-to-all-start.6 = ((bf16[8,32,3584]{2,1,0:T(8,128)(2,1)}), bf16[8,32,3584]{2,1,0:T(8,128)(2,1)S(1)}, u32[]{:S(2)}, u32[]{:S(2)}) async-start(bf16[8,32,3584]{2,1,0:T(8,128)(2,1)} %bitcast.110), calls=%async_computation.6 | async-start | bytes 3670016 | tf_op jit(solution)/shard_map/all_to_all | solution.py:89
  218.5 48.3 %all-to-all-start.5 = ((bf16[8,32,7168]{2,1,0:T(8,128)(2,1)}), bf16[8,32,7168]{2,1,0:T(8,128)(2,1)}, u32[]{:S(2)}, u32[]{:S(2)}) async-start(bf16[8,32,7168]{2,1,0:T(8,128)(2,1)} %bitcast.102), calls=%async_computation.5 | async-start | bytes 7340032 | tf_op jit(solution)/shard_map/all_to_all | solution.py:89
  266.7 32.1 %all-to-all-start.7 = ((bf16[8,32,3584]{2,1,0:T(8,128)(2,1)}), bf16[8,32,3584]{2,1,0:T(8,128)(2,1)S(1)}, u32[]{:S(2)}, u32[]{:S(2)}) async-start(bf16[8,32,3584]{2,1,0:T(8,128)(2,1)} %bitcast.109), calls=%async_computation.7 | async-start | bytes 3670016 | tf_op jit(solution)/shard_map/all_to_all | solution.py:89
  270.3 29.8 %collective-permute-start.3 = (bf16[128,3584]{1,0:T(8,128)(2,1)}, bf16[128,3584]{1,0:T(8,128)(2,1)}, u32[]{:S(2)}, u32[]{:S(2)}) collective-permute-start(bf16[128,3584]{1,0:T(8,128)(2,1)} %convolution_convert_fusion.10), channel_id=1, source_target_pairs={{0,24},{8,0},{16,8},{24,16},{1,25},{9,1},{17,9},{25,17},{2,26},{10... | collective-permute-start | bytes 2752520 | tf_op jit(solution)/shard_map/ppermute | solution.py:47
  300.2 27.9 %all-to-all-start.8 = ((bf16[8,32,3584]{2,1,0:T(8,128)(2,1)}), bf16[8,32,3584]{2,1,0:T(8,128)(2,1)S(1)}, u32[]{:S(2)}, u32[]{:S(2)}) async-start(bf16[8,32,3584]{2,1,0:T(8,128)(2,1)} %bitcast.111), calls=%async_computation.8 | async-start | bytes 3670016 | tf_op jit(solution)/shard_map/all_to_all | solution.py:89
  304.2 43.6 %collective-permute-start.4 = (bf16[128,3584]{1,0:T(8,128)(2,1)}, bf16[128,3584]{1,0:T(8,128)(2,1)}, u32[]{:S(2)}, u32[]{:S(2)}) collective-permute-start(bf16[128,3584]{1,0:T(8,128)(2,1)} %convolution_convert_fusion.9), channel_id=1, source_target_pairs={{0,16},{8,24},{16,0},{24,8},{1,17},{9,25},{17,1},{25,9},{2,18},{10... | collective-permute-start | bytes 2752520 | tf_op jit(solution)/shard_map/ppermute | solution.py:47
  347.9 23.8 %collective-permute-start.5 = (bf16[128,3584]{1,0:T(8,128)(2,1)S(1)}, bf16[128,3584]{1,0:T(8,128)(2,1)S(1)}, u32[]{:S(2)}, u32[]{:S(2)}) collective-permute-start(bf16[128,3584]{1,0:T(8,128)(2,1)S(1)} %convolution_convert_fusion.8), channel_id=1, source_target_pairs={{0,8},{8,16},{16,24},{24,0},{1,9},{9,17},{17,25},{25,1},{2,10},{10... | collective-permute-start | bytes 2752520 | tf_op jit(solution)/shard_map/ppermute | solution.py:47

commit v6 on v5

--- a/solution.py
+++ b/solution.py
@@ -93,12 +93,9 @@
     def fetch(step, previous):
         return shift(previous, n_node, 1)
 
-    def send(step, chunk):
-        return spread(select_rows(dispatch[step], chunk))
-
     def compute(step, received):
         saved = lax.dynamic_slice_in_dim(gate_saved, sources[step] * chunk_rows, chunk_rows, 0)
-        rows = received.reshape(chunk_rows, 2 * model_width)
+        rows = received
         return expert_backward(
             rows[:, :model_width],
             rows[:, model_width:],
@@ -108,37 +105,40 @@
             weight_out,
         )
 
-    def gather_back(step, contrib):
-        returned = spread(contrib).reshape(chunk_rows, model_width)
-        return jnp.dot(dispatch[step], returned, preferred_element_type=jnp.float32).astype(
-            jnp.bfloat16
-        )
-
     def send_home(step, node_sum):
         return shift(node_sum, n_node, -step)
 
     chunks = {0: jnp.concatenate([hidden_in, out_grad], axis=1)}
     received = {}
     contribs = {}
-    sums = {}
     homes = {}
-    for slot in range(-1, n_node + 2):
+    for slot in range(-1, n_node + 1):
         produced = {}
         if 0 < slot + 2 < n_node:
             produced["chunk", slot + 2] = fetch(slot + 2, chunks[slot + 1])
-        if 0 <= slot + 1 < n_node:
-            produced["received", slot + 1] = send(slot + 1, chunks[slot + 1])
         if 0 <= slot < n_node:
             produced["contrib", slot] = compute(slot, received[slot])
+        outgoing = []
+        if 0 <= slot + 1 < n_node:
+            outgoing.append(select_rows(dispatch[slot + 1], chunks[slot + 1]))
         if 0 <= slot - 1 < n_node:
-            produced["sum", slot - 1] = gather_back(slot - 1, contribs[slot - 1])
-        if 0 <= slot - 2 < n_node:
-            produced["home", slot - 2] = send_home(slot - 2, sums[slot - 2])
+            outgoing.append(contribs[slot - 1])
+        arrived = spread(jnp.concatenate(outgoing, axis=1) if len(outgoing) > 1 else outgoing[0])
+        arrived = arrived.reshape(chunk_rows, arrived.shape[-1])
+        if 0 <= slot + 1 < n_node:
+            produced["received", slot + 1] = arrived[:, : 2 * model_width]
+        if 0 <= slot - 1 < n_node:
+            returned = arrived[:, arrived.shape[-1] - model_width :]
+            node_sum = jnp.dot(
+                dispatch[slot - 1], returned, preferred_element_type=jnp.float32
+            ).astype(jnp.bfloat16)
+            produced["home", slot - 1] = send_home(slot - 1, node_sum)
         keys = list(produced)
         values = lax.optimization_barrier([produced[key] for key in keys])
         for (kind, step), value in zip(keys, values):
-            {"chunk": chunks, "received": received, "contrib": contribs, "sum": sums,
-             "home": homes}[kind][step] = value
+            {"chunk": chunks, "received": received, "contrib": contribs, "home": homes}[kind][
+                step
+            ] = value
 
     total = homes[0].astype(jnp.float32)
     for step in range(1, n_node):

time: 381 us -> 421 us (1.10)
  blocking collectives: 0 us -> 28.4 us
  waiting for transfers between devices: 187 us -> 203 us
  matrix products: 134 us -> 124 us
  starting transfers between devices: 43.7 us -> 33.8 us
  local copies, waits for them, and re-layouts: 4.61 us -> 14.3 us
  other arithmetic: 4.64 us -> 9.96 us
    all_to_all x0 -> x1, blocking collectives: none -> 28.4 us  [spread(): lax.all_to_all(rows.reshape(n_local, capacity, rows.shape[-1]), 'local',...]
    all_to_all x8 -> x5, waiting for transfers between devices: 113 us -> 135 us  [spread(): lax.all_to_all(rows.reshape(n_local, capacity, rows.shape[-1]), 'local',...]
    all_to_all x8 -> x5, starting transfers between devices: 34.5 us -> 23.2 us  [spread(): lax.all_to_all(rows.reshape(n_local, capacity, rows.shape[-1]), 'local',...]
    slice x0 -> x2, local copies, waits for them, and re-layouts: none -> 8.34 us  [on_device(): produced['received', slot + 1] = arrived[:, :2 * model_width]]
    dot_general x4, matrix products: 64.7 us -> 57.9 us  [expert_backward(): lax.dot_general(grad_pre, weight_in, (((1,), (1,)), ((), ())), preferred_...]
    concatenate x0 -> x2, other arithmetic: none -> 5.61 us  [on_device(): jnp.concatenate(outgoing, axis=1)]
    ppermute x6, waiting for transfers between devices: 74.1 us -> 68.5 us  [shift(): lax.ppermute(value, 'node', [(i, (i + step) % n_node) for i in range(n_no...]
    dot_general x4, matrix products: 16.4 us -> 11.2 us  [select_rows(): lax.dot_general(onehot, rows, (((0,), (0,)), ((), ())), preferred_element...]
  transfers between devices with their start and end apart: 15 -> 12, of which waited for: 10 -> 8; matrix products, arithmetic and copies ran while one was open for 36% -> 30% of each run, Pallas kernels for 0% -> 0%
where the time goes in v6:
time: 421 us; the launch traced here: 415 us
  waiting for transfers between devices  203 us (48%)
  matrix products  124 us (29%)
  starting transfers between devices  33.8 us (8%)
  blocking collectives  28.4 us (7%)
  local copies, waits for them, and re-layouts  14.3 us (3%)
  other arithmetic  9.96 us (2%)
    all_to_all x5, waiting for transfers between devices, spread(): lax.all_to_all(rows.reshape(n_local, capacity, rows.shape[-1]), 'local',...  135 us
    ppermute x6, waiting for transfers between devices, shift(): lax.ppermute(value, 'node', [(i, (i + step) % n_node) for i in range(n_no...  68.5 us
    dot_general x4, matrix products, expert_backward(): lax.dot_general(grad_pre, weight_in, (((1,), (1,)), ((), ())), preferred_...  57.9 us
    all_to_all x1, blocking collectives, spread(): lax.all_to_all(rows.reshape(n_local, capacity, rows.shape[-1]), 'local',...  28.4 us
    dot_general x4, matrix products, expert_backward(): jnp.dot(rows_x, weight_in[:, FF:], preferred_element_type=jnp.float32)  23.6 us
    dot_general x4, matrix products, expert_backward(): lax.dot_general(rows_dy, weight_out, (((1,), (1,)), ((), ())), preferred_...  23.6 us
    all_to_all x5, starting transfers between devices, spread(): lax.all_to_all(rows.reshape(n_local, capacity, rows.shape[-1]), 'local',...  23.2 us
    dot_general x4, matrix products, select_rows(): lax.dot_general(onehot, rows, (((0,), (0,)), ((), ())), preferred_element...  11.2 us
  transfers between devices with their start and end apart: 12, of which 8 were waited for; matrix products, arithmetic and copies ran while one was open for 30% of the time, Pallas kernels for 0%

profile of v6, /device:TPU:0, one launch (start us, length us, event | category | flops | bytes accessed | tf_op | source)
XLA Modules:
  0.0 414.9 jit_solution(2794798676831612614)
XLA Ops:
  0.0 0.9 copy.11
  0.9 0.2 reshape.76
  1.1 0.6 fusion.135
  2.0 0.4 fusion.182
  2.5 1.3 constant_dynamic-update-slice_fusion
  3.7 3.0 convolution_convert_fusion.3
  6.7 5.3 %all-to-all-start = ((bf16[8,32,7168]{2,1,0:T(8,128)(2,1)}), bf16[8,32,7168]{2,1,0:T(8,128)(2,1)}, u32[]{:S(2)}, u32[]{:S(2)}) async-start(bf16[8,32,7168]{2,1,0:T(8,128)(2,1)} %bitcast.97), calls=%async_computation | async-start | bytes 7340032 | tf_op jit(solution)/shard_map/all_to_all | solution.py:89
  12.0 2.4 collective-permute-start
  14.5 0.1 copy.13
  14.6 0.1 copy.16
  14.7 0.1 copy.15
  14.8 0.1 copy.14
  15.1 0.4 fusion.179
  15.5 0.1 stack_reshape.13
  15.7 0.4 fusion.175
  16.3 0.4 fusion.177
  16.8 0.4 fusion.180
  17.4 0.6 copy.12
  18.0 0.4 fusion.183
  18.4 37.2 %all-to-all-done = bf16[8,32,7168]{2,1,0:T(8,128)(2,1)} async-done(((bf16[8,32,7168]{2,1,0:T(8,128)(2,1)}), bf16[8,32,7168]{2,1,0:T(8,128)(2,1)}, u32[]{:S(2)}, u32[]{:S(2)}) %all-to-all-start) | async-done | bytes 3670048 | tf_op jit(solution)/shard_map/all_to_all | solution.py:89
  55.6 3.3 all-to-all-start.1
  59.0 4.5 %convolution_convert_fusion.2 = bf16[256,7168]{1,0:T(8,128)(2,1)} fusion(bf16[128,256]{1,0:T(8,128)(2,1)S(1)} %fusion.183, bf16[128,7168]{1,0:T(8,128)(2,1)} %collective-permute-done), kind=kOutput, calls=%fused_computation.2 | convolution fusion | flops 471597056 | bytes 5570560 | tf_op jit(solution)/shard_map/dot_general | solution.py:38
  63.4 0.2 all-to-all-done.1
  63.6 4.5 %all-to-all-start.2 = ((bf16[8,32,7168]{2,1,0:T(8,128)(2,1)}), bf16[8,32,7168]{2,1,0:T(8,128)(2,1)}, u32[]{:S(2)}, u32[]{:S(2)}) async-start(bf16[8,32,7168]{2,1,0:T(8,128)(2,1)} %bitcast.98), calls=%async_computation.2 | async-start | bytes 7340032 | tf_op jit(solution)/shard_map/all_to_all | solution.py:89
  68.1 0.4 fusion.184
  68.7 2.8 collective-permute-start.1
  71.5 5.8 %fusion.143 = (bf16[256,1024]{1,0:T(8,128)(2,1)S(1)}, f32[256,1024]{1,0:T(8,128)S(1)}) fusion(bf16[1024,1024]{1,0:T(8,128)(2,1)} %param.11, s32[]{:T(128)S(6)} %select_n.75, f32[256]{0:T(256)S(1)} %reshape.89, bf16[1,1024,3584]{2,1,0:T(8,128)(2,1)} %param.13, bf16[256,7168]{1,0:T(8,128)(2,1)} %bitcast.3), kind=kOutput, calls=%fused_computation.84 | convolution fusion | flops 1881145344 | bytes 11273220 | tf_op jit(solution)/shard_map/dot_general | solution.py:22
  77.3 5.9 %fusion.109 = bf16[256,1024]{1,0:T(8,128)(2,1)S(1)} fusion(f32[256,1024]{1,0:T(8,128)S(1)} %get-tuple-element.46, bf16[3584,2048]{1,0:T(8,128)(2,1)} %bitcast.103, bf16[256,7168]{1,0:T(8,128)(2,1)} %bitcast.3, bf16[1024,1024]{1,0:T(8,128)(2,1)} %param.11, s32[]{:T(128)S(6)} %select_n.75), kind=kOutput, calls=%fused_computation.72 | convolution fusion | flops 1881931776 | bytes 11272196 | tf_op jit(solution)/shard_map/dot_general | solution.py:21
  83.2 16.2 %convolution_convert_fusion.7 = bf16[256,3584]{1,0:T(8,128)(2,1)} fusion(bf16[256,1024]{1,0:T(8,128)(2,1)S(1)} %get-tuple-element.45, bf16[256,1024]{1,0:T(8,128)(2,1)S(1)} %fusion.109, bf16[1,3584,2048]{2,1,0:T(8,128)(2,1)} %param.12), kind=kOutput, calls=%fused_computation.17 | convolution fusion | flops 3761111040 | bytes 17563648 | tf_op jit(solution)/shard_map/dot_general | solution.py:31
  99.4 14.8 %collective-permute-done.1 = bf16[128,7168]{1,0:T(8,128)(2,1)S(1)} collective-permute-done((bf16[128,7168]{1,0:T(8,128)(2,1)}, bf16[128,7168]{1,0:T(8,128)(2,1)S(1)}, u32[]{:S(2)}, u32[]{:S(2)}) %collective-permute-start.1) | collective-permute-done | bytes 1835040 | tf_op jit(solution)/shard_map/ppermute | solution.py:47
  114.2 1.1 convolution_convert_fusion.1
  115.4 0.4 copy-done.3
  115.7 2.8 pad_maximum_fusion
  118.5 4.7 %all-to-all-start.3 = ((bf16[8,32,10752]{2,1,0:T(8,128)(2,1)}), bf16[8,32,10752]{2,1,0:T(8,128)(2,1)}, u32[]{:S(2)}, u32[]{:S(2)}) async-start(bf16[8,32,10752]{2,1,0:T(8,128)(2,1)} %bitcast.96), calls=%async_computation.3 | async-start | bytes 11010048 | tf_op jit(solution)/shard_map/all_to_all | solution.py:89
  123.2 0.4 fusion.185
  123.7 0.2 collective-permute-start.2
  123.9 5.8 %fusion.149 = (bf16[256,1024]{1,0:T(8,128)(2,1)S(1)}, f32[256,1024]{1,0:T(8,128)S(1)}) fusion(bf16[1024,1024]{1,0:T(8,128)(2,1)} %param.11, s32[]{:T(128)S(6)} %select_n.76, f32[256]{0:T(256)S(1)} %reshape.90, bf16[1,1024,3584]{2,1,0:T(8,128)(2,1)} %param.13, bf16[256,7168]{1,0:T(8,128)(2,1)} %bitcast.19), kind=kOutput, calls=%fused_computation.90 | convolution fusion | flops 1881145344 | bytes 11273220 | tf_op jit(solution)/shard_map/dot_general | solution.py:22
  129.7 5.9 %fusion.114 = bf16[256,1024]{1,0:T(8,128)(2,1)S(1)} fusion(f32[256,1024]{1,0:T(8,128)S(1)} %get-tuple-element.48, bf16[3584,2048]{1,0:T(8,128)(2,1)} %bitcast.104, bf16[256,7168]{1,0:T(8,128)(2,1)} %bitcast.19, bf16[1024,1024]{1,0:T(8,128)(2,1)} %param.11, s32[]{:T(128)S(6)} %select_n.76), kind=kOutput, calls=%fused_computation.73 | convolution fusion | flops 1881931776 | bytes 11272196 | tf_op jit(solution)/shard_map/dot_general | solution.py:21
  135.6 16.2 %convolution_convert_fusion.6 = bf16[256,3584]{1,0:T(8,128)(2,1)} fusion(bf16[256,1024]{1,0:T(8,128)(2,1)S(1)} %get-tuple-element.47, bf16[256,1024]{1,0:T(8,128)(2,1)S(1)} %fusion.114, bf16[1,3584,2048]{2,1,0:T(8,128)(2,1)} %param.12), kind=kOutput, calls=%fused_computation.16 | convolution fusion | flops 3761111040 | bytes 17563648 | tf_op jit(solution)/shard_map/dot_general | solution.py:31
  151.8 34.6 %all-to-all-done.3 = bf16[8,32,10752]{2,1,0:T(8,128)(2,1)} async-done(((bf16[8,32,10752]{2,1,0:T(8,128)(2,1)}), bf16[8,32,10752]{2,1,0:T(8,128)(2,1)}, u32[]{:S(2)}, u32[]{:S(2)}) %all-to-all-start.3) | async-done | bytes 5505056 | tf_op jit(solution)/shard_map/all_to_all | solution.py:89
  186.4 4.2 %slice.74 = bf16[256,7168]{1,0:T(8,128)(2,1)} slice(bf16[256,10752]{1,0:T(8,128)(2,1)} %bitcast.21), slice={[0:256], [0:7168]} | slice | bytes 7340032 | tf_op jit(solution)/shard_map/slice | solution.py:129
  190.6 2.0 convolution_convert_fusion.11
  192.6 2.6 convolution_convert_fusion
  195.3 2.8 pad_maximum_fusion.1
  198.1 4.9 %all-to-all-start.4 = ((bf16[8,32,10752]{2,1,0:T(8,128)(2,1)}), bf16[8,32,10752]{2,1,0:T(8,128)(2,1)}, u32[]{:S(2)}, u32[]{:S(2)}) async-start(bf16[8,32,10752]{2,1,0:T(8,128)(2,1)} %bitcast.95), calls=%async_computation.4 | async-start | bytes 11010048 | tf_op jit(solution)/shard_map/all_to_all | solution.py:89
  203.2 6.0 %fusion.155 = (bf16[256,1024]{1,0:T(8,128)(2,1)S(1)}, f32[256,1024]{1,0:T(8,128)S(1)}) fusion(bf16[1024,1024]{1,0:T(8,128)(2,1)} %param.11, s32[]{:T(128)S(6)} %select_n.77, f32[256]{0:T(256)S(1)} %reshape.91, bf16[1,1024,3584]{2,1,0:T(8,128)(2,1)} %param.13, bf16[256,7168]{1,0:T(8,128)(2,1)} %slice.74), kind=kOutput, calls=%fused_computation.96 | convolution fusion | flops 1881145344 | bytes 11273220 | tf_op jit(solution)/shard_map/dot_general | solution.py:22
  209.2 5.5 %fusion.119 = bf16[256,1024]{1,0:T(8,128)(2,1)S(1)} fusion(f32[256,1024]{1,0:T(8,128)S(1)} %get-tuple-element.50, bf16[3584,2048]{1,0:T(8,128)(2,1)} %bitcast.105, bf16[256,7168]{1,0:T(8,128)(2,1)S(1)} %copy-done, bf16[1024,1024]{1,0:T(8,128)(2,1)} %param.11, s32[]{:T(128)S(6)} %select_n.77), kind=kOutput, calls=%fused_computation.74 | convolution fusion | flops 1881931776 | bytes 11272196 | tf_op jit(solution)/shard_map/dot_general | solution.py:21
  214.7 51.5 %all-to-all-done.4 = bf16[8,32,10752]{2,1,0:T(8,128)(2,1)} async-done(((bf16[8,32,10752]{2,1,0:T(8,128)(2,1)}), bf16[8,32,10752]{2,1,0:T(8,128)(2,1)}, u32[]{:S(2)}, u32[]{:S(2)}) %all-to-all-start.4) | async-done | bytes 5505056 | tf_op jit(solution)/shard_map/all_to_all | solution.py:89
  266.2 1.9 convolution_convert_fusion.10
  268.1 1.8 collective-permute-start.3
  269.9 16.2 %convolution_convert_fusion.5 = bf16[256,3584]{1,0:T(8,128)(2,1)} fusion(bf16[256,1024]{1,0:T(8,128)(2,1)S(1)} %get-tuple-element.49, bf16[256,1024]{1,0:T(8,128)(2,1)S(1)} %fusion.119, bf16[1,3584,2048]{2,1,0:T(8,128)(2,1)} %param.12), kind=kOutput, calls=%fused_computation.15 | convolution fusion | flops 3761111040 | bytes 17563648 | tf_op jit(solution)/shard_map/dot_general | solution.py:31
  286.0 4.1 slice.77
  290.2 0.9 copy-done.5
  291.1 3.8 all-to-all-start.5
  295.0 6.0 %fusion.161 = (bf16[256,1024]{1,0:T(8,128)(2,1)S(1)}, f32[256,1024]{1,0:T(8,128)S(1)}) fusion(bf16[1024,1024]{1,0:T(8,128)(2,1)} %param.11, s32[]{:T(128)S(6)} %select_n.78, f32[256]{0:T(256)S(1)} %reshape.92, bf16[1,1024,3584]{2,1,0:T(8,128)(2,1)} %param.13, bf16[256,7168]{1,0:T(8,128)(2,1)} %slice.77), kind=kOutput, calls=%fused_computation.102 | convolution fusion | flops 1881145344 | bytes 11273220 | tf_op jit(solution)/shard_map/dot_general | solution.py:22
  301.0 6.3 %fusion.124 = bf16[256,1024]{1,0:T(8,128)(2,1)} fusion(f32[256,1024]{1,0:T(8,128)S(1)} %get-tuple-element.52, bf16[3584,2048]{1,0:T(8,128)(2,1)} %bitcast.106, bf16[256,7168]{1,0:T(8,128)(2,1)S(1)} %copy-done.1, bf16[1024,1024]{1,0:T(8,128)(2,1)} %param.11, s32[]{:T(128)S(6)} %select_n.78), kind=kOutput, calls=%fused_computation.75 | convolution fusion | flops 1881931776 | bytes 11272196 | tf_op jit(solution)/shard_map/dot_general | solution.py:21
  307.3 11.5 %all-to-all-done.5 = bf16[8,32,3584]{2,1,0:T(8,128)(2,1)S(1)} async-done(((bf16[8,32,3584]{2,1,0:T(8,128)(2,1)}), bf16[8,32,3584]{2,1,0:T(8,128)(2,1)S(1)}, u32[]{:S(2)}, u32[]{:S(2)}) %all-to-all-start.5) | async-done | bytes 1835040 | tf_op jit(solution)/shard_map/all_to_all | solution.py:89
  318.7 1.3 convolution_convert_fusion.9
  320.1 9.3 %convolution_convert_fusion.4 = bf16[256,3584]{1,0:T(8,128)(2,1)S(1)} fusion(bf16[256,1024]{1,0:T(8,128)(2,1)S(1)} %get-tuple-element.51, bf16[256,1024]{1,0:T(8,128)(2,1)} %fusion.124, bf16[1,3584,2048]{2,1,0:T(8,128)(2,1)} %param.12), kind=kOutput, calls=%fused_computation.14 | convolution fusion | flops 3761111040 | bytes 17563648 | tf_op jit(solution)/shard_map/dot_general | solution.py:31
  329.4 30.5 %collective-permute-done.4 = bf16[128,3584]{1,0:T(8,128)(2,1)} collective-permute-done((bf16[128,3584]{1,0:T(8,128)(2,1)}, bf16[128,3584]{1,0:T(8,128)(2,1)}, u32[]{:S(2)}, u32[]{:S(2)}) %collective-permute-start.4) | collective-permute-done | bytes 917536 | tf_op jit(solution)/shard_map/ppermute | solution.py:47
  359.9 28.4 %all_to_all.35 = bf16[8,32,3584]{2,1,0:T(8,128)(2,1)S(1)} all-to-all(bf16[8,32,3584]{2,1,0:T(8,128)(2,1)S(1)} %bitcast.102), channel_id=1, replica_groups=mesh['node'=4,'local'=8] {'local'}, dimensions={0} | all-to-all | bytes 3670016 | tf_op jit(solution)/shard_map/all_to_all | solution.py:89
  388.4 0.4 convolution_convert_fusion.8
  388.8 23.2 %collective-permute-done.5 = bf16[128,3584]{1,0:T(8,128)(2,1)S(1)} collective-permute-done((bf16[128,3584]{1,0:T(8,128)(2,1)S(1)}, bf16[128,3584]{1,0:T(8,128)(2,1)S(1)}, u32[]{:S(2)}, u32[]{:S(2)}) %collective-permute-start.5) | collective-permute-done | bytes 917536 | tf_op jit(solution)/shard_map/ppermute | solution.py:47
  412.1 2.6 add_convert_fusion
  (42 shorter events, 1.3 us)
Async XLA Ops:
  0.0 2.4 copy-start.4
  6.7 7.7 %copy-start.7 = (s32[4,128,8]{1,2,0:T(8,128)S(1)}, s32[4,128,8]{1,2,0:T(8,128)}, u32[]{:S(2)}) copy-start(s32[4,128,8]{1,2,0:T(8,128)} %param.10) | copy-start | bytes 49156
  6.7 48.9 %all-to-all-start = ((bf16[8,32,7168]{2,1,0:T(8,128)(2,1)}), bf16[8,32,7168]{2,1,0:T(8,128)(2,1)}, u32[]{:S(2)}, u32[]{:S(2)}) async-start(bf16[8,32,7168]{2,1,0:T(8,128)(2,1)} %bitcast.97), calls=%async_computation | async-start | bytes 7340032 | tf_op jit(solution)/shard_map/all_to_all | solution.py:89
  12.0 46.9 %collective-permute-start = (bf16[128,7168]{1,0:T(8,128)(2,1)S(1)}, bf16[128,7168]{1,0:T(8,128)(2,1)}, u32[]{:S(2)}, u32[]{:S(2)}) collective-permute-start(bf16[128,7168]{1,0:T(8,128)(2,1)S(1)} %constant_dynamic-update-slice_fusion), channel_id=1, source_target_pairs={{0,8},{8,16},{16,24},{24,0},{1,9},{9,17},{17,25},{25,1},{2,10},{10... | collective-permute-start | bytes 5505032 | tf_op jit(solution)/shard_map/ppermute | solution.py:47
  55.6 8.0 %all-to-all-start.1 = ((bf16[8,4,32]{2,1,0:T(4,128)(2,1)}), bf16[8,4,32]{2,1,0:T(4,128)(2,1)S(1)}, u32[]{:S(2)}, u32[]{:S(2)}) async-start(bf16[8,4,32]{2,1,0:T(4,128)(2,1)} %copy.12), calls=%async_computation.1 | async-start | bytes 16384 | tf_op jit(solution)/shard_map/all_to_all | solution.py:86
  63.6 50.6 %all-to-all-start.2 = ((bf16[8,32,7168]{2,1,0:T(8,128)(2,1)}), bf16[8,32,7168]{2,1,0:T(8,128)(2,1)}, u32[]{:S(2)}, u32[]{:S(2)}) async-start(bf16[8,32,7168]{2,1,0:T(8,128)(2,1)} %bitcast.98), calls=%async_computation.2 | async-start | bytes 7340032 | tf_op jit(solution)/shard_map/all_to_all | solution.py:89
  68.7 45.6 %collective-permute-start.1 = (bf16[128,7168]{1,0:T(8,128)(2,1)}, bf16[128,7168]{1,0:T(8,128)(2,1)S(1)}, u32[]{:S(2)}, u32[]{:S(2)}) collective-permute-start(bf16[128,7168]{1,0:T(8,128)(2,1)} %collective-permute-done), channel_id=1, source_target_pairs={{0,8},{8,16},{16,24},{24,0},{1,9},{9,17},{17,25},{25,1},{2,10},{10... | collective-permute-start | bytes 5505032 | tf_op jit(solution)/shard_map/ppermute | solution.py:47
  114.2 1.5 copy-start.3
  118.5 67.9 %all-to-all-start.3 = ((bf16[8,32,10752]{2,1,0:T(8,128)(2,1)}), bf16[8,32,10752]{2,1,0:T(8,128)(2,1)}, u32[]{:S(2)}, u32[]{:S(2)}) async-start(bf16[8,32,10752]{2,1,0:T(8,128)(2,1)} %bitcast.96), calls=%async_computation.3 | async-start | bytes 11010048 | tf_op jit(solution)/shard_map/all_to_all | solution.py:89
  123.7 68.9 %collective-permute-start.2 = (bf16[128,7168]{1,0:T(8,128)(2,1)S(1)}, bf16[128,7168]{1,0:T(8,128)(2,1)}, u32[]{:S(2)}, u32[]{:S(2)}) collective-permute-start(bf16[128,7168]{1,0:T(8,128)(2,1)S(1)} %collective-permute-done.1), channel_id=1, source_target_pairs={{0,8},{8,16},{16,24},{24,0},{1,9},{9,17},{17,25},{25,1},{2,10},{10... | collective-permute-start | bytes 5505032 | tf_op jit(solution)/shard_map/ppermute | solution.py:47
  190.6 4.7 %copy-start.2 = (bf16[256,3584]{1,0:T(8,128)(2,1)S(1)}, bf16[256,3584]{1,0:T(8,128)(2,1)}, u32[]{:S(2)}) copy-start(bf16[256,3584]{1,0:T(8,128)(2,1)} %convolution_convert_fusion.6) | copy-start | bytes 5505028
  198.1 68.1 %all-to-all-start.4 = ((bf16[8,32,10752]{2,1,0:T(8,128)(2,1)}), bf16[8,32,10752]{2,1,0:T(8,128)(2,1)}, u32[]{:S(2)}, u32[]{:S(2)}) async-start(bf16[8,32,10752]{2,1,0:T(8,128)(2,1)} %bitcast.95), calls=%async_computation.4 | async-start | bytes 11010048 | tf_op jit(solution)/shard_map/all_to_all | solution.py:89
  203.2 6.0 %copy-start = (bf16[256,7168]{1,0:T(8,128)(2,1)S(1)}, bf16[256,7168]{1,0:T(8,128)(2,1)}, u32[]{:S(2)}) copy-start(bf16[256,7168]{1,0:T(8,128)(2,1)} %slice.74) | copy-start | bytes 11010052
  268.1 22.1 %collective-permute-start.3 = (bf16[128,3584]{1,0:T(8,128)(2,1)S(1)}, bf16[128,3584]{1,0:T(8,128)(2,1)S(1)}, u32[]{:S(2)}, u32[]{:S(2)}) collective-permute-start(bf16[128,3584]{1,0:T(8,128)(2,1)S(1)} %convolution_convert_fusion.10), channel_id=1, source_target_pairs={{0,24},{8,0},{16,8},{24,16},{1,25},{9,1},{17,9},{25,17},{2,26},{10... | collective-permute-start | bytes 2752520 | tf_op jit(solution)/shard_map/ppermute | solution.py:47
  290.2 0.9 copy-start.5
  291.1 27.6 %all-to-all-start.5 = ((bf16[8,32,3584]{2,1,0:T(8,128)(2,1)}), bf16[8,32,3584]{2,1,0:T(8,128)(2,1)S(1)}, u32[]{:S(2)}, u32[]{:S(2)}) async-start(bf16[8,32,3584]{2,1,0:T(8,128)(2,1)} %bitcast.101), calls=%async_computation.5 | async-start | bytes 3670016 | tf_op jit(solution)/shard_map/all_to_all | solution.py:89
  295.0 6.0 %copy-start.1 = (bf16[256,7168]{1,0:T(8,128)(2,1)S(1)}, bf16[256,7168]{1,0:T(8,128)(2,1)}, u32[]{:S(2)}) copy-start(bf16[256,7168]{1,0:T(8,128)(2,1)} %slice.77) | copy-start | bytes 11010052
  320.1 39.8 %collective-permute-start.4 = (bf16[128,3584]{1,0:T(8,128)(2,1)}, bf16[128,3584]{1,0:T(8,128)(2,1)}, u32[]{:S(2)}, u32[]{:S(2)}) collective-permute-start(bf16[128,3584]{1,0:T(8,128)(2,1)} %convolution_convert_fusion.9), channel_id=1, source_target_pairs={{0,16},{8,24},{16,0},{24,8},{1,17},{9,25},{17,1},{25,9},{2,18},{10... | collective-permute-start | bytes 2752520 | tf_op jit(solution)/shard_map/ppermute | solution.py:47
  329.4 82.6 %copy-start.6 = (bf16[128,3584]{1,0:T(8,128)(2,1)S(1)}, bf16[128,3584]{1,0:T(8,128)(2,1)}, u32[]{:S(2)}) copy-start(bf16[128,3584]{1,0:T(8,128)(2,1)} %copy-done.5) | copy-start | bytes 2752516
  388.8 23.3 %collective-permute-start.5 = (bf16[128,3584]{1,0:T(8,128)(2,1)S(1)}, bf16[128,3584]{1,0:T(8,128)(2,1)S(1)}, u32[]{:S(2)}, u32[]{:S(2)}) collective-permute-start(bf16[128,3584]{1,0:T(8,128)(2,1)S(1)} %convolution_convert_fusion.8), channel_id=1, source_target_pairs={{0,8},{8,16},{16,24},{24,0},{1,9},{9,17},{17,25},{25,1},{2,10},{10... | collective-permute-start | bytes 2752520 | tf_op jit(solution)/shard_map/ppermute | solution.py:47

commit v7 on v5

--- a/solution.py
+++ b/solution.py
@@ -17,7 +17,7 @@
     return jnp.sum(before * onehot.astype(jnp.float32), axis=-1).astype(jnp.int32)
 
 
-def expert_backward(rows_x, rows_dy, rows_gate, saved, weight_in, weight_out):
+def expert_grad_pre(rows_x, rows_dy, rows_gate, saved, weight_in, weight_out):
     up_pre = jnp.dot(rows_x, weight_in[:, FF:], preferred_element_type=jnp.float32)
     grad_hidden = lax.dot_general(
         rows_dy, weight_out, (((1,), (1,)), ((), ())), preferred_element_type=jnp.float32
@@ -27,7 +27,10 @@
     sigmoid_gate = jax.nn.sigmoid(gate_pre)
     grad_gate = grad_hidden * up_pre * sigmoid_gate * (1.0 + gate_pre * (1.0 - sigmoid_gate))
     grad_up = grad_hidden * gate_pre * sigmoid_gate
-    grad_pre = jnp.concatenate([grad_gate, grad_up], axis=1).astype(jnp.bfloat16)
+    return jnp.concatenate([grad_gate, grad_up], axis=1).astype(jnp.bfloat16)
+
+
+def expert_part(grad_pre, weight_in):
     contrib = lax.dot_general(
         grad_pre, weight_in, (((1,), (1,)), ((), ())), preferred_element_type=jnp.float32
     )
@@ -99,7 +102,7 @@
     def compute(step, received):
         saved = lax.dynamic_slice_in_dim(gate_saved, sources[step] * chunk_rows, chunk_rows, 0)
         rows = received.reshape(chunk_rows, 2 * model_width)
-        return expert_backward(
+        return expert_grad_pre(
             rows[:, :model_width],
             rows[:, model_width:],
             gates[:, step].reshape(chunk_rows),
@@ -119,26 +122,39 @@
 
     chunks = {0: jnp.concatenate([hidden_in, out_grad], axis=1)}
     received = {}
+    grads = {}
     contribs = {}
-    sums = {}
     homes = {}
-    for slot in range(-1, n_node + 2):
-        produced = {}
-        if 0 < slot + 2 < n_node:
-            produced["chunk", slot + 2] = fetch(slot + 2, chunks[slot + 1])
-        if 0 <= slot + 1 < n_node:
-            produced["received", slot + 1] = send(slot + 1, chunks[slot + 1])
-        if 0 <= slot < n_node:
-            produced["contrib", slot] = compute(slot, received[slot])
-        if 0 <= slot - 1 < n_node:
-            produced["sum", slot - 1] = gather_back(slot - 1, contribs[slot - 1])
-        if 0 <= slot - 2 < n_node:
-            produced["home", slot - 2] = send_home(slot - 2, sums[slot - 2])
+    stores = {"chunk": chunks, "received": received, "grad": grads, "contrib": contribs,
+              "home": homes}
+
+    def settle(produced):
         keys = list(produced)
         values = lax.optimization_barrier([produced[key] for key in keys])
         for (kind, step), value in zip(keys, values):
-            {"chunk": chunks, "received": received, "contrib": contribs, "sum": sums,
-             "home": homes}[kind][step] = value
+            stores[kind][step] = value
+
+    carried = {}
+    for slot in range(-1, n_node + 1):
+        first = dict(carried)
+        fetched = {}
+        if 0 < slot + 2 < n_node:
+            fetched["chunk", slot + 2] = fetch(slot + 2, chunks[slot + 1])
+        if 0 <= slot + 1 < n_node:
+            first["received", slot + 1] = send(slot + 1, chunks[slot + 1])
+        if 0 <= slot < n_node:
+            first["grad", slot] = compute(slot, received[slot])
+        if first:
+            settle(first)
+        second = dict(fetched)
+        carried = {}
+        if 0 <= slot < n_node:
+            second["contrib", slot] = expert_part(grads[slot], weight_in)
+        if 0 <= slot - 1 < n_node:
+            carried["home", slot - 1] = send_home(slot - 1, gather_back(slot - 1, contribs[slot - 1]))
+        if second:
+            settle(second)
+    settle(carried)
 
     total = homes[0].astype(jnp.float32)
     for step in range(1, n_node):

time: 381 us -> 423 us (1.11)
  waiting for transfers between devices: 187 us -> 229 us
    all_to_all x8, waiting for transfers between devices: 113 us -> 148 us  [spread(): lax.all_to_all(rows.reshape(n_local, capacity, rows.shape[-1]), 'local',...]
    ppermute x6, waiting for transfers between devices: 74.1 us -> 81 us  [shift(): lax.ppermute(value, 'node', [(i, (i + step) % n_node) for i in range(n_no...]
  transfers between devices with their start and end apart: 15 -> 15, of which waited for: 10 -> 9; matrix products, arithmetic and copies ran while one was open for 36% -> 27% of each run, Pallas kernels for 0% -> 0%
where the time goes in v7:
time: 423 us; the launch traced here: 416 us
  waiting for transfers between devices  229 us (54%)
  matrix products  131 us (31%)
  starting transfers between devices  44 us (10%)
  local copies, waits for them, and re-layouts  6.96 us (2%)
  other arithmetic  4.59 us (1%)
    all_to_all x8, waiting for transfers between devices, spread(): lax.all_to_all(rows.reshape(n_local, capacity, rows.shape[-1]), 'local',...  148 us
    ppermute x6, waiting for transfers between devices, shift(): lax.ppermute(value, 'node', [(i, (i + step) % n_node) for i in range(n_no...  81 us
    dot_general x4, matrix products, expert_part(): lax.dot_general(grad_pre, weight_in, (((1,), (1,)), ((), ())), preferred_...  59.5 us
    all_to_all x8, starting transfers between devices, spread(): lax.all_to_all(rows.reshape(n_local, capacity, rows.shape[-1]), 'local',...  34.2 us
    dot_general x4, matrix products, expert_grad_pre(): lax.dot_general(rows_dy, weight_out, (((1,), (1,)), ((), ())), preferred_...  24.2 us
    dot_general x4, matrix products, expert_grad_pre(): jnp.dot(rows_x, weight_in[:, FF:], preferred_element_type=jnp.float32)  24 us
    dot_general x4, matrix products, select_rows(): lax.dot_general(onehot, rows, (((0,), (0,)), ((), ())), preferred_element...  15 us
  transfers between devices with their start and end apart: 15, of which 9 were waited for; matrix products, arithmetic and copies ran while one was open for 27% of the time, Pallas kernels for 0%

profile of v7, /device:TPU:0, one launch (start us, length us, event | category | flops | bytes accessed | tf_op | source)
XLA Modules:
  0.0 416.3 jit_solution(12525653439489131362)
XLA Ops:
  0.0 0.9 copy.11
  0.9 0.2 reshape.88
  1.0 0.6 fusion.133
  1.9 0.1 copy.13
  2.1 0.4 fusion.166
  2.5 0.1 stack_reshape.12
  2.6 0.1 copy.14
  2.8 0.4 fusion.164
  3.3 0.1 copy.15
  3.6 0.4 fusion.163
  4.1 0.1 copy.16
  4.3 0.4 fusion.161
  4.8 0.6 copy.12
  5.5 5.2 %all-to-all-start.2 = ((bf16[8,4,32]{2,1,0:T(4,128)(2,1)}), bf16[8,4,32]{2,1,0:T(4,128)(2,1)S(1)}, u32[]{:S(2)}, u32[]{:S(2)}) async-start(bf16[8,4,32]{2,1,0:T(4,128)(2,1)} %copy.12), calls=%async_computation.2 | async-start | bytes 16384 | tf_op jit(solution)/shard_map/all_to_all | solution.py:89
  10.6 0.4 fusion.168
  11.1 1.3 constant_dynamic-update-slice_fusion
  12.4 3.0 convolution_convert_fusion.2
  15.4 4.5 %all-to-all-start.1 = ((bf16[8,32,7168]{2,1,0:T(8,128)(2,1)}), bf16[8,32,7168]{2,1,0:T(8,128)(2,1)}, u32[]{:S(2)}, u32[]{:S(2)}) async-start(bf16[8,32,7168]{2,1,0:T(8,128)(2,1)} %bitcast.108), calls=%async_computation.1 | async-start | bytes 7340032 | tf_op jit(solution)/shard_map/all_to_all | solution.py:92
  19.9 1.6 collective-permute-start
  21.5 0.4 fusion.169
  21.9 42.3 %collective-permute-done = bf16[128,7168]{1,0:T(8,128)(2,1)S(1)} collective-permute-done((bf16[128,7168]{1,0:T(8,128)(2,1)S(1)}, bf16[128,7168]{1,0:T(8,128)(2,1)S(1)}, u32[]{:S(2)}, u32[]{:S(2)}) %collective-permute-start) | collective-permute-done | bytes 1835040 | tf_op jit(solution)/shard_map/ppermute | solution.py:50
  64.2 1.2 copy-done
  65.4 3.0 convolution_convert_fusion.3
  68.5 4.6 %all-to-all-start = ((bf16[8,32,7168]{2,1,0:T(8,128)(2,1)}), bf16[8,32,7168]{2,1,0:T(8,128)(2,1)}, u32[]{:S(2)}, u32[]{:S(2)}) async-start(bf16[8,32,7168]{2,1,0:T(8,128)(2,1)} %bitcast.106), calls=%async_computation | async-start | bytes 7340032 | tf_op jit(solution)/shard_map/all_to_all | solution.py:92
  73.1 0.4 fusion.170
  73.7 0.2 collective-permute-start.1
  73.9 5.8 %fusion.141 = (bf16[256,1024]{1,0:T(8,128)(2,1)S(1)}, f32[256,1024]{1,0:T(8,128)S(1)}) fusion(bf16[1024,1024]{1,0:T(8,128)(2,1)} %param.11, s32[]{:T(128)S(6)} %select_n.75, f32[256]{0:T(256)S(1)} %reshape.105, bf16[1,1024,3584]{2,1,0:T(8,128)(2,1)} %param.13, bf16[256,7168]{1,0:T(8,128)(2,1)} %bitcast.4), kind=kOutput, calls=%fused_computation.80 | convolution fusion | flops 1881145344 | bytes 11273220 | tf_op jit(solution)/shard_map/dot_general | solution.py:22
  79.7 5.9 %fusion.107 = bf16[256,1024]{1,0:T(8,128)(2,1)S(1)} fusion(f32[256,1024]{1,0:T(8,128)S(1)} %get-tuple-element.44, bf16[3584,2048]{1,0:T(8,128)(2,1)} %bitcast.115, bf16[256,7168]{1,0:T(8,128)(2,1)} %bitcast.4, bf16[1024,1024]{1,0:T(8,128)(2,1)} %param.11, s32[]{:T(128)S(6)} %select_n.75), kind=kOutput, calls=%fused_computation.68 | convolution fusion | flops 1881931776 | bytes 11272196 | tf_op jit(solution)/shard_map/dot_general | solution.py:21
  85.7 30.9 %all-to-all-done = bf16[8,32,7168]{2,1,0:T(8,128)(2,1)} async-done(((bf16[8,32,7168]{2,1,0:T(8,128)(2,1)}), bf16[8,32,7168]{2,1,0:T(8,128)(2,1)}, u32[]{:S(2)}, u32[]{:S(2)}) %all-to-all-start) | async-done | bytes 3670048 | tf_op jit(solution)/shard_map/all_to_all | solution.py:92
  116.6 16.1 %convolution_convert_fusion.7 = bf16[256,3584]{1,0:T(8,128)(2,1)} fusion(bf16[256,2048]{1,0:T(8,128)(2,1)S(1)} %pad_maximum_fusion, bf16[1,3584,2048]{2,1,0:T(8,128)(2,1)} %param.12), kind=kOutput, calls=%fused_computation.15 | convolution fusion | flops 3759013888 | bytes 17563648 | tf_op jit(solution)/shard_map/dot_general | solution.py:34
  132.7 4.5 %convolution_convert_fusion.1 = bf16[256,7168]{1,0:T(8,128)(2,1)} fusion(bf16[128,256]{1,0:T(8,128)(2,1)S(1)} %fusion.170, bf16[128,7168]{1,0:T(8,128)(2,1)} %collective-permute-done.1), kind=kOutput, calls=%fused_computation.1 | convolution fusion | flops 471597056 | bytes 5570560 | tf_op jit(solution)/shard_map/dot_general | solution.py:41
  137.3 4.5 %all-to-all-start.4 = ((bf16[8,32,7168]{2,1,0:T(8,128)(2,1)}), bf16[8,32,7168]{2,1,0:T(8,128)(2,1)}, u32[]{:S(2)}, u32[]{:S(2)}) async-start(bf16[8,32,7168]{2,1,0:T(8,128)(2,1)} %bitcast.107), calls=%async_computation.4 | async-start | bytes 7340032 | tf_op jit(solution)/shard_map/all_to_all | solution.py:92
  141.8 6.8 %fusion.147 = (bf16[256,1024]{1,0:T(8,128)(2,1)S(1)}, f32[256,1024]{1,0:T(8,128)}) fusion(bf16[1024,1024]{1,0:T(8,128)(2,1)} %param.11, s32[]{:T(128)S(6)} %select_n.76, f32[256]{0:T(256)S(1)} %reshape.106, bf16[1,1024,3584]{2,1,0:T(8,128)(2,1)} %param.13, bf16[256,7168]{1,0:T(8,128)(2,1)} %bitcast.22), kind=kOutput, calls=%fused_computation.86 | convolution fusion | flops 1881145344 | bytes 11273220 | tf_op jit(solution)/shard_map/dot_general | solution.py:22
  148.6 36.6 %all-to-all-done.4 = bf16[8,32,7168]{2,1,0:T(8,128)(2,1)} async-done(((bf16[8,32,7168]{2,1,0:T(8,128)(2,1)}), bf16[8,32,7168]{2,1,0:T(8,128)(2,1)}, u32[]{:S(2)}, u32[]{:S(2)}) %all-to-all-start.4) | async-done | bytes 3670048 | tf_op jit(solution)/shard_map/all_to_all | solution.py:92
  185.3 3.8 all-to-all-start.3
  189.1 6.2 %fusion.112 = bf16[256,1024]{1,0:T(8,128)(2,1)S(1)} fusion(f32[256,1024]{1,0:T(8,128)} %get-tuple-element.46, bf16[3584,2048]{1,0:T(8,128)(2,1)} %bitcast.116, bf16[256,7168]{1,0:T(8,128)(2,1)} %bitcast.22, bf16[1024,1024]{1,0:T(8,128)(2,1)} %param.11, s32[]{:T(128)S(6)} %select_n.76), kind=kOutput, calls=%fused_computation.69 | convolution fusion | flops 1881931776 | bytes 11272196 | tf_op jit(solution)/shard_map/dot_general | solution.py:21
  195.4 16.2 %convolution_convert_fusion.6 = bf16[256,3584]{1,0:T(8,128)(2,1)} fusion(bf16[256,2048]{1,0:T(8,128)(2,1)S(1)} %pad_maximum_fusion.1, bf16[1,3584,2048]{2,1,0:T(8,128)(2,1)} %param.12), kind=kOutput, calls=%fused_computation.14 | convolution fusion | flops 3759013888 | bytes 17563648 | tf_op jit(solution)/shard_map/dot_general | solution.py:34
  211.6 1.3 all-to-all-done.3
  212.8 4.3 %all-to-all-start.6 = ((bf16[8,32,3584]{2,1,0:T(8,128)(2,1)}), bf16[8,32,3584]{2,1,0:T(8,128)(2,1)}, u32[]{:S(2)}, u32[]{:S(2)}) async-start(bf16[8,32,3584]{2,1,0:T(8,128)(2,1)} %bitcast.112), calls=%async_computation.6 | async-start | bytes 3670016 | tf_op jit(solution)/shard_map/all_to_all | solution.py:92
  217.2 0.4 fusion.171
  217.6 4.5 %convolution_convert_fusion = bf16[256,7168]{1,0:T(8,128)(2,1)} fusion(bf16[128,256]{1,0:T(8,128)(2,1)S(1)} %fusion.171, bf16[128,7168]{1,0:T(8,128)(2,1)} %collective-permute-done.2), kind=kOutput, calls=%fused_computation | convolution fusion | flops 471597056 | bytes 5570560 | tf_op jit(solution)/shard_map/dot_general | solution.py:41
  222.1 19.0 %all-to-all-done.6 = bf16[8,32,3584]{2,1,0:T(8,128)(2,1)} async-done(((bf16[8,32,3584]{2,1,0:T(8,128)(2,1)}), bf16[8,32,3584]{2,1,0:T(8,128)(2,1)}, u32[]{:S(2)}, u32[]{:S(2)}) %all-to-all-start.6) | async-done | bytes 1835040 | tf_op jit(solution)/shard_map/all_to_all | solution.py:92
  241.0 4.5 %all-to-all-start.5 = ((bf16[8,32,7168]{2,1,0:T(8,128)(2,1)}), bf16[8,32,7168]{2,1,0:T(8,128)(2,1)}, u32[]{:S(2)}, u32[]{:S(2)}) async-start(bf16[8,32,7168]{2,1,0:T(8,128)(2,1)} %bitcast.105), calls=%async_computation.5 | async-start | bytes 7340032 | tf_op jit(solution)/shard_map/all_to_all | solution.py:92
  245.7 0.4 convolution_convert_fusion.11
  246.1 1.2 copy-done.6
  247.3 5.8 %fusion.153 = (bf16[256,1024]{1,0:T(8,128)(2,1)S(1)}, f32[256,1024]{1,0:T(8,128)S(1)}) fusion(bf16[1024,1024]{1,0:T(8,128)(2,1)S(1)} %copy-done.6, s32[]{:T(128)S(6)} %select_n.77, f32[256]{0:T(256)S(1)} %reshape.107, bf16[1,1024,3584]{2,1,0:T(8,128)(2,1)} %param.13, bf16[256,7168]{1,0:T(8,128)(2,1)} %bitcast.24), kind=kOutput, calls=%fused_computation.92 | convolution fusion | flops 1881145344 | bytes 11273220 | tf_op jit(solution)/shard_map/dot_general | solution.py:22
  253.1 5.9 %fusion.117 = bf16[256,1024]{1,0:T(8,128)(2,1)S(1)} fusion(f32[256,1024]{1,0:T(8,128)S(1)} %get-tuple-element.48, bf16[3584,2048]{1,0:T(8,128)(2,1)} %bitcast.117, bf16[256,7168]{1,0:T(8,128)(2,1)} %bitcast.24, bf16[1024,1024]{1,0:T(8,128)(2,1)S(1)} %copy-done.6, s32[]{:T(128)S(6)} %select_n.77), kind=kOutput, calls=%fused_computation.70 | convolution fusion | flops 1881931776 | bytes 11272196 | tf_op jit(solution)/shard_map/dot_general | solution.py:21
  259.1 1.1 pad_maximum_fusion.2
  260.2 1.9 convolution_convert_fusion.10
  262.1 2.1 collective-permute-start.3
  264.2 24.8 %all-to-all-done.5 = bf16[8,32,7168]{2,1,0:T(8,128)(2,1)} async-done(((bf16[8,32,7168]{2,1,0:T(8,128)(2,1)}), bf16[8,32,7168]{2,1,0:T(8,128)(2,1)}, u32[]{:S(2)}, u32[]{:S(2)}) %all-to-all-start.5) | async-done | bytes 3670048 | tf_op jit(solution)/shard_map/all_to_all | solution.py:92
  289.0 5.8 %fusion.159 = (bf16[256,1024]{1,0:T(8,128)(2,1)S(1)}, f32[256,1024]{1,0:T(8,128)S(1)}) fusion(bf16[1024,1024]{1,0:T(8,128)(2,1)} %param.11, s32[]{:T(128)S(6)} %select_n.78, f32[256]{0:T(256)S(1)} %reshape.108, bf16[1,1024,3584]{2,1,0:T(8,128)(2,1)} %param.13, bf16[256,7168]{1,0:T(8,128)(2,1)} %bitcast.27), kind=kOutput, calls=%fused_computation.98 | convolution fusion | flops 1881145344 | bytes 11273220 | tf_op jit(solution)/shard_map/dot_general | solution.py:22
  294.8 5.9 %fusion.122 = bf16[256,1024]{1,0:T(8,128)(2,1)S(1)} fusion(f32[256,1024]{1,0:T(8,128)S(1)} %get-tuple-element.50, bf16[3584,2048]{1,0:T(8,128)(2,1)} %bitcast.118, bf16[256,7168]{1,0:T(8,128)(2,1)} %bitcast.27, bf16[1024,1024]{1,0:T(8,128)(2,1)} %param.11, s32[]{:T(128)S(6)} %select_n.78), kind=kOutput, calls=%fused_computation.71 | convolution fusion | flops 1881931776 | bytes 11272196 | tf_op jit(solution)/shard_map/dot_general | solution.py:21
  300.9 16.5 %convolution_convert_fusion.4 = bf16[256,3584]{1,0:T(8,128)(2,1)} fusion(bf16[256,2048]{1,0:T(8,128)(2,1)S(1)} %pad_maximum_fusion.3, bf16[1,3584,2048]{2,1,0:T(8,128)(2,1)} %param.12), kind=kOutput, calls=%fused_computation.12 | convolution fusion | flops 3759013888 | bytes 17563648 | tf_op jit(solution)/shard_map/dot_general | solution.py:34
  317.4 3.6 all-to-all-start.8
  321.0 10.8 %convolution_convert_fusion.5 = bf16[256,3584]{1,0:T(8,128)(2,1)} fusion(bf16[256,2048]{1,0:T(8,128)(2,1)} %pad_maximum_fusion.2, bf16[1,3584,2048]{2,1,0:T(8,128)(2,1)} %param.12), kind=kOutput, calls=%fused_computation.13 | convolution fusion | flops 3759013888 | bytes 17563648 | tf_op jit(solution)/shard_map/dot_general | solution.py:34
  331.7 13.0 %all-to-all-done.8 = bf16[8,32,3584]{2,1,0:T(8,128)(2,1)S(1)} async-done(((bf16[8,32,3584]{2,1,0:T(8,128)(2,1)}), bf16[8,32,3584]{2,1,0:T(8,128)(2,1)S(1)}, u32[]{:S(2)}, u32[]{:S(2)}) %all-to-all-start.8) | async-done | bytes 1835040 | tf_op jit(solution)/shard_map/all_to_all | solution.py:92
  344.7 4.3 %all-to-all-start.7 = ((bf16[8,32,3584]{2,1,0:T(8,128)(2,1)}), bf16[8,32,3584]{2,1,0:T(8,128)(2,1)}, u32[]{:S(2)}, u32[]{:S(2)}) async-start(bf16[8,32,3584]{2,1,0:T(8,128)(2,1)} %bitcast.113), calls=%async_computation.7 | async-start | bytes 3670016 | tf_op jit(solution)/shard_map/all_to_all | solution.py:92
  349.1 1.3 convolution_convert_fusion.8
  350.4 22.5 %all-to-all-done.7 = bf16[8,32,3584]{2,1,0:T(8,128)(2,1)} async-done(((bf16[8,32,3584]{2,1,0:T(8,128)(2,1)}), bf16[8,32,3584]{2,1,0:T(8,128)(2,1)}, u32[]{:S(2)}, u32[]{:S(2)}) %all-to-all-start.7) | async-done | bytes 1835040 | tf_op jit(solution)/shard_map/all_to_all | solution.py:92
  372.9 1.9 convolution_convert_fusion.9
  374.8 0.8 collective-permute-start.4
  375.6 38.7 %collective-permute-done.4 = bf16[128,3584]{1,0:T(8,128)(2,1)S(1)} collective-permute-done((bf16[128,3584]{1,0:T(8,128)(2,1)S(1)}, bf16[128,3584]{1,0:T(8,128)(2,1)S(1)}, u32[]{:S(2)}, u32[]{:S(2)}) %collective-permute-start.4) | collective-permute-done | bytes 917536 | tf_op jit(solution)/shard_map/ppermute | solution.py:50
  414.4 1.5 add_convert_fusion
  (45 shorter events, 1.5 us)
Async XLA Ops:
  0.0 1.9 copy-start.5
  2.1 9.0 %copy-start.2 = (bf16[128,3584]{1,0:T(8,128)(2,1)S(1)}, bf16[128,3584]{1,0:T(8,128)(2,1)}, u32[]{:S(2)}) copy-start(bf16[128,3584]{1,0:T(8,128)(2,1)} %param.7) | copy-start | bytes 2752516
  5.5 9.9 %all-to-all-start.2 = ((bf16[8,4,32]{2,1,0:T(4,128)(2,1)}), bf16[8,4,32]{2,1,0:T(4,128)(2,1)S(1)}, u32[]{:S(2)}, u32[]{:S(2)}) async-start(bf16[8,4,32]{2,1,0:T(4,128)(2,1)} %copy.12), calls=%async_computation.2 | async-start | bytes 16384 | tf_op jit(solution)/shard_map/all_to_all | solution.py:89
  15.4 53.1 %all-to-all-start.1 = ((bf16[8,32,7168]{2,1,0:T(8,128)(2,1)}), bf16[8,32,7168]{2,1,0:T(8,128)(2,1)}, u32[]{:S(2)}, u32[]{:S(2)}) async-start(bf16[8,32,7168]{2,1,0:T(8,128)(2,1)} %bitcast.108), calls=%async_computation.1 | async-start | bytes 7340032 | tf_op jit(solution)/shard_map/all_to_all | solution.py:92
  19.9 44.3 %collective-permute-start = (bf16[128,7168]{1,0:T(8,128)(2,1)S(1)}, bf16[128,7168]{1,0:T(8,128)(2,1)S(1)}, u32[]{:S(2)}, u32[]{:S(2)}) collective-permute-start(bf16[128,7168]{1,0:T(8,128)(2,1)S(1)} %constant_dynamic-update-slice_fusion), channel_id=1, source_target_pairs={{0,8},{8,16},{16,24},{24,0},{1,9},{9,17},{17,25},{25,1},{2,10},{10... | collective-permute-start | bytes 5505032 | tf_op jit(solution)/shard_map/ppermute | solution.py:50
  64.2 1.2 copy-start
  68.5 5.2 %copy-start.1 = (bf16[128,7168]{1,0:T(8,128)(2,1)S(1)}, bf16[128,7168]{1,0:T(8,128)(2,1)}, u32[]{:S(2)}) copy-start(bf16[128,7168]{1,0:T(8,128)(2,1)} %copy-done) | copy-start | bytes 5505028
  68.5 48.1 %all-to-all-start = ((bf16[8,32,7168]{2,1,0:T(8,128)(2,1)}), bf16[8,32,7168]{2,1,0:T(8,128)(2,1)}, u32[]{:S(2)}, u32[]{:S(2)}) async-start(bf16[8,32,7168]{2,1,0:T(8,128)(2,1)} %bitcast.106), calls=%async_computation | async-start | bytes 7340032 | tf_op jit(solution)/shard_map/all_to_all | solution.py:92
  73.7 59.0 %collective-permute-start.1 = (bf16[128,7168]{1,0:T(8,128)(2,1)S(1)}, bf16[128,7168]{1,0:T(8,128)(2,1)}, u32[]{:S(2)}, u32[]{:S(2)}) collective-permute-start(bf16[128,7168]{1,0:T(8,128)(2,1)S(1)} %copy-done.1), channel_id=1, source_target_pairs={{0,8},{8,16},{16,24},{24,0},{1,9},{9,17},{17,25},{25,1},{2,10},{10... | collective-permute-start | bytes 5505032 | tf_op jit(solution)/shard_map/ppermute | solution.py:50
  137.3 48.0 %all-to-all-start.4 = ((bf16[8,32,7168]{2,1,0:T(8,128)(2,1)}), bf16[8,32,7168]{2,1,0:T(8,128)(2,1)}, u32[]{:S(2)}, u32[]{:S(2)}) async-start(bf16[8,32,7168]{2,1,0:T(8,128)(2,1)} %bitcast.107), calls=%async_computation.4 | async-start | bytes 7340032 | tf_op jit(solution)/shard_map/all_to_all | solution.py:92
  141.8 69.7 %collective-permute-start.2 = (bf16[128,7168]{1,0:T(8,128)(2,1)}, bf16[128,7168]{1,0:T(8,128)(2,1)}, u32[]{:S(2)}, u32[]{:S(2)}) collective-permute-start(bf16[128,7168]{1,0:T(8,128)(2,1)} %collective-permute-done.1), channel_id=1, source_target_pairs={{0,8},{8,16},{16,24},{24,0},{1,9},{9,17},{17,25},{25,1},{2,10},{10... | collective-permute-start | bytes 5505032 | tf_op jit(solution)/shard_map/ppermute | solution.py:50
  185.3 27.6 %all-to-all-start.3 = ((bf16[8,32,3584]{2,1,0:T(8,128)(2,1)}), bf16[8,32,3584]{2,1,0:T(8,128)(2,1)S(1)}, u32[]{:S(2)}, u32[]{:S(2)}) async-start(bf16[8,32,3584]{2,1,0:T(8,128)(2,1)} %bitcast.111), calls=%async_computation.3 | async-start | bytes 3670016 | tf_op jit(solution)/shard_map/all_to_all | solution.py:92
  212.8 28.2 %all-to-all-start.6 = ((bf16[8,32,3584]{2,1,0:T(8,128)(2,1)}), bf16[8,32,3584]{2,1,0:T(8,128)(2,1)}, u32[]{:S(2)}, u32[]{:S(2)}) async-start(bf16[8,32,3584]{2,1,0:T(8,128)(2,1)} %bitcast.112), calls=%async_computation.6 | async-start | bytes 3670016 | tf_op jit(solution)/shard_map/all_to_all | solution.py:92
  241.0 48.0 %all-to-all-start.5 = ((bf16[8,32,7168]{2,1,0:T(8,128)(2,1)}), bf16[8,32,7168]{2,1,0:T(8,128)(2,1)}, u32[]{:S(2)}, u32[]{:S(2)}) async-start(bf16[8,32,7168]{2,1,0:T(8,128)(2,1)} %bitcast.105), calls=%async_computation.5 | async-start | bytes 7340032 | tf_op jit(solution)/shard_map/all_to_all | solution.py:92
  245.7 1.6 copy-start.6
  262.1 38.8 %collective-permute-start.3 = (bf16[128,3584]{1,0:T(8,128)(2,1)S(1)}, bf16[128,3584]{1,0:T(8,128)(2,1)S(1)}, u32[]{:S(2)}, u32[]{:S(2)}) collective-permute-start(bf16[128,3584]{1,0:T(8,128)(2,1)S(1)} %convolution_convert_fusion.10), channel_id=1, source_target_pairs={{0,24},{8,0},{16,8},{24,16},{1,25},{9,1},{17,9},{25,17},{2,26},{10... | collective-permute-start | bytes 2752520 | tf_op jit(solution)/shard_map/ppermute | solution.py:50
  300.9 16.5 %copy-start.3 = (bf16[128,3584]{1,0:T(8,128)(2,1)}, bf16[128,3584]{1,0:T(8,128)(2,1)S(1)}, u32[]{:S(2)}) copy-start(bf16[128,3584]{1,0:T(8,128)(2,1)S(1)} %collective-permute-done.3) | copy-start | bytes 2752516
  317.4 27.4 %all-to-all-start.8 = ((bf16[8,32,3584]{2,1,0:T(8,128)(2,1)}), bf16[8,32,3584]{2,1,0:T(8,128)(2,1)S(1)}, u32[]{:S(2)}, u32[]{:S(2)}) async-start(bf16[8,32,3584]{2,1,0:T(8,128)(2,1)} %bitcast.114), calls=%async_computation.8 | async-start | bytes 3670016 | tf_op jit(solution)/shard_map/all_to_all | solution.py:92
  344.7 28.2 %all-to-all-start.7 = ((bf16[8,32,3584]{2,1,0:T(8,128)(2,1)}), bf16[8,32,3584]{2,1,0:T(8,128)(2,1)}, u32[]{:S(2)}, u32[]{:S(2)}) async-start(bf16[8,32,3584]{2,1,0:T(8,128)(2,1)} %bitcast.113), calls=%async_computation.7 | async-start | bytes 3670016 | tf_op jit(solution)/shard_map/all_to_all | solution.py:92
  350.4 64.0 %copy-start.4 = (bf16[128,3584]{1,0:T(8,128)(2,1)S(1)}, bf16[128,3584]{1,0:T(8,128)(2,1)}, u32[]{:S(2)}) copy-start(bf16[128,3584]{1,0:T(8,128)(2,1)} %copy-done.3) | copy-start | bytes 2752516
  350.4 25.2 %collective-permute-start.5 = (bf16[128,3584]{1,0:T(8,128)(2,1)}, bf16[128,3584]{1,0:T(8,128)(2,1)S(1)}, u32[]{:S(2)}, u32[]{:S(2)}) collective-permute-start(bf16[128,3584]{1,0:T(8,128)(2,1)} %convolution_convert_fusion.8), channel_id=1, source_target_pairs={{0,8},{8,16},{16,24},{24,0},{1,9},{9,17},{17,25},{25,1},{2,10},{10... | collective-permute-start | bytes 2752520 | tf_op jit(solution)/shard_map/ppermute | solution.py:50
  374.8 39.5 %collective-permute-start.4 = (bf16[128,3584]{1,0:T(8,128)(2,1)S(1)}, bf16[128,3584]{1,0:T(8,128)(2,1)S(1)}, u32[]{:S(2)}, u32[]{:S(2)}) collective-permute-start(bf16[128,3584]{1,0:T(8,128)(2,1)S(1)} %convolution_convert_fusion.9), channel_id=1, source_target_pairs={{0,16},{8,24},{16,0},{24,8},{1,17},{9,25},{17,1},{25,9},{2,18},{10... | collective-permute-start | bytes 2752520 | tf_op jit(solution)/shard_map/ppermute | solution.py:50

commit v8 on v5

--- a/solution.py
+++ b/solution.py
@@ -108,11 +108,23 @@
             weight_out,
         )
 
+    local_here = lax.axis_index("local")
+
     def gather_back(step, contrib):
-        returned = spread(contrib).reshape(chunk_rows, model_width)
-        return jnp.dot(dispatch[step], returned, preferred_element_type=jnp.float32).astype(
-            jnp.bfloat16
-        )
+        blocks = contrib.reshape(n_local, capacity, model_width)
+        total_sum = None
+        for offset in range(n_local):
+            target = (local_here + offset) % n_local
+            piece = lax.dynamic_index_in_dim(blocks, target, 0, keepdims=False)
+            if offset:
+                piece = lax.ppermute(
+                    piece, "local", [(i, (i + offset) % n_local) for i in range(n_local)]
+                )
+            origin = (local_here - offset) % n_local
+            columns = lax.dynamic_slice_in_dim(dispatch[step], origin * capacity, capacity, 1)
+            part = jnp.dot(columns, piece, preferred_element_type=jnp.float32)
+            total_sum = part if total_sum is None else total_sum + part
+        return total_sum.astype(jnp.bfloat16)
 
     def send_home(step, node_sum):
         return shift(node_sum, n_node, -step)

time: 381 us -> 423 us (1.11)
  waiting for transfers between devices: 187 us -> 205 us
  starting transfers between devices: 43.7 us -> 58.8 us
  matrix products: 134 us -> 142 us
    ppermute x0 -> x28, waiting for transfers between devices: none -> 120 us  [gather_back(): lax.ppermute(piece, 'local', [(i, (i + offset) % n_local) for i in range(...]
    all_to_all x8 -> x4, waiting for transfers between devices: 113 us -> 37.3 us  [spread(): lax.all_to_all(rows.reshape(n_local, capacity, rows.shape[-1]), 'local',...]
    ppermute x0 -> x28, starting transfers between devices: none -> 29.2 us  [gather_back(): lax.ppermute(piece, 'local', [(i, (i + offset) % n_local) for i in range(...]
    ppermute x6, waiting for transfers between devices: 74.1 us -> 47.3 us  [shift(): lax.ppermute(value, 'node', [(i, (i + step) % n_node) for i in range(n_no...]
    dot_general x4 -> x32, matrix products: 3.52 us -> 23.2 us  [gather_back(): part = jnp.dot(columns, piece, preferred_element_type=jnp.float32)]
    dot_general x4, matrix products: 64.7 us -> 48.3 us  [expert_backward(): lax.dot_general(grad_pre, weight_in, (((1,), (1,)), ((), ())), preferred_...]
    all_to_all x8 -> x4, starting transfers between devices: 34.5 us -> 19.2 us  [spread(): lax.all_to_all(rows.reshape(n_local, capacity, rows.shape[-1]), 'local',...]
  transfers between devices with their start and end apart: 15 -> 39, of which waited for: 10 -> 17; matrix products, arithmetic and copies ran while one was open for 36% -> 28% of each run, Pallas kernels for 0% -> 0%
where the time goes in v8:
time: 423 us; the launch traced here: 417 us
  waiting for transfers between devices  205 us (48%)
  matrix products  142 us (34%)
  starting transfers between devices  58.8 us (14%)
  local copies, waits for them, and re-layouts  7.14 us (2%)
    ppermute x28, waiting for transfers between devices, gather_back(): lax.ppermute(piece, 'local', [(i, (i + offset) % n_local) for i in range(...  120 us
    dot_general x4, matrix products, expert_backward(): lax.dot_general(grad_pre, weight_in, (((1,), (1,)), ((), ())), preferred_...  48.3 us
    ppermute x6, waiting for transfers between devices, shift(): lax.ppermute(value, 'node', [(i, (i + step) % n_node) for i in range(n_no...  47.3 us
    all_to_all x4, waiting for transfers between devices, spread(): lax.all_to_all(rows.reshape(n_local, capacity, rows.shape[-1]), 'local',...  37.3 us
    ppermute x28, starting transfers between devices, gather_back(): lax.ppermute(piece, 'local', [(i, (i + offset) % n_local) for i in range(...  29.2 us
    dot_general x4, matrix products, expert_backward(): jnp.dot(rows_x, weight_in[:, FF:], preferred_element_type=jnp.float32)  26.5 us
    dot_general x4, matrix products, expert_backward(): lax.dot_general(rows_dy, weight_out, (((1,), (1,)), ((), ())), preferred_...  24.8 us
    dot_general x32, matrix products, gather_back(): part = jnp.dot(columns, piece, preferred_element_type=jnp.float32)  23.2 us
  transfers between devices with their start and end apart: 39, of which 17 were waited for; matrix products, arithmetic and copies ran while one was open for 28% of the time, Pallas kernels for 0%

profile of v8, /device:TPU:0, one launch (start us, length us, event | category | flops | bytes accessed | tf_op | source)
XLA Modules:
  0.0 416.9 jit_solution(14474850128820270473)
XLA Ops:
  0.0 0.9 copy.11
  2.5 1.3 constant_dynamic-update-slice_fusion
  3.7 3.0 convolution_convert_fusion.3
  6.7 5.3 %all-to-all-start = ((bf16[8,32,7168]{2,1,0:T(8,128)(2,1)}), bf16[8,32,7168]{2,1,0:T(8,128)(2,1)}, u32[]{:S(2)}, u32[]{:S(2)}) async-start(bf16[8,32,7168]{2,1,0:T(8,128)(2,1)} %bitcast.185), calls=%async_computation | async-start | bytes 7340032 | tf_op jit(solution)/shard_map/all_to_all | solution.py:89
  12.0 2.4 collective-permute-start
  18.4 37.3 %all-to-all-done = bf16[8,32,7168]{2,1,0:T(8,128)(2,1)} async-done(((bf16[8,32,7168]{2,1,0:T(8,128)(2,1)}), bf16[8,32,7168]{2,1,0:T(8,128)(2,1)}, u32[]{:S(2)}, u32[]{:S(2)}) %all-to-all-start) | async-done | bytes 3670048 | tf_op jit(solution)/shard_map/all_to_all | solution.py:89
  55.6 3.3 all-to-all-start.2
  59.0 4.6 %convolution_convert_fusion.2 = bf16[256,7168]{1,0:T(8,128)(2,1)} fusion(bf16[128,256]{1,0:T(8,128)(2,1)S(1)} %fusion.206, bf16[128,7168]{1,0:T(8,128)(2,1)} %collective-permute-done), kind=kOutput, calls=%fused_computation.2 | convolution fusion | flops 471597056 | bytes 5570560 | tf_op jit(solution)/shard_map/dot_general | solution.py:38
  63.6 4.5 %all-to-all-start.1 = ((bf16[8,32,7168]{2,1,0:T(8,128)(2,1)}), bf16[8,32,7168]{2,1,0:T(8,128)(2,1)}, u32[]{:S(2)}, u32[]{:S(2)}) async-start(bf16[8,32,7168]{2,1,0:T(8,128)(2,1)} %bitcast.188), calls=%async_computation.1 | async-start | bytes 7340032 | tf_op jit(solution)/shard_map/all_to_all | solution.py:89
  69.3 2.7 collective-permute-start.1
  72.0 5.8 %fusion.165 = (bf16[256,1024]{1,0:T(8,128)(2,1)S(1)}, f32[256,1024]{1,0:T(8,128)S(1)}) fusion(bf16[1024,1024]{1,0:T(8,128)(2,1)} %param.11, s32[]{:T(128)S(6)} %select_n.330, f32[256]{0:T(256)S(1)} %reshape.89, bf16[1,1024,3584]{2,1,0:T(8,128)(2,1)} %param.13, bf16[256,7168]{1,0:T(8,128)(2,1)} %bitcast.4), kind=kOutput, calls=%fused_computation.108 | convolution fusion | flops 1881145344 | bytes 11273220 | tf_op jit(solution)/shard_map/dot_general | solution.py:22
  77.8 5.9 %fusion.131 = bf16[256,1024]{1,0:T(8,128)(2,1)S(1)} fusion(f32[256,1024]{1,0:T(8,128)S(1)} %get-tuple-element.82, bf16[3584,2048]{1,0:T(8,128)(2,1)} %bitcast.197, bf16[256,7168]{1,0:T(8,128)(2,1)} %bitcast.4, bf16[1024,1024]{1,0:T(8,128)(2,1)} %param.11, s32[]{:T(128)S(6)} %select_n.330), kind=kOutput, calls=%fused_computation.96 | convolution fusion | flops 1881931776 | bytes 11272196 | tf_op jit(solution)/shard_map/dot_general | solution.py:21
  83.8 16.1 %convolution_convert_fusion.7 = bf16[256,3584]{1,0:T(8,128)(2,1)} fusion(bf16[256,1024]{1,0:T(8,128)(2,1)S(1)} %get-tuple-element.81, bf16[256,1024]{1,0:T(8,128)(2,1)S(1)} %fusion.131, bf16[1,3584,2048]{2,1,0:T(8,128)(2,1)} %param.12), kind=kOutput, calls=%fused_computation.15 | convolution fusion | flops 3761111040 | bytes 17563648 | tf_op jit(solution)/shard_map/dot_general | solution.py:31
  99.9 15.0 %collective-permute-done.1 = bf16[128,7168]{1,0:T(8,128)(2,1)} collective-permute-done((bf16[128,7168]{1,0:T(8,128)(2,1)}, bf16[128,7168]{1,0:T(8,128)(2,1)}, u32[]{:S(2)}, u32[]{:S(2)}) %collective-permute-start.1) | collective-permute-done | bytes 1835040 | tf_op jit(solution)/shard_map/ppermute | solution.py:47
  114.9 5.8 %fusion.171 = (bf16[256,1024]{1,0:T(8,128)(2,1)S(1)}, f32[256,1024]{1,0:T(8,128)S(1)}) fusion(bf16[1024,1024]{1,0:T(8,128)(2,1)} %param.11, s32[]{:T(128)S(6)} %select_n.331, f32[256]{0:T(256)S(1)} %reshape.90, bf16[1,1024,3584]{2,1,0:T(8,128)(2,1)} %param.13, bf16[256,7168]{1,0:T(8,128)(2,1)} %bitcast.20), kind=kOutput, calls=%fused_computation.114 | convolution fusion | flops 1881145344 | bytes 11273220 | tf_op jit(solution)/shard_map/dot_general | solution.py:22
  120.7 6.9 %fusion.136 = bf16[256,1024]{1,0:T(8,128)(2,1)} fusion(f32[256,1024]{1,0:T(8,128)S(1)} %get-tuple-element.84, bf16[3584,2048]{1,0:T(8,128)(2,1)} %bitcast.198, bf16[256,7168]{1,0:T(8,128)(2,1)} %bitcast.20, bf16[1024,1024]{1,0:T(8,128)(2,1)} %param.11, s32[]{:T(128)S(6)} %select_n.331), kind=kOutput, calls=%fused_computation.97 | convolution fusion | flops 1881931776 | bytes 11272196 | tf_op jit(solution)/shard_map/dot_general | solution.py:21
  127.7 1.7 collective-permute-start.4
  129.8 1.5 collective-permute-start.8
  131.3 4.5 %convolution_convert_fusion.1 = bf16[256,7168]{1,0:T(8,128)(2,1)} fusion(bf16[128,256]{1,0:T(8,128)(2,1)S(1)} %fusion.207, bf16[128,7168]{1,0:T(8,128)(2,1)} %collective-permute-done.1), kind=kOutput, calls=%fused_computation.1 | convolution fusion | flops 471597056 | bytes 5570560 | tf_op jit(solution)/shard_map/dot_general | solution.py:38
  135.9 4.7 %all-to-all-start.3 = ((bf16[8,32,7168]{2,1,0:T(8,128)(2,1)}), bf16[8,32,7168]{2,1,0:T(8,128)(2,1)}, u32[]{:S(2)}, u32[]{:S(2)}) async-start(bf16[8,32,7168]{2,1,0:T(8,128)(2,1)} %bitcast.186), calls=%async_computation.3 | async-start | bytes 7340032 | tf_op jit(solution)/shard_map/all_to_all | solution.py:89
  140.5 10.7 %convolution_convert_fusion.6 = bf16[256,3584]{1,0:T(8,128)(2,1)} fusion(bf16[256,1024]{1,0:T(8,128)(2,1)S(1)} %get-tuple-element.83, bf16[256,1024]{1,0:T(8,128)(2,1)} %fusion.136, bf16[1,3584,2048]{2,1,0:T(8,128)(2,1)} %param.12), kind=kOutput, calls=%fused_computation.14 | convolution fusion | flops 3761111040 | bytes 17563648 | tf_op jit(solution)/shard_map/dot_general | solution.py:31
  151.2 1.4 fusion.220
  152.6 2.2 collective-permute-start.5
  155.2 33.1 %collective-permute-done.5 = bf16[32,3584]{1,0:T(8,128)(2,1)S(1)} collective-permute-done((bf16[32,3584]{1,0:T(8,128)(2,1)S(1)}, bf16[32,3584]{1,0:T(8,128)(2,1)S(1)}, u32[]{:S(2)}, u32[]{:S(2)}) %collective-permute-start.5) | collective-permute-done | bytes 229408 | tf_op jit(solution)/shard_map/ppermute | solution.py:120
  189.7 5.3 %collective-permute-done.6 = bf16[32,3584]{1,0:T(8,128)(2,1)S(1)} collective-permute-done((bf16[32,3584]{1,0:T(8,128)(2,1)S(1)}, bf16[32,3584]{1,0:T(8,128)(2,1)S(1)}, u32[]{:S(2)}, u32[]{:S(2)}) %collective-permute-start.6) | collective-permute-done | bytes 229408 | tf_op jit(solution)/shard_map/ppermute | solution.py:120
  195.5 5.0 %collective-permute-done.7 = bf16[32,3584]{1,0:T(8,128)(2,1)S(1)} collective-permute-done((bf16[32,3584]{1,0:T(8,128)(2,1)S(1)}, bf16[32,3584]{1,0:T(8,128)(2,1)S(1)}, u32[]{:S(2)}, u32[]{:S(2)}) %collective-permute-start.7) | collective-permute-done | bytes 229408 | tf_op jit(solution)/shard_map/ppermute | solution.py:120
  202.7 6.6 %fusion.177 = (bf16[256,1024]{1,0:T(8,128)(2,1)}, f32[256,1024]{1,0:T(8,128)S(1)}) fusion(bf16[1024,1024]{1,0:T(8,128)(2,1)} %param.11, s32[]{:T(128)S(6)} %select_n.363, f32[256]{0:T(256)S(1)} %reshape.91, bf16[1,1024,3584]{2,1,0:T(8,128)(2,1)} %param.13, bf16[256,7168]{1,0:T(8,128)(2,1)} %bitcast.31), kind=kOutput, calls=%fused_computation.120 | convolution fusion | flops 1881145344 | bytes 11273220 | tf_op jit(solution)/shard_map/dot_general | solution.py:22
  209.3 6.9 %fusion.141 = bf16[256,1024]{1,0:T(8,128)(2,1)} fusion(f32[256,1024]{1,0:T(8,128)S(1)} %get-tuple-element.86, bf16[3584,2048]{1,0:T(8,128)(2,1)} %bitcast.199, bf16[256,7168]{1,0:T(8,128)(2,1)} %bitcast.31, bf16[1024,1024]{1,0:T(8,128)(2,1)} %param.11, s32[]{:T(128)S(6)} %select_n.363), kind=kOutput, calls=%fused_computation.98 | convolution fusion | flops 1881931776 | bytes 11272196 | tf_op jit(solution)/shard_map/dot_general | solution.py:21
  217.0 1.8 collective-permute-start.11
  218.8 1.0 collective-permute-start.16
  219.9 1.7 collective-permute-start.15
  222.5 4.5 %convolution_convert_fusion = bf16[256,7168]{1,0:T(8,128)(2,1)} fusion(bf16[128,256]{1,0:T(8,128)(2,1)S(1)} %fusion.204, bf16[128,7168]{1,0:T(8,128)(2,1)} %collective-permute-done.2), kind=kOutput, calls=%fused_computation | convolution fusion | flops 471597056 | bytes 5570560 | tf_op jit(solution)/shard_map/dot_general | solution.py:38
  227.0 4.7 %all-to-all-start.4 = ((bf16[8,32,7168]{2,1,0:T(8,128)(2,1)}), bf16[8,32,7168]{2,1,0:T(8,128)(2,1)}, u32[]{:S(2)}, u32[]{:S(2)}) async-start(bf16[8,32,7168]{2,1,0:T(8,128)(2,1)} %bitcast.187), calls=%async_computation.4 | async-start | bytes 7340032 | tf_op jit(solution)/shard_map/all_to_all | solution.py:89
  231.7 10.7 %convolution_convert_fusion.5 = bf16[256,3584]{1,0:T(8,128)(2,1)} fusion(bf16[256,1024]{1,0:T(8,128)(2,1)} %get-tuple-element.85, bf16[256,1024]{1,0:T(8,128)(2,1)} %fusion.141, bf16[1,3584,2048]{2,1,0:T(8,128)(2,1)} %param.12), kind=kOutput, calls=%fused_computation.13 | convolution fusion | flops 3761111040 | bytes 17563648 | tf_op jit(solution)/shard_map/dot_general | solution.py:31
  242.4 1.4 fusion.218
  243.8 1.8 collective-permute-start.12
  245.6 1.4 convolution_add_fusion.5
  247.0 34.5 %collective-permute-done.12 = bf16[32,3584]{1,0:T(8,128)(2,1)S(1)} collective-permute-done((bf16[32,3584]{1,0:T(8,128)(2,1)S(1)}, bf16[32,3584]{1,0:T(8,128)(2,1)S(1)}, u32[]{:S(2)}, u32[]{:S(2)}) %collective-permute-start.12) | collective-permute-done | bytes 229408 | tf_op jit(solution)/shard_map/ppermute | solution.py:120
  282.3 5.3 %collective-permute-done.13 = bf16[32,3584]{1,0:T(8,128)(2,1)S(1)} collective-permute-done((bf16[32,3584]{1,0:T(8,128)(2,1)S(1)}, bf16[32,3584]{1,0:T(8,128)(2,1)S(1)}, u32[]{:S(2)}, u32[]{:S(2)}) %collective-permute-start.13) | collective-permute-done | bytes 229408 | tf_op jit(solution)/shard_map/ppermute | solution.py:120
  289.4 2.7 fusion.29
  292.1 1.9 collective-permute-start.24
  293.9 6.6 %fusion.183 = (bf16[256,1024]{1,0:T(8,128)(2,1)}, f32[256,1024]{1,0:T(8,128)S(1)}) fusion(bf16[1024,1024]{1,0:T(8,128)(2,1)} %param.11, s32[]{:T(128)S(6)} %select_n.364, f32[256]{0:T(256)S(1)} %reshape.92, bf16[1,1024,3584]{2,1,0:T(8,128)(2,1)} %param.13, bf16[256,7168]{1,0:T(8,128)(2,1)} %bitcast.41), kind=kOutput, calls=%fused_computation.126 | convolution fusion | flops 1881145344 | bytes 11273220 | tf_op jit(solution)/shard_map/dot_general | solution.py:22
  300.5 6.9 %fusion.146 = bf16[256,1024]{1,0:T(8,128)(2,1)} fusion(f32[256,1024]{1,0:T(8,128)S(1)} %get-tuple-element.88, bf16[3584,2048]{1,0:T(8,128)(2,1)} %bitcast.200, bf16[256,7168]{1,0:T(8,128)(2,1)} %bitcast.41, bf16[1024,1024]{1,0:T(8,128)(2,1)} %param.11, s32[]{:T(128)S(6)} %select_n.364), kind=kOutput, calls=%fused_computation.99 | convolution fusion | flops 1881931776 | bytes 11272196 | tf_op jit(solution)/shard_map/dot_general | solution.py:21
  307.4 1.0 dynamic-slice_bitcast_fusion.12
  308.4 2.9 collective-permute-start.22
  311.8 10.8 %convolution_convert_fusion.4 = bf16[256,3584]{1,0:T(8,128)(2,1)} fusion(bf16[256,1024]{1,0:T(8,128)(2,1)} %get-tuple-element.87, bf16[256,1024]{1,0:T(8,128)(2,1)} %fusion.146, bf16[1,3584,2048]{2,1,0:T(8,128)(2,1)} %param.12), kind=kOutput, calls=%fused_computation.12 | convolution fusion | flops 3761111040 | bytes 17563648 | tf_op jit(solution)/shard_map/dot_general | solution.py:31
  323.5 1.9 collective-permute-start.19
  325.4 1.4 convolution_add_fusion.3
  326.7 4.7 %collective-permute-done.19 = bf16[32,3584]{1,0:T(8,128)(2,1)S(1)} collective-permute-done((bf16[32,3584]{1,0:T(8,128)(2,1)S(1)}, bf16[32,3584]{1,0:T(8,128)(2,1)S(1)}, u32[]{:S(2)}, u32[]{:S(2)}) %collective-permute-start.19) | collective-permute-done | bytes 229408 | tf_op jit(solution)/shard_map/ppermute | solution.py:120
  331.4 0.9 collective-permute-start.20
  332.8 4.7 %collective-permute-done.20 = bf16[32,3584]{1,0:T(8,128)(2,1)S(1)} collective-permute-done((bf16[32,3584]{1,0:T(8,128)(2,1)S(1)}, bf16[32,3584]{1,0:T(8,128)(2,1)S(1)}, u32[]{:S(2)}, u32[]{:S(2)}) %collective-permute-start.20) | collective-permute-done | bytes 229408 | tf_op jit(solution)/shard_map/ppermute | solution.py:120
  337.9 5.0 %collective-permute-done.21 = bf16[32,3584]{1,0:T(8,128)(2,1)S(1)} collective-permute-done((bf16[32,3584]{1,0:T(8,128)(2,1)S(1)}, bf16[32,3584]{1,0:T(8,128)(2,1)S(1)}, u32[]{:S(2)}, u32[]{:S(2)}) %collective-permute-start.21) | collective-permute-done | bytes 229408 | tf_op jit(solution)/shard_map/ppermute | solution.py:120
  343.4 1.4 fusion.241
  345.2 1.9 fusion.30
  347.4 3.6 collective-permute-start.26
  353.1 3.2 collective-permute-done.25
  356.8 10.5 %collective-permute-done.27 = bf16[32,3584]{1,0:T(8,128)(2,1)S(1)} collective-permute-done((bf16[32,3584]{1,0:T(8,128)(2,1)S(1)}, bf16[32,3584]{1,0:T(8,128)(2,1)S(1)}, u32[]{:S(2)}, u32[]{:S(2)}) %collective-permute-start.27) | collective-permute-done | bytes 229408 | tf_op jit(solution)/shard_map/ppermute | solution.py:120
  367.2 1.2 collective-permute-start.28
  368.9 5.6 %collective-permute-done.28 = bf16[32,3584]{1,0:T(8,128)(2,1)S(1)} collective-permute-done((bf16[32,3584]{1,0:T(8,128)(2,1)S(1)}, bf16[32,3584]{1,0:T(8,128)(2,1)S(1)}, u32[]{:S(2)}, u32[]{:S(2)}) %collective-permute-start.28) | collective-permute-done | bytes 229408 | tf_op jit(solution)/shard_map/ppermute | solution.py:120
  374.6 2.1 collective-permute-start.29
  377.1 3.4 collective-permute-done.29
  382.7 8.1 %collective-permute-done.32 = bf16[128,3584]{1,0:T(8,128)(2,1)S(1)} collective-permute-done((bf16[128,3584]{1,0:T(8,128)(2,1)S(1)}, bf16[128,3584]{1,0:T(8,128)(2,1)S(1)}, u32[]{:S(2)}, u32[]{:S(2)}) %collective-permute-start.32) | collective-permute-done | bytes 917536 | tf_op jit(solution)/shard_map/ppermute | solution.py:47
  390.9 24.2 %collective-permute-done.33 = bf16[128,3584]{1,0:T(8,128)(2,1)S(1)} collective-permute-done((bf16[128,3584]{1,0:T(8,128)(2,1)S(1)}, bf16[128,3584]{1,0:T(8,128)(2,1)S(1)}, u32[]{:S(2)}, u32[]{:S(2)}) %collective-permute-start.33) | collective-permute-done | bytes 917536 | tf_op jit(solution)/shard_map/ppermute | solution.py:47
  415.1 1.4 add_convert_fusion
  (125 shorter events, 24.8 us)
Async XLA Ops:
  0.0 2.4 copy-start.4
  6.7 7.7 %copy-start.8 = (s32[4,128,8]{1,2,0:T(8,128)S(1)}, s32[4,128,8]{1,2,0:T(8,128)}, u32[]{:S(2)}) copy-start(s32[4,128,8]{1,2,0:T(8,128)} %param.10) | copy-start | bytes 49156
  6.7 48.9 %all-to-all-start = ((bf16[8,32,7168]{2,1,0:T(8,128)(2,1)}), bf16[8,32,7168]{2,1,0:T(8,128)(2,1)}, u32[]{:S(2)}, u32[]{:S(2)}) async-start(bf16[8,32,7168]{2,1,0:T(8,128)(2,1)} %bitcast.185), calls=%async_computation | async-start | bytes 7340032 | tf_op jit(solution)/shard_map/all_to_all | solution.py:89
  12.0 46.9 %collective-permute-start = (bf16[128,7168]{1,0:T(8,128)(2,1)S(1)}, bf16[128,7168]{1,0:T(8,128)(2,1)}, u32[]{:S(2)}, u32[]{:S(2)}) collective-permute-start(bf16[128,7168]{1,0:T(8,128)(2,1)S(1)} %constant_dynamic-update-slice_fusion), channel_id=1, source_target_pairs={{0,8},{8,16},{16,24},{24,0},{1,9},{9,17},{17,25},{25,1},{2,10},{10... | collective-permute-start | bytes 5505032 | tf_op jit(solution)/shard_map/ppermute | solution.py:47
  55.6 8.0 %all-to-all-start.2 = ((bf16[8,4,32]{2,1,0:T(4,128)(2,1)}), bf16[8,4,32]{2,1,0:T(4,128)(2,1)S(1)}, u32[]{:S(2)}, u32[]{:S(2)}) async-start(bf16[8,4,32]{2,1,0:T(4,128)(2,1)} %copy.12), calls=%async_computation.2 | async-start | bytes 16384 | tf_op jit(solution)/shard_map/all_to_all | solution.py:86
  63.6 51.3 %all-to-all-start.1 = ((bf16[8,32,7168]{2,1,0:T(8,128)(2,1)}), bf16[8,32,7168]{2,1,0:T(8,128)(2,1)}, u32[]{:S(2)}, u32[]{:S(2)}) async-start(bf16[8,32,7168]{2,1,0:T(8,128)(2,1)} %bitcast.188), calls=%async_computation.1 | async-start | bytes 7340032 | tf_op jit(solution)/shard_map/all_to_all | solution.py:89
  69.3 45.6 %collective-permute-start.1 = (bf16[128,7168]{1,0:T(8,128)(2,1)}, bf16[128,7168]{1,0:T(8,128)(2,1)}, u32[]{:S(2)}, u32[]{:S(2)}) collective-permute-start(bf16[128,7168]{1,0:T(8,128)(2,1)} %collective-permute-done), channel_id=1, source_target_pairs={{0,8},{8,16},{16,24},{24,0},{1,9},{9,17},{17,25},{25,1},{2,10},{10... | collective-permute-start | bytes 5505032 | tf_op jit(solution)/shard_map/ppermute | solution.py:47
  120.7 6.9 %copy-start.3 = (bf16[256,3584]{1,0:T(8,128)(2,1)S(1)}, bf16[256,3584]{1,0:T(8,128)(2,1)}, u32[]{:S(2)}) copy-start(bf16[256,3584]{1,0:T(8,128)(2,1)} %convolution_convert_fusion.7) | copy-start | bytes 5505028
  127.7 74.2 %collective-permute-start.4 = (bf16[32,3584]{1,0:T(8,128)(2,1)S(1)}, bf16[32,3584]{1,0:T(8,128)(2,1)S(1)}, u32[]{:S(2)}, u32[]{:S(2)}) collective-permute-start(bf16[32,3584]{1,0:T(8,128)(2,1)S(1)} %get-tuple-element.70), channel_id=1, source_target_pairs={{0,2},{1,3},{2,4},{3,5},{4,6},{5,7},{6,0},{7,1},{8,10},{9,11},{10,... | collective-permute-start | bytes 688136 | tf_op jit(solution)/shard_map/ppermute | solution.py:120
  129.4 72.0 %collective-permute-start.9 = (bf16[32,3584]{1,0:T(8,128)(2,1)S(1)}, bf16[32,3584]{1,0:T(8,128)(2,1)S(1)}, u32[]{:S(2)}, u32[]{:S(2)}) collective-permute-start(bf16[32,3584]{1,0:T(8,128)(2,1)S(1)} %get-tuple-element.71), channel_id=1, source_target_pairs={{0,7},{1,0},{2,1},{3,2},{4,3},{5,4},{6,5},{7,6},{8,15},{9,8},{10,9... | collective-permute-start | bytes 688136 | tf_op jit(solution)/shard_map/ppermute | solution.py:120
  129.8 71.1 %collective-permute-start.8 = (bf16[32,3584]{1,0:T(8,128)(2,1)S(1)}, bf16[32,3584]{1,0:T(8,128)(2,1)S(1)}, u32[]{:S(2)}, u32[]{:S(2)}) collective-permute-start(bf16[32,3584]{1,0:T(8,128)(2,1)S(1)} %get-tuple-element.72), channel_id=1, source_target_pairs={{0,6},{1,7},{2,0},{3,1},{4,2},{5,3},{6,4},{7,5},{8,14},{9,15},{10,... | collective-permute-start | bytes 688136 | tf_op jit(solution)/shard_map/ppermute | solution.py:120
  131.3 21.2 %collective-permute-start.3 = (bf16[32,3584]{1,0:T(8,128)(2,1)S(1)}, bf16[32,3584]{1,0:T(8,128)(2,1)S(1)}, u32[]{:S(2)}, u32[]{:S(2)}) collective-permute-start(bf16[32,3584]{1,0:T(8,128)(2,1)S(1)} %get-tuple-element.76), channel_id=1, source_target_pairs={{0,1},{1,2},{2,3},{3,4},{4,5},{5,6},{6,7},{7,0},{8,9},{9,10},{10,1... | collective-permute-start | bytes 688136 | tf_op jit(solution)/shard_map/ppermute | solution.py:120
  131.3 71.4 %collective-permute-start.2 = (bf16[128,7168]{1,0:T(8,128)(2,1)}, bf16[128,7168]{1,0:T(8,128)(2,1)}, u32[]{:S(2)}, u32[]{:S(2)}) collective-permute-start(bf16[128,7168]{1,0:T(8,128)(2,1)} %collective-permute-done.1), channel_id=1, source_target_pairs={{0,8},{8,16},{16,24},{24,0},{1,9},{9,17},{17,25},{25,1},{2,10},{10... | collective-permute-start | bytes 5505032 | tf_op jit(solution)/shard_map/ppermute | solution.py:47
  135.9 66.9 %all-to-all-start.3 = ((bf16[8,32,7168]{2,1,0:T(8,128)(2,1)}), bf16[8,32,7168]{2,1,0:T(8,128)(2,1)}, u32[]{:S(2)}, u32[]{:S(2)}) async-start(bf16[8,32,7168]{2,1,0:T(8,128)(2,1)} %bitcast.186), calls=%async_computation.3 | async-start | bytes 7340032 | tf_op jit(solution)/shard_map/all_to_all | solution.py:89
  152.6 35.8 %collective-permute-start.5 = (bf16[32,3584]{1,0:T(8,128)(2,1)S(1)}, bf16[32,3584]{1,0:T(8,128)(2,1)S(1)}, u32[]{:S(2)}, u32[]{:S(2)}) collective-permute-start(bf16[32,3584]{1,0:T(8,128)(2,1)S(1)} %get-tuple-element.75), channel_id=1, source_target_pairs={{0,3},{1,4},{2,5},{3,6},{4,7},{5,0},{6,1},{7,2},{8,11},{9,12},{10,... | collective-permute-start | bytes 688136 | tf_op jit(solution)/shard_map/ppermute | solution.py:120
  188.4 6.7 %collective-permute-start.6 = (bf16[32,3584]{1,0:T(8,128)(2,1)S(1)}, bf16[32,3584]{1,0:T(8,128)(2,1)S(1)}, u32[]{:S(2)}, u32[]{:S(2)}) collective-permute-start(bf16[32,3584]{1,0:T(8,128)(2,1)S(1)} %get-tuple-element.74), channel_id=1, source_target_pairs={{0,4},{1,5},{2,6},{3,7},{4,0},{5,1},{6,2},{7,3},{8,12},{9,13},{10,... | collective-permute-start | bytes 688136 | tf_op jit(solution)/shard_map/ppermute | solution.py:120
  195.1 5.4 %collective-permute-start.7 = (bf16[32,3584]{1,0:T(8,128)(2,1)S(1)}, bf16[32,3584]{1,0:T(8,128)(2,1)S(1)}, u32[]{:S(2)}, u32[]{:S(2)}) collective-permute-start(bf16[32,3584]{1,0:T(8,128)(2,1)S(1)} %get-tuple-element.73), channel_id=1, source_target_pairs={{0,5},{1,6},{2,7},{3,0},{4,1},{5,2},{6,3},{7,4},{8,13},{9,14},{10,... | collective-permute-start | bytes 688136 | tf_op jit(solution)/shard_map/ppermute | solution.py:120
  209.3 6.9 %copy-start = (bf16[256,3584]{1,0:T(8,128)(2,1)S(1)}, bf16[256,3584]{1,0:T(8,128)(2,1)}, u32[]{:S(2)}) copy-start(bf16[256,3584]{1,0:T(8,128)(2,1)} %convolution_convert_fusion.6) | copy-start | bytes 5505028
  217.0 72.4 %collective-permute-start.11 = (bf16[32,3584]{1,0:T(8,128)(2,1)S(1)}, bf16[32,3584]{1,0:T(8,128)(2,1)}, u32[]{:S(2)}, u32[]{:S(2)}) collective-permute-start(bf16[32,3584]{1,0:T(8,128)(2,1)S(1)} %get-tuple-element.63), channel_id=1, source_target_pairs={{0,2},{1,3},{2,4},{3,5},{4,6},{5,7},{6,0},{7,1},{8,10},{9,11},{10,... | collective-permute-start | bytes 688136 | tf_op jit(solution)/shard_map/ppermute | solution.py:120
  218.8 70.1 %collective-permute-start.16 = (bf16[32,3584]{1,0:T(8,128)(2,1)S(1)}, bf16[32,3584]{1,0:T(8,128)(2,1)S(1)}, u32[]{:S(2)}, u32[]{:S(2)}) collective-permute-start(bf16[32,3584]{1,0:T(8,128)(2,1)S(1)} %get-tuple-element.64), channel_id=1, source_target_pairs={{0,7},{1,0},{2,1},{3,2},{4,3},{5,4},{6,5},{7,6},{8,15},{9,8},{10,9... | collective-permute-start | bytes 688136 | tf_op jit(solution)/shard_map/ppermute | solution.py:120
  219.9 68.6 %collective-permute-start.15 = (bf16[32,3584]{1,0:T(8,128)(2,1)S(1)}, bf16[32,3584]{1,0:T(8,128)(2,1)S(1)}, u32[]{:S(2)}, u32[]{:S(2)}) collective-permute-start(bf16[32,3584]{1,0:T(8,128)(2,1)S(1)} %get-tuple-element.65), channel_id=1, source_target_pairs={{0,6},{1,7},{2,0},{3,1},{4,2},{5,3},{6,4},{7,5},{8,14},{9,15},{10,... | collective-permute-start | bytes 688136 | tf_op jit(solution)/shard_map/ppermute | solution.py:120
  221.6 66.4 %collective-permute-start.14 = (bf16[32,3584]{1,0:T(8,128)(2,1)S(1)}, bf16[32,3584]{1,0:T(8,128)(2,1)S(1)}, u32[]{:S(2)}, u32[]{:S(2)}) collective-permute-start(bf16[32,3584]{1,0:T(8,128)(2,1)S(1)} %get-tuple-element.66), channel_id=1, source_target_pairs={{0,5},{1,6},{2,7},{3,0},{4,1},{5,2},{6,3},{7,4},{8,13},{9,14},{10,... | collective-permute-start | bytes 688136 | tf_op jit(solution)/shard_map/ppermute | solution.py:120
  221.6 22.2 %collective-permute-start.10 = (bf16[32,3584]{1,0:T(8,128)(2,1)}, bf16[32,3584]{1,0:T(8,128)(2,1)}, u32[]{:S(2)}, u32[]{:S(2)}) collective-permute-start(bf16[32,3584]{1,0:T(8,128)(2,1)} %get-tuple-element.69), channel_id=1, source_target_pairs={{0,1},{1,2},{2,3},{3,4},{4,5},{5,6},{6,7},{7,0},{8,9},{9,10},{10,1... | collective-permute-start | bytes 688136 | tf_op jit(solution)/shard_map/ppermute | solution.py:120
  227.0 65.1 %all-to-all-start.4 = ((bf16[8,32,7168]{2,1,0:T(8,128)(2,1)}), bf16[8,32,7168]{2,1,0:T(8,128)(2,1)}, u32[]{:S(2)}, u32[]{:S(2)}) async-start(bf16[8,32,7168]{2,1,0:T(8,128)(2,1)} %bitcast.187), calls=%async_computation.4 | async-start | bytes 7340032 | tf_op jit(solution)/shard_map/all_to_all | solution.py:89
  243.8 37.7 %collective-permute-start.12 = (bf16[32,3584]{1,0:T(8,128)(2,1)S(1)}, bf16[32,3584]{1,0:T(8,128)(2,1)S(1)}, u32[]{:S(2)}, u32[]{:S(2)}) collective-permute-start(bf16[32,3584]{1,0:T(8,128)(2,1)S(1)} %get-tuple-element.68), channel_id=1, source_target_pairs={{0,3},{1,4},{2,5},{3,6},{4,7},{5,0},{6,1},{7,2},{8,11},{9,12},{10,... | collective-permute-start | bytes 688136 | tf_op jit(solution)/shard_map/ppermute | solution.py:120
  281.5 6.1 %collective-permute-start.13 = (bf16[32,3584]{1,0:T(8,128)(2,1)S(1)}, bf16[32,3584]{1,0:T(8,128)(2,1)S(1)}, u32[]{:S(2)}, u32[]{:S(2)}) collective-permute-start(bf16[32,3584]{1,0:T(8,128)(2,1)S(1)} %get-tuple-element.67), channel_id=1, source_target_pairs={{0,4},{1,5},{2,6},{3,7},{4,0},{5,1},{6,2},{7,3},{8,12},{9,13},{10,... | collective-permute-start | bytes 688136 | tf_op jit(solution)/shard_map/ppermute | solution.py:120
  292.1 55.1 %collective-permute-start.24 = (bf16[128,3584]{1,0:T(8,128)(2,1)}, bf16[128,3584]{1,0:T(8,128)(2,1)S(1)}, u32[]{:S(2)}, u32[]{:S(2)}) collective-permute-start(bf16[128,3584]{1,0:T(8,128)(2,1)} %fusion.29), channel_id=1, source_target_pairs={{0,24},{8,0},{16,8},{24,16},{1,25},{9,1},{17,9},{25,17},{2,26},{10... | collective-permute-start | bytes 2752520 | tf_op jit(solution)/shard_map/ppermute | solution.py:47
  300.5 6.9 %copy-start.1 = (bf16[256,3584]{1,0:T(8,128)(2,1)S(1)}, bf16[256,3584]{1,0:T(8,128)(2,1)}, u32[]{:S(2)}) copy-start(bf16[256,3584]{1,0:T(8,128)(2,1)} %convolution_convert_fusion.5) | copy-start | bytes 5505028
  308.4 36.8 %collective-permute-start.18 = (bf16[32,3584]{1,0:T(8,128)(2,1)S(1)}, bf16[32,3584]{1,0:T(8,128)(2,1)}, u32[]{:S(2)}, u32[]{:S(2)}) collective-permute-start(bf16[32,3584]{1,0:T(8,128)(2,1)S(1)} %get-tuple-element.56), channel_id=1, source_target_pairs={{0,2},{1,3},{2,4},{3,5},{4,6},{5,7},{6,0},{7,1},{8,10},{9,11},{10,... | collective-permute-start | bytes 688136 | tf_op jit(solution)/shard_map/ppermute | solution.py:120
  308.4 36.4 %collective-permute-start.23 = (bf16[32,3584]{1,0:T(8,128)(2,1)S(1)}, bf16[32,3584]{1,0:T(8,128)(2,1)S(1)}, u32[]{:S(2)}, u32[]{:S(2)}) collective-permute-start(bf16[32,3584]{1,0:T(8,128)(2,1)S(1)} %get-tuple-element.57), channel_id=1, source_target_pairs={{0,7},{1,0},{2,1},{3,2},{4,3},{5,4},{6,5},{7,6},{8,15},{9,8},{10,9... | collective-permute-start | bytes 688136 | tf_op jit(solution)/shard_map/ppermute | solution.py:120
  308.4 35.0 %collective-permute-start.22 = (bf16[32,3584]{1,0:T(8,128)(2,1)S(1)}, bf16[32,3584]{1,0:T(8,128)(2,1)}, u32[]{:S(2)}, u32[]{:S(2)}) collective-permute-start(bf16[32,3584]{1,0:T(8,128)(2,1)S(1)} %get-tuple-element.58), channel_id=1, source_target_pairs={{0,6},{1,7},{2,0},{3,1},{4,2},{5,3},{6,4},{7,5},{8,14},{9,15},{10,... | collective-permute-start | bytes 688136 | tf_op jit(solution)/shard_map/ppermute | solution.py:120
  311.3 11.7 %collective-permute-start.17 = (bf16[32,3584]{1,0:T(8,128)(2,1)}, bf16[32,3584]{1,0:T(8,128)(2,1)}, u32[]{:S(2)}, u32[]{:S(2)}) collective-permute-start(bf16[32,3584]{1,0:T(8,128)(2,1)} %get-tuple-element.62), channel_id=1, source_target_pairs={{0,1},{1,2},{2,3},{3,4},{4,5},{5,6},{6,7},{7,0},{8,9},{9,10},{10,1... | collective-permute-start | bytes 688136 | tf_op jit(solution)/shard_map/ppermute | solution.py:120
  322.6 0.9 copy-start.7
  323.5 7.9 %copy-start.6 = (bf16[32,3584]{1,0:T(8,128)(2,1)S(1)}, bf16[32,3584]{1,0:T(8,128)(2,1)}, u32[]{:S(2)}) copy-start(bf16[32,3584]{1,0:T(8,128)(2,1)} %get-tuple-element.60) | copy-start | bytes 688132
  323.5 7.9 %collective-permute-start.19 = (bf16[32,3584]{1,0:T(8,128)(2,1)S(1)}, bf16[32,3584]{1,0:T(8,128)(2,1)S(1)}, u32[]{:S(2)}, u32[]{:S(2)}) collective-permute-start(bf16[32,3584]{1,0:T(8,128)(2,1)S(1)} %copy-done.7), channel_id=1, source_target_pairs={{0,3},{1,4},{2,5},{3,6},{4,7},{5,0},{6,1},{7,2},{8,11},{9,12},{10,... | collective-permute-start | bytes 688136 | tf_op jit(solution)/shard_map/ppermute | solution.py:120
  326.7 10.7 %copy-start.5 = (bf16[32,3584]{1,0:T(8,128)(2,1)S(1)}, bf16[32,3584]{1,0:T(8,128)(2,1)}, u32[]{:S(2)}) copy-start(bf16[32,3584]{1,0:T(8,128)(2,1)} %get-tuple-element.59) | copy-start | bytes 688132
  331.4 6.1 %collective-permute-start.20 = (bf16[32,3584]{1,0:T(8,128)(2,1)S(1)}, bf16[32,3584]{1,0:T(8,128)(2,1)S(1)}, u32[]{:S(2)}, u32[]{:S(2)}) collective-permute-start(bf16[32,3584]{1,0:T(8,128)(2,1)S(1)} %copy-done.6), channel_id=1, source_target_pairs={{0,4},{1,5},{2,6},{3,7},{4,0},{5,1},{6,2},{7,3},{8,12},{9,13},{10,... | collective-permute-start | bytes 688136 | tf_op jit(solution)/shard_map/ppermute | solution.py:120
  337.5 5.4 %collective-permute-start.21 = (bf16[32,3584]{1,0:T(8,128)(2,1)S(1)}, bf16[32,3584]{1,0:T(8,128)(2,1)S(1)}, u32[]{:S(2)}, u32[]{:S(2)}) collective-permute-start(bf16[32,3584]{1,0:T(8,128)(2,1)S(1)} %copy-done.5), channel_id=1, source_target_pairs={{0,5},{1,6},{2,7},{3,0},{4,1},{5,2},{6,3},{7,4},{8,13},{9,14},{10,... | collective-permute-start | bytes 688136 | tf_op jit(solution)/shard_map/ppermute | solution.py:120
  345.2 1.9 copy-start.2
  347.3 9.0 %collective-permute-start.25 = (bf16[32,3584]{1,0:T(8,128)(2,1)S(1)}, bf16[32,3584]{1,0:T(8,128)(2,1)S(1)}, u32[]{:S(2)}, u32[]{:S(2)}) collective-permute-start(bf16[32,3584]{1,0:T(8,128)(2,1)S(1)} %get-tuple-element.55), channel_id=1, source_target_pairs={{0,1},{1,2},{2,3},{3,4},{4,5},{5,6},{6,7},{7,0},{8,9},{9,10},{10,1... | collective-permute-start | bytes 688136 | tf_op jit(solution)/shard_map/ppermute | solution.py:120
  347.4 43.5 %collective-permute-start.32 = (bf16[128,3584]{1,0:T(8,128)(2,1)S(1)}, bf16[128,3584]{1,0:T(8,128)(2,1)S(1)}, u32[]{:S(2)}, u32[]{:S(2)}) collective-permute-start(bf16[128,3584]{1,0:T(8,128)(2,1)S(1)} %fusion.30), channel_id=1, source_target_pairs={{0,16},{8,24},{16,0},{24,8},{1,17},{9,25},{17,1},{25,9},{2,18},{10... | collective-permute-start | bytes 2752520 | tf_op jit(solution)/shard_map/ppermute | solution.py:47
  347.4 34.5 %collective-permute-start.26 = (bf16[32,3584]{1,0:T(8,128)(2,1)S(1)}, bf16[32,3584]{1,0:T(8,128)(2,1)S(1)}, u32[]{:S(2)}, u32[]{:S(2)}) collective-permute-start(bf16[32,3584]{1,0:T(8,128)(2,1)S(1)} %get-tuple-element.49), channel_id=1, source_target_pairs={{0,2},{1,3},{2,4},{3,5},{4,6},{5,7},{6,0},{7,1},{8,10},{9,11},{10,... | collective-permute-start | bytes 688136 | tf_op jit(solution)/shard_map/ppermute | solution.py:120
  351.1 30.4 %collective-permute-start.31 = (bf16[32,3584]{1,0:T(8,128)(2,1)S(1)}, bf16[32,3584]{1,0:T(8,128)(2,1)S(1)}, u32[]{:S(2)}, u32[]{:S(2)}) collective-permute-start(bf16[32,3584]{1,0:T(8,128)(2,1)S(1)} %get-tuple-element.50), channel_id=1, source_target_pairs={{0,7},{1,0},{2,1},{3,2},{4,3},{5,4},{6,5},{7,6},{8,15},{9,8},{10,9... | collective-permute-start | bytes 688136 | tf_op jit(solution)/shard_map/ppermute | solution.py:120
  351.8 29.2 %collective-permute-start.30 = (bf16[32,3584]{1,0:T(8,128)(2,1)S(1)}, bf16[32,3584]{1,0:T(8,128)(2,1)S(1)}, u32[]{:S(2)}, u32[]{:S(2)}) collective-permute-start(bf16[32,3584]{1,0:T(8,128)(2,1)S(1)} %get-tuple-element.51), channel_id=1, source_target_pairs={{0,6},{1,7},{2,0},{3,1},{4,2},{5,3},{6,4},{7,5},{8,14},{9,15},{10,... | collective-permute-start | bytes 688136 | tf_op jit(solution)/shard_map/ppermute | solution.py:120
  356.3 10.9 %collective-permute-start.27 = (bf16[32,3584]{1,0:T(8,128)(2,1)S(1)}, bf16[32,3584]{1,0:T(8,128)(2,1)S(1)}, u32[]{:S(2)}, u32[]{:S(2)}) collective-permute-start(bf16[32,3584]{1,0:T(8,128)(2,1)S(1)} %get-tuple-element.54), channel_id=1, source_target_pairs={{0,3},{1,4},{2,5},{3,6},{4,7},{5,0},{6,1},{7,2},{8,11},{9,12},{10,... | collective-permute-start | bytes 688136 | tf_op jit(solution)/shard_map/ppermute | solution.py:120
  367.2 7.3 %collective-permute-start.28 = (bf16[32,3584]{1,0:T(8,128)(2,1)S(1)}, bf16[32,3584]{1,0:T(8,128)(2,1)S(1)}, u32[]{:S(2)}, u32[]{:S(2)}) collective-permute-start(bf16[32,3584]{1,0:T(8,128)(2,1)S(1)} %get-tuple-element.53), channel_id=1, source_target_pairs={{0,4},{1,5},{2,6},{3,7},{4,0},{5,1},{6,2},{7,3},{8,12},{9,13},{10,... | collective-permute-start | bytes 688136 | tf_op jit(solution)/shard_map/ppermute | solution.py:120
  374.6 6.0 %collective-permute-start.29 = (bf16[32,3584]{1,0:T(8,128)(2,1)S(1)}, bf16[32,3584]{1,0:T(8,128)(2,1)S(1)}, u32[]{:S(2)}, u32[]{:S(2)}) collective-permute-start(bf16[32,3584]{1,0:T(8,128)(2,1)S(1)} %get-tuple-element.52), channel_id=1, source_target_pairs={{0,5},{1,6},{2,7},{3,0},{4,1},{5,2},{6,3},{7,4},{8,13},{9,14},{10,... | collective-permute-start | bytes 688136 | tf_op jit(solution)/shard_map/ppermute | solution.py:120
  390.9 24.2 %collective-permute-start.33 = (bf16[128,3584]{1,0:T(8,128)(2,1)S(1)}, bf16[128,3584]{1,0:T(8,128)(2,1)S(1)}, u32[]{:S(2)}, u32[]{:S(2)}) collective-permute-start(bf16[128,3584]{1,0:T(8,128)(2,1)S(1)} %fusion.31), channel_id=1, source_target_pairs={{0,8},{8,16},{16,24},{24,0},{1,9},{9,17},{17,25},{25,1},{2,10},{10... | collective-permute-start | bytes 2752520 | tf_op jit(solution)/shard_map/ppermute | solution.py:47

commit v9 on v5

--- a/solution.py
+++ b/solution.py
@@ -1,6 +1,7 @@
 import jax
 import jax.numpy as jnp
 from jax import lax
+from jax.experimental import pallas as pl
 from jax.sharding import PartitionSpec as P
 
 FF = 1024
@@ -17,6 +18,29 @@
     return jnp.sum(before * onehot.astype(jnp.float32), axis=-1).astype(jnp.int32)
 
 
+def part_kernel(grad_ref, weight_ref, out_ref):
+    out_ref[...] = lax.dot_general(
+        grad_ref[...], weight_ref[...], (((1,), (1,)), ((), ())),
+        preferred_element_type=jnp.float32,
+    ).astype(out_ref.dtype)
+
+
+def part_matmul(grad_pre, weight_in):
+    rows, depth = grad_pre.shape
+    width = weight_in.shape[0]
+    tile = 512 if width % 512 == 0 else width
+    return pl.pallas_call(
+        part_kernel,
+        grid=(width // tile,),
+        in_specs=[
+            pl.BlockSpec((rows, depth), lambda j: (0, 0)),
+            pl.BlockSpec((tile, depth), lambda j: (j, 0)),
+        ],
+        out_specs=pl.BlockSpec((rows, tile), lambda j: (0, j)),
+        out_shape=jax.ShapeDtypeStruct((rows, width), jnp.bfloat16),
+    )(grad_pre, weight_in)
+
+
 def expert_backward(rows_x, rows_dy, rows_gate, saved, weight_in, weight_out):
     up_pre = jnp.dot(rows_x, weight_in[:, FF:], preferred_element_type=jnp.float32)
     grad_hidden = lax.dot_general(
@@ -28,10 +52,7 @@
     grad_gate = grad_hidden * up_pre * sigmoid_gate * (1.0 + gate_pre * (1.0 - sigmoid_gate))
     grad_up = grad_hidden * gate_pre * sigmoid_gate
     grad_pre = jnp.concatenate([grad_gate, grad_up], axis=1).astype(jnp.bfloat16)
-    contrib = lax.dot_general(
-        grad_pre, weight_in, (((1,), (1,)), ((), ())), preferred_element_type=jnp.float32
-    )
-    return contrib.astype(jnp.bfloat16)
+    return part_matmul(grad_pre, weight_in)
 
 
 def select_rows(onehot, rows):

time: 381 us -> 372 us (0.976); the launches traced: 375 us -> 370 us
  matrix products: 134 us -> 69.2 us
  Pallas kernels: 0 us -> 43 us
  waiting for transfers between devices: 187 us -> 200 us
  other arithmetic: 4.64 us -> 8.95 us
    dot_general x4 -> x0, matrix products: 64.7 us -> none  [expert_backward(): lax.dot_general(grad_pre, weight_in, (((1,), (1,)), ((), ())), preferred_...]
    pallas_call x0 -> x4, Pallas kernels: none -> 43 us  [part_matmul(): pl.pallas_call(part_kernel, grid=(width // tile,), in_specs=[pl.BlockSpec...]
    ppermute x6, waiting for transfers between devices: 74.1 us -> 82.7 us  [shift(): lax.ppermute(value, 'node', [(i, (i + step) % n_node) for i in range(n_no...]
    concatenate x0 -> x4, other arithmetic: none -> 4.31 us  [expert_backward(): jnp.concatenate([grad_gate, grad_up], axis=1).astype(jnp.bfloat16)]
    all_to_all x8, waiting for transfers between devices: 113 us -> 117 us  [spread(): lax.all_to_all(rows.reshape(n_local, capacity, rows.shape[-1]), 'local',...]
  transfers between devices with their start and end apart: 15 -> 15, of which waited for: 10 -> 10; matrix products, arithmetic and copies ran while one was open for 36% -> 20% of each run, Pallas kernels for 0% -> 12%
where the time goes in v9:
time: 372 us; the launch traced here: 370 us
  waiting for transfers between devices  200 us (54%)
  matrix products  69.2 us (19%)
  Pallas kernels  43 us (12%)
  starting transfers between devices  42.8 us (12%)
  other arithmetic  8.95 us (2%)
  local copies, waits for them, and re-layouts  5.85 us (2%)
    all_to_all x8, waiting for transfers between devices, spread(): lax.all_to_all(rows.reshape(n_local, capacity, rows.shape[-1]), 'local',...  117 us
    ppermute x6, waiting for transfers between devices, shift(): lax.ppermute(value, 'node', [(i, (i + step) % n_node) for i in range(n_no...  82.7 us
    pallas_call x4, Pallas kernels, part_matmul(): pl.pallas_call(part_kernel, grid=(width // tile,), in_specs=[pl.BlockSpec...  43 us
    all_to_all x8, starting transfers between devices, spread(): lax.all_to_all(rows.reshape(n_local, capacity, rows.shape[-1]), 'local',...  34.2 us
    dot_general x4, matrix products, expert_backward(): jnp.dot(rows_x, weight_in[:, FF:], preferred_element_type=jnp.float32)  23.7 us
    dot_general x4, matrix products, expert_backward(): lax.dot_general(rows_dy, weight_out, (((1,), (1,)), ((), ())), preferred_...  23.3 us
    dot_general x4, matrix products, select_rows(): lax.dot_general(onehot, rows, (((0,), (0,)), ((), ())), preferred_element...  16.4 us
  transfers between devices with their start and end apart: 15, of which 10 were waited for; matrix products, arithmetic and copies ran while one was open for 20% of the time, Pallas kernels for 12%

profile of v9, /device:TPU:0, one launch (start us, length us, event | category | flops | bytes accessed | tf_op | source)
XLA Modules:
  0.0 370.4 jit_solution(16296005640931225965)
XLA Ops:
  0.0 0.9 copy.11
  0.9 0.2 reshape.88
  1.1 0.6 fusion.133
  2.0 0.4 fusion.169
  2.5 1.3 constant_dynamic-update-slice_fusion
  3.7 2.9 convolution_convert_fusion.3
  6.7 5.3 %all-to-all-start = ((bf16[8,32,7168]{2,1,0:T(8,128)(2,1)}), bf16[8,32,7168]{2,1,0:T(8,128)(2,1)}, u32[]{:S(2)}, u32[]{:S(2)}) async-start(bf16[8,32,7168]{2,1,0:T(8,128)(2,1)} %bitcast.101), calls=%async_computation | async-start | bytes 7340032 | tf_op jit(solution)/shard_map/all_to_all | solution.py:110
  12.0 2.4 collective-permute-start
  14.4 0.1 copy.13
  14.7 0.1 copy.15
  14.8 0.1 copy.14
  15.0 0.4 fusion.161
  15.6 0.4 fusion.162
  16.1 0.4 fusion.164
  16.8 0.4 fusion.166
  17.3 0.6 copy.12
  17.9 0.4 fusion.170
  18.3 37.3 %all-to-all-done = bf16[8,32,7168]{2,1,0:T(8,128)(2,1)} async-done(((bf16[8,32,7168]{2,1,0:T(8,128)(2,1)}), bf16[8,32,7168]{2,1,0:T(8,128)(2,1)}, u32[]{:S(2)}, u32[]{:S(2)}) %all-to-all-start) | async-done | bytes 3670048 | tf_op jit(solution)/shard_map/all_to_all | solution.py:110
  55.6 3.3 all-to-all-start.2
  58.9 4.5 %convolution_convert_fusion.2 = bf16[256,7168]{1,0:T(8,128)(2,1)} fusion(bf16[128,256]{1,0:T(8,128)(2,1)S(1)} %fusion.170, bf16[128,7168]{1,0:T(8,128)(2,1)} %collective-permute-done), kind=kOutput, calls=%fused_computation.2 | convolution fusion | flops 471597056 | bytes 5570560 | tf_op jit(solution)/shard_map/dot_general | solution.py:59
  63.4 0.1 all-to-all-done.2
  63.6 4.5 %all-to-all-start.1 = ((bf16[8,32,7168]{2,1,0:T(8,128)(2,1)}), bf16[8,32,7168]{2,1,0:T(8,128)(2,1)}, u32[]{:S(2)}, u32[]{:S(2)}) async-start(bf16[8,32,7168]{2,1,0:T(8,128)(2,1)} %bitcast.103), calls=%async_computation.1 | async-start | bytes 7340032 | tf_op jit(solution)/shard_map/all_to_all | solution.py:110
  68.2 2.3 collective-permute-start.1
  70.5 5.8 %fusion.141 = (bf16[256,1024]{1,0:T(8,128)(2,1)S(1)}, f32[256,1024]{1,0:T(8,128)S(1)}) fusion(bf16[1024,1024]{1,0:T(8,128)(2,1)} %param.11, s32[]{:T(128)S(6)} %select_n.75, f32[256]{0:T(256)S(1)} %reshape.105, bf16[1,1024,3584]{2,1,0:T(8,128)(2,1)} %param.13, bf16[256,7168]{1,0:T(8,128)(2,1)} %bitcast.4), kind=kOutput, calls=%fused_computation.76 | convolution fusion | flops 1881145344 | bytes 11273220 | tf_op jit(solution)/shard_map/dot_general | solution.py:46
  76.3 5.9 %fusion.107 = bf16[256,1024]{1,0:T(8,128)(2,1)S(1)} fusion(f32[256,1024]{1,0:T(8,128)S(1)} %get-tuple-element.54, bf16[3584,2048]{1,0:T(8,128)(2,1)} %bitcast.93, bf16[256,7168]{1,0:T(8,128)(2,1)} %bitcast.4, bf16[1024,1024]{1,0:T(8,128)(2,1)} %param.11, s32[]{:T(128)S(6)} %select_n.75), kind=kOutput, calls=%fused_computation.64 | convolution fusion | flops 1881931776 | bytes 11272196 | tf_op jit(solution)/shard_map/dot_general | solution.py:45
  82.2 1.1 pad_maximum_fusion.grad_ref
  83.3 10.8 %shard_map.73 = bf16[256,3584]{1,0:T(8,128)(2,1)} custom-call(bf16[256,2048]{1,0:T(8,128)(2,1)} %pad_maximum_fusion.grad_ref, bf16[3584,2048]{1,0:T(8,128)(2,1)} %bitcast.94), custom_call_target="tpu_custom_call" | custom-call | tf_op jit(solution)/shard_map/pallas_call | solution.py:32
  94.1 19.2 %collective-permute-done.1 = bf16[128,7168]{1,0:T(8,128)(2,1)S(1)} collective-permute-done((bf16[128,7168]{1,0:T(8,128)(2,1)}, bf16[128,7168]{1,0:T(8,128)(2,1)S(1)}, u32[]{:S(2)}, u32[]{:S(2)}) %collective-permute-start.1) | collective-permute-done | bytes 1835040 | tf_op jit(solution)/shard_map/ppermute | solution.py:68
  113.2 1.2 copy-done
  114.5 3.9 %all-to-all-start.4 = ((bf16[8,32,3584]{2,1,0:T(8,128)(2,1)}), bf16[8,32,3584]{2,1,0:T(8,128)(2,1)S(1)}, u32[]{:S(2)}, u32[]{:S(2)}) async-start(bf16[8,32,3584]{2,1,0:T(8,128)(2,1)} %bitcast.105), calls=%async_computation.4 | async-start | bytes 3670016 | tf_op jit(solution)/shard_map/all_to_all | solution.py:110
  118.4 0.4 fusion.171
  118.8 4.5 %convolution_convert_fusion.1 = bf16[256,7168]{1,0:T(8,128)(2,1)} fusion(bf16[128,256]{1,0:T(8,128)(2,1)S(1)} %fusion.171, bf16[128,7168]{1,0:T(8,128)(2,1)} %copy-done), kind=kOutput, calls=%fused_computation.1 | convolution fusion | flops 471597056 | bytes 5570560 | tf_op jit(solution)/shard_map/dot_general | solution.py:59
  123.3 18.9 %all-to-all-done.4 = bf16[8,32,3584]{2,1,0:T(8,128)(2,1)S(1)} async-done(((bf16[8,32,3584]{2,1,0:T(8,128)(2,1)}), bf16[8,32,3584]{2,1,0:T(8,128)(2,1)S(1)}, u32[]{:S(2)}, u32[]{:S(2)}) %all-to-all-start.4) | async-done | bytes 1835040 | tf_op jit(solution)/shard_map/all_to_all | solution.py:110
  142.2 4.7 %all-to-all-start.3 = ((bf16[8,32,7168]{2,1,0:T(8,128)(2,1)}), bf16[8,32,7168]{2,1,0:T(8,128)(2,1)}, u32[]{:S(2)}, u32[]{:S(2)}) async-start(bf16[8,32,7168]{2,1,0:T(8,128)(2,1)} %bitcast.104), calls=%async_computation.3 | async-start | bytes 7340032 | tf_op jit(solution)/shard_map/all_to_all | solution.py:110
  147.0 5.8 %fusion.147 = (bf16[256,1024]{1,0:T(8,128)(2,1)S(1)}, f32[256,1024]{1,0:T(8,128)S(1)}) fusion(bf16[1024,1024]{1,0:T(8,128)(2,1)} %param.11, s32[]{:T(128)S(6)} %select_n.76, f32[256]{0:T(256)S(1)} %reshape.106, bf16[1,1024,3584]{2,1,0:T(8,128)(2,1)} %param.13, bf16[256,7168]{1,0:T(8,128)(2,1)} %bitcast.20), kind=kOutput, calls=%fused_computation.82 | convolution fusion | flops 1881145344 | bytes 11273220 | tf_op jit(solution)/shard_map/dot_general | solution.py:46
  152.8 5.9 %fusion.112 = bf16[256,1024]{1,0:T(8,128)(2,1)S(1)} fusion(f32[256,1024]{1,0:T(8,128)S(1)} %get-tuple-element.56, bf16[3584,2048]{1,0:T(8,128)(2,1)} %bitcast.95, bf16[256,7168]{1,0:T(8,128)(2,1)} %bitcast.20, bf16[1024,1024]{1,0:T(8,128)(2,1)} %param.11, s32[]{:T(128)S(6)} %select_n.76), kind=kOutput, calls=%fused_computation.65 | convolution fusion | flops 1881931776 | bytes 11272196 | tf_op jit(solution)/shard_map/dot_general | solution.py:45
  158.7 1.1 pad_maximum_fusion.1.grad_ref
  159.8 10.7 %shard_map.74 = bf16[256,3584]{1,0:T(8,128)(2,1)} custom-call(bf16[256,2048]{1,0:T(8,128)(2,1)} %pad_maximum_fusion.1.grad_ref, bf16[3584,2048]{1,0:T(8,128)(2,1)} %bitcast.96), custom_call_target="tpu_custom_call" | custom-call | tf_op jit(solution)/shard_map/pallas_call | solution.py:32
  170.6 0.4 convolution_convert_fusion.7
  171.0 20.4 %collective-permute-done.2 = bf16[128,7168]{1,0:T(8,128)(2,1)} collective-permute-done((bf16[128,7168]{1,0:T(8,128)(2,1)}, bf16[128,7168]{1,0:T(8,128)(2,1)}, u32[]{:S(2)}, u32[]{:S(2)}) %collective-permute-start.2) | collective-permute-done | bytes 1835040 | tf_op jit(solution)/shard_map/ppermute | solution.py:68
  191.4 3.9 %all-to-all-start.6 = ((bf16[8,32,3584]{2,1,0:T(8,128)(2,1)}), bf16[8,32,3584]{2,1,0:T(8,128)(2,1)S(1)}, u32[]{:S(2)}, u32[]{:S(2)}) async-start(bf16[8,32,3584]{2,1,0:T(8,128)(2,1)} %bitcast.25), calls=%async_computation.6 | async-start | bytes 3670016 | tf_op jit(solution)/shard_map/all_to_all | solution.py:110
  195.2 0.4 fusion.168
  195.7 4.4 %convolution_convert_fusion = bf16[256,7168]{1,0:T(8,128)(2,1)} fusion(bf16[128,256]{1,0:T(8,128)(2,1)S(1)} %fusion.168, bf16[128,7168]{1,0:T(8,128)(2,1)} %collective-permute-done.2), kind=kOutput, calls=%fused_computation | convolution fusion | flops 471597056 | bytes 5570560 | tf_op jit(solution)/shard_map/dot_general | solution.py:59
  200.1 19.0 %all-to-all-done.6 = bf16[8,32,3584]{2,1,0:T(8,128)(2,1)S(1)} async-done(((bf16[8,32,3584]{2,1,0:T(8,128)(2,1)}), bf16[8,32,3584]{2,1,0:T(8,128)(2,1)S(1)}, u32[]{:S(2)}, u32[]{:S(2)}) %all-to-all-start.6) | async-done | bytes 1835040 | tf_op jit(solution)/shard_map/all_to_all | solution.py:110
  219.1 4.5 %all-to-all-start.5 = ((bf16[8,32,7168]{2,1,0:T(8,128)(2,1)}), bf16[8,32,7168]{2,1,0:T(8,128)(2,1)}, u32[]{:S(2)}, u32[]{:S(2)}) async-start(bf16[8,32,7168]{2,1,0:T(8,128)(2,1)} %bitcast.102), calls=%async_computation.5 | async-start | bytes 7340032 | tf_op jit(solution)/shard_map/all_to_all | solution.py:110
  223.7 5.8 %fusion.153 = (bf16[256,1024]{1,0:T(8,128)(2,1)S(1)}, f32[256,1024]{1,0:T(8,128)S(1)}) fusion(bf16[1024,1024]{1,0:T(8,128)(2,1)} %param.11, s32[]{:T(128)S(6)} %select_n.77, f32[256]{0:T(256)S(1)} %reshape.107, bf16[1,1024,3584]{2,1,0:T(8,128)(2,1)} %param.13, bf16[256,7168]{1,0:T(8,128)(2,1)} %bitcast.24), kind=kOutput, calls=%fused_computation.88 | convolution fusion | flops 1881145344 | bytes 11273220 | tf_op jit(solution)/shard_map/dot_general | solution.py:46
  229.6 5.9 %fusion.117 = bf16[256,1024]{1,0:T(8,128)(2,1)S(1)} fusion(f32[256,1024]{1,0:T(8,128)S(1)} %get-tuple-element.58, bf16[3584,2048]{1,0:T(8,128)(2,1)} %bitcast.97, bf16[256,7168]{1,0:T(8,128)(2,1)} %bitcast.24, bf16[1024,1024]{1,0:T(8,128)(2,1)} %param.11, s32[]{:T(128)S(6)} %select_n.77), kind=kOutput, calls=%fused_computation.66 | convolution fusion | flops 1881931776 | bytes 11272196 | tf_op jit(solution)/shard_map/dot_general | solution.py:45
  235.5 1.1 pad_maximum_fusion.2.grad_ref
  236.6 10.7 %shard_map.75 = bf16[256,3584]{1,0:T(8,128)(2,1)} custom-call(bf16[256,2048]{1,0:T(8,128)(2,1)} %pad_maximum_fusion.2.grad_ref, bf16[3584,2048]{1,0:T(8,128)(2,1)} %bitcast.98), custom_call_target="tpu_custom_call" | custom-call | tf_op jit(solution)/shard_map/pallas_call | solution.py:32
  247.3 1.4 convolution_convert_fusion.6
  248.7 18.4 %all-to-all-done.5 = bf16[8,32,7168]{2,1,0:T(8,128)(2,1)} async-done(((bf16[8,32,7168]{2,1,0:T(8,128)(2,1)}), bf16[8,32,7168]{2,1,0:T(8,128)(2,1)}, u32[]{:S(2)}, u32[]{:S(2)}) %all-to-all-start.5) | async-done | bytes 3670048 | tf_op jit(solution)/shard_map/all_to_all | solution.py:110
  267.1 3.6 all-to-all-start.7
  270.7 0.7 collective-permute-start.3
  271.4 5.8 %fusion.159 = (bf16[256,1024]{1,0:T(8,128)(2,1)S(1)}, f32[256,1024]{1,0:T(8,128)S(1)}) fusion(bf16[1024,1024]{1,0:T(8,128)(2,1)} %param.11, s32[]{:T(128)S(6)} %select_n.78, f32[256]{0:T(256)S(1)} %reshape.108, bf16[1,1024,3584]{2,1,0:T(8,128)(2,1)} %param.13, bf16[256,7168]{1,0:T(8,128)(2,1)} %bitcast.27), kind=kOutput, calls=%fused_computation.94 | convolution fusion | flops 1881145344 | bytes 11273220 | tf_op jit(solution)/shard_map/dot_general | solution.py:46
  277.2 5.9 %fusion.122 = bf16[256,1024]{1,0:T(8,128)(2,1)S(1)} fusion(f32[256,1024]{1,0:T(8,128)S(1)} %get-tuple-element.60, bf16[3584,2048]{1,0:T(8,128)(2,1)} %bitcast.99, bf16[256,7168]{1,0:T(8,128)(2,1)} %bitcast.27, bf16[1024,1024]{1,0:T(8,128)(2,1)} %param.11, s32[]{:T(128)S(6)} %select_n.78), kind=kOutput, calls=%fused_computation.67 | convolution fusion | flops 1881931776 | bytes 11272196 | tf_op jit(solution)/shard_map/dot_general | solution.py:45
  283.1 1.1 pad_maximum_fusion.3.grad_ref
  284.2 10.7 %shard_map.76 = bf16[256,3584]{1,0:T(8,128)(2,1)} custom-call(bf16[256,2048]{1,0:T(8,128)(2,1)} %pad_maximum_fusion.3.grad_ref, bf16[3584,2048]{1,0:T(8,128)(2,1)} %bitcast.100), custom_call_target="tpu_custom_call" | custom-call | tf_op jit(solution)/shard_map/pallas_call | solution.py:32
  294.9 1.3 convolution_convert_fusion.5
  296.3 3.9 %all-to-all-start.8 = ((bf16[8,32,3584]{2,1,0:T(8,128)(2,1)}), bf16[8,32,3584]{2,1,0:T(8,128)(2,1)S(1)}, u32[]{:S(2)}, u32[]{:S(2)}) async-start(bf16[8,32,3584]{2,1,0:T(8,128)(2,1)} %bitcast.30), calls=%async_computation.8 | async-start | bytes 3670016 | tf_op jit(solution)/shard_map/all_to_all | solution.py:110
  300.1 23.8 %all-to-all-done.8 = bf16[8,32,3584]{2,1,0:T(8,128)(2,1)S(1)} async-done(((bf16[8,32,3584]{2,1,0:T(8,128)(2,1)}), bf16[8,32,3584]{2,1,0:T(8,128)(2,1)S(1)}, u32[]{:S(2)}, u32[]{:S(2)}) %all-to-all-start.8) | async-done | bytes 1835040 | tf_op jit(solution)/shard_map/all_to_all | solution.py:110
  324.0 0.4 convolution_convert_fusion.4
  324.4 19.4 %collective-permute-done.4 = bf16[128,3584]{1,0:T(8,128)(2,1)} collective-permute-done((bf16[128,3584]{1,0:T(8,128)(2,1)}, bf16[128,3584]{1,0:T(8,128)(2,1)}, u32[]{:S(2)}, u32[]{:S(2)}) %collective-permute-start.4) | collective-permute-done | bytes 917536 | tf_op jit(solution)/shard_map/ppermute | solution.py:68
  343.8 23.8 %collective-permute-done.5 = bf16[128,3584]{1,0:T(8,128)(2,1)S(1)} collective-permute-done((bf16[128,3584]{1,0:T(8,128)(2,1)S(1)}, bf16[128,3584]{1,0:T(8,128)(2,1)S(1)}, u32[]{:S(2)}, u32[]{:S(2)}) %collective-permute-start.5) | collective-permute-done | bytes 917536 | tf_op jit(solution)/shard_map/ppermute | solution.py:68
  367.6 2.9 add_convert_fusion
  (37 shorter events, 1.4 us)
Async XLA Ops:
  0.0 2.4 copy-start.1
  6.7 7.7 %copy-start.2 = (s32[4,128,8]{1,2,0:T(8,128)S(1)}, s32[4,128,8]{1,2,0:T(8,128)}, u32[]{:S(2)}) copy-start(s32[4,128,8]{1,2,0:T(8,128)} %param.10) | copy-start | bytes 49156
  6.7 48.9 %all-to-all-start = ((bf16[8,32,7168]{2,1,0:T(8,128)(2,1)}), bf16[8,32,7168]{2,1,0:T(8,128)(2,1)}, u32[]{:S(2)}, u32[]{:S(2)}) async-start(bf16[8,32,7168]{2,1,0:T(8,128)(2,1)} %bitcast.101), calls=%async_computation | async-start | bytes 7340032 | tf_op jit(solution)/shard_map/all_to_all | solution.py:110
  12.0 46.9 %collective-permute-start = (bf16[128,7168]{1,0:T(8,128)(2,1)S(1)}, bf16[128,7168]{1,0:T(8,128)(2,1)}, u32[]{:S(2)}, u32[]{:S(2)}) collective-permute-start(bf16[128,7168]{1,0:T(8,128)(2,1)S(1)} %constant_dynamic-update-slice_fusion), channel_id=1, source_target_pairs={{0,8},{8,16},{16,24},{24,0},{1,9},{9,17},{17,25},{25,1},{2,10},{10... | collective-permute-start | bytes 5505032 | tf_op jit(solution)/shard_map/ppermute | solution.py:68
  55.6 8.0 %all-to-all-start.2 = ((bf16[8,4,32]{2,1,0:T(4,128)(2,1)}), bf16[8,4,32]{2,1,0:T(4,128)(2,1)S(1)}, u32[]{:S(2)}, u32[]{:S(2)}) async-start(bf16[8,4,32]{2,1,0:T(4,128)(2,1)} %copy.12), calls=%async_computation.2 | async-start | bytes 16384 | tf_op jit(solution)/shard_map/all_to_all | solution.py:107
  63.6 49.7 %all-to-all-start.1 = ((bf16[8,32,7168]{2,1,0:T(8,128)(2,1)}), bf16[8,32,7168]{2,1,0:T(8,128)(2,1)}, u32[]{:S(2)}, u32[]{:S(2)}) async-start(bf16[8,32,7168]{2,1,0:T(8,128)(2,1)} %bitcast.103), calls=%async_computation.1 | async-start | bytes 7340032 | tf_op jit(solution)/shard_map/all_to_all | solution.py:110
  68.2 45.0 %collective-permute-start.1 = (bf16[128,7168]{1,0:T(8,128)(2,1)}, bf16[128,7168]{1,0:T(8,128)(2,1)S(1)}, u32[]{:S(2)}, u32[]{:S(2)}) collective-permute-start(bf16[128,7168]{1,0:T(8,128)(2,1)} %collective-permute-done), channel_id=1, source_target_pairs={{0,8},{8,16},{16,24},{24,0},{1,9},{9,17},{17,25},{25,1},{2,10},{10... | collective-permute-start | bytes 5505032 | tf_op jit(solution)/shard_map/ppermute | solution.py:68
  113.2 1.2 copy-start
  114.5 27.7 %all-to-all-start.4 = ((bf16[8,32,3584]{2,1,0:T(8,128)(2,1)}), bf16[8,32,3584]{2,1,0:T(8,128)(2,1)S(1)}, u32[]{:S(2)}, u32[]{:S(2)}) async-start(bf16[8,32,3584]{2,1,0:T(8,128)(2,1)} %bitcast.105), calls=%async_computation.4 | async-start | bytes 3670016 | tf_op jit(solution)/shard_map/all_to_all | solution.py:110
  142.2 49.2 %all-to-all-start.3 = ((bf16[8,32,7168]{2,1,0:T(8,128)(2,1)}), bf16[8,32,7168]{2,1,0:T(8,128)(2,1)}, u32[]{:S(2)}, u32[]{:S(2)}) async-start(bf16[8,32,7168]{2,1,0:T(8,128)(2,1)} %bitcast.104), calls=%async_computation.3 | async-start | bytes 7340032 | tf_op jit(solution)/shard_map/all_to_all | solution.py:110
  147.0 44.4 %collective-permute-start.2 = (bf16[128,7168]{1,0:T(8,128)(2,1)}, bf16[128,7168]{1,0:T(8,128)(2,1)}, u32[]{:S(2)}, u32[]{:S(2)}) collective-permute-start(bf16[128,7168]{1,0:T(8,128)(2,1)} %copy-done), channel_id=1, source_target_pairs={{0,8},{8,16},{16,24},{24,0},{1,9},{9,17},{17,25},{25,1},{2,10},{10... | collective-permute-start | bytes 5505032 | tf_op jit(solution)/shard_map/ppermute | solution.py:68
  191.4 27.7 %all-to-all-start.6 = ((bf16[8,32,3584]{2,1,0:T(8,128)(2,1)}), bf16[8,32,3584]{2,1,0:T(8,128)(2,1)S(1)}, u32[]{:S(2)}, u32[]{:S(2)}) async-start(bf16[8,32,3584]{2,1,0:T(8,128)(2,1)} %bitcast.25), calls=%async_computation.6 | async-start | bytes 3670016 | tf_op jit(solution)/shard_map/all_to_all | solution.py:110
  219.1 48.0 %all-to-all-start.5 = ((bf16[8,32,7168]{2,1,0:T(8,128)(2,1)}), bf16[8,32,7168]{2,1,0:T(8,128)(2,1)}, u32[]{:S(2)}, u32[]{:S(2)}) async-start(bf16[8,32,7168]{2,1,0:T(8,128)(2,1)} %bitcast.102), calls=%async_computation.5 | async-start | bytes 7340032 | tf_op jit(solution)/shard_map/all_to_all | solution.py:110
  267.1 27.9 %all-to-all-start.7 = ((bf16[8,32,3584]{2,1,0:T(8,128)(2,1)}), bf16[8,32,3584]{2,1,0:T(8,128)(2,1)S(1)}, u32[]{:S(2)}, u32[]{:S(2)}) async-start(bf16[8,32,3584]{2,1,0:T(8,128)(2,1)} %bitcast.28), calls=%async_computation.7 | async-start | bytes 3670016 | tf_op jit(solution)/shard_map/all_to_all | solution.py:110
  270.7 25.6 %collective-permute-start.3 = (bf16[128,3584]{1,0:T(8,128)(2,1)}, bf16[128,3584]{1,0:T(8,128)(2,1)}, u32[]{:S(2)}, u32[]{:S(2)}) collective-permute-start(bf16[128,3584]{1,0:T(8,128)(2,1)} %convolution_convert_fusion.6), channel_id=1, source_target_pairs={{0,24},{8,0},{16,8},{24,16},{1,25},{9,1},{17,9},{25,17},{2,26},{10... | collective-permute-start | bytes 2752520 | tf_op jit(solution)/shard_map/ppermute | solution.py:68
  296.3 27.7 %all-to-all-start.8 = ((bf16[8,32,3584]{2,1,0:T(8,128)(2,1)}), bf16[8,32,3584]{2,1,0:T(8,128)(2,1)S(1)}, u32[]{:S(2)}, u32[]{:S(2)}) async-start(bf16[8,32,3584]{2,1,0:T(8,128)(2,1)} %bitcast.30), calls=%async_computation.8 | async-start | bytes 3670016 | tf_op jit(solution)/shard_map/all_to_all | solution.py:110
  300.1 43.6 %collective-permute-start.4 = (bf16[128,3584]{1,0:T(8,128)(2,1)}, bf16[128,3584]{1,0:T(8,128)(2,1)}, u32[]{:S(2)}, u32[]{:S(2)}) collective-permute-start(bf16[128,3584]{1,0:T(8,128)(2,1)} %convolution_convert_fusion.5), channel_id=1, source_target_pairs={{0,16},{8,24},{16,0},{24,8},{1,17},{9,25},{17,1},{25,9},{2,18},{10... | collective-permute-start | bytes 2752520 | tf_op jit(solution)/shard_map/ppermute | solution.py:68
  343.8 23.8 %collective-permute-start.5 = (bf16[128,3584]{1,0:T(8,128)(2,1)S(1)}, bf16[128,3584]{1,0:T(8,128)(2,1)S(1)}, u32[]{:S(2)}, u32[]{:S(2)}) collective-permute-start(bf16[128,3584]{1,0:T(8,128)(2,1)S(1)} %convolution_convert_fusion.4), channel_id=1, source_target_pairs={{0,8},{8,16},{16,24},{24,0},{1,9},{9,17},{17,25},{25,1},{2,10},{10... | collective-permute-start | bytes 2752520 | tf_op jit(solution)/shard_map/ppermute | solution.py:68

commit v10 on v9

--- a/solution.py
+++ b/solution.py
@@ -19,29 +19,28 @@
 
 
 def part_kernel(grad_ref, weight_ref, out_ref):
-    out_ref[...] = lax.dot_general(
-        grad_ref[...], weight_ref[...], (((1,), (1,)), ((), ())),
-        preferred_element_type=jnp.float32,
+    out_ref[...] = jnp.dot(
+        grad_ref[...], weight_ref[...], preferred_element_type=jnp.float32
     ).astype(out_ref.dtype)
 
 
-def part_matmul(grad_pre, weight_in):
+def part_matmul(grad_pre, weight_in_t):
     rows, depth = grad_pre.shape
-    width = weight_in.shape[0]
+    width = weight_in_t.shape[1]
     tile = 512 if width % 512 == 0 else width
     return pl.pallas_call(
         part_kernel,
         grid=(width // tile,),
         in_specs=[
             pl.BlockSpec((rows, depth), lambda j: (0, 0)),
-            pl.BlockSpec((tile, depth), lambda j: (j, 0)),
+            pl.BlockSpec((depth, tile), lambda j: (0, j)),
         ],
         out_specs=pl.BlockSpec((rows, tile), lambda j: (0, j)),
         out_shape=jax.ShapeDtypeStruct((rows, width), jnp.bfloat16),
-    )(grad_pre, weight_in)
+    )(grad_pre, weight_in_t)
 
 
-def expert_backward(rows_x, rows_dy, rows_gate, saved, weight_in, weight_out):
+def expert_backward(rows_x, rows_dy, rows_gate, saved, weight_in, weight_in_t, weight_out):
     up_pre = jnp.dot(rows_x, weight_in[:, FF:], preferred_element_type=jnp.float32)
     grad_hidden = lax.dot_general(
         rows_dy, weight_out, (((1,), (1,)), ((), ())), preferred_element_type=jnp.float32
@@ -52,7 +51,7 @@
     grad_gate = grad_hidden * up_pre * sigmoid_gate * (1.0 + gate_pre * (1.0 - sigmoid_gate))
     grad_up = grad_hidden * gate_pre * sigmoid_gate
     grad_pre = jnp.concatenate([grad_gate, grad_up], axis=1).astype(jnp.bfloat16)
-    return part_matmul(grad_pre, weight_in)
+    return part_matmul(grad_pre, weight_in_t)
 
 
 def select_rows(onehot, rows):
@@ -78,6 +77,7 @@
     model_width = hidden_in.shape[1]
     node_here = lax.axis_index("node")
     weight_in = w_in[0]
+    weight_in_t = jnp.transpose(weight_in)
     weight_out = w_out[0]
 
     ids = expert_ids.reshape(n_node, tok * TOPK)
@@ -126,6 +126,7 @@
             gates[:, step].reshape(chunk_rows),
             saved,
             weight_in,
+            weight_in_t,
             weight_out,
         )
 

time: 372 us -> 391 us (1.051)
  local copies, waits for them, and re-layouts: 5.85 us -> 26.6 us
    unnamed x8 -> x11, local copies, waits for them, and re-layouts: 2.25 us -> 23 us
  transfers between devices with their start and end apart: 15 -> 15, of which waited for: 10 -> 10; matrix products, arithmetic and copies ran while one was open for 20% -> 23% of each run, Pallas kernels for 12% -> 11%
where the time goes in v10:
time: 391 us; the launch traced here: 389 us
  waiting for transfers between devices  201 us (51%)
  matrix products  67.3 us (17%)
  starting transfers between devices  42.9 us (11%)
  Pallas kernels  42.6 us (11%)
  local copies, waits for them, and re-layouts  26.6 us (7%)
  other arithmetic  8.92 us (2%)
    all_to_all x8, waiting for transfers between devices, spread(): lax.all_to_all(rows.reshape(n_local, capacity, rows.shape[-1]), 'local',...  117 us
    ppermute x6, waiting for transfers between devices, shift(): lax.ppermute(value, 'node', [(i, (i + step) % n_node) for i in range(n_no...  83.1 us
    pallas_call x4, Pallas kernels, part_matmul(): pl.pallas_call(part_kernel, grid=(width // tile,), in_specs=[pl.BlockSpec...  42.6 us
    all_to_all x8, starting transfers between devices, spread(): lax.all_to_all(rows.reshape(n_local, capacity, rows.shape[-1]), 'local',...  34.2 us
    dot_general x4, matrix products, expert_backward(): lax.dot_general(rows_dy, weight_out, (((1,), (1,)), ((), ())), preferred_...  23.6 us
    unnamed x11, local copies, waits for them, and re-layouts  23 us
    dot_general x4, matrix products, expert_backward(): jnp.dot(rows_x, weight_in[:, FF:], preferred_element_type=jnp.float32)  21.4 us
    dot_general x4, matrix products, select_rows(): lax.dot_general(onehot, rows, (((0,), (0,)), ((), ())), preferred_element...  16.4 us
  transfers between devices with their start and end apart: 15, of which 10 were waited for; matrix products, arithmetic and copies ran while one was open for 23% of the time, Pallas kernels for 11%

profile of v10, /device:TPU:0, one launch (start us, length us, event | category | flops | bytes accessed | tf_op | source)
XLA Modules:
  0.0 389.3 jit_solution(3111292904194098595)
XLA Ops:
  0.0 0.9 copy.14
  0.9 0.2 reshape.88
  1.1 0.6 fusion.133
  2.0 0.4 fusion.169
  2.5 1.3 constant_dynamic-update-slice_fusion
  3.7 2.9 convolution_convert_fusion.3
  6.7 5.3 %all-to-all-start = ((bf16[8,32,7168]{2,1,0:T(8,128)(2,1)}), bf16[8,32,7168]{2,1,0:T(8,128)(2,1)}, u32[]{:S(2)}, u32[]{:S(2)}) async-start(bf16[8,32,7168]{2,1,0:T(8,128)(2,1)} %bitcast.103), calls=%async_computation | async-start | bytes 7340032 | tf_op jit(solution)/shard_map/all_to_all | solution.py:110
  12.0 2.4 collective-permute-start
  14.4 0.1 copy.17
  15.0 0.4 fusion.161
  15.6 0.4 fusion.162
  16.2 0.4 fusion.164
  16.8 0.4 fusion.166
  17.3 0.6 copy.15
  17.9 0.4 fusion.170
  18.3 37.3 %all-to-all-done = bf16[8,32,7168]{2,1,0:T(8,128)(2,1)} async-done(((bf16[8,32,7168]{2,1,0:T(8,128)(2,1)}), bf16[8,32,7168]{2,1,0:T(8,128)(2,1)}, u32[]{:S(2)}, u32[]{:S(2)}) %all-to-all-start) | async-done | bytes 3670048 | tf_op jit(solution)/shard_map/all_to_all | solution.py:110
  55.6 3.3 all-to-all-start.2
  58.9 4.5 %convolution_convert_fusion.2 = bf16[256,7168]{1,0:T(8,128)(2,1)} fusion(bf16[128,256]{1,0:T(8,128)(2,1)S(1)} %fusion.170, bf16[128,7168]{1,0:T(8,128)(2,1)} %collective-permute-done), kind=kOutput, calls=%fused_computation.2 | convolution fusion | flops 471597056 | bytes 5570560 | tf_op jit(solution)/shard_map/dot_general | solution.py:58
  63.4 0.1 all-to-all-done.2
  63.6 4.5 %all-to-all-start.1 = ((bf16[8,32,7168]{2,1,0:T(8,128)(2,1)}), bf16[8,32,7168]{2,1,0:T(8,128)(2,1)}, u32[]{:S(2)}, u32[]{:S(2)}) async-start(bf16[8,32,7168]{2,1,0:T(8,128)(2,1)} %bitcast.105), calls=%async_computation.1 | async-start | bytes 7340032 | tf_op jit(solution)/shard_map/all_to_all | solution.py:110
  68.1 18.8 %copy.16 = bf16[1,3584,2048]{1,2,0:T(8,128)(2,1)} copy(bf16[1,3584,2048]{2,1,0:T(8,128)(2,1)} %param.12) | data formatting | bytes 29360128 | tf_op args[5]
  87.0 2.3 collective-permute-start.1
  89.3 6.0 %fusion.141 = (bf16[256,1024]{1,0:T(8,128)(2,1)S(1)}, f32[256,1024]{1,0:T(8,128)S(1)}) fusion(bf16[1024,1024]{1,0:T(8,128)(2,1)} %param.11, s32[]{:T(128)S(6)} %select_n.75, f32[256]{0:T(256)S(1)} %reshape.105, bf16[1,1024,3584]{2,1,0:T(8,128)(2,1)} %param.13, bf16[256,7168]{1,0:T(8,128)(2,1)} %bitcast.4), kind=kOutput, calls=%fused_computation.76 | convolution fusion | flops 1881145344 | bytes 11273220 | tf_op jit(solution)/shard_map/dot_general | solution.py:45
  95.2 2.0 copy-done
  97.2 3.8 fusion.107
  101.0 1.1 pad_maximum_fusion.grad_ref
  102.1 10.6 %shard_map.73 = bf16[256,3584]{1,0:T(8,128)(2,1)} custom-call(bf16[256,2048]{1,0:T(8,128)(2,1)} %pad_maximum_fusion.grad_ref, bf16[2048,3584]{1,0:T(8,128)(2,1)} %bitcast.95), custom_call_target="tpu_custom_call" | custom-call | tf_op jit(solution)/shard_map/pallas_call | solution.py:31
  112.7 19.3 %collective-permute-done.1 = bf16[128,7168]{1,0:T(8,128)(2,1)S(1)} collective-permute-done((bf16[128,7168]{1,0:T(8,128)(2,1)}, bf16[128,7168]{1,0:T(8,128)(2,1)S(1)}, u32[]{:S(2)}, u32[]{:S(2)}) %collective-permute-start.1) | collective-permute-done | bytes 1835040 | tf_op jit(solution)/shard_map/ppermute | solution.py:67
  132.0 1.3 copy-done.1
  133.3 3.9 all-to-all-start.4
  137.2 0.4 fusion.171
  137.6 4.5 %convolution_convert_fusion.1 = bf16[256,7168]{1,0:T(8,128)(2,1)} fusion(bf16[128,256]{1,0:T(8,128)(2,1)S(1)} %fusion.171, bf16[128,7168]{1,0:T(8,128)(2,1)} %copy-done.1), kind=kOutput, calls=%fused_computation.1 | convolution fusion | flops 471597056 | bytes 5570560 | tf_op jit(solution)/shard_map/dot_general | solution.py:58
  142.1 18.9 %all-to-all-done.4 = bf16[8,32,3584]{2,1,0:T(8,128)(2,1)S(1)} async-done(((bf16[8,32,3584]{2,1,0:T(8,128)(2,1)}), bf16[8,32,3584]{2,1,0:T(8,128)(2,1)S(1)}, u32[]{:S(2)}, u32[]{:S(2)}) %all-to-all-start.4) | async-done | bytes 1835040 | tf_op jit(solution)/shard_map/all_to_all | solution.py:110
  161.0 4.7 %all-to-all-start.3 = ((bf16[8,32,7168]{2,1,0:T(8,128)(2,1)}), bf16[8,32,7168]{2,1,0:T(8,128)(2,1)}, u32[]{:S(2)}, u32[]{:S(2)}) async-start(bf16[8,32,7168]{2,1,0:T(8,128)(2,1)} %bitcast.106), calls=%async_computation.3 | async-start | bytes 7340032 | tf_op jit(solution)/shard_map/all_to_all | solution.py:110
  165.8 5.8 %fusion.147 = (bf16[256,1024]{1,0:T(8,128)(2,1)S(1)}, f32[256,1024]{1,0:T(8,128)S(1)}) fusion(bf16[1024,1024]{1,0:T(8,128)(2,1)} %param.11, s32[]{:T(128)S(6)} %select_n.76, f32[256]{0:T(256)S(1)} %reshape.106, bf16[1,1024,3584]{2,1,0:T(8,128)(2,1)} %param.13, bf16[256,7168]{1,0:T(8,128)(2,1)} %bitcast.21), kind=kOutput, calls=%fused_computation.82 | convolution fusion | flops 1881145344 | bytes 11273220 | tf_op jit(solution)/shard_map/dot_general | solution.py:45
  171.7 5.9 %fusion.112 = bf16[256,1024]{1,0:T(8,128)(2,1)S(1)} fusion(f32[256,1024]{1,0:T(8,128)S(1)} %get-tuple-element.56, bf16[3584,2048]{0,1:T(8,128)(2,1)} %bitcast.96, bf16[256,7168]{1,0:T(8,128)(2,1)} %bitcast.21, bf16[1024,1024]{1,0:T(8,128)(2,1)} %param.11, s32[]{:T(128)S(6)} %select_n.76), kind=kOutput, calls=%fused_computation.65 | convolution fusion | flops 1881931776 | bytes 11272196 | tf_op jit(solution)/shard_map/dot_general | solution.py:44
  177.5 1.1 pad_maximum_fusion.1.grad_ref
  178.6 10.6 %shard_map.74 = bf16[256,3584]{1,0:T(8,128)(2,1)} custom-call(bf16[256,2048]{1,0:T(8,128)(2,1)} %pad_maximum_fusion.1.grad_ref, bf16[2048,3584]{1,0:T(8,128)(2,1)} %bitcast.97), custom_call_target="tpu_custom_call" | custom-call | tf_op jit(solution)/shard_map/pallas_call | solution.py:31
  189.2 0.4 convolution_convert_fusion.7
  189.7 20.6 %collective-permute-done.2 = bf16[128,7168]{1,0:T(8,128)(2,1)} collective-permute-done((bf16[128,7168]{1,0:T(8,128)(2,1)}, bf16[128,7168]{1,0:T(8,128)(2,1)}, u32[]{:S(2)}, u32[]{:S(2)}) %collective-permute-start.2) | collective-permute-done | bytes 1835040 | tf_op jit(solution)/shard_map/ppermute | solution.py:67
  210.2 3.9 all-to-all-start.6
  214.1 0.4 fusion.168
  214.5 4.5 %convolution_convert_fusion = bf16[256,7168]{1,0:T(8,128)(2,1)} fusion(bf16[128,256]{1,0:T(8,128)(2,1)S(1)} %fusion.168, bf16[128,7168]{1,0:T(8,128)(2,1)} %collective-permute-done.2), kind=kOutput, calls=%fused_computation | convolution fusion | flops 471597056 | bytes 5570560 | tf_op jit(solution)/shard_map/dot_general | solution.py:58
  219.0 18.9 %all-to-all-done.6 = bf16[8,32,3584]{2,1,0:T(8,128)(2,1)S(1)} async-done(((bf16[8,32,3584]{2,1,0:T(8,128)(2,1)}), bf16[8,32,3584]{2,1,0:T(8,128)(2,1)S(1)}, u32[]{:S(2)}, u32[]{:S(2)}) %all-to-all-start.6) | async-done | bytes 1835040 | tf_op jit(solution)/shard_map/all_to_all | solution.py:110
  237.9 4.6 %all-to-all-start.5 = ((bf16[8,32,7168]{2,1,0:T(8,128)(2,1)}), bf16[8,32,7168]{2,1,0:T(8,128)(2,1)}, u32[]{:S(2)}, u32[]{:S(2)}) async-start(bf16[8,32,7168]{2,1,0:T(8,128)(2,1)} %bitcast.104), calls=%async_computation.5 | async-start | bytes 7340032 | tf_op jit(solution)/shard_map/all_to_all | solution.py:110
  242.7 5.9 %fusion.153 = (bf16[256,1024]{1,0:T(8,128)(2,1)S(1)}, f32[256,1024]{1,0:T(8,128)S(1)}) fusion(bf16[1024,1024]{1,0:T(8,128)(2,1)} %param.11, s32[]{:T(128)S(6)} %select_n.77, f32[256]{0:T(256)S(1)} %reshape.107, bf16[1,1024,3584]{2,1,0:T(8,128)(2,1)} %param.13, bf16[256,7168]{1,0:T(8,128)(2,1)} %bitcast.26), kind=kOutput, calls=%fused_computation.88 | convolution fusion | flops 1881145344 | bytes 11273220 | tf_op jit(solution)/shard_map/dot_general | solution.py:45
  248.6 5.9 %fusion.117 = bf16[256,1024]{1,0:T(8,128)(2,1)S(1)} fusion(f32[256,1024]{1,0:T(8,128)S(1)} %get-tuple-element.58, bf16[3584,2048]{0,1:T(8,128)(2,1)} %bitcast.98, bf16[256,7168]{1,0:T(8,128)(2,1)} %bitcast.26, bf16[1024,1024]{1,0:T(8,128)(2,1)} %param.11, s32[]{:T(128)S(6)} %select_n.77), kind=kOutput, calls=%fused_computation.66 | convolution fusion | flops 1881931776 | bytes 11272196 | tf_op jit(solution)/shard_map/dot_general | solution.py:44
  254.5 1.1 pad_maximum_fusion.2.grad_ref
  255.5 10.6 %shard_map.75 = bf16[256,3584]{1,0:T(8,128)(2,1)} custom-call(bf16[256,2048]{1,0:T(8,128)(2,1)} %pad_maximum_fusion.2.grad_ref, bf16[2048,3584]{1,0:T(8,128)(2,1)} %bitcast.99), custom_call_target="tpu_custom_call" | custom-call | tf_op jit(solution)/shard_map/pallas_call | solution.py:31
  266.2 1.4 convolution_convert_fusion.6
  267.6 18.5 %all-to-all-done.5 = bf16[8,32,7168]{2,1,0:T(8,128)(2,1)} async-done(((bf16[8,32,7168]{2,1,0:T(8,128)(2,1)}), bf16[8,32,7168]{2,1,0:T(8,128)(2,1)}, u32[]{:S(2)}, u32[]{:S(2)}) %all-to-all-start.5) | async-done | bytes 3670048 | tf_op jit(solution)/shard_map/all_to_all | solution.py:110
  286.0 3.6 all-to-all-start.7
  289.6 0.7 collective-permute-start.3
  290.3 5.9 %fusion.159 = (bf16[256,1024]{1,0:T(8,128)(2,1)S(1)}, f32[256,1024]{1,0:T(8,128)S(1)}) fusion(bf16[1024,1024]{1,0:T(8,128)(2,1)} %param.11, s32[]{:T(128)S(6)} %select_n.78, f32[256]{0:T(256)S(1)} %reshape.108, bf16[1,1024,3584]{2,1,0:T(8,128)(2,1)} %param.13, bf16[256,7168]{1,0:T(8,128)(2,1)} %bitcast.29), kind=kOutput, calls=%fused_computation.94 | convolution fusion | flops 1881145344 | bytes 11273220 | tf_op jit(solution)/shard_map/dot_general | solution.py:45
  296.2 5.9 %fusion.122 = bf16[256,1024]{1,0:T(8,128)(2,1)S(1)} fusion(f32[256,1024]{1,0:T(8,128)S(1)} %get-tuple-element.60, bf16[3584,2048]{0,1:T(8,128)(2,1)} %bitcast.100, bf16[256,7168]{1,0:T(8,128)(2,1)} %bitcast.29, bf16[1024,1024]{1,0:T(8,128)(2,1)} %param.11, s32[]{:T(128)S(6)} %select_n.78), kind=kOutput, calls=%fused_computation.67 | convolution fusion | flops 1881931776 | bytes 11272196 | tf_op jit(solution)/shard_map/dot_general | solution.py:44
  302.0 1.1 pad_maximum_fusion.3.grad_ref
  303.1 10.6 %shard_map.76 = bf16[256,3584]{1,0:T(8,128)(2,1)} custom-call(bf16[256,2048]{1,0:T(8,128)(2,1)} %pad_maximum_fusion.3.grad_ref, bf16[2048,3584]{1,0:T(8,128)(2,1)} %bitcast.101), custom_call_target="tpu_custom_call" | custom-call | tf_op jit(solution)/shard_map/pallas_call | solution.py:31
  313.8 1.3 convolution_convert_fusion.5
  315.1 3.8 all-to-all-start.8
  319.0 23.8 %all-to-all-done.8 = bf16[8,32,3584]{2,1,0:T(8,128)(2,1)S(1)} async-done(((bf16[8,32,3584]{2,1,0:T(8,128)(2,1)}), bf16[8,32,3584]{2,1,0:T(8,128)(2,1)S(1)}, u32[]{:S(2)}, u32[]{:S(2)}) %all-to-all-start.8) | async-done | bytes 1835040 | tf_op jit(solution)/shard_map/all_to_all | solution.py:110
  342.8 0.4 convolution_convert_fusion.4
  343.2 19.4 %collective-permute-done.4 = bf16[128,3584]{1,0:T(8,128)(2,1)} collective-permute-done((bf16[128,3584]{1,0:T(8,128)(2,1)}, bf16[128,3584]{1,0:T(8,128)(2,1)}, u32[]{:S(2)}, u32[]{:S(2)}) %collective-permute-start.4) | collective-permute-done | bytes 917536 | tf_op jit(solution)/shard_map/ppermute | solution.py:67
  362.6 23.8 %collective-permute-done.5 = bf16[128,3584]{1,0:T(8,128)(2,1)S(1)} collective-permute-done((bf16[128,3584]{1,0:T(8,128)(2,1)S(1)}, bf16[128,3584]{1,0:T(8,128)(2,1)S(1)}, u32[]{:S(2)}, u32[]{:S(2)}) %collective-permute-start.5) | collective-permute-done | bytes 917536 | tf_op jit(solution)/shard_map/ppermute | solution.py:67
  386.4 2.9 add_convert_fusion
  (40 shorter events, 1.7 us)
Async XLA Ops:
  0.0 2.4 copy-start.2
  6.7 7.7 %copy-start.3 = (s32[4,128,8]{1,2,0:T(8,128)S(1)}, s32[4,128,8]{1,2,0:T(8,128)}, u32[]{:S(2)}) copy-start(s32[4,128,8]{1,2,0:T(8,128)} %param.10) | copy-start | bytes 49156
  6.7 48.9 %all-to-all-start = ((bf16[8,32,7168]{2,1,0:T(8,128)(2,1)}), bf16[8,32,7168]{2,1,0:T(8,128)(2,1)}, u32[]{:S(2)}, u32[]{:S(2)}) async-start(bf16[8,32,7168]{2,1,0:T(8,128)(2,1)} %bitcast.103), calls=%async_computation | async-start | bytes 7340032 | tf_op jit(solution)/shard_map/all_to_all | solution.py:110
  12.0 46.9 %collective-permute-start = (bf16[128,7168]{1,0:T(8,128)(2,1)S(1)}, bf16[128,7168]{1,0:T(8,128)(2,1)}, u32[]{:S(2)}, u32[]{:S(2)}) collective-permute-start(bf16[128,7168]{1,0:T(8,128)(2,1)S(1)} %constant_dynamic-update-slice_fusion), channel_id=1, source_target_pairs={{0,8},{8,16},{16,24},{24,0},{1,9},{9,17},{17,25},{25,1},{2,10},{10... | collective-permute-start | bytes 5505032 | tf_op jit(solution)/shard_map/ppermute | solution.py:67
  55.6 8.0 %all-to-all-start.2 = ((bf16[8,4,32]{2,1,0:T(4,128)(2,1)}), bf16[8,4,32]{2,1,0:T(4,128)(2,1)S(1)}, u32[]{:S(2)}, u32[]{:S(2)}) async-start(bf16[8,4,32]{2,1,0:T(4,128)(2,1)} %copy.15), calls=%async_computation.2 | async-start | bytes 16384 | tf_op jit(solution)/shard_map/all_to_all | solution.py:107
  63.6 68.5 %all-to-all-start.1 = ((bf16[8,32,7168]{2,1,0:T(8,128)(2,1)}), bf16[8,32,7168]{2,1,0:T(8,128)(2,1)}, u32[]{:S(2)}, u32[]{:S(2)}) async-start(bf16[8,32,7168]{2,1,0:T(8,128)(2,1)} %bitcast.105), calls=%async_computation.1 | async-start | bytes 7340032 | tf_op jit(solution)/shard_map/all_to_all | solution.py:110
  87.0 45.0 %collective-permute-start.1 = (bf16[128,7168]{1,0:T(8,128)(2,1)}, bf16[128,7168]{1,0:T(8,128)(2,1)S(1)}, u32[]{:S(2)}, u32[]{:S(2)}) collective-permute-start(bf16[128,7168]{1,0:T(8,128)(2,1)} %collective-permute-done), channel_id=1, source_target_pairs={{0,8},{8,16},{16,24},{24,0},{1,9},{9,17},{17,25},{25,1},{2,10},{10... | collective-permute-start | bytes 5505032 | tf_op jit(solution)/shard_map/ppermute | solution.py:67
  89.3 7.9 %copy-start = (bf16[1,3584,2048]{1,2,0:T(8,128)(2,1)S(1)}, bf16[1,3584,2048]{1,2,0:T(8,128)(2,1)}, u32[]{:S(2)}) copy-start(bf16[1,3584,2048]{1,2,0:T(8,128)(2,1)} %copy.16) | copy-start | bytes 44040196
  132.0 1.3 copy-start.1
  133.3 27.7 %all-to-all-start.4 = ((bf16[8,32,3584]{2,1,0:T(8,128)(2,1)}), bf16[8,32,3584]{2,1,0:T(8,128)(2,1)S(1)}, u32[]{:S(2)}, u32[]{:S(2)}) async-start(bf16[8,32,3584]{2,1,0:T(8,128)(2,1)} %bitcast.107), calls=%async_computation.4 | async-start | bytes 3670016 | tf_op jit(solution)/shard_map/all_to_all | solution.py:110
  161.0 49.2 %all-to-all-start.3 = ((bf16[8,32,7168]{2,1,0:T(8,128)(2,1)}), bf16[8,32,7168]{2,1,0:T(8,128)(2,1)}, u32[]{:S(2)}, u32[]{:S(2)}) async-start(bf16[8,32,7168]{2,1,0:T(8,128)(2,1)} %bitcast.106), calls=%async_computation.3 | async-start | bytes 7340032 | tf_op jit(solution)/shard_map/all_to_all | solution.py:110
  165.8 44.4 %collective-permute-start.2 = (bf16[128,7168]{1,0:T(8,128)(2,1)}, bf16[128,7168]{1,0:T(8,128)(2,1)}, u32[]{:S(2)}, u32[]{:S(2)}) collective-permute-start(bf16[128,7168]{1,0:T(8,128)(2,1)} %copy-done.1), channel_id=1, source_target_pairs={{0,8},{8,16},{16,24},{24,0},{1,9},{9,17},{17,25},{25,1},{2,10},{10... | collective-permute-start | bytes 5505032 | tf_op jit(solution)/shard_map/ppermute | solution.py:67
  210.2 27.7 %all-to-all-start.6 = ((bf16[8,32,3584]{2,1,0:T(8,128)(2,1)}), bf16[8,32,3584]{2,1,0:T(8,128)(2,1)S(1)}, u32[]{:S(2)}, u32[]{:S(2)}) async-start(bf16[8,32,3584]{2,1,0:T(8,128)(2,1)} %bitcast.27), calls=%async_computation.6 | async-start | bytes 3670016 | tf_op jit(solution)/shard_map/all_to_all | solution.py:110
  237.9 48.1 %all-to-all-start.5 = ((bf16[8,32,7168]{2,1,0:T(8,128)(2,1)}), bf16[8,32,7168]{2,1,0:T(8,128)(2,1)}, u32[]{:S(2)}, u32[]{:S(2)}) async-start(bf16[8,32,7168]{2,1,0:T(8,128)(2,1)} %bitcast.104), calls=%async_computation.5 | async-start | bytes 7340032 | tf_op jit(solution)/shard_map/all_to_all | solution.py:110
  286.0 27.8 %all-to-all-start.7 = ((bf16[8,32,3584]{2,1,0:T(8,128)(2,1)}), bf16[8,32,3584]{2,1,0:T(8,128)(2,1)S(1)}, u32[]{:S(2)}, u32[]{:S(2)}) async-start(bf16[8,32,3584]{2,1,0:T(8,128)(2,1)} %bitcast.30), calls=%async_computation.7 | async-start | bytes 3670016 | tf_op jit(solution)/shard_map/all_to_all | solution.py:110
  289.6 25.5 %collective-permute-start.3 = (bf16[128,3584]{1,0:T(8,128)(2,1)}, bf16[128,3584]{1,0:T(8,128)(2,1)}, u32[]{:S(2)}, u32[]{:S(2)}) collective-permute-start(bf16[128,3584]{1,0:T(8,128)(2,1)} %convolution_convert_fusion.6), channel_id=1, source_target_pairs={{0,24},{8,0},{16,8},{24,16},{1,25},{9,1},{17,9},{25,17},{2,26},{10... | collective-permute-start | bytes 2752520 | tf_op jit(solution)/shard_map/ppermute | solution.py:67
  315.1 27.7 %all-to-all-start.8 = ((bf16[8,32,3584]{2,1,0:T(8,128)(2,1)}), bf16[8,32,3584]{2,1,0:T(8,128)(2,1)S(1)}, u32[]{:S(2)}, u32[]{:S(2)}) async-start(bf16[8,32,3584]{2,1,0:T(8,128)(2,1)} %bitcast.32), calls=%async_computation.8 | async-start | bytes 3670016 | tf_op jit(solution)/shard_map/all_to_all | solution.py:110
  319.0 43.6 %collective-permute-start.4 = (bf16[128,3584]{1,0:T(8,128)(2,1)}, bf16[128,3584]{1,0:T(8,128)(2,1)}, u32[]{:S(2)}, u32[]{:S(2)}) collective-permute-start(bf16[128,3584]{1,0:T(8,128)(2,1)} %convolution_convert_fusion.5), channel_id=1, source_target_pairs={{0,16},{8,24},{16,0},{24,8},{1,17},{9,25},{17,1},{25,9},{2,18},{10... | collective-permute-start | bytes 2752520 | tf_op jit(solution)/shard_map/ppermute | solution.py:67
  362.6 23.8 %collective-permute-start.5 = (bf16[128,3584]{1,0:T(8,128)(2,1)S(1)}, bf16[128,3584]{1,0:T(8,128)(2,1)S(1)}, u32[]{:S(2)}, u32[]{:S(2)}) collective-permute-start(bf16[128,3584]{1,0:T(8,128)(2,1)S(1)} %convolution_convert_fusion.4), channel_id=1, source_target_pairs={{0,8},{8,16},{16,24},{24,0},{1,9},{9,17},{17,25},{25,1},{2,10},{10... | collective-permute-start | bytes 2752520 | tf_op jit(solution)/shard_map/ppermute | solution.py:67

commit v11 on v9

--- a/solution.py
+++ b/solution.py
@@ -141,9 +141,8 @@
     chunks = {0: jnp.concatenate([hidden_in, out_grad], axis=1)}
     received = {}
     contribs = {}
-    sums = {}
     homes = {}
-    for slot in range(-1, n_node + 2):
+    for slot in range(-1, n_node + 1):
         produced = {}
         if 0 < slot + 2 < n_node:
             produced["chunk", slot + 2] = fetch(slot + 2, chunks[slot + 1])
@@ -152,14 +151,15 @@
         if 0 <= slot < n_node:
             produced["contrib", slot] = compute(slot, received[slot])
         if 0 <= slot - 1 < n_node:
-            produced["sum", slot - 1] = gather_back(slot - 1, contribs[slot - 1])
-        if 0 <= slot - 2 < n_node:
-            produced["home", slot - 2] = send_home(slot - 2, sums[slot - 2])
+            produced["home", slot - 1] = send_home(
+                slot - 1, gather_back(slot - 1, contribs[slot - 1])
+            )
         keys = list(produced)
         values = lax.optimization_barrier([produced[key] for key in keys])
         for (kind, step), value in zip(keys, values):
-            {"chunk": chunks, "received": received, "contrib": contribs, "sum": sums,
-             "home": homes}[kind][step] = value
+            {"chunk": chunks, "received": received, "contrib": contribs, "home": homes}[kind][
+                step
+            ] = value
 
     total = homes[0].astype(jnp.float32)
     for step in range(1, n_node):

time: 372 us -> 389 us (1.046)
  blocking collectives: 0 us -> 28.8 us
  waiting for transfers between devices: 200 us -> 193 us
    all_to_all x0 -> x1, blocking collectives: none -> 28.8 us  [spread(): lax.all_to_all(rows.reshape(n_local, capacity, rows.shape[-1]), 'local',...]
    all_to_all x8 -> x7, waiting for transfers between devices: 117 us -> 105 us  [spread(): lax.all_to_all(rows.reshape(n_local, capacity, rows.shape[-1]), 'local',...]
    ppermute x6, waiting for transfers between devices: 82.7 us -> 87.5 us  [shift(): lax.ppermute(value, 'node', [(i, (i + step) % n_node) for i in range(n_no...]
    all_to_all x8 -> x7, starting transfers between devices: 34.2 us -> 30.5 us  [spread(): lax.all_to_all(rows.reshape(n_local, capacity, rows.shape[-1]), 'local',...]
  transfers between devices with their start and end apart: 15 -> 14, of which waited for: 10 -> 11; matrix products, arithmetic and copies ran while one was open for 20% -> 19% of each run, Pallas kernels for 12% -> 11%
where the time goes in v11:
time: 389 us; the launch traced here: 388 us
  waiting for transfers between devices  193 us (50%)
  matrix products  70.3 us (18%)
  Pallas kernels  43 us (11%)
  starting transfers between devices  39 us (10%)
  blocking collectives  28.8 us (7%)
  other arithmetic  7.5 us (2%)
  local copies, waits for them, and re-layouts  5.86 us (2%)
    all_to_all x7, waiting for transfers between devices, spread(): lax.all_to_all(rows.reshape(n_local, capacity, rows.shape[-1]), 'local',...  105 us
    ppermute x6, waiting for transfers between devices, shift(): lax.ppermute(value, 'node', [(i, (i + step) % n_node) for i in range(n_no...  87.5 us
    pallas_call x4, Pallas kernels, part_matmul(): pl.pallas_call(part_kernel, grid=(width // tile,), in_specs=[pl.BlockSpec...  43 us
    all_to_all x7, starting transfers between devices, spread(): lax.all_to_all(rows.reshape(n_local, capacity, rows.shape[-1]), 'local',...  30.5 us
    all_to_all x1, blocking collectives, spread(): lax.all_to_all(rows.reshape(n_local, capacity, rows.shape[-1]), 'local',...  28.8 us
    dot_general x4, matrix products, expert_backward(): lax.dot_general(rows_dy, weight_out, (((1,), (1,)), ((), ())), preferred_...  24.2 us
    dot_general x4, matrix products, expert_backward(): jnp.dot(rows_x, weight_in[:, FF:], preferred_element_type=jnp.float32)  23.7 us
    dot_general x4, matrix products, select_rows(): lax.dot_general(onehot, rows, (((0,), (0,)), ((), ())), preferred_element...  16.5 us
  transfers between devices with their start and end apart: 14, of which 11 were waited for; matrix products, arithmetic and copies ran while one was open for 19% of the time, Pallas kernels for 11%

profile of v11, /device:TPU:0, one launch (start us, length us, event | category | flops | bytes accessed | tf_op | source)
XLA Modules:
  0.0 387.6 jit_solution(8224097091714834330)
XLA Ops:
  0.0 0.9 copy.11
  0.9 0.2 reshape.88
  1.1 0.6 fusion.133
  2.0 0.4 fusion.168
  2.5 1.3 constant_dynamic-update-slice_fusion
  3.7 2.9 convolution_convert_fusion.3
  6.7 5.3 %all-to-all-start = ((bf16[8,32,7168]{2,1,0:T(8,128)(2,1)}), bf16[8,32,7168]{2,1,0:T(8,128)(2,1)}, u32[]{:S(2)}, u32[]{:S(2)}) async-start(bf16[8,32,7168]{2,1,0:T(8,128)(2,1)} %bitcast.101), calls=%async_computation | async-start | bytes 7340032 | tf_op jit(solution)/shard_map/all_to_all | solution.py:110
  12.0 2.4 collective-permute-start
  14.4 0.1 copy.13
  14.8 0.1 copy.14
  15.0 0.4 fusion.163
  15.6 0.4 fusion.161
  16.2 0.4 fusion.164
  16.8 0.4 fusion.166
  17.3 0.6 copy.12
  17.9 0.4 fusion.169
  18.3 37.3 %all-to-all-done = bf16[8,32,7168]{2,1,0:T(8,128)(2,1)} async-done(((bf16[8,32,7168]{2,1,0:T(8,128)(2,1)}), bf16[8,32,7168]{2,1,0:T(8,128)(2,1)}, u32[]{:S(2)}, u32[]{:S(2)}) %all-to-all-start) | async-done | bytes 3670048 | tf_op jit(solution)/shard_map/all_to_all | solution.py:110
  55.6 3.3 all-to-all-start.2
  58.9 4.5 %convolution_convert_fusion.2 = bf16[256,7168]{1,0:T(8,128)(2,1)} fusion(bf16[128,256]{1,0:T(8,128)(2,1)S(1)} %fusion.169, bf16[128,7168]{1,0:T(8,128)(2,1)} %collective-permute-done), kind=kOutput, calls=%fused_computation.2 | convolution fusion | flops 471597056 | bytes 5570560 | tf_op jit(solution)/shard_map/dot_general | solution.py:59
  63.4 0.1 all-to-all-done.2
  63.6 4.5 %all-to-all-start.1 = ((bf16[8,32,7168]{2,1,0:T(8,128)(2,1)}), bf16[8,32,7168]{2,1,0:T(8,128)(2,1)}, u32[]{:S(2)}, u32[]{:S(2)}) async-start(bf16[8,32,7168]{2,1,0:T(8,128)(2,1)} %bitcast.102), calls=%async_computation.1 | async-start | bytes 7340032 | tf_op jit(solution)/shard_map/all_to_all | solution.py:110
  68.2 2.3 collective-permute-start.1
  70.5 5.8 %fusion.141 = (bf16[256,1024]{1,0:T(8,128)(2,1)S(1)}, f32[256,1024]{1,0:T(8,128)S(1)}) fusion(bf16[1024,1024]{1,0:T(8,128)(2,1)} %param.11, s32[]{:T(128)S(6)} %select_n.75, f32[256]{0:T(256)S(1)} %reshape.105, bf16[1,1024,3584]{2,1,0:T(8,128)(2,1)} %param.13, bf16[256,7168]{1,0:T(8,128)(2,1)} %bitcast.4), kind=kOutput, calls=%fused_computation.76 | convolution fusion | flops 1881145344 | bytes 11273220 | tf_op jit(solution)/shard_map/dot_general | solution.py:46
  76.3 5.9 %fusion.107 = bf16[256,1024]{1,0:T(8,128)(2,1)S(1)} fusion(f32[256,1024]{1,0:T(8,128)S(1)} %get-tuple-element.46, bf16[3584,2048]{1,0:T(8,128)(2,1)} %bitcast.93, bf16[256,7168]{1,0:T(8,128)(2,1)} %bitcast.4, bf16[1024,1024]{1,0:T(8,128)(2,1)} %param.11, s32[]{:T(128)S(6)} %select_n.75), kind=kOutput, calls=%fused_computation.64 | convolution fusion | flops 1881931776 | bytes 11272196 | tf_op jit(solution)/shard_map/dot_general | solution.py:45
  82.2 1.1 pad_maximum_fusion.grad_ref
  83.3 10.8 %shard_map.73 = bf16[256,3584]{1,0:T(8,128)(2,1)} custom-call(bf16[256,2048]{1,0:T(8,128)(2,1)} %pad_maximum_fusion.grad_ref, bf16[3584,2048]{1,0:T(8,128)(2,1)} %bitcast.94), custom_call_target="tpu_custom_call" | custom-call | tf_op jit(solution)/shard_map/pallas_call | solution.py:32
  94.1 19.2 %collective-permute-done.1 = bf16[128,7168]{1,0:T(8,128)(2,1)S(1)} collective-permute-done((bf16[128,7168]{1,0:T(8,128)(2,1)}, bf16[128,7168]{1,0:T(8,128)(2,1)S(1)}, u32[]{:S(2)}, u32[]{:S(2)}) %collective-permute-start.1) | collective-permute-done | bytes 1835040 | tf_op jit(solution)/shard_map/ppermute | solution.py:68
  113.2 1.2 copy-done
  114.5 3.9 all-to-all-start.4
  118.4 0.4 fusion.170
  118.8 4.5 %convolution_convert_fusion.1 = bf16[256,7168]{1,0:T(8,128)(2,1)} fusion(bf16[128,256]{1,0:T(8,128)(2,1)S(1)} %fusion.170, bf16[128,7168]{1,0:T(8,128)(2,1)} %copy-done), kind=kOutput, calls=%fused_computation.1 | convolution fusion | flops 471597056 | bytes 5570560 | tf_op jit(solution)/shard_map/dot_general | solution.py:59
  123.3 18.9 %all-to-all-done.4 = bf16[8,32,3584]{2,1,0:T(8,128)(2,1)S(1)} async-done(((bf16[8,32,3584]{2,1,0:T(8,128)(2,1)}), bf16[8,32,3584]{2,1,0:T(8,128)(2,1)S(1)}, u32[]{:S(2)}, u32[]{:S(2)}) %all-to-all-start.4) | async-done | bytes 1835040 | tf_op jit(solution)/shard_map/all_to_all | solution.py:110
  142.2 4.7 %all-to-all-start.3 = ((bf16[8,32,7168]{2,1,0:T(8,128)(2,1)}), bf16[8,32,7168]{2,1,0:T(8,128)(2,1)}, u32[]{:S(2)}, u32[]{:S(2)}) async-start(bf16[8,32,7168]{2,1,0:T(8,128)(2,1)} %bitcast.104), calls=%async_computation.3 | async-start | bytes 7340032 | tf_op jit(solution)/shard_map/all_to_all | solution.py:110
  147.0 5.8 %fusion.147 = (bf16[256,1024]{1,0:T(8,128)(2,1)S(1)}, f32[256,1024]{1,0:T(8,128)S(1)}) fusion(bf16[1024,1024]{1,0:T(8,128)(2,1)} %param.11, s32[]{:T(128)S(6)} %select_n.76, f32[256]{0:T(256)S(1)} %reshape.106, bf16[1,1024,3584]{2,1,0:T(8,128)(2,1)} %param.13, bf16[256,7168]{1,0:T(8,128)(2,1)} %bitcast.20), kind=kOutput, calls=%fused_computation.82 | convolution fusion | flops 1881145344 | bytes 11273220 | tf_op jit(solution)/shard_map/dot_general | solution.py:46
  152.8 5.9 %fusion.112 = bf16[256,1024]{1,0:T(8,128)(2,1)S(1)} fusion(f32[256,1024]{1,0:T(8,128)S(1)} %get-tuple-element.48, bf16[3584,2048]{1,0:T(8,128)(2,1)} %bitcast.95, bf16[256,7168]{1,0:T(8,128)(2,1)} %bitcast.20, bf16[1024,1024]{1,0:T(8,128)(2,1)} %param.11, s32[]{:T(128)S(6)} %select_n.76), kind=kOutput, calls=%fused_computation.65 | convolution fusion | flops 1881931776 | bytes 11272196 | tf_op jit(solution)/shard_map/dot_general | solution.py:45
  158.7 1.1 pad_maximum_fusion.1.grad_ref
  159.8 10.7 %shard_map.74 = bf16[256,3584]{1,0:T(8,128)(2,1)} custom-call(bf16[256,2048]{1,0:T(8,128)(2,1)} %pad_maximum_fusion.1.grad_ref, bf16[3584,2048]{1,0:T(8,128)(2,1)} %bitcast.96), custom_call_target="tpu_custom_call" | custom-call | tf_op jit(solution)/shard_map/pallas_call | solution.py:32
  170.5 0.4 convolution_convert_fusion.7
  171.0 20.4 %collective-permute-done.2 = bf16[128,7168]{1,0:T(8,128)(2,1)} collective-permute-done((bf16[128,7168]{1,0:T(8,128)(2,1)}, bf16[128,7168]{1,0:T(8,128)(2,1)}, u32[]{:S(2)}, u32[]{:S(2)}) %collective-permute-start.2) | collective-permute-done | bytes 1835040 | tf_op jit(solution)/shard_map/ppermute | solution.py:68
  191.4 3.9 %all-to-all-start.6 = ((bf16[8,32,3584]{2,1,0:T(8,128)(2,1)}), bf16[8,32,3584]{2,1,0:T(8,128)(2,1)S(1)}, u32[]{:S(2)}, u32[]{:S(2)}) async-start(bf16[8,32,3584]{2,1,0:T(8,128)(2,1)} %bitcast.25), calls=%async_computation.6 | async-start | bytes 3670016 | tf_op jit(solution)/shard_map/all_to_all | solution.py:110
  195.2 0.4 fusion.171
  195.7 4.5 %convolution_convert_fusion = bf16[256,7168]{1,0:T(8,128)(2,1)} fusion(bf16[128,256]{1,0:T(8,128)(2,1)S(1)} %fusion.171, bf16[128,7168]{1,0:T(8,128)(2,1)} %collective-permute-done.2), kind=kOutput, calls=%fused_computation | convolution fusion | flops 471597056 | bytes 5570560 | tf_op jit(solution)/shard_map/dot_general | solution.py:59
  200.2 18.9 %all-to-all-done.6 = bf16[8,32,3584]{2,1,0:T(8,128)(2,1)S(1)} async-done(((bf16[8,32,3584]{2,1,0:T(8,128)(2,1)}), bf16[8,32,3584]{2,1,0:T(8,128)(2,1)S(1)}, u32[]{:S(2)}, u32[]{:S(2)}) %all-to-all-start.6) | async-done | bytes 1835040 | tf_op jit(solution)/shard_map/all_to_all | solution.py:110
  219.1 4.5 %all-to-all-start.5 = ((bf16[8,32,7168]{2,1,0:T(8,128)(2,1)}), bf16[8,32,7168]{2,1,0:T(8,128)(2,1)}, u32[]{:S(2)}, u32[]{:S(2)}) async-start(bf16[8,32,7168]{2,1,0:T(8,128)(2,1)} %bitcast.103), calls=%async_computation.5 | async-start | bytes 7340032 | tf_op jit(solution)/shard_map/all_to_all | solution.py:110
  223.7 5.8 %fusion.153 = (bf16[256,1024]{1,0:T(8,128)(2,1)S(1)}, f32[256,1024]{1,0:T(8,128)S(1)}) fusion(bf16[1024,1024]{1,0:T(8,128)(2,1)} %param.11, s32[]{:T(128)S(6)} %select_n.77, f32[256]{0:T(256)S(1)} %reshape.107, bf16[1,1024,3584]{2,1,0:T(8,128)(2,1)} %param.13, bf16[256,7168]{1,0:T(8,128)(2,1)} %bitcast.24), kind=kOutput, calls=%fused_computation.88 | convolution fusion | flops 1881145344 | bytes 11273220 | tf_op jit(solution)/shard_map/dot_general | solution.py:46
  229.5 1.3 convolution_convert_fusion.6
  230.8 0.4 collective-permute-start.3
  231.3 5.9 %fusion.117 = bf16[256,1024]{1,0:T(8,128)(2,1)S(1)} fusion(f32[256,1024]{1,0:T(8,128)S(1)} %get-tuple-element.50, bf16[3584,2048]{1,0:T(8,128)(2,1)} %bitcast.97, bf16[256,7168]{1,0:T(8,128)(2,1)} %bitcast.24, bf16[1024,1024]{1,0:T(8,128)(2,1)} %param.11, s32[]{:T(128)S(6)} %select_n.77), kind=kOutput, calls=%fused_computation.66 | convolution fusion | flops 1881931776 | bytes 11272196 | tf_op jit(solution)/shard_map/dot_general | solution.py:45
  237.2 1.1 pad_maximum_fusion.2.grad_ref
  238.3 10.7 %shard_map.75 = bf16[256,3584]{1,0:T(8,128)(2,1)} custom-call(bf16[256,2048]{1,0:T(8,128)(2,1)} %pad_maximum_fusion.2.grad_ref, bf16[3584,2048]{1,0:T(8,128)(2,1)} %bitcast.98), custom_call_target="tpu_custom_call" | custom-call | tf_op jit(solution)/shard_map/pallas_call | solution.py:32
  249.0 4.7 %collective-permute-done.3 = bf16[128,3584]{1,0:T(8,128)(2,1)S(1)} collective-permute-done((bf16[128,3584]{1,0:T(8,128)(2,1)}, bf16[128,3584]{1,0:T(8,128)(2,1)S(1)}, u32[]{:S(2)}, u32[]{:S(2)}) %collective-permute-start.3) | collective-permute-done | bytes 917536 | tf_op jit(solution)/shard_map/ppermute | solution.py:68
  253.7 13.4 %all-to-all-done.5 = bf16[8,32,7168]{2,1,0:T(8,128)(2,1)} async-done(((bf16[8,32,7168]{2,1,0:T(8,128)(2,1)}), bf16[8,32,7168]{2,1,0:T(8,128)(2,1)}, u32[]{:S(2)}, u32[]{:S(2)}) %all-to-all-start.5) | async-done | bytes 3670048 | tf_op jit(solution)/shard_map/all_to_all | solution.py:110
  267.1 3.8 all-to-all-start.7
  271.0 6.8 %fusion.159 = (bf16[256,1024]{1,0:T(8,128)(2,1)S(1)}, f32[256,1024]{1,0:T(8,128)}) fusion(bf16[1024,1024]{1,0:T(8,128)(2,1)} %param.11, s32[]{:T(128)S(6)} %select_n.78, f32[256]{0:T(256)S(1)} %reshape.108, bf16[1,1024,3584]{2,1,0:T(8,128)(2,1)} %param.13, bf16[256,7168]{1,0:T(8,128)(2,1)} %bitcast.27), kind=kOutput, calls=%fused_computation.94 | convolution fusion | flops 1881145344 | bytes 11273220 | tf_op jit(solution)/shard_map/dot_general | solution.py:46
  277.8 16.7 %all-to-all-done.7 = bf16[8,32,3584]{2,1,0:T(8,128)(2,1)S(1)} async-done(((bf16[8,32,3584]{2,1,0:T(8,128)(2,1)}), bf16[8,32,3584]{2,1,0:T(8,128)(2,1)S(1)}, u32[]{:S(2)}, u32[]{:S(2)}) %all-to-all-start.7) | async-done | bytes 1835040 | tf_op jit(solution)/shard_map/all_to_all | solution.py:110
  294.5 1.3 convolution_convert_fusion.5
  295.8 5.9 %fusion.122 = bf16[256,1024]{1,0:T(8,128)(2,1)S(1)} fusion(f32[256,1024]{1,0:T(8,128)S(1)} %copy-done.5, bf16[3584,2048]{1,0:T(8,128)(2,1)} %bitcast.99, bf16[256,7168]{1,0:T(8,128)(2,1)} %bitcast.27, bf16[1024,1024]{1,0:T(8,128)(2,1)} %param.11, s32[]{:T(128)S(6)} %select_n.78), kind=kOutput, calls=%fused_computation.67 | convolution fusion | flops 1881931776 | bytes 11272196 | tf_op jit(solution)/shard_map/dot_general | solution.py:45
  301.8 1.1 pad_maximum_fusion.3.grad_ref
  302.8 10.7 %shard_map.76 = bf16[256,3584]{1,0:T(8,128)(2,1)} custom-call(bf16[256,2048]{1,0:T(8,128)(2,1)} %pad_maximum_fusion.3.grad_ref, bf16[3584,2048]{1,0:T(8,128)(2,1)} %bitcast.100), custom_call_target="tpu_custom_call" | custom-call | tf_op jit(solution)/shard_map/pallas_call | solution.py:32
  313.6 20.0 %collective-permute-done.4 = bf16[128,3584]{1,0:T(8,128)(2,1)S(1)} collective-permute-done((bf16[128,3584]{1,0:T(8,128)(2,1)}, bf16[128,3584]{1,0:T(8,128)(2,1)S(1)}, u32[]{:S(2)}, u32[]{:S(2)}) %collective-permute-start.4) | collective-permute-done | bytes 917536 | tf_op jit(solution)/shard_map/ppermute | solution.py:68
  333.6 28.8 %all_to_all.45 = bf16[8,32,3584]{2,1,0:T(8,128)(2,1)S(1)} all-to-all(bf16[8,32,3584]{2,1,0:T(8,128)(2,1)} %bitcast.107), channel_id=1, replica_groups=mesh['node'=4,'local'=8] {'local'}, dimensions={0} | all-to-all | bytes 3670016 | tf_op jit(solution)/shard_map/all_to_all | solution.py:110
  362.4 0.4 convolution_convert_fusion.4
  362.9 23.2 %collective-permute-done.5 = bf16[128,3584]{1,0:T(8,128)(2,1)S(1)} collective-permute-done((bf16[128,3584]{1,0:T(8,128)(2,1)S(1)}, bf16[128,3584]{1,0:T(8,128)(2,1)S(1)}, u32[]{:S(2)}, u32[]{:S(2)}) %collective-permute-start.5) | collective-permute-done | bytes 917536 | tf_op jit(solution)/shard_map/ppermute | solution.py:68
  386.1 1.4 add_convert_fusion
  (42 shorter events, 1.6 us)
Async XLA Ops:
  0.0 2.4 copy-start.1
  6.7 7.7 %copy-start.4 = (s32[4,128,8]{1,2,0:T(8,128)S(1)}, s32[4,128,8]{1,2,0:T(8,128)}, u32[]{:S(2)}) copy-start(s32[4,128,8]{1,2,0:T(8,128)} %param.10) | copy-start | bytes 49156
  6.7 48.9 %all-to-all-start = ((bf16[8,32,7168]{2,1,0:T(8,128)(2,1)}), bf16[8,32,7168]{2,1,0:T(8,128)(2,1)}, u32[]{:S(2)}, u32[]{:S(2)}) async-start(bf16[8,32,7168]{2,1,0:T(8,128)(2,1)} %bitcast.101), calls=%async_computation | async-start | bytes 7340032 | tf_op jit(solution)/shard_map/all_to_all | solution.py:110
  12.0 46.9 %collective-permute-start = (bf16[128,7168]{1,0:T(8,128)(2,1)S(1)}, bf16[128,7168]{1,0:T(8,128)(2,1)}, u32[]{:S(2)}, u32[]{:S(2)}) collective-permute-start(bf16[128,7168]{1,0:T(8,128)(2,1)S(1)} %constant_dynamic-update-slice_fusion), channel_id=1, source_target_pairs={{0,8},{8,16},{16,24},{24,0},{1,9},{9,17},{17,25},{25,1},{2,10},{10... | collective-permute-start | bytes 5505032 | tf_op jit(solution)/shard_map/ppermute | solution.py:68
  55.6 8.0 %all-to-all-start.2 = ((bf16[8,4,32]{2,1,0:T(4,128)(2,1)}), bf16[8,4,32]{2,1,0:T(4,128)(2,1)S(1)}, u32[]{:S(2)}, u32[]{:S(2)}) async-start(bf16[8,4,32]{2,1,0:T(4,128)(2,1)} %copy.12), calls=%async_computation.2 | async-start | bytes 16384 | tf_op jit(solution)/shard_map/all_to_all | solution.py:107
  63.6 49.7 %all-to-all-start.1 = ((bf16[8,32,7168]{2,1,0:T(8,128)(2,1)}), bf16[8,32,7168]{2,1,0:T(8,128)(2,1)}, u32[]{:S(2)}, u32[]{:S(2)}) async-start(bf16[8,32,7168]{2,1,0:T(8,128)(2,1)} %bitcast.102), calls=%async_computation.1 | async-start | bytes 7340032 | tf_op jit(solution)/shard_map/all_to_all | solution.py:110
  68.2 45.0 %collective-permute-start.1 = (bf16[128,7168]{1,0:T(8,128)(2,1)}, bf16[128,7168]{1,0:T(8,128)(2,1)S(1)}, u32[]{:S(2)}, u32[]{:S(2)}) collective-permute-start(bf16[128,7168]{1,0:T(8,128)(2,1)} %collective-permute-done), channel_id=1, source_target_pairs={{0,8},{8,16},{16,24},{24,0},{1,9},{9,17},{17,25},{25,1},{2,10},{10... | collective-permute-start | bytes 5505032 | tf_op jit(solution)/shard_map/ppermute | solution.py:68
  113.2 1.2 copy-start
  114.5 27.7 %all-to-all-start.4 = ((bf16[8,32,3584]{2,1,0:T(8,128)(2,1)}), bf16[8,32,3584]{2,1,0:T(8,128)(2,1)S(1)}, u32[]{:S(2)}, u32[]{:S(2)}) async-start(bf16[8,32,3584]{2,1,0:T(8,128)(2,1)} %bitcast.106), calls=%async_computation.4 | async-start | bytes 3670016 | tf_op jit(solution)/shard_map/all_to_all | solution.py:110
  142.2 49.2 %all-to-all-start.3 = ((bf16[8,32,7168]{2,1,0:T(8,128)(2,1)}), bf16[8,32,7168]{2,1,0:T(8,128)(2,1)}, u32[]{:S(2)}, u32[]{:S(2)}) async-start(bf16[8,32,7168]{2,1,0:T(8,128)(2,1)} %bitcast.104), calls=%async_computation.3 | async-start | bytes 7340032 | tf_op jit(solution)/shard_map/all_to_all | solution.py:110
  147.0 44.4 %collective-permute-start.2 = (bf16[128,7168]{1,0:T(8,128)(2,1)}, bf16[128,7168]{1,0:T(8,128)(2,1)}, u32[]{:S(2)}, u32[]{:S(2)}) collective-permute-start(bf16[128,7168]{1,0:T(8,128)(2,1)} %copy-done), channel_id=1, source_target_pairs={{0,8},{8,16},{16,24},{24,0},{1,9},{9,17},{17,25},{25,1},{2,10},{10... | collective-permute-start | bytes 5505032 | tf_op jit(solution)/shard_map/ppermute | solution.py:68
  191.4 27.7 %all-to-all-start.6 = ((bf16[8,32,3584]{2,1,0:T(8,128)(2,1)}), bf16[8,32,3584]{2,1,0:T(8,128)(2,1)S(1)}, u32[]{:S(2)}, u32[]{:S(2)}) async-start(bf16[8,32,3584]{2,1,0:T(8,128)(2,1)} %bitcast.25), calls=%async_computation.6 | async-start | bytes 3670016 | tf_op jit(solution)/shard_map/all_to_all | solution.py:110
  219.1 48.0 %all-to-all-start.5 = ((bf16[8,32,7168]{2,1,0:T(8,128)(2,1)}), bf16[8,32,7168]{2,1,0:T(8,128)(2,1)}, u32[]{:S(2)}, u32[]{:S(2)}) async-start(bf16[8,32,7168]{2,1,0:T(8,128)(2,1)} %bitcast.103), calls=%async_computation.5 | async-start | bytes 7340032 | tf_op jit(solution)/shard_map/all_to_all | solution.py:110
  230.8 22.8 %collective-permute-start.3 = (bf16[128,3584]{1,0:T(8,128)(2,1)}, bf16[128,3584]{1,0:T(8,128)(2,1)S(1)}, u32[]{:S(2)}, u32[]{:S(2)}) collective-permute-start(bf16[128,3584]{1,0:T(8,128)(2,1)} %convolution_convert_fusion.6), channel_id=1, source_target_pairs={{0,24},{8,0},{16,8},{24,16},{1,25},{9,1},{17,9},{25,17},{2,26},{10... | collective-permute-start | bytes 2752520 | tf_op jit(solution)/shard_map/ppermute | solution.py:68
  253.7 13.4 %copy-start.2 = (bf16[128,3584]{1,0:T(8,128)(2,1)}, bf16[128,3584]{1,0:T(8,128)(2,1)S(1)}, u32[]{:S(2)}) copy-start(bf16[128,3584]{1,0:T(8,128)(2,1)S(1)} %collective-permute-done.3) | copy-start | bytes 2752516
  267.1 27.4 %all-to-all-start.7 = ((bf16[8,32,3584]{2,1,0:T(8,128)(2,1)}), bf16[8,32,3584]{2,1,0:T(8,128)(2,1)S(1)}, u32[]{:S(2)}, u32[]{:S(2)}) async-start(bf16[8,32,3584]{2,1,0:T(8,128)(2,1)} %bitcast.105), calls=%async_computation.7 | async-start | bytes 3670016 | tf_op jit(solution)/shard_map/all_to_all | solution.py:110
  294.5 1.4 copy-start.5
  295.8 37.8 %collective-permute-start.4 = (bf16[128,3584]{1,0:T(8,128)(2,1)}, bf16[128,3584]{1,0:T(8,128)(2,1)S(1)}, u32[]{:S(2)}, u32[]{:S(2)}) collective-permute-start(bf16[128,3584]{1,0:T(8,128)(2,1)} %convolution_convert_fusion.5), channel_id=1, source_target_pairs={{0,16},{8,24},{16,0},{24,8},{1,17},{9,25},{17,1},{25,9},{2,18},{10... | collective-permute-start | bytes 2752520 | tf_op jit(solution)/shard_map/ppermute | solution.py:68
  362.4 23.7 %copy-start.3 = (bf16[128,3584]{1,0:T(8,128)(2,1)S(1)}, bf16[128,3584]{1,0:T(8,128)(2,1)}, u32[]{:S(2)}) copy-start(bf16[128,3584]{1,0:T(8,128)(2,1)} %copy-done.2) | copy-start | bytes 2752516
  362.8 23.3 %collective-permute-start.5 = (bf16[128,3584]{1,0:T(8,128)(2,1)S(1)}, bf16[128,3584]{1,0:T(8,128)(2,1)S(1)}, u32[]{:S(2)}, u32[]{:S(2)}) collective-permute-start(bf16[128,3584]{1,0:T(8,128)(2,1)S(1)} %convolution_convert_fusion.4), channel_id=1, source_target_pairs={{0,8},{8,16},{16,24},{24,0},{1,9},{9,17},{17,25},{25,1},{2,10},{10... | collective-permute-start | bytes 2752520 | tf_op jit(solution)/shard_map/ppermute | solution.py:68

commit v12 on v9

--- a/solution.py
+++ b/solution.py
@@ -104,7 +104,7 @@
             .astype(jnp.bfloat16)
             .reshape(n_local, capacity)
         )
-    gates = lax.all_to_all(jnp.stack(send_gate, axis=1), "local", 0, 0, tiled=True)
+    gate_store = {}
 
     def spread(rows):
         return lax.all_to_all(
@@ -123,7 +123,7 @@
         return expert_backward(
             rows[:, :model_width],
             rows[:, model_width:],
-            gates[:, step].reshape(chunk_rows),
+            gate_store[0][:, step].reshape(chunk_rows),
             saved,
             weight_in,
             weight_out,
@@ -145,6 +145,10 @@
     homes = {}
     for slot in range(-1, n_node + 2):
         produced = {}
+        if slot == -1:
+            produced["gates", 0] = lax.all_to_all(
+                jnp.stack(send_gate, axis=1), "local", 0, 0, tiled=True
+            )
         if 0 < slot + 2 < n_node:
             produced["chunk", slot + 2] = fetch(slot + 2, chunks[slot + 1])
         if 0 <= slot + 1 < n_node:
@@ -159,7 +163,7 @@
         values = lax.optimization_barrier([produced[key] for key in keys])
         for (kind, step), value in zip(keys, values):
             {"chunk": chunks, "received": received, "contrib": contribs, "sum": sums,
-             "home": homes}[kind][step] = value
+             "home": homes, "gates": gate_store}[kind][step] = value
 
     total = homes[0].astype(jnp.float32)
     for step in range(1, n_node):

time: 372 us -> 376 us (1.011)
  waiting for transfers between devices: 200 us -> 206 us
    ppermute x6, waiting for transfers between devices: 82.7 us -> 126 us  [shift(): lax.ppermute(value, 'node', [(i, (i + step) % n_node) for i in range(n_no...]
    all_to_all x8, waiting for transfers between devices: 117 us -> 80.1 us  [spread(): lax.all_to_all(rows.reshape(n_local, capacity, rows.shape[-1]), 'local',...]
  transfers between devices with their start and end apart: 15 -> 15, of which waited for: 10 -> 9; matrix products, arithmetic and copies ran while one was open for 20% -> 19% of each run, Pallas kernels for 12% -> 11%
where the time goes in v12:
time: 376 us; the launch traced here: 375 us
  waiting for transfers between devices  206 us (55%)
  matrix products  69.2 us (18%)
  Pallas kernels  43 us (11%)
  starting transfers between devices  41.2 us (11%)
  other arithmetic  9.66 us (3%)
  local copies, waits for them, and re-layouts  5.76 us (2%)
    ppermute x6, waiting for transfers between devices, shift(): lax.ppermute(value, 'node', [(i, (i + step) % n_node) for i in range(n_no...  126 us
    all_to_all x8, waiting for transfers between devices, spread(): lax.all_to_all(rows.reshape(n_local, capacity, rows.shape[-1]), 'local',...  80.1 us
    pallas_call x4, Pallas kernels, part_matmul(): pl.pallas_call(part_kernel, grid=(width // tile,), in_specs=[pl.BlockSpec...  43 us
    all_to_all x8, starting transfers between devices, spread(): lax.all_to_all(rows.reshape(n_local, capacity, rows.shape[-1]), 'local',...  33.3 us
    dot_general x4, matrix products, expert_backward(): jnp.dot(rows_x, weight_in[:, FF:], preferred_element_type=jnp.float32)  23.7 us
    dot_general x4, matrix products, expert_backward(): lax.dot_general(rows_dy, weight_out, (((1,), (1,)), ((), ())), preferred_...  23.3 us
    dot_general x4, matrix products, select_rows(): lax.dot_general(onehot, rows, (((0,), (0,)), ((), ())), preferred_element...  16.4 us
  transfers between devices with their start and end apart: 15, of which 9 were waited for; matrix products, arithmetic and copies ran while one was open for 19% of the time, Pallas kernels for 11%

profile of v12, /device:TPU:0, one launch (start us, length us, event | category | flops | bytes accessed | tf_op | source)
XLA Modules:
  0.0 375.0 jit_solution(4313506047481188305)
XLA Ops:
  0.0 0.7 multiply_convert_fusion
  0.7 0.1 copy.13
  0.9 0.1 copy.16
  1.1 0.1 copy.14
  1.2 0.8 copy.11
  2.1 0.2 reshape.88
  2.3 0.6 fusion.133
  3.1 0.4 fusion.165
  3.7 0.4 fusion.161
  4.3 0.4 fusion.163
  5.0 0.4 fusion.166
  5.5 0.6 copy.12
  6.1 5.2 %all-to-all-start = ((bf16[8,4,32]{2,1,0:T(4,128)(2,1)}), bf16[8,4,32]{2,1,0:T(4,128)(2,1)S(1)}, u32[]{:S(2)}, u32[]{:S(2)}) async-start(bf16[8,4,32]{2,1,0:T(4,128)(2,1)} %copy.12), calls=%async_computation | async-start | bytes 16384 | tf_op jit(solution)/shard_map/all_to_all | solution.py:149
  11.3 0.4 fusion.169
  11.8 1.3 constant_dynamic-update-slice_fusion
  13.1 2.9 convolution_convert_fusion.3
  16.0 4.5 %all-to-all-start.1 = ((bf16[8,32,7168]{2,1,0:T(8,128)(2,1)}), bf16[8,32,7168]{2,1,0:T(8,128)(2,1)}, u32[]{:S(2)}, u32[]{:S(2)}) async-start(bf16[8,32,7168]{2,1,0:T(8,128)(2,1)} %bitcast.104), calls=%async_computation.1 | async-start | bytes 7340032 | tf_op jit(solution)/shard_map/all_to_all | solution.py:110
  20.5 1.6 collective-permute-start
  22.1 0.4 fusion.170
  22.5 42.4 %collective-permute-done = bf16[128,7168]{1,0:T(8,128)(2,1)} collective-permute-done((bf16[128,7168]{1,0:T(8,128)(2,1)S(1)}, bf16[128,7168]{1,0:T(8,128)(2,1)}, u32[]{:S(2)}, u32[]{:S(2)}) %collective-permute-start) | collective-permute-done | bytes 1835040 | tf_op jit(solution)/shard_map/ppermute | solution.py:68
  64.9 4.5 %convolution_convert_fusion.2 = bf16[256,7168]{1,0:T(8,128)(2,1)} fusion(bf16[128,256]{1,0:T(8,128)(2,1)S(1)} %fusion.170, bf16[128,7168]{1,0:T(8,128)(2,1)} %collective-permute-done), kind=kOutput, calls=%fused_computation.2 | convolution fusion | flops 471597056 | bytes 5570560 | tf_op jit(solution)/shard_map/dot_general | solution.py:59
  69.4 4.5 %all-to-all-start.2 = ((bf16[8,32,7168]{2,1,0:T(8,128)(2,1)}), bf16[8,32,7168]{2,1,0:T(8,128)(2,1)}, u32[]{:S(2)}, u32[]{:S(2)}) async-start(bf16[8,32,7168]{2,1,0:T(8,128)(2,1)} %bitcast.103), calls=%async_computation.2 | async-start | bytes 7340032 | tf_op jit(solution)/shard_map/all_to_all | solution.py:110
  73.9 0.8 collective-permute-start.1
  74.8 5.8 %fusion.141 = (bf16[256,1024]{1,0:T(8,128)(2,1)S(1)}, f32[256,1024]{1,0:T(8,128)S(1)}) fusion(bf16[1024,1024]{1,0:T(8,128)(2,1)} %param.11, s32[]{:T(128)S(6)} %select_n.75, f32[256]{0:T(256)S(1)} %reshape.105, bf16[1,1024,3584]{2,1,0:T(8,128)(2,1)} %param.13, bf16[256,7168]{1,0:T(8,128)(2,1)} %bitcast.16), kind=kOutput, calls=%fused_computation.76 | convolution fusion | flops 1881145344 | bytes 11273220 | tf_op jit(solution)/shard_map/dot_general | solution.py:46
  80.6 5.9 %fusion.107 = bf16[256,1024]{1,0:T(8,128)(2,1)S(1)} fusion(f32[256,1024]{1,0:T(8,128)S(1)} %get-tuple-element.56, bf16[3584,2048]{1,0:T(8,128)(2,1)} %bitcast.93, bf16[256,7168]{1,0:T(8,128)(2,1)} %bitcast.16, bf16[1024,1024]{1,0:T(8,128)(2,1)} %param.11, s32[]{:T(128)S(6)} %select_n.75), kind=kOutput, calls=%fused_computation.64 | convolution fusion | flops 1881931776 | bytes 11272196 | tf_op jit(solution)/shard_map/dot_general | solution.py:45
  86.5 1.1 pad_maximum_fusion.grad_ref
  87.6 10.8 %shard_map.73 = bf16[256,3584]{1,0:T(8,128)(2,1)} custom-call(bf16[256,2048]{1,0:T(8,128)(2,1)} %pad_maximum_fusion.grad_ref, bf16[3584,2048]{1,0:T(8,128)(2,1)} %bitcast.94), custom_call_target="tpu_custom_call" | custom-call | tf_op jit(solution)/shard_map/pallas_call | solution.py:32
  98.4 19.8 %collective-permute-done.1 = bf16[128,7168]{1,0:T(8,128)(2,1)S(1)} collective-permute-done((bf16[128,7168]{1,0:T(8,128)(2,1)}, bf16[128,7168]{1,0:T(8,128)(2,1)S(1)}, u32[]{:S(2)}, u32[]{:S(2)}) %collective-permute-start.1) | collective-permute-done | bytes 1835040 | tf_op jit(solution)/shard_map/ppermute | solution.py:68
  118.2 1.2 copy-done
  119.4 3.9 %all-to-all-start.4 = ((bf16[8,32,3584]{2,1,0:T(8,128)(2,1)}), bf16[8,32,3584]{2,1,0:T(8,128)(2,1)S(1)}, u32[]{:S(2)}, u32[]{:S(2)}) async-start(bf16[8,32,3584]{2,1,0:T(8,128)(2,1)} %bitcast.105), calls=%async_computation.4 | async-start | bytes 3670016 | tf_op jit(solution)/shard_map/all_to_all | solution.py:110
  123.3 0.4 fusion.171
  123.7 4.5 %convolution_convert_fusion.1 = bf16[256,7168]{1,0:T(8,128)(2,1)} fusion(bf16[128,256]{1,0:T(8,128)(2,1)S(1)} %fusion.171, bf16[128,7168]{1,0:T(8,128)(2,1)} %copy-done), kind=kOutput, calls=%fused_computation.1 | convolution fusion | flops 471597056 | bytes 5570560 | tf_op jit(solution)/shard_map/dot_general | solution.py:59
  128.2 18.9 %all-to-all-done.4 = bf16[8,32,3584]{2,1,0:T(8,128)(2,1)S(1)} async-done(((bf16[8,32,3584]{2,1,0:T(8,128)(2,1)}), bf16[8,32,3584]{2,1,0:T(8,128)(2,1)S(1)}, u32[]{:S(2)}, u32[]{:S(2)}) %all-to-all-start.4) | async-done | bytes 1835040 | tf_op jit(solution)/shard_map/all_to_all | solution.py:110
  147.1 4.7 %all-to-all-start.3 = ((bf16[8,32,7168]{2,1,0:T(8,128)(2,1)}), bf16[8,32,7168]{2,1,0:T(8,128)(2,1)}, u32[]{:S(2)}, u32[]{:S(2)}) async-start(bf16[8,32,7168]{2,1,0:T(8,128)(2,1)} %bitcast.102), calls=%async_computation.3 | async-start | bytes 7340032 | tf_op jit(solution)/shard_map/all_to_all | solution.py:110
  151.9 5.8 %fusion.147 = (bf16[256,1024]{1,0:T(8,128)(2,1)S(1)}, f32[256,1024]{1,0:T(8,128)S(1)}) fusion(bf16[1024,1024]{1,0:T(8,128)(2,1)} %param.11, s32[]{:T(128)S(6)} %select_n.76, f32[256]{0:T(256)S(1)} %reshape.106, bf16[1,1024,3584]{2,1,0:T(8,128)(2,1)} %param.13, bf16[256,7168]{1,0:T(8,128)(2,1)} %bitcast.20), kind=kOutput, calls=%fused_computation.82 | convolution fusion | flops 1881145344 | bytes 11273220 | tf_op jit(solution)/shard_map/dot_general | solution.py:46
  157.7 5.9 %fusion.112 = bf16[256,1024]{1,0:T(8,128)(2,1)S(1)} fusion(f32[256,1024]{1,0:T(8,128)S(1)} %get-tuple-element.58, bf16[3584,2048]{1,0:T(8,128)(2,1)} %bitcast.95, bf16[256,7168]{1,0:T(8,128)(2,1)} %bitcast.20, bf16[1024,1024]{1,0:T(8,128)(2,1)} %param.11, s32[]{:T(128)S(6)} %select_n.76), kind=kOutput, calls=%fused_computation.65 | convolution fusion | flops 1881931776 | bytes 11272196 | tf_op jit(solution)/shard_map/dot_general | solution.py:45
  163.7 1.1 pad_maximum_fusion.1.grad_ref
  164.7 10.7 %shard_map.74 = bf16[256,3584]{1,0:T(8,128)(2,1)} custom-call(bf16[256,2048]{1,0:T(8,128)(2,1)} %pad_maximum_fusion.1.grad_ref, bf16[3584,2048]{1,0:T(8,128)(2,1)} %bitcast.96), custom_call_target="tpu_custom_call" | custom-call | tf_op jit(solution)/shard_map/pallas_call | solution.py:32
  175.5 0.4 convolution_convert_fusion.7
  175.9 20.4 %collective-permute-done.2 = bf16[128,7168]{1,0:T(8,128)(2,1)} collective-permute-done((bf16[128,7168]{1,0:T(8,128)(2,1)}, bf16[128,7168]{1,0:T(8,128)(2,1)}, u32[]{:S(2)}, u32[]{:S(2)}) %collective-permute-start.2) | collective-permute-done | bytes 1835040 | tf_op jit(solution)/shard_map/ppermute | solution.py:68
  196.3 3.9 %all-to-all-start.6 = ((bf16[8,32,3584]{2,1,0:T(8,128)(2,1)}), bf16[8,32,3584]{2,1,0:T(8,128)(2,1)S(1)}, u32[]{:S(2)}, u32[]{:S(2)}) async-start(bf16[8,32,3584]{2,1,0:T(8,128)(2,1)} %bitcast.25), calls=%async_computation.6 | async-start | bytes 3670016 | tf_op jit(solution)/shard_map/all_to_all | solution.py:110
  200.2 0.4 fusion.168
  200.6 4.4 %convolution_convert_fusion = bf16[256,7168]{1,0:T(8,128)(2,1)} fusion(bf16[128,256]{1,0:T(8,128)(2,1)S(1)} %fusion.168, bf16[128,7168]{1,0:T(8,128)(2,1)} %collective-permute-done.2), kind=kOutput, calls=%fused_computation | convolution fusion | flops 471597056 | bytes 5570560 | tf_op jit(solution)/shard_map/dot_general | solution.py:59
  205.0 19.0 %all-to-all-done.6 = bf16[8,32,3584]{2,1,0:T(8,128)(2,1)S(1)} async-done(((bf16[8,32,3584]{2,1,0:T(8,128)(2,1)}), bf16[8,32,3584]{2,1,0:T(8,128)(2,1)S(1)}, u32[]{:S(2)}, u32[]{:S(2)}) %all-to-all-start.6) | async-done | bytes 1835040 | tf_op jit(solution)/shard_map/all_to_all | solution.py:110
  224.0 4.5 %all-to-all-start.5 = ((bf16[8,32,7168]{2,1,0:T(8,128)(2,1)}), bf16[8,32,7168]{2,1,0:T(8,128)(2,1)}, u32[]{:S(2)}, u32[]{:S(2)}) async-start(bf16[8,32,7168]{2,1,0:T(8,128)(2,1)} %bitcast.101), calls=%async_computation.5 | async-start | bytes 7340032 | tf_op jit(solution)/shard_map/all_to_all | solution.py:110
  228.7 5.8 %fusion.153 = (bf16[256,1024]{1,0:T(8,128)(2,1)S(1)}, f32[256,1024]{1,0:T(8,128)S(1)}) fusion(bf16[1024,1024]{1,0:T(8,128)(2,1)} %param.11, s32[]{:T(128)S(6)} %select_n.77, f32[256]{0:T(256)S(1)} %reshape.107, bf16[1,1024,3584]{2,1,0:T(8,128)(2,1)} %param.13, bf16[256,7168]{1,0:T(8,128)(2,1)} %bitcast.24), kind=kOutput, calls=%fused_computation.88 | convolution fusion | flops 1881145344 | bytes 11273220 | tf_op jit(solution)/shard_map/dot_general | solution.py:46
  234.5 5.9 %fusion.117 = bf16[256,1024]{1,0:T(8,128)(2,1)S(1)} fusion(f32[256,1024]{1,0:T(8,128)S(1)} %get-tuple-element.60, bf16[3584,2048]{1,0:T(8,128)(2,1)} %bitcast.97, bf16[256,7168]{1,0:T(8,128)(2,1)} %bitcast.24, bf16[1024,1024]{1,0:T(8,128)(2,1)} %param.11, s32[]{:T(128)S(6)} %select_n.77), kind=kOutput, calls=%fused_computation.66 | convolution fusion | flops 1881931776 | bytes 11272196 | tf_op jit(solution)/shard_map/dot_general | solution.py:45
  240.4 1.1 pad_maximum_fusion.2.grad_ref
  241.5 10.7 %shard_map.75 = bf16[256,3584]{1,0:T(8,128)(2,1)} custom-call(bf16[256,2048]{1,0:T(8,128)(2,1)} %pad_maximum_fusion.2.grad_ref, bf16[3584,2048]{1,0:T(8,128)(2,1)} %bitcast.98), custom_call_target="tpu_custom_call" | custom-call | tf_op jit(solution)/shard_map/pallas_call | solution.py:32
  252.3 1.4 convolution_convert_fusion.6
  253.6 18.4 %all-to-all-done.5 = bf16[8,32,7168]{2,1,0:T(8,128)(2,1)} async-done(((bf16[8,32,7168]{2,1,0:T(8,128)(2,1)}), bf16[8,32,7168]{2,1,0:T(8,128)(2,1)}, u32[]{:S(2)}, u32[]{:S(2)}) %all-to-all-start.5) | async-done | bytes 3670048 | tf_op jit(solution)/shard_map/all_to_all | solution.py:110
  272.0 3.6 all-to-all-start.7
  275.6 0.3 collective-permute-start.3
  275.9 5.8 %fusion.159 = (bf16[256,1024]{1,0:T(8,128)(2,1)S(1)}, f32[256,1024]{1,0:T(8,128)S(1)}) fusion(bf16[1024,1024]{1,0:T(8,128)(2,1)} %param.11, s32[]{:T(128)S(6)} %select_n.78, f32[256]{0:T(256)S(1)} %reshape.108, bf16[1,1024,3584]{2,1,0:T(8,128)(2,1)} %param.13, bf16[256,7168]{1,0:T(8,128)(2,1)} %bitcast.27), kind=kOutput, calls=%fused_computation.94 | convolution fusion | flops 1881145344 | bytes 11273220 | tf_op jit(solution)/shard_map/dot_general | solution.py:46
  281.7 5.9 %fusion.122 = bf16[256,1024]{1,0:T(8,128)(2,1)S(1)} fusion(f32[256,1024]{1,0:T(8,128)S(1)} %get-tuple-element.62, bf16[3584,2048]{1,0:T(8,128)(2,1)} %bitcast.99, bf16[256,7168]{1,0:T(8,128)(2,1)} %bitcast.27, bf16[1024,1024]{1,0:T(8,128)(2,1)} %param.11, s32[]{:T(128)S(6)} %select_n.78), kind=kOutput, calls=%fused_computation.67 | convolution fusion | flops 1881931776 | bytes 11272196 | tf_op jit(solution)/shard_map/dot_general | solution.py:45
  287.7 1.1 pad_maximum_fusion.3.grad_ref
  288.7 10.7 %shard_map.76 = bf16[256,3584]{1,0:T(8,128)(2,1)} custom-call(bf16[256,2048]{1,0:T(8,128)(2,1)} %pad_maximum_fusion.3.grad_ref, bf16[3584,2048]{1,0:T(8,128)(2,1)} %bitcast.100), custom_call_target="tpu_custom_call" | custom-call | tf_op jit(solution)/shard_map/pallas_call | solution.py:32
  299.5 1.3 convolution_convert_fusion.5
  300.8 3.8 %all-to-all-start.8 = ((bf16[8,32,3584]{2,1,0:T(8,128)(2,1)}), bf16[8,32,3584]{2,1,0:T(8,128)(2,1)S(1)}, u32[]{:S(2)}, u32[]{:S(2)}) async-start(bf16[8,32,3584]{2,1,0:T(8,128)(2,1)} %bitcast.30), calls=%async_computation.8 | async-start | bytes 3670016 | tf_op jit(solution)/shard_map/all_to_all | solution.py:110
  304.7 23.8 %all-to-all-done.8 = bf16[8,32,3584]{2,1,0:T(8,128)(2,1)S(1)} async-done(((bf16[8,32,3584]{2,1,0:T(8,128)(2,1)}), bf16[8,32,3584]{2,1,0:T(8,128)(2,1)S(1)}, u32[]{:S(2)}, u32[]{:S(2)}) %all-to-all-start.8) | async-done | bytes 1835040 | tf_op jit(solution)/shard_map/all_to_all | solution.py:110
  328.5 0.4 convolution_convert_fusion.4
  328.9 19.4 %collective-permute-done.4 = bf16[128,3584]{1,0:T(8,128)(2,1)} collective-permute-done((bf16[128,3584]{1,0:T(8,128)(2,1)}, bf16[128,3584]{1,0:T(8,128)(2,1)}, u32[]{:S(2)}, u32[]{:S(2)}) %collective-permute-start.4) | collective-permute-done | bytes 917536 | tf_op jit(solution)/shard_map/ppermute | solution.py:68
  348.3 23.8 %collective-permute-done.5 = bf16[128,3584]{1,0:T(8,128)(2,1)S(1)} collective-permute-done((bf16[128,3584]{1,0:T(8,128)(2,1)S(1)}, bf16[128,3584]{1,0:T(8,128)(2,1)S(1)}, u32[]{:S(2)}, u32[]{:S(2)}) %collective-permute-start.5) | collective-permute-done | bytes 917536 | tf_op jit(solution)/shard_map/ppermute | solution.py:68
  372.1 2.9 add_convert_fusion
  (35 shorter events, 1.4 us)
Async XLA Ops:
  3.1 8.6 %copy-start.1 = (bf16[128,3584]{1,0:T(8,128)(2,1)S(1)}, bf16[128,3584]{1,0:T(8,128)(2,1)}, u32[]{:S(2)}) copy-start(bf16[128,3584]{1,0:T(8,128)(2,1)} %param.7) | copy-start | bytes 2752516
  6.1 9.9 %all-to-all-start = ((bf16[8,4,32]{2,1,0:T(4,128)(2,1)}), bf16[8,4,32]{2,1,0:T(4,128)(2,1)S(1)}, u32[]{:S(2)}, u32[]{:S(2)}) async-start(bf16[8,4,32]{2,1,0:T(4,128)(2,1)} %copy.12), calls=%async_computation | async-start | bytes 16384 | tf_op jit(solution)/shard_map/all_to_all | solution.py:149
  16.0 48.9 %all-to-all-start.1 = ((bf16[8,32,7168]{2,1,0:T(8,128)(2,1)}), bf16[8,32,7168]{2,1,0:T(8,128)(2,1)}, u32[]{:S(2)}, u32[]{:S(2)}) async-start(bf16[8,32,7168]{2,1,0:T(8,128)(2,1)} %bitcast.104), calls=%async_computation.1 | async-start | bytes 7340032 | tf_op jit(solution)/shard_map/all_to_all | solution.py:110
  20.5 44.4 %collective-permute-start = (bf16[128,7168]{1,0:T(8,128)(2,1)S(1)}, bf16[128,7168]{1,0:T(8,128)(2,1)}, u32[]{:S(2)}, u32[]{:S(2)}) collective-permute-start(bf16[128,7168]{1,0:T(8,128)(2,1)S(1)} %constant_dynamic-update-slice_fusion), channel_id=1, source_target_pairs={{0,8},{8,16},{16,24},{24,0},{1,9},{9,17},{17,25},{25,1},{2,10},{10... | collective-permute-start | bytes 5505032 | tf_op jit(solution)/shard_map/ppermute | solution.py:68
  69.4 48.8 %all-to-all-start.2 = ((bf16[8,32,7168]{2,1,0:T(8,128)(2,1)}), bf16[8,32,7168]{2,1,0:T(8,128)(2,1)}, u32[]{:S(2)}, u32[]{:S(2)}) async-start(bf16[8,32,7168]{2,1,0:T(8,128)(2,1)} %bitcast.103), calls=%async_computation.2 | async-start | bytes 7340032 | tf_op jit(solution)/shard_map/all_to_all | solution.py:110
  73.9 44.3 %collective-permute-start.1 = (bf16[128,7168]{1,0:T(8,128)(2,1)}, bf16[128,7168]{1,0:T(8,128)(2,1)S(1)}, u32[]{:S(2)}, u32[]{:S(2)}) collective-permute-start(bf16[128,7168]{1,0:T(8,128)(2,1)} %collective-permute-done), channel_id=1, source_target_pairs={{0,8},{8,16},{16,24},{24,0},{1,9},{9,17},{17,25},{25,1},{2,10},{10... | collective-permute-start | bytes 5505032 | tf_op jit(solution)/shard_map/ppermute | solution.py:68
  118.2 1.2 copy-start
  119.4 27.7 %all-to-all-start.4 = ((bf16[8,32,3584]{2,1,0:T(8,128)(2,1)}), bf16[8,32,3584]{2,1,0:T(8,128)(2,1)S(1)}, u32[]{:S(2)}, u32[]{:S(2)}) async-start(bf16[8,32,3584]{2,1,0:T(8,128)(2,1)} %bitcast.105), calls=%async_computation.4 | async-start | bytes 3670016 | tf_op jit(solution)/shard_map/all_to_all | solution.py:110
  147.1 49.2 %all-to-all-start.3 = ((bf16[8,32,7168]{2,1,0:T(8,128)(2,1)}), bf16[8,32,7168]{2,1,0:T(8,128)(2,1)}, u32[]{:S(2)}, u32[]{:S(2)}) async-start(bf16[8,32,7168]{2,1,0:T(8,128)(2,1)} %bitcast.102), calls=%async_computation.3 | async-start | bytes 7340032 | tf_op jit(solution)/shard_map/all_to_all | solution.py:110
  151.9 44.4 %collective-permute-start.2 = (bf16[128,7168]{1,0:T(8,128)(2,1)}, bf16[128,7168]{1,0:T(8,128)(2,1)}, u32[]{:S(2)}, u32[]{:S(2)}) collective-permute-start(bf16[128,7168]{1,0:T(8,128)(2,1)} %copy-done), channel_id=1, source_target_pairs={{0,8},{8,16},{16,24},{24,0},{1,9},{9,17},{17,25},{25,1},{2,10},{10... | collective-permute-start | bytes 5505032 | tf_op jit(solution)/shard_map/ppermute | solution.py:68
  196.3 27.7 %all-to-all-start.6 = ((bf16[8,32,3584]{2,1,0:T(8,128)(2,1)}), bf16[8,32,3584]{2,1,0:T(8,128)(2,1)S(1)}, u32[]{:S(2)}, u32[]{:S(2)}) async-start(bf16[8,32,3584]{2,1,0:T(8,128)(2,1)} %bitcast.25), calls=%async_computation.6 | async-start | bytes 3670016 | tf_op jit(solution)/shard_map/all_to_all | solution.py:110
  224.0 48.0 %all-to-all-start.5 = ((bf16[8,32,7168]{2,1,0:T(8,128)(2,1)}), bf16[8,32,7168]{2,1,0:T(8,128)(2,1)}, u32[]{:S(2)}, u32[]{:S(2)}) async-start(bf16[8,32,7168]{2,1,0:T(8,128)(2,1)} %bitcast.101), calls=%async_computation.5 | async-start | bytes 7340032 | tf_op jit(solution)/shard_map/all_to_all | solution.py:110
  272.0 27.5 %all-to-all-start.7 = ((bf16[8,32,3584]{2,1,0:T(8,128)(2,1)}), bf16[8,32,3584]{2,1,0:T(8,128)(2,1)S(1)}, u32[]{:S(2)}, u32[]{:S(2)}) async-start(bf16[8,32,3584]{2,1,0:T(8,128)(2,1)} %bitcast.28), calls=%async_computation.7 | async-start | bytes 3670016 | tf_op jit(solution)/shard_map/all_to_all | solution.py:110
  275.6 25.2 %collective-permute-start.3 = (bf16[128,3584]{1,0:T(8,128)(2,1)}, bf16[128,3584]{1,0:T(8,128)(2,1)}, u32[]{:S(2)}, u32[]{:S(2)}) collective-permute-start(bf16[128,3584]{1,0:T(8,128)(2,1)} %convolution_convert_fusion.6), channel_id=1, source_target_pairs={{0,24},{8,0},{16,8},{24,16},{1,25},{9,1},{17,9},{25,17},{2,26},{10... | collective-permute-start | bytes 2752520 | tf_op jit(solution)/shard_map/ppermute | solution.py:68
  300.8 27.7 %all-to-all-start.8 = ((bf16[8,32,3584]{2,1,0:T(8,128)(2,1)}), bf16[8,32,3584]{2,1,0:T(8,128)(2,1)S(1)}, u32[]{:S(2)}, u32[]{:S(2)}) async-start(bf16[8,32,3584]{2,1,0:T(8,128)(2,1)} %bitcast.30), calls=%async_computation.8 | async-start | bytes 3670016 | tf_op jit(solution)/shard_map/all_to_all | solution.py:110
  304.7 43.6 %collective-permute-start.4 = (bf16[128,3584]{1,0:T(8,128)(2,1)}, bf16[128,3584]{1,0:T(8,128)(2,1)}, u32[]{:S(2)}, u32[]{:S(2)}) collective-permute-start(bf16[128,3584]{1,0:T(8,128)(2,1)} %convolution_convert_fusion.5), channel_id=1, source_target_pairs={{0,16},{8,24},{16,0},{24,8},{1,17},{9,25},{17,1},{25,9},{2,18},{10... | collective-permute-start | bytes 2752520 | tf_op jit(solution)/shard_map/ppermute | solution.py:68
  348.3 23.8 %collective-permute-start.5 = (bf16[128,3584]{1,0:T(8,128)(2,1)S(1)}, bf16[128,3584]{1,0:T(8,128)(2,1)S(1)}, u32[]{:S(2)}, u32[]{:S(2)}) collective-permute-start(bf16[128,3584]{1,0:T(8,128)(2,1)S(1)} %convolution_convert_fusion.4), channel_id=1, source_target_pairs={{0,8},{8,16},{16,24},{24,0},{1,9},{9,17},{17,25},{25,1},{2,10},{10... | collective-permute-start | bytes 2752520 | tf_op jit(solution)/shard_map/ppermute | solution.py:68

commit v13 on v9

--- a/solution.py
+++ b/solution.py
@@ -28,7 +28,7 @@
 def part_matmul(grad_pre, weight_in):
     rows, depth = grad_pre.shape
     width = weight_in.shape[0]
-    tile = 512 if width % 512 == 0 else width
+    tile = 896 if width % 896 == 0 else width
     return pl.pallas_call(
         part_kernel,
         grid=(width // tile,),

time: 372 us -> 370 us (level)
  Pallas kernels: 43 us -> 37.8 us
  waiting for transfers between devices: 200 us -> 205 us
    pallas_call x4, Pallas kernels: 43 us -> 37.8 us  [part_matmul(): pl.pallas_call(part_kernel, grid=(width // tile,), in_specs=[pl.BlockSpec...]
  transfers between devices with their start and end apart: 15 -> 15, of which waited for: 10 -> 11; matrix products, arithmetic and copies ran while one was open for 20% -> 20% of each run, Pallas kernels for 12% -> 10%
where the time goes in v13:
time: 370 us; the launch traced here: 369 us
  waiting for transfers between devices  205 us (55%)
  matrix products  69.3 us (19%)
  starting transfers between devices  42.5 us (11%)
  Pallas kernels  37.8 us (10%)
  other arithmetic  8.95 us (2%)
  local copies, waits for them, and re-layouts  5.85 us (2%)
    all_to_all x8, waiting for transfers between devices, spread(): lax.all_to_all(rows.reshape(n_local, capacity, rows.shape[-1]), 'local',...  119 us
    ppermute x6, waiting for transfers between devices, shift(): lax.ppermute(value, 'node', [(i, (i + step) % n_node) for i in range(n_no...  85.1 us
    pallas_call x4, Pallas kernels, part_matmul(): pl.pallas_call(part_kernel, grid=(width // tile,), in_specs=[pl.BlockSpec...  37.8 us
    all_to_all x8, starting transfers between devices, spread(): lax.all_to_all(rows.reshape(n_local, capacity, rows.shape[-1]), 'local',...  33.9 us
    dot_general x4, matrix products, expert_backward(): jnp.dot(rows_x, weight_in[:, FF:], preferred_element_type=jnp.float32)  23.7 us
    dot_general x4, matrix products, expert_backward(): lax.dot_general(rows_dy, weight_out, (((1,), (1,)), ((), ())), preferred_...  23.2 us
    dot_general x4, matrix products, select_rows(): lax.dot_general(onehot, rows, (((0,), (0,)), ((), ())), preferred_element...  16.4 us
  transfers between devices with their start and end apart: 15, of which 11 were waited for; matrix products, arithmetic and copies ran while one was open for 20% of the time, Pallas kernels for 10%

profile of v13, /device:TPU:0, one launch (start us, length us, event | category | flops | bytes accessed | tf_op | source)
XLA Modules:
  0.0 369.2 jit_solution(13124991540653035524)
XLA Ops:
  0.0 0.9 copy.11
  0.9 0.2 reshape.88
  1.1 0.6 fusion.133
  2.0 0.4 fusion.169
  2.5 1.3 constant_dynamic-update-slice_fusion
  3.7 2.9 convolution_convert_fusion.3
  6.7 5.3 %all-to-all-start = ((bf16[8,32,7168]{2,1,0:T(8,128)(2,1)}), bf16[8,32,7168]{2,1,0:T(8,128)(2,1)}, u32[]{:S(2)}, u32[]{:S(2)}) async-start(bf16[8,32,7168]{2,1,0:T(8,128)(2,1)} %bitcast.101), calls=%async_computation | async-start | bytes 7340032 | tf_op jit(solution)/shard_map/all_to_all | solution.py:110
  12.0 2.4 collective-permute-start
  14.4 0.1 copy.13
  14.5 0.1 copy.16
  15.0 0.4 fusion.161
  15.6 0.4 fusion.162
  16.1 0.4 fusion.164
  16.8 0.4 fusion.166
  17.3 0.6 copy.12
  17.9 0.4 fusion.170
  18.3 37.3 %all-to-all-done = bf16[8,32,7168]{2,1,0:T(8,128)(2,1)} async-done(((bf16[8,32,7168]{2,1,0:T(8,128)(2,1)}), bf16[8,32,7168]{2,1,0:T(8,128)(2,1)}, u32[]{:S(2)}, u32[]{:S(2)}) %all-to-all-start) | async-done | bytes 3670048 | tf_op jit(solution)/shard_map/all_to_all | solution.py:110
  55.6 3.3 all-to-all-start.2
  58.9 4.5 %convolution_convert_fusion.2 = bf16[256,7168]{1,0:T(8,128)(2,1)} fusion(bf16[128,256]{1,0:T(8,128)(2,1)S(1)} %fusion.170, bf16[128,7168]{1,0:T(8,128)(2,1)} %collective-permute-done), kind=kOutput, calls=%fused_computation.2 | convolution fusion | flops 471597056 | bytes 5570560 | tf_op jit(solution)/shard_map/dot_general | solution.py:59
  63.4 0.1 all-to-all-done.2
  63.6 4.5 %all-to-all-start.1 = ((bf16[8,32,7168]{2,1,0:T(8,128)(2,1)}), bf16[8,32,7168]{2,1,0:T(8,128)(2,1)}, u32[]{:S(2)}, u32[]{:S(2)}) async-start(bf16[8,32,7168]{2,1,0:T(8,128)(2,1)} %bitcast.103), calls=%async_computation.1 | async-start | bytes 7340032 | tf_op jit(solution)/shard_map/all_to_all | solution.py:110
  68.2 2.3 collective-permute-start.1
  70.5 5.8 %fusion.141 = (bf16[256,1024]{1,0:T(8,128)(2,1)S(1)}, f32[256,1024]{1,0:T(8,128)S(1)}) fusion(bf16[1024,1024]{1,0:T(8,128)(2,1)} %param.11, s32[]{:T(128)S(6)} %select_n.75, f32[256]{0:T(256)S(1)} %reshape.105, bf16[1,1024,3584]{2,1,0:T(8,128)(2,1)} %param.13, bf16[256,7168]{1,0:T(8,128)(2,1)} %bitcast.4), kind=kOutput, calls=%fused_computation.76 | convolution fusion | flops 1881145344 | bytes 11273220 | tf_op jit(solution)/shard_map/dot_general | solution.py:46
  76.3 5.9 %fusion.107 = bf16[256,1024]{1,0:T(8,128)(2,1)S(1)} fusion(f32[256,1024]{1,0:T(8,128)S(1)} %get-tuple-element.54, bf16[3584,2048]{1,0:T(8,128)(2,1)} %bitcast.93, bf16[256,7168]{1,0:T(8,128)(2,1)} %bitcast.4, bf16[1024,1024]{1,0:T(8,128)(2,1)} %param.11, s32[]{:T(128)S(6)} %select_n.75), kind=kOutput, calls=%fused_computation.64 | convolution fusion | flops 1881931776 | bytes 11272196 | tf_op jit(solution)/shard_map/dot_general | solution.py:45
  82.2 1.1 pad_maximum_fusion.grad_ref
  83.3 9.4 %shard_map.73 = bf16[256,3584]{1,0:T(8,128)(2,1)} custom-call(bf16[256,2048]{1,0:T(8,128)(2,1)} %pad_maximum_fusion.grad_ref, bf16[3584,2048]{1,0:T(8,128)(2,1)} %bitcast.94), custom_call_target="tpu_custom_call" | custom-call | tf_op jit(solution)/shard_map/pallas_call | solution.py:32
  92.7 20.5 %collective-permute-done.1 = bf16[128,7168]{1,0:T(8,128)(2,1)S(1)} collective-permute-done((bf16[128,7168]{1,0:T(8,128)(2,1)}, bf16[128,7168]{1,0:T(8,128)(2,1)S(1)}, u32[]{:S(2)}, u32[]{:S(2)}) %collective-permute-start.1) | collective-permute-done | bytes 1835040 | tf_op jit(solution)/shard_map/ppermute | solution.py:68
  113.2 1.2 copy-done
  114.5 3.9 %all-to-all-start.4 = ((bf16[8,32,3584]{2,1,0:T(8,128)(2,1)}), bf16[8,32,3584]{2,1,0:T(8,128)(2,1)S(1)}, u32[]{:S(2)}, u32[]{:S(2)}) async-start(bf16[8,32,3584]{2,1,0:T(8,128)(2,1)} %bitcast.105), calls=%async_computation.4 | async-start | bytes 3670016 | tf_op jit(solution)/shard_map/all_to_all | solution.py:110
  118.4 0.4 fusion.171
  118.8 4.5 %convolution_convert_fusion.1 = bf16[256,7168]{1,0:T(8,128)(2,1)} fusion(bf16[128,256]{1,0:T(8,128)(2,1)S(1)} %fusion.171, bf16[128,7168]{1,0:T(8,128)(2,1)} %copy-done), kind=kOutput, calls=%fused_computation.1 | convolution fusion | flops 471597056 | bytes 5570560 | tf_op jit(solution)/shard_map/dot_general | solution.py:59
  123.3 18.9 %all-to-all-done.4 = bf16[8,32,3584]{2,1,0:T(8,128)(2,1)S(1)} async-done(((bf16[8,32,3584]{2,1,0:T(8,128)(2,1)}), bf16[8,32,3584]{2,1,0:T(8,128)(2,1)S(1)}, u32[]{:S(2)}, u32[]{:S(2)}) %all-to-all-start.4) | async-done | bytes 1835040 | tf_op jit(solution)/shard_map/all_to_all | solution.py:110
  142.2 4.5 %all-to-all-start.3 = ((bf16[8,32,7168]{2,1,0:T(8,128)(2,1)}), bf16[8,32,7168]{2,1,0:T(8,128)(2,1)}, u32[]{:S(2)}, u32[]{:S(2)}) async-start(bf16[8,32,7168]{2,1,0:T(8,128)(2,1)} %bitcast.104), calls=%async_computation.3 | async-start | bytes 7340032 | tf_op jit(solution)/shard_map/all_to_all | solution.py:110
  146.8 5.8 %fusion.147 = (bf16[256,1024]{1,0:T(8,128)(2,1)S(1)}, f32[256,1024]{1,0:T(8,128)S(1)}) fusion(bf16[1024,1024]{1,0:T(8,128)(2,1)} %param.11, s32[]{:T(128)S(6)} %select_n.76, f32[256]{0:T(256)S(1)} %reshape.106, bf16[1,1024,3584]{2,1,0:T(8,128)(2,1)} %param.13, bf16[256,7168]{1,0:T(8,128)(2,1)} %bitcast.20), kind=kOutput, calls=%fused_computation.82 | convolution fusion | flops 1881145344 | bytes 11273220 | tf_op jit(solution)/shard_map/dot_general | solution.py:46
  152.6 5.9 %fusion.112 = bf16[256,1024]{1,0:T(8,128)(2,1)S(1)} fusion(f32[256,1024]{1,0:T(8,128)S(1)} %get-tuple-element.56, bf16[3584,2048]{1,0:T(8,128)(2,1)} %bitcast.95, bf16[256,7168]{1,0:T(8,128)(2,1)} %bitcast.20, bf16[1024,1024]{1,0:T(8,128)(2,1)} %param.11, s32[]{:T(128)S(6)} %select_n.76), kind=kOutput, calls=%fused_computation.65 | convolution fusion | flops 1881931776 | bytes 11272196 | tf_op jit(solution)/shard_map/dot_general | solution.py:45
  158.6 1.1 pad_maximum_fusion.1.grad_ref
  159.6 9.5 %shard_map.74 = bf16[256,3584]{1,0:T(8,128)(2,1)} custom-call(bf16[256,2048]{1,0:T(8,128)(2,1)} %pad_maximum_fusion.1.grad_ref, bf16[3584,2048]{1,0:T(8,128)(2,1)} %bitcast.96), custom_call_target="tpu_custom_call" | custom-call | tf_op jit(solution)/shard_map/pallas_call | solution.py:32
  169.1 0.4 convolution_convert_fusion.7
  169.5 21.7 %collective-permute-done.2 = bf16[128,7168]{1,0:T(8,128)(2,1)} collective-permute-done((bf16[128,7168]{1,0:T(8,128)(2,1)}, bf16[128,7168]{1,0:T(8,128)(2,1)}, u32[]{:S(2)}, u32[]{:S(2)}) %collective-permute-start.2) | collective-permute-done | bytes 1835040 | tf_op jit(solution)/shard_map/ppermute | solution.py:68
  191.2 3.9 %all-to-all-start.6 = ((bf16[8,32,3584]{2,1,0:T(8,128)(2,1)}), bf16[8,32,3584]{2,1,0:T(8,128)(2,1)S(1)}, u32[]{:S(2)}, u32[]{:S(2)}) async-start(bf16[8,32,3584]{2,1,0:T(8,128)(2,1)} %bitcast.25), calls=%async_computation.6 | async-start | bytes 3670016 | tf_op jit(solution)/shard_map/all_to_all | solution.py:110
  195.1 0.4 fusion.168
  195.5 4.4 %convolution_convert_fusion = bf16[256,7168]{1,0:T(8,128)(2,1)} fusion(bf16[128,256]{1,0:T(8,128)(2,1)S(1)} %fusion.168, bf16[128,7168]{1,0:T(8,128)(2,1)} %collective-permute-done.2), kind=kOutput, calls=%fused_computation | convolution fusion | flops 471597056 | bytes 5570560 | tf_op jit(solution)/shard_map/dot_general | solution.py:59
  199.9 19.0 %all-to-all-done.6 = bf16[8,32,3584]{2,1,0:T(8,128)(2,1)S(1)} async-done(((bf16[8,32,3584]{2,1,0:T(8,128)(2,1)}), bf16[8,32,3584]{2,1,0:T(8,128)(2,1)S(1)}, u32[]{:S(2)}, u32[]{:S(2)}) %all-to-all-start.6) | async-done | bytes 1835040 | tf_op jit(solution)/shard_map/all_to_all | solution.py:110
  218.9 4.7 %all-to-all-start.5 = ((bf16[8,32,7168]{2,1,0:T(8,128)(2,1)}), bf16[8,32,7168]{2,1,0:T(8,128)(2,1)}, u32[]{:S(2)}, u32[]{:S(2)}) async-start(bf16[8,32,7168]{2,1,0:T(8,128)(2,1)} %bitcast.102), calls=%async_computation.5 | async-start | bytes 7340032 | tf_op jit(solution)/shard_map/all_to_all | solution.py:110
  223.8 5.8 %fusion.153 = (bf16[256,1024]{1,0:T(8,128)(2,1)S(1)}, f32[256,1024]{1,0:T(8,128)S(1)}) fusion(bf16[1024,1024]{1,0:T(8,128)(2,1)} %param.11, s32[]{:T(128)S(6)} %select_n.77, f32[256]{0:T(256)S(1)} %reshape.107, bf16[1,1024,3584]{2,1,0:T(8,128)(2,1)} %param.13, bf16[256,7168]{1,0:T(8,128)(2,1)} %bitcast.24), kind=kOutput, calls=%fused_computation.88 | convolution fusion | flops 1881145344 | bytes 11273220 | tf_op jit(solution)/shard_map/dot_general | solution.py:46
  229.6 5.9 %fusion.117 = bf16[256,1024]{1,0:T(8,128)(2,1)S(1)} fusion(f32[256,1024]{1,0:T(8,128)S(1)} %get-tuple-element.58, bf16[3584,2048]{1,0:T(8,128)(2,1)} %bitcast.97, bf16[256,7168]{1,0:T(8,128)(2,1)} %bitcast.24, bf16[1024,1024]{1,0:T(8,128)(2,1)} %param.11, s32[]{:T(128)S(6)} %select_n.77), kind=kOutput, calls=%fused_computation.66 | convolution fusion | flops 1881931776 | bytes 11272196 | tf_op jit(solution)/shard_map/dot_general | solution.py:45
  235.6 1.1 pad_maximum_fusion.2.grad_ref
  236.6 9.5 %shard_map.75 = bf16[256,3584]{1,0:T(8,128)(2,1)} custom-call(bf16[256,2048]{1,0:T(8,128)(2,1)} %pad_maximum_fusion.2.grad_ref, bf16[3584,2048]{1,0:T(8,128)(2,1)} %bitcast.98), custom_call_target="tpu_custom_call" | custom-call | tf_op jit(solution)/shard_map/pallas_call | solution.py:32
  246.1 1.4 convolution_convert_fusion.6
  247.5 19.4 %all-to-all-done.5 = bf16[8,32,7168]{2,1,0:T(8,128)(2,1)} async-done(((bf16[8,32,7168]{2,1,0:T(8,128)(2,1)}), bf16[8,32,7168]{2,1,0:T(8,128)(2,1)}, u32[]{:S(2)}, u32[]{:S(2)}) %all-to-all-start.5) | async-done | bytes 3670048 | tf_op jit(solution)/shard_map/all_to_all | solution.py:110
  266.9 3.6 all-to-all-start.7
  270.5 0.5 collective-permute-start.3
  271.0 5.8 %fusion.159 = (bf16[256,1024]{1,0:T(8,128)(2,1)S(1)}, f32[256,1024]{1,0:T(8,128)S(1)}) fusion(bf16[1024,1024]{1,0:T(8,128)(2,1)} %param.11, s32[]{:T(128)S(6)} %select_n.78, f32[256]{0:T(256)S(1)} %reshape.108, bf16[1,1024,3584]{2,1,0:T(8,128)(2,1)} %param.13, bf16[256,7168]{1,0:T(8,128)(2,1)} %bitcast.27), kind=kOutput, calls=%fused_computation.94 | convolution fusion | flops 1881145344 | bytes 11273220 | tf_op jit(solution)/shard_map/dot_general | solution.py:46
  276.8 5.9 %fusion.122 = bf16[256,1024]{1,0:T(8,128)(2,1)S(1)} fusion(f32[256,1024]{1,0:T(8,128)S(1)} %get-tuple-element.60, bf16[3584,2048]{1,0:T(8,128)(2,1)} %bitcast.99, bf16[256,7168]{1,0:T(8,128)(2,1)} %bitcast.27, bf16[1024,1024]{1,0:T(8,128)(2,1)} %param.11, s32[]{:T(128)S(6)} %select_n.78), kind=kOutput, calls=%fused_computation.67 | convolution fusion | flops 1881931776 | bytes 11272196 | tf_op jit(solution)/shard_map/dot_general | solution.py:45
  282.7 1.1 pad_maximum_fusion.3.grad_ref
  283.8 9.4 %shard_map.76 = bf16[256,3584]{1,0:T(8,128)(2,1)} custom-call(bf16[256,2048]{1,0:T(8,128)(2,1)} %pad_maximum_fusion.3.grad_ref, bf16[3584,2048]{1,0:T(8,128)(2,1)} %bitcast.100), custom_call_target="tpu_custom_call" | custom-call | tf_op jit(solution)/shard_map/pallas_call | solution.py:32
  293.2 1.0 all-to-all-done.7
  294.3 1.3 convolution_convert_fusion.5
  295.6 3.6 all-to-all-start.8
  299.3 23.7 %all-to-all-done.8 = bf16[8,32,3584]{2,1,0:T(8,128)(2,1)S(1)} async-done(((bf16[8,32,3584]{2,1,0:T(8,128)(2,1)}), bf16[8,32,3584]{2,1,0:T(8,128)(2,1)S(1)}, u32[]{:S(2)}, u32[]{:S(2)}) %all-to-all-start.8) | async-done | bytes 1835040 | tf_op jit(solution)/shard_map/all_to_all | solution.py:110
  323.0 0.4 convolution_convert_fusion.4
  323.4 19.4 %collective-permute-done.4 = bf16[128,3584]{1,0:T(8,128)(2,1)} collective-permute-done((bf16[128,3584]{1,0:T(8,128)(2,1)}, bf16[128,3584]{1,0:T(8,128)(2,1)}, u32[]{:S(2)}, u32[]{:S(2)}) %collective-permute-start.4) | collective-permute-done | bytes 917536 | tf_op jit(solution)/shard_map/ppermute | solution.py:68
  342.7 23.6 %collective-permute-done.5 = bf16[128,3584]{1,0:T(8,128)(2,1)S(1)} collective-permute-done((bf16[128,3584]{1,0:T(8,128)(2,1)S(1)}, bf16[128,3584]{1,0:T(8,128)(2,1)S(1)}, u32[]{:S(2)}, u32[]{:S(2)}) %collective-permute-start.5) | collective-permute-done | bytes 917536 | tf_op jit(solution)/shard_map/ppermute | solution.py:68
  366.3 2.9 add_convert_fusion
  (37 shorter events, 1.6 us)
Async XLA Ops:
  0.0 2.4 copy-start.1
  6.7 7.7 %copy-start.2 = (s32[4,128,8]{1,2,0:T(8,128)S(1)}, s32[4,128,8]{1,2,0:T(8,128)}, u32[]{:S(2)}) copy-start(s32[4,128,8]{1,2,0:T(8,128)} %param.10) | copy-start | bytes 49156
  6.7 48.9 %all-to-all-start = ((bf16[8,32,7168]{2,1,0:T(8,128)(2,1)}), bf16[8,32,7168]{2,1,0:T(8,128)(2,1)}, u32[]{:S(2)}, u32[]{:S(2)}) async-start(bf16[8,32,7168]{2,1,0:T(8,128)(2,1)} %bitcast.101), calls=%async_computation | async-start | bytes 7340032 | tf_op jit(solution)/shard_map/all_to_all | solution.py:110
  12.0 46.9 %collective-permute-start = (bf16[128,7168]{1,0:T(8,128)(2,1)S(1)}, bf16[128,7168]{1,0:T(8,128)(2,1)}, u32[]{:S(2)}, u32[]{:S(2)}) collective-permute-start(bf16[128,7168]{1,0:T(8,128)(2,1)S(1)} %constant_dynamic-update-slice_fusion), channel_id=1, source_target_pairs={{0,8},{8,16},{16,24},{24,0},{1,9},{9,17},{17,25},{25,1},{2,10},{10... | collective-permute-start | bytes 5505032 | tf_op jit(solution)/shard_map/ppermute | solution.py:68
  55.6 8.0 %all-to-all-start.2 = ((bf16[8,4,32]{2,1,0:T(4,128)(2,1)}), bf16[8,4,32]{2,1,0:T(4,128)(2,1)S(1)}, u32[]{:S(2)}, u32[]{:S(2)}) async-start(bf16[8,4,32]{2,1,0:T(4,128)(2,1)} %copy.12), calls=%async_computation.2 | async-start | bytes 16384 | tf_op jit(solution)/shard_map/all_to_all | solution.py:107
  63.6 49.7 %all-to-all-start.1 = ((bf16[8,32,7168]{2,1,0:T(8,128)(2,1)}), bf16[8,32,7168]{2,1,0:T(8,128)(2,1)}, u32[]{:S(2)}, u32[]{:S(2)}) async-start(bf16[8,32,7168]{2,1,0:T(8,128)(2,1)} %bitcast.103), calls=%async_computation.1 | async-start | bytes 7340032 | tf_op jit(solution)/shard_map/all_to_all | solution.py:110
  68.2 45.0 %collective-permute-start.1 = (bf16[128,7168]{1,0:T(8,128)(2,1)}, bf16[128,7168]{1,0:T(8,128)(2,1)S(1)}, u32[]{:S(2)}, u32[]{:S(2)}) collective-permute-start(bf16[128,7168]{1,0:T(8,128)(2,1)} %collective-permute-done), channel_id=1, source_target_pairs={{0,8},{8,16},{16,24},{24,0},{1,9},{9,17},{17,25},{25,1},{2,10},{10... | collective-permute-start | bytes 5505032 | tf_op jit(solution)/shard_map/ppermute | solution.py:68
  113.2 1.2 copy-start
  114.5 27.7 %all-to-all-start.4 = ((bf16[8,32,3584]{2,1,0:T(8,128)(2,1)}), bf16[8,32,3584]{2,1,0:T(8,128)(2,1)S(1)}, u32[]{:S(2)}, u32[]{:S(2)}) async-start(bf16[8,32,3584]{2,1,0:T(8,128)(2,1)} %bitcast.105), calls=%async_computation.4 | async-start | bytes 3670016 | tf_op jit(solution)/shard_map/all_to_all | solution.py:110
  142.2 49.0 %all-to-all-start.3 = ((bf16[8,32,7168]{2,1,0:T(8,128)(2,1)}), bf16[8,32,7168]{2,1,0:T(8,128)(2,1)}, u32[]{:S(2)}, u32[]{:S(2)}) async-start(bf16[8,32,7168]{2,1,0:T(8,128)(2,1)} %bitcast.104), calls=%async_computation.3 | async-start | bytes 7340032 | tf_op jit(solution)/shard_map/all_to_all | solution.py:110
  146.8 44.4 %collective-permute-start.2 = (bf16[128,7168]{1,0:T(8,128)(2,1)}, bf16[128,7168]{1,0:T(8,128)(2,1)}, u32[]{:S(2)}, u32[]{:S(2)}) collective-permute-start(bf16[128,7168]{1,0:T(8,128)(2,1)} %copy-done), channel_id=1, source_target_pairs={{0,8},{8,16},{16,24},{24,0},{1,9},{9,17},{17,25},{25,1},{2,10},{10... | collective-permute-start | bytes 5505032 | tf_op jit(solution)/shard_map/ppermute | solution.py:68
  191.2 27.7 %all-to-all-start.6 = ((bf16[8,32,3584]{2,1,0:T(8,128)(2,1)}), bf16[8,32,3584]{2,1,0:T(8,128)(2,1)S(1)}, u32[]{:S(2)}, u32[]{:S(2)}) async-start(bf16[8,32,3584]{2,1,0:T(8,128)(2,1)} %bitcast.25), calls=%async_computation.6 | async-start | bytes 3670016 | tf_op jit(solution)/shard_map/all_to_all | solution.py:110
  218.9 48.0 %all-to-all-start.5 = ((bf16[8,32,7168]{2,1,0:T(8,128)(2,1)}), bf16[8,32,7168]{2,1,0:T(8,128)(2,1)}, u32[]{:S(2)}, u32[]{:S(2)}) async-start(bf16[8,32,7168]{2,1,0:T(8,128)(2,1)} %bitcast.102), calls=%async_computation.5 | async-start | bytes 7340032 | tf_op jit(solution)/shard_map/all_to_all | solution.py:110
  266.9 27.4 %all-to-all-start.7 = ((bf16[8,32,3584]{2,1,0:T(8,128)(2,1)}), bf16[8,32,3584]{2,1,0:T(8,128)(2,1)S(1)}, u32[]{:S(2)}, u32[]{:S(2)}) async-start(bf16[8,32,3584]{2,1,0:T(8,128)(2,1)} %bitcast.28), calls=%async_computation.7 | async-start | bytes 3670016 | tf_op jit(solution)/shard_map/all_to_all | solution.py:110
  270.5 25.1 %collective-permute-start.3 = (bf16[128,3584]{1,0:T(8,128)(2,1)}, bf16[128,3584]{1,0:T(8,128)(2,1)}, u32[]{:S(2)}, u32[]{:S(2)}) collective-permute-start(bf16[128,3584]{1,0:T(8,128)(2,1)} %convolution_convert_fusion.6), channel_id=1, source_target_pairs={{0,24},{8,0},{16,8},{24,16},{1,25},{9,1},{17,9},{25,17},{2,26},{10... | collective-permute-start | bytes 2752520 | tf_op jit(solution)/shard_map/ppermute | solution.py:68
  295.6 27.4 %all-to-all-start.8 = ((bf16[8,32,3584]{2,1,0:T(8,128)(2,1)}), bf16[8,32,3584]{2,1,0:T(8,128)(2,1)S(1)}, u32[]{:S(2)}, u32[]{:S(2)}) async-start(bf16[8,32,3584]{2,1,0:T(8,128)(2,1)} %bitcast.30), calls=%async_computation.8 | async-start | bytes 3670016 | tf_op jit(solution)/shard_map/all_to_all | solution.py:110
  299.2 43.5 %collective-permute-start.4 = (bf16[128,3584]{1,0:T(8,128)(2,1)}, bf16[128,3584]{1,0:T(8,128)(2,1)}, u32[]{:S(2)}, u32[]{:S(2)}) collective-permute-start(bf16[128,3584]{1,0:T(8,128)(2,1)} %convolution_convert_fusion.5), channel_id=1, source_target_pairs={{0,16},{8,24},{16,0},{24,8},{1,17},{9,25},{17,1},{25,9},{2,18},{10... | collective-permute-start | bytes 2752520 | tf_op jit(solution)/shard_map/ppermute | solution.py:68
  342.7 23.6 %collective-permute-start.5 = (bf16[128,3584]{1,0:T(8,128)(2,1)S(1)}, bf16[128,3584]{1,0:T(8,128)(2,1)S(1)}, u32[]{:S(2)}, u32[]{:S(2)}) collective-permute-start(bf16[128,3584]{1,0:T(8,128)(2,1)S(1)} %convolution_convert_fusion.4), channel_id=1, source_target_pairs={{0,8},{8,16},{16,24},{24,0},{1,9},{9,17},{17,25},{25,1},{2,10},{10... | collective-permute-start | bytes 2752520 | tf_op jit(solution)/shard_map/ppermute | solution.py:68

commit v14 on v13

--- a/solution.py
+++ b/solution.py
@@ -18,41 +18,75 @@
     return jnp.sum(before * onehot.astype(jnp.float32), axis=-1).astype(jnp.int32)
 
 
-def part_kernel(grad_ref, weight_ref, out_ref):
-    out_ref[...] = lax.dot_general(
-        grad_ref[...], weight_ref[...], (((1,), (1,)), ((), ())),
+def grad_kernel(x_ref, dy_ref, gate_ref, saved_ref, up_ref, out_w_ref, gate_out_ref, up_out_ref):
+    up_pre = jnp.dot(x_ref[...], up_ref[...], preferred_element_type=jnp.float32)
+    grad_hidden = lax.dot_general(
+        dy_ref[...], out_w_ref[...], (((1,), (1,)), ((), ())),
         preferred_element_type=jnp.float32,
-    ).astype(out_ref.dtype)
-
-
-def part_matmul(grad_pre, weight_in):
-    rows, depth = grad_pre.shape
+    ) * gate_ref[...].astype(jnp.float32)
+    gate_pre = saved_ref[...].astype(jnp.float32)
+    sigmoid_gate = 1.0 / (1.0 + jnp.exp(-gate_pre))
+    gate_out_ref[...] = (
+        grad_hidden * up_pre * sigmoid_gate * (1.0 + gate_pre * (1.0 - sigmoid_gate))
+    ).astype(gate_out_ref.dtype)
+    up_out_ref[...] = (grad_hidden * gate_pre * sigmoid_gate).astype(up_out_ref.dtype)
+
+
+def grad_pre_halves(rows_x, rows_dy, rows_gate, saved, weight_in, weight_out):
+    rows, width = rows_x.shape
+    hidden = weight_out.shape[0]
+    tile = 256 if hidden % 256 == 0 else hidden
+    steps = hidden // tile
+    return pl.pallas_call(
+        grad_kernel,
+        grid=(steps,),
+        in_specs=[
+            pl.BlockSpec((rows, width), lambda j: (0, 0)),
+            pl.BlockSpec((rows, width), lambda j: (0, 0)),
+            pl.BlockSpec((rows, 1), lambda j: (0, 0)),
+            pl.BlockSpec((rows, tile), lambda j: (0, j)),
+            pl.BlockSpec((width, tile), lambda j: (0, steps + j)),
+            pl.BlockSpec((tile, width), lambda j: (j, 0)),
+        ],
+        out_specs=[
+            pl.BlockSpec((rows, tile), lambda j: (0, j)),
+            pl.BlockSpec((rows, tile), lambda j: (0, j)),
+        ],
+        out_shape=[jax.ShapeDtypeStruct((rows, hidden), jnp.bfloat16)] * 2,
+    )(rows_x, rows_dy, rows_gate.reshape(rows, 1), saved, weight_in, weight_out)
+
+
+def part_kernel(gate_ref, up_ref, weight_ref, out_ref):
+    hidden = gate_ref.shape[1]
+    contract = (((1,), (1,)), ((), ()))
+    total = lax.dot_general(
+        gate_ref[...], weight_ref[:, :hidden], contract, preferred_element_type=jnp.float32
+    ) + lax.dot_general(
+        up_ref[...], weight_ref[:, hidden:], contract, preferred_element_type=jnp.float32
+    )
+    out_ref[...] = total.astype(out_ref.dtype)
+
+
+def part_matmul(grad_gate, grad_up, weight_in):
+    rows, hidden = grad_gate.shape
     width = weight_in.shape[0]
     tile = 896 if width % 896 == 0 else width
     return pl.pallas_call(
         part_kernel,
         grid=(width // tile,),
         in_specs=[
-            pl.BlockSpec((rows, depth), lambda j: (0, 0)),
-            pl.BlockSpec((tile, depth), lambda j: (j, 0)),
+            pl.BlockSpec((rows, hidden), lambda j: (0, 0)),
+            pl.BlockSpec((rows, hidden), lambda j: (0, 0)),
+            pl.BlockSpec((tile, 2 * hidden), lambda j: (j, 0)),
         ],
         out_specs=pl.BlockSpec((rows, tile), lambda j: (0, j)),
         out_shape=jax.ShapeDtypeStruct((rows, width), jnp.bfloat16),
-    )(grad_pre, weight_in)
+    )(grad_gate, grad_up, weight_in)
 
 
 def expert_backward(rows_x, rows_dy, rows_gate, saved, weight_in, weight_out):
-    up_pre = jnp.dot(rows_x, weight_in[:, FF:], preferred_element_type=jnp.float32)
-    grad_hidden = lax.dot_general(
-        rows_dy, weight_out, (((1,), (1,)), ((), ())), preferred_element_type=jnp.float32
-    )
-    grad_hidden = grad_hidden * rows_gate.astype(jnp.float32)[:, None]
-    gate_pre = saved.astype(jnp.float32)
-    sigmoid_gate = jax.nn.sigmoid(gate_pre)
-    grad_gate = grad_hidden * up_pre * sigmoid_gate * (1.0 + gate_pre * (1.0 - sigmoid_gate))
-    grad_up = grad_hidden * gate_pre * sigmoid_gate
-    grad_pre = jnp.concatenate([grad_gate, grad_up], axis=1).astype(jnp.bfloat16)
-    return part_matmul(grad_pre, weight_in)
+    grad_gate, grad_up = grad_pre_halves(rows_x, rows_dy, rows_gate, saved, weight_in, weight_out)
+    return part_matmul(grad_gate, grad_up, weight_in)
 
 
 def select_rows(onehot, rows):

time: 370 us -> 372 us (level)
  matrix products: 69.3 us -> 22.4 us
  Pallas kernels: 37.8 us -> 79.8 us
  local copies, waits for them, and re-layouts: 5.85 us -> 25.4 us
  waiting for transfers between devices: 205 us -> 195 us
  other arithmetic: 8.95 us -> 4.59 us
    dot_general x8 -> x0, matrix products: 47 us -> none  [the longest x4 23.7 us: expert_backward(): jnp.dot(rows_x, weight_in[:, FF:], preferred_element_type=jnp.float32)]
    pallas_call x0 -> x4, Pallas kernels: none -> 42.1 us  [grad_pre_halves(): pl.pallas_call(grad_kernel, grid=(steps,), in_specs=[pl.BlockSpec((rows,...]
    slice x0 -> x5, local copies, waits for them, and re-layouts: none -> 16.6 us  [the longest x4 16.5 us: compute(): rows[:, model_width:]]
    ppermute x6, waiting for transfers between devices: 85.1 us -> 78.4 us  [shift(): lax.ppermute(value, 'node', [(i, (i + step) % n_node) for i in range(n_no...]
    concatenate x4 -> x0, other arithmetic: 4.31 us -> none  [expert_backward(): jnp.concatenate([grad_gate, grad_up], axis=1).astype(jnp.bfloat16)]
  transfers between devices with their start and end apart: 15 -> 15, of which waited for: 11 -> 10; matrix products, arithmetic and copies ran while one was open for 20% -> 12% of each run, Pallas kernels for 10% -> 22%
where the time goes in v14:
time: 372 us; the launch traced here: 371 us
  waiting for transfers between devices  195 us (52%)
  Pallas kernels  79.8 us (21%)
  starting transfers between devices  44 us (12%)
  local copies, waits for them, and re-layouts  25.4 us (7%)
  matrix products  22.4 us (6%)
  other arithmetic  4.59 us (1%)
    all_to_all x8, waiting for transfers between devices, spread(): lax.all_to_all(rows.reshape(n_local, capacity, rows.shape[-1]), 'local',...  116 us
    ppermute x6, waiting for transfers between devices, shift(): lax.ppermute(value, 'node', [(i, (i + step) % n_node) for i in range(n_no...  78.4 us
    pallas_call x4, Pallas kernels, grad_pre_halves(): pl.pallas_call(grad_kernel, grid=(steps,), in_specs=[pl.BlockSpec((rows,...  42.1 us
    pallas_call x4, Pallas kernels, part_matmul(): pl.pallas_call(part_kernel, grid=(width // tile,), in_specs=[pl.BlockSpec...  37.7 us
    all_to_all x8, starting transfers between devices, spread(): lax.all_to_all(rows.reshape(n_local, capacity, rows.shape[-1]), 'local',...  34.4 us
    slice x4, local copies, waits for them, and re-layouts, compute(): rows[:, model_width:]  16.5 us
    dot_general x4, matrix products, select_rows(): lax.dot_general(onehot, rows, (((0,), (0,)), ((), ())), preferred_element...  16.5 us
  transfers between devices with their start and end apart: 15, of which 10 were waited for; matrix products, arithmetic and copies ran while one was open for 12% of the time, Pallas kernels for 22%

profile of v14, /device:TPU:0, one launch (start us, length us, event | category | flops | bytes accessed | tf_op | source)
XLA Modules:
  0.0 371.0 jit_solution(5842497700347336356)
XLA Ops:
  0.0 0.9 copy.24
  0.9 0.2 reshape.60
  1.1 0.6 fusion.9
  2.0 0.4 fusion.21
  2.5 1.3 constant_dynamic-update-slice_fusion
  3.7 2.9 convolution_convert_fusion.3
  6.7 5.3 %all-to-all-start = ((bf16[8,32,7168]{2,1,0:T(8,128)(2,1)}), bf16[8,32,7168]{2,1,0:T(8,128)(2,1)}, u32[]{:S(2)}, u32[]{:S(2)}) async-start(bf16[8,32,7168]{2,1,0:T(8,128)(2,1)} %bitcast.82), calls=%async_computation | async-start | bytes 7340032 | tf_op jit(solution)/shard_map/all_to_all | solution.py:144
  12.0 2.4 collective-permute-start
  14.4 0.1 copy.30
  14.7 0.1 copy.32
  15.0 0.4 fusion.13
  15.6 0.4 fusion.14
  16.2 0.4 fusion.16
  16.8 0.4 fusion.18
  17.3 0.6 copy.25
  17.9 0.4 fusion.22
  18.3 37.3 %all-to-all-done = bf16[8,32,7168]{2,1,0:T(8,128)(2,1)} async-done(((bf16[8,32,7168]{2,1,0:T(8,128)(2,1)}), bf16[8,32,7168]{2,1,0:T(8,128)(2,1)}, u32[]{:S(2)}, u32[]{:S(2)}) %all-to-all-start) | async-done | bytes 3670048 | tf_op jit(solution)/shard_map/all_to_all | solution.py:144
  55.6 3.3 all-to-all-start.2
  58.9 4.5 %convolution_convert_fusion.2 = bf16[256,7168]{1,0:T(8,128)(2,1)} fusion(bf16[128,256]{1,0:T(8,128)(2,1)S(1)} %fusion.22, bf16[128,7168]{1,0:T(8,128)(2,1)} %collective-permute-done), kind=kOutput, calls=%fused_computation.2 | convolution fusion | flops 471597056 | bytes 5570560 | tf_op jit(solution)/shard_map/dot_general | solution.py:93
  63.4 0.2 all-to-all-done.2
  63.6 4.6 %all-to-all-start.1 = ((bf16[8,32,7168]{2,1,0:T(8,128)(2,1)}), bf16[8,32,7168]{2,1,0:T(8,128)(2,1)}, u32[]{:S(2)}, u32[]{:S(2)}) async-start(bf16[8,32,7168]{2,1,0:T(8,128)(2,1)} %bitcast.81), calls=%async_computation.1 | async-start | bytes 7340032 | tf_op jit(solution)/shard_map/all_to_all | solution.py:144
  68.2 2.3 collective-permute-start.1
  70.5 1.4 constant_dynamic-slice_fusion
  71.9 0.8 reshape_reshape_squeeze.16.gate_ref
  72.7 4.1 %fusion.43 = (bf16[256,3584]{1,0:T(8,128)(2,1)}, bf16[256,3584]{1,0:T(8,128)(2,1)}) fusion(bf16[256,7168]{1,0:T(8,128)(2,1)} %bitcast.4), kind=kLoop, calls=%fused_computation.77 | loop fusion | bytes 7340032 | tf_op jit(solution)/shard_map/slice | solution.py:159
  76.8 10.5 %shard_map.73 = (bf16[256,1024]{1,0:T(8,128)(2,1)}, bf16[256,1024]{1,0:T(8,128)(2,1)}) custom-call(bf16[256,3584]{1,0:T(8,128)(2,1)} %get-tuple-element.72.x_ref, bf16[256,3584]{1,0:T(8,128)(2,1)} %get-tuple-element.71.dy_ref, bf16[256,1]{1,0:T(8,128)(2,1)} %reshape_reshape_squeeze.16.gate_ref, bf16[256,1024]{1,0:T(8,128)(2,1)} %get-tuple-element.75.saved_ref, ...), custom_call_target="tpu_custom_call" | custom-call | tf_op jit(solution)/shard_map/pallas_call | solution.py:40
  87.3 9.4 %shard_map.74 = bf16[256,3584]{1,0:T(8,128)(2,1)} custom-call(bf16[256,1024]{1,0:T(8,128)(2,1)} %get-tuple-element.33.gate_ref, bf16[256,1024]{1,0:T(8,128)(2,1)} %get-tuple-element.34.up_ref, bf16[3584,2048]{1,0:T(8,128)(2,1)} %bitcast.70), custom_call_target="tpu_custom_call" | custom-call | tf_op jit(solution)/shard_map/pallas_call | solution.py:74
  96.8 16.6 %collective-permute-done.1 = bf16[128,7168]{1,0:T(8,128)(2,1)} collective-permute-done((bf16[128,7168]{1,0:T(8,128)(2,1)}, bf16[128,7168]{1,0:T(8,128)(2,1)}, u32[]{:S(2)}, u32[]{:S(2)}) %collective-permute-start.1) | collective-permute-done | bytes 1835040 | tf_op jit(solution)/shard_map/ppermute | solution.py:102
  113.3 3.9 %all-to-all-start.4 = ((bf16[8,32,3584]{2,1,0:T(8,128)(2,1)}), bf16[8,32,3584]{2,1,0:T(8,128)(2,1)S(1)}, u32[]{:S(2)}, u32[]{:S(2)}) async-start(bf16[8,32,3584]{2,1,0:T(8,128)(2,1)} %bitcast.85), calls=%async_computation.4 | async-start | bytes 3670016 | tf_op jit(solution)/shard_map/all_to_all | solution.py:144
  117.2 0.4 fusion.23
  117.6 4.5 %convolution_convert_fusion.1 = bf16[256,7168]{1,0:T(8,128)(2,1)} fusion(bf16[128,256]{1,0:T(8,128)(2,1)S(1)} %fusion.23, bf16[128,7168]{1,0:T(8,128)(2,1)} %collective-permute-done.1), kind=kOutput, calls=%fused_computation.1 | convolution fusion | flops 471597056 | bytes 5570560 | tf_op jit(solution)/shard_map/dot_general | solution.py:93
  122.2 18.9 %all-to-all-done.4 = bf16[8,32,3584]{2,1,0:T(8,128)(2,1)S(1)} async-done(((bf16[8,32,3584]{2,1,0:T(8,128)(2,1)}), bf16[8,32,3584]{2,1,0:T(8,128)(2,1)S(1)}, u32[]{:S(2)}, u32[]{:S(2)}) %all-to-all-start.4) | async-done | bytes 1835040 | tf_op jit(solution)/shard_map/all_to_all | solution.py:144
  141.1 4.5 %all-to-all-start.3 = ((bf16[8,32,7168]{2,1,0:T(8,128)(2,1)}), bf16[8,32,7168]{2,1,0:T(8,128)(2,1)}, u32[]{:S(2)}, u32[]{:S(2)}) async-start(bf16[8,32,7168]{2,1,0:T(8,128)(2,1)} %bitcast.83), calls=%async_computation.3 | async-start | bytes 7340032 | tf_op jit(solution)/shard_map/all_to_all | solution.py:144
  145.6 0.5 collective-permute-start.2
  146.1 0.8 reshape_reshape_squeeze.17.gate_ref
  146.9 4.1 %fusion.42 = (bf16[256,3584]{1,0:T(8,128)(2,1)}, bf16[256,3584]{1,0:T(8,128)(2,1)}) fusion(bf16[256,7168]{1,0:T(8,128)(2,1)} %bitcast.20), kind=kLoop, calls=%fused_computation.76 | loop fusion | bytes 7340032 | tf_op jit(solution)/shard_map/slice | solution.py:159
  150.9 10.5 %shard_map.75 = (bf16[256,1024]{1,0:T(8,128)(2,1)}, bf16[256,1024]{1,0:T(8,128)(2,1)}) custom-call(bf16[256,3584]{1,0:T(8,128)(2,1)} %get-tuple-element.70.x_ref, bf16[256,3584]{1,0:T(8,128)(2,1)} %get-tuple-element.69.dy_ref, bf16[256,1]{1,0:T(8,128)(2,1)} %reshape_reshape_squeeze.17.gate_ref, bf16[256,1024]{1,0:T(8,128)(2,1)} %get-tuple-element.74.saved_ref, ...), custom_call_target="tpu_custom_call" | custom-call | tf_op jit(solution)/shard_map/pallas_call | solution.py:40
  161.5 9.4 %shard_map.76 = bf16[256,3584]{1,0:T(8,128)(2,1)} custom-call(bf16[256,1024]{1,0:T(8,128)(2,1)} %get-tuple-element.37.gate_ref, bf16[256,1024]{1,0:T(8,128)(2,1)} %get-tuple-element.38.up_ref, bf16[3584,2048]{1,0:T(8,128)(2,1)} %bitcast.72), custom_call_target="tpu_custom_call" | custom-call | tf_op jit(solution)/shard_map/pallas_call | solution.py:74
  170.9 0.4 convolution_convert_fusion.7
  171.3 18.7 %collective-permute-done.2 = bf16[128,7168]{1,0:T(8,128)(2,1)} collective-permute-done((bf16[128,7168]{1,0:T(8,128)(2,1)}, bf16[128,7168]{1,0:T(8,128)(2,1)}, u32[]{:S(2)}, u32[]{:S(2)}) %collective-permute-start.2) | collective-permute-done | bytes 1835040 | tf_op jit(solution)/shard_map/ppermute | solution.py:102
  190.0 3.9 %all-to-all-start.6 = ((bf16[8,32,3584]{2,1,0:T(8,128)(2,1)}), bf16[8,32,3584]{2,1,0:T(8,128)(2,1)S(1)}, u32[]{:S(2)}, u32[]{:S(2)}) async-start(bf16[8,32,3584]{2,1,0:T(8,128)(2,1)} %bitcast.25), calls=%async_computation.6 | async-start | bytes 3670016 | tf_op jit(solution)/shard_map/all_to_all | solution.py:144
  193.9 0.4 fusion.20
  194.3 4.5 %convolution_convert_fusion = bf16[256,7168]{1,0:T(8,128)(2,1)} fusion(bf16[128,256]{1,0:T(8,128)(2,1)S(1)} %fusion.20, bf16[128,7168]{1,0:T(8,128)(2,1)} %collective-permute-done.2), kind=kOutput, calls=%fused_computation | convolution fusion | flops 471597056 | bytes 5570560 | tf_op jit(solution)/shard_map/dot_general | solution.py:93
  198.8 18.9 %all-to-all-done.6 = bf16[8,32,3584]{2,1,0:T(8,128)(2,1)S(1)} async-done(((bf16[8,32,3584]{2,1,0:T(8,128)(2,1)}), bf16[8,32,3584]{2,1,0:T(8,128)(2,1)S(1)}, u32[]{:S(2)}, u32[]{:S(2)}) %all-to-all-start.6) | async-done | bytes 1835040 | tf_op jit(solution)/shard_map/all_to_all | solution.py:144
  217.7 4.5 %all-to-all-start.5 = ((bf16[8,32,7168]{2,1,0:T(8,128)(2,1)}), bf16[8,32,7168]{2,1,0:T(8,128)(2,1)}, u32[]{:S(2)}, u32[]{:S(2)}) async-start(bf16[8,32,7168]{2,1,0:T(8,128)(2,1)} %bitcast.84), calls=%async_computation.5 | async-start | bytes 7340032 | tf_op jit(solution)/shard_map/all_to_all | solution.py:144
  222.2 0.8 reshape_reshape_squeeze.18.gate_ref
  223.0 4.2 %fusion.41 = (bf16[256,3584]{1,0:T(8,128)(2,1)}, bf16[256,3584]{1,0:T(8,128)(2,1)}) fusion(bf16[256,7168]{1,0:T(8,128)(2,1)} %bitcast.24), kind=kLoop, calls=%fused_computation.75 | loop fusion | bytes 7340032 | tf_op jit(solution)/shard_map/slice | solution.py:159
  227.2 10.5 %shard_map.77 = (bf16[256,1024]{1,0:T(8,128)(2,1)}, bf16[256,1024]{1,0:T(8,128)(2,1)}) custom-call(bf16[256,3584]{1,0:T(8,128)(2,1)} %get-tuple-element.68.x_ref, bf16[256,3584]{1,0:T(8,128)(2,1)} %get-tuple-element.67.dy_ref, bf16[256,1]{1,0:T(8,128)(2,1)} %reshape_reshape_squeeze.18.gate_ref, bf16[256,1024]{1,0:T(8,128)(2,1)} %get-tuple-element.76.saved_ref, ...), custom_call_target="tpu_custom_call" | custom-call | tf_op jit(solution)/shard_map/pallas_call | solution.py:40
  237.7 9.4 %shard_map.78 = bf16[256,3584]{1,0:T(8,128)(2,1)} custom-call(bf16[256,1024]{1,0:T(8,128)(2,1)} %get-tuple-element.42.gate_ref, bf16[256,1024]{1,0:T(8,128)(2,1)} %get-tuple-element.43.up_ref, bf16[3584,2048]{1,0:T(8,128)(2,1)} %bitcast.74), custom_call_target="tpu_custom_call" | custom-call | tf_op jit(solution)/shard_map/pallas_call | solution.py:74
  247.1 1.4 convolution_convert_fusion.6
  248.5 17.3 %all-to-all-done.5 = bf16[8,32,7168]{2,1,0:T(8,128)(2,1)} async-done(((bf16[8,32,7168]{2,1,0:T(8,128)(2,1)}), bf16[8,32,7168]{2,1,0:T(8,128)(2,1)}, u32[]{:S(2)}, u32[]{:S(2)}) %all-to-all-start.5) | async-done | bytes 3670048 | tf_op jit(solution)/shard_map/all_to_all | solution.py:144
  265.7 3.6 all-to-all-start.7
  269.3 0.8 reshape_reshape_squeeze.19.gate_ref
  270.1 1.0 collective-permute-start.3
  271.1 4.2 %fusion.40 = (bf16[256,3584]{1,0:T(8,128)(2,1)}, bf16[256,3584]{1,0:T(8,128)(2,1)}) fusion(bf16[256,7168]{1,0:T(8,128)(2,1)} %bitcast.27), kind=kLoop, calls=%fused_computation.74 | loop fusion | bytes 7340032 | tf_op jit(solution)/shard_map/slice | solution.py:159
  275.3 10.5 %shard_map.79 = (bf16[256,1024]{1,0:T(8,128)(2,1)}, bf16[256,1024]{1,0:T(8,128)(2,1)}) custom-call(bf16[256,3584]{1,0:T(8,128)(2,1)} %get-tuple-element.66.x_ref, bf16[256,3584]{1,0:T(8,128)(2,1)} %get-tuple-element.65.dy_ref, bf16[256,1]{1,0:T(8,128)(2,1)} %reshape_reshape_squeeze.19.gate_ref, bf16[256,1024]{1,0:T(8,128)(2,1)} %get-tuple-element.73.saved_ref, ...), custom_call_target="tpu_custom_call" | custom-call | tf_op jit(solution)/shard_map/pallas_call | solution.py:40
  285.8 9.4 %shard_map.80 = bf16[256,3584]{1,0:T(8,128)(2,1)} custom-call(bf16[256,1024]{1,0:T(8,128)(2,1)} %get-tuple-element.48.gate_ref, bf16[256,1024]{1,0:T(8,128)(2,1)} %get-tuple-element.49.up_ref, bf16[3584,2048]{1,0:T(8,128)(2,1)} %bitcast.76), custom_call_target="tpu_custom_call" | custom-call | tf_op jit(solution)/shard_map/pallas_call | solution.py:74
  295.2 1.3 convolution_convert_fusion.5
  296.6 4.1 %all-to-all-start.8 = ((bf16[8,32,3584]{2,1,0:T(8,128)(2,1)}), bf16[8,32,3584]{2,1,0:T(8,128)(2,1)S(1)}, u32[]{:S(2)}, u32[]{:S(2)}) async-start(bf16[8,32,3584]{2,1,0:T(8,128)(2,1)} %bitcast.30), calls=%async_computation.8 | async-start | bytes 3670016 | tf_op jit(solution)/shard_map/all_to_all | solution.py:144
  300.7 23.8 %all-to-all-done.8 = bf16[8,32,3584]{2,1,0:T(8,128)(2,1)S(1)} async-done(((bf16[8,32,3584]{2,1,0:T(8,128)(2,1)}), bf16[8,32,3584]{2,1,0:T(8,128)(2,1)S(1)}, u32[]{:S(2)}, u32[]{:S(2)}) %all-to-all-start.8) | async-done | bytes 1835040 | tf_op jit(solution)/shard_map/all_to_all | solution.py:144
  324.5 0.4 convolution_convert_fusion.4
  325.0 19.4 %collective-permute-done.4 = bf16[128,3584]{1,0:T(8,128)(2,1)} collective-permute-done((bf16[128,3584]{1,0:T(8,128)(2,1)}, bf16[128,3584]{1,0:T(8,128)(2,1)}, u32[]{:S(2)}, u32[]{:S(2)}) %collective-permute-start.4) | collective-permute-done | bytes 917536 | tf_op jit(solution)/shard_map/ppermute | solution.py:102
  344.4 23.8 %collective-permute-done.5 = bf16[128,3584]{1,0:T(8,128)(2,1)S(1)} collective-permute-done((bf16[128,3584]{1,0:T(8,128)(2,1)S(1)}, bf16[128,3584]{1,0:T(8,128)(2,1)S(1)}, u32[]{:S(2)}, u32[]{:S(2)}) %collective-permute-start.5) | collective-permute-done | bytes 917536 | tf_op jit(solution)/shard_map/ppermute | solution.py:102
  368.1 2.9 add_convert_fusion
  (34 shorter events, 1.3 us)
Async XLA Ops:
  0.0 2.4 copy-start.1
  6.7 7.7 %copy-start.2 = (s32[4,128,8]{1,2,0:T(8,128)S(1)}, s32[4,128,8]{1,2,0:T(8,128)}, u32[]{:S(2)}) copy-start(s32[4,128,8]{1,2,0:T(8,128)} %param.10) | copy-start | bytes 49156
  6.7 48.9 %all-to-all-start = ((bf16[8,32,7168]{2,1,0:T(8,128)(2,1)}), bf16[8,32,7168]{2,1,0:T(8,128)(2,1)}, u32[]{:S(2)}, u32[]{:S(2)}) async-start(bf16[8,32,7168]{2,1,0:T(8,128)(2,1)} %bitcast.82), calls=%async_computation | async-start | bytes 7340032 | tf_op jit(solution)/shard_map/all_to_all | solution.py:144
  12.0 46.9 %collective-permute-start = (bf16[128,7168]{1,0:T(8,128)(2,1)S(1)}, bf16[128,7168]{1,0:T(8,128)(2,1)}, u32[]{:S(2)}, u32[]{:S(2)}) collective-permute-start(bf16[128,7168]{1,0:T(8,128)(2,1)S(1)} %constant_dynamic-update-slice_fusion), channel_id=1, source_target_pairs={{0,8},{8,16},{16,24},{24,0},{1,9},{9,17},{17,25},{25,1},{2,10},{10... | collective-permute-start | bytes 5505032 | tf_op jit(solution)/shard_map/ppermute | solution.py:102
  55.6 8.0 %all-to-all-start.2 = ((bf16[8,4,32]{2,1,0:T(4,128)(2,1)}), bf16[8,4,32]{2,1,0:T(4,128)(2,1)S(1)}, u32[]{:S(2)}, u32[]{:S(2)}) async-start(bf16[8,4,32]{2,1,0:T(4,128)(2,1)} %copy.25), calls=%async_computation.2 | async-start | bytes 16384 | tf_op jit(solution)/shard_map/all_to_all | solution.py:141
  63.6 6.9 %copy-start = (bf16[1024,1024]{1,0:T(8,128)(2,1)S(1)}, bf16[1024,1024]{1,0:T(8,128)(2,1)}, u32[]{:S(2)}) copy-start(bf16[1024,1024]{1,0:T(8,128)(2,1)} %param.11) | copy-start | bytes 6291460
  63.6 49.8 %all-to-all-start.1 = ((bf16[8,32,7168]{2,1,0:T(8,128)(2,1)}), bf16[8,32,7168]{2,1,0:T(8,128)(2,1)}, u32[]{:S(2)}, u32[]{:S(2)}) async-start(bf16[8,32,7168]{2,1,0:T(8,128)(2,1)} %bitcast.81), calls=%async_computation.1 | async-start | bytes 7340032 | tf_op jit(solution)/shard_map/all_to_all | solution.py:144
  68.2 45.1 %collective-permute-start.1 = (bf16[128,7168]{1,0:T(8,128)(2,1)}, bf16[128,7168]{1,0:T(8,128)(2,1)}, u32[]{:S(2)}, u32[]{:S(2)}) collective-permute-start(bf16[128,7168]{1,0:T(8,128)(2,1)} %collective-permute-done), channel_id=1, source_target_pairs={{0,8},{8,16},{16,24},{24,0},{1,9},{9,17},{17,25},{25,1},{2,10},{10... | collective-permute-start | bytes 5505032 | tf_op jit(solution)/shard_map/ppermute | solution.py:102
  113.3 27.7 %all-to-all-start.4 = ((bf16[8,32,3584]{2,1,0:T(8,128)(2,1)}), bf16[8,32,3584]{2,1,0:T(8,128)(2,1)S(1)}, u32[]{:S(2)}, u32[]{:S(2)}) async-start(bf16[8,32,3584]{2,1,0:T(8,128)(2,1)} %bitcast.85), calls=%async_computation.4 | async-start | bytes 3670016 | tf_op jit(solution)/shard_map/all_to_all | solution.py:144
  141.1 48.9 %all-to-all-start.3 = ((bf16[8,32,7168]{2,1,0:T(8,128)(2,1)}), bf16[8,32,7168]{2,1,0:T(8,128)(2,1)}, u32[]{:S(2)}, u32[]{:S(2)}) async-start(bf16[8,32,7168]{2,1,0:T(8,128)(2,1)} %bitcast.83), calls=%async_computation.3 | async-start | bytes 7340032 | tf_op jit(solution)/shard_map/all_to_all | solution.py:144
  145.6 44.4 %collective-permute-start.2 = (bf16[128,7168]{1,0:T(8,128)(2,1)}, bf16[128,7168]{1,0:T(8,128)(2,1)}, u32[]{:S(2)}, u32[]{:S(2)}) collective-permute-start(bf16[128,7168]{1,0:T(8,128)(2,1)} %collective-permute-done.1), channel_id=1, source_target_pairs={{0,8},{8,16},{16,24},{24,0},{1,9},{9,17},{17,25},{25,1},{2,10},{10... | collective-permute-start | bytes 5505032 | tf_op jit(solution)/shard_map/ppermute | solution.py:102
  190.0 27.7 %all-to-all-start.6 = ((bf16[8,32,3584]{2,1,0:T(8,128)(2,1)}), bf16[8,32,3584]{2,1,0:T(8,128)(2,1)S(1)}, u32[]{:S(2)}, u32[]{:S(2)}) async-start(bf16[8,32,3584]{2,1,0:T(8,128)(2,1)} %bitcast.25), calls=%async_computation.6 | async-start | bytes 3670016 | tf_op jit(solution)/shard_map/all_to_all | solution.py:144
  217.7 48.0 %all-to-all-start.5 = ((bf16[8,32,7168]{2,1,0:T(8,128)(2,1)}), bf16[8,32,7168]{2,1,0:T(8,128)(2,1)}, u32[]{:S(2)}, u32[]{:S(2)}) async-start(bf16[8,32,7168]{2,1,0:T(8,128)(2,1)} %bitcast.84), calls=%async_computation.5 | async-start | bytes 7340032 | tf_op jit(solution)/shard_map/all_to_all | solution.py:144
  265.7 29.5 %all-to-all-start.7 = ((bf16[8,32,3584]{2,1,0:T(8,128)(2,1)}), bf16[8,32,3584]{2,1,0:T(8,128)(2,1)S(1)}, u32[]{:S(2)}, u32[]{:S(2)}) async-start(bf16[8,32,3584]{2,1,0:T(8,128)(2,1)} %bitcast.28), calls=%async_computation.7 | async-start | bytes 3670016 | tf_op jit(solution)/shard_map/all_to_all | solution.py:144
  270.1 26.5 %collective-permute-start.3 = (bf16[128,3584]{1,0:T(8,128)(2,1)}, bf16[128,3584]{1,0:T(8,128)(2,1)}, u32[]{:S(2)}, u32[]{:S(2)}) collective-permute-start(bf16[128,3584]{1,0:T(8,128)(2,1)} %convolution_convert_fusion.6), channel_id=1, source_target_pairs={{0,24},{8,0},{16,8},{24,16},{1,25},{9,1},{17,9},{25,17},{2,26},{10... | collective-permute-start | bytes 2752520 | tf_op jit(solution)/shard_map/ppermute | solution.py:102
  296.6 28.0 %all-to-all-start.8 = ((bf16[8,32,3584]{2,1,0:T(8,128)(2,1)}), bf16[8,32,3584]{2,1,0:T(8,128)(2,1)S(1)}, u32[]{:S(2)}, u32[]{:S(2)}) async-start(bf16[8,32,3584]{2,1,0:T(8,128)(2,1)} %bitcast.30), calls=%async_computation.8 | async-start | bytes 3670016 | tf_op jit(solution)/shard_map/all_to_all | solution.py:144
  300.7 43.6 %collective-permute-start.4 = (bf16[128,3584]{1,0:T(8,128)(2,1)}, bf16[128,3584]{1,0:T(8,128)(2,1)}, u32[]{:S(2)}, u32[]{:S(2)}) collective-permute-start(bf16[128,3584]{1,0:T(8,128)(2,1)} %convolution_convert_fusion.5), channel_id=1, source_target_pairs={{0,16},{8,24},{16,0},{24,8},{1,17},{9,25},{17,1},{25,9},{2,18},{10... | collective-permute-start | bytes 2752520 | tf_op jit(solution)/shard_map/ppermute | solution.py:102
  344.3 23.8 %collective-permute-start.5 = (bf16[128,3584]{1,0:T(8,128)(2,1)S(1)}, bf16[128,3584]{1,0:T(8,128)(2,1)S(1)}, u32[]{:S(2)}, u32[]{:S(2)}) collective-permute-start(bf16[128,3584]{1,0:T(8,128)(2,1)S(1)} %convolution_convert_fusion.4), channel_id=1, source_target_pairs={{0,8},{8,16},{16,24},{24,0},{1,9},{9,17},{17,25},{25,1},{2,10},{10... | collective-permute-start | bytes 2752520 | tf_op jit(solution)/shard_map/ppermute | solution.py:102

commit v15 on v13

--- a/solution.py
+++ b/solution.py
@@ -104,7 +104,9 @@
             .astype(jnp.bfloat16)
             .reshape(n_local, capacity)
         )
-    gates = lax.all_to_all(jnp.stack(send_gate, axis=1), "local", 0, 0, tiled=True)
+    gate_columns = jnp.stack(send_gate, axis=-1)
+    gate_columns = jnp.pad(gate_columns, ((0, 0), (0, 0), (0, 128 - n_node % 128)))
+    gate_store = {}
 
     def spread(rows):
         return lax.all_to_all(
@@ -115,15 +117,22 @@
         return shift(previous, n_node, 1)
 
     def send(step, chunk):
-        return spread(select_rows(dispatch[step], chunk))
+        rows = select_rows(dispatch[step], chunk)
+        if step == 0:
+            rows = jnp.concatenate(
+                [rows, gate_columns.reshape(chunk_rows, gate_columns.shape[-1])], axis=1
+            )
+        return spread(rows)
 
     def compute(step, received):
         saved = lax.dynamic_slice_in_dim(gate_saved, sources[step] * chunk_rows, chunk_rows, 0)
-        rows = received.reshape(chunk_rows, 2 * model_width)
+        rows = received.reshape(chunk_rows, received.shape[-1])
+        if step == 0:
+            gate_store[0] = rows[:, 2 * model_width : 2 * model_width + n_node]
         return expert_backward(
             rows[:, :model_width],
-            rows[:, model_width:],
-            gates[:, step].reshape(chunk_rows),
+            rows[:, model_width : 2 * model_width],
+            gate_store[0][:, step],
             saved,
             weight_in,
             weight_out,

time: 370 us -> 371 us (level)
  other arithmetic: 8.95 us -> 13 us
  starting transfers between devices: 42.5 us -> 38.5 us
    ppermute x6, waiting for transfers between devices: 85.1 us -> 126 us  [shift(): lax.ppermute(value, 'node', [(i, (i + step) % n_node) for i in range(n_no...]
    all_to_all x8, waiting for transfers between devices: 119 us -> 82.2 us  [spread(): lax.all_to_all(rows.reshape(n_local, capacity, rows.shape[-1]), 'local',...]
  transfers between devices with their start and end apart: 15 -> 14, of which waited for: 11 -> 10; matrix products, arithmetic and copies ran while one was open for 20% -> 18% of each run, Pallas kernels for 10% -> 10%
where the time goes in v15:
time: 371 us; the launch traced here: 370 us
  waiting for transfers between devices  208 us (56%)
  matrix products  67.4 us (18%)
  starting transfers between devices  38.5 us (10%)
  Pallas kernels  37.8 us (10%)
  other arithmetic  13 us (4%)
  local copies, waits for them, and re-layouts  5.08 us (1%)
    ppermute x6, waiting for transfers between devices, shift(): lax.ppermute(value, 'node', [(i, (i + step) % n_node) for i in range(n_no...  126 us
    all_to_all x8, waiting for transfers between devices, spread(): lax.all_to_all(rows.reshape(n_local, capacity, rows.shape[-1]), 'local',...  82.2 us
    pallas_call x4, Pallas kernels, part_matmul(): pl.pallas_call(part_kernel, grid=(width // tile,), in_specs=[pl.BlockSpec...  37.8 us
    all_to_all x8, starting transfers between devices, spread(): lax.all_to_all(rows.reshape(n_local, capacity, rows.shape[-1]), 'local',...  33.8 us
    dot_general x4, matrix products, expert_backward(): jnp.dot(rows_x, weight_in[:, FF:], preferred_element_type=jnp.float32)  23.7 us
    dot_general x4, matrix products, expert_backward(): lax.dot_general(rows_dy, weight_out, (((1,), (1,)), ((), ())), preferred_...  23.3 us
    dot_general x4, matrix products, select_rows(): lax.dot_general(onehot, rows, (((0,), (0,)), ((), ())), preferred_element...  14.5 us
  transfers between devices with their start and end apart: 14, of which 10 were waited for; matrix products, arithmetic and copies ran while one was open for 18% of the time, Pallas kernels for 10%

profile of v15, /device:TPU:0, one launch (start us, length us, event | category | flops | bytes accessed | tf_op | source)
XLA Modules:
  0.0 370.2 jit_solution(17521004501820682381)
XLA Ops:
  0.0 0.7 multiply_convert_fusion
  0.7 0.1 copy.15
  1.2 0.8 copy.13
  2.1 0.2 reshape.62
  2.3 0.6 fusion.135
  3.1 0.4 fusion.171
  3.5 0.4 fusion.166
  4.1 0.4 fusion.163
  4.7 0.4 fusion.165
  5.4 0.4 fusion.168
  5.9 0.1 copy.19
  6.1 1.3 constant_dynamic-update-slice_fusion
  7.4 1.1 convolution_convert_fusion.3
  8.6 2.1 fusion.20
  10.6 5.2 %all-to-all-start = ((bf16[8,32,7296]{2,1,0:T(8,128)(2,1)}), bf16[8,32,7296]{2,1,0:T(8,128)(2,1)}, u32[]{:S(2)}, u32[]{:S(2)}) async-start(bf16[8,32,7296]{2,1,0:T(8,128)(2,1)} %fusion.20), calls=%async_computation | async-start | bytes 7471104 | tf_op jit(solution)/shard_map/all_to_all | solution.py:112
  15.8 2.5 collective-permute-start
  18.3 0.4 fusion.172
  18.7 42.2 %collective-permute-done = bf16[128,7168]{1,0:T(8,128)(2,1)} collective-permute-done((bf16[128,7168]{1,0:T(8,128)(2,1)S(1)}, bf16[128,7168]{1,0:T(8,128)(2,1)}, u32[]{:S(2)}, u32[]{:S(2)}) %collective-permute-start) | collective-permute-done | bytes 1835040 | tf_op jit(solution)/shard_map/ppermute | solution.py:68
  60.9 4.5 %convolution_convert_fusion.2 = bf16[256,7168]{1,0:T(8,128)(2,1)} fusion(bf16[128,256]{1,0:T(8,128)(2,1)S(1)} %fusion.172, bf16[128,7168]{1,0:T(8,128)(2,1)} %collective-permute-done), kind=kOutput, calls=%fused_computation.2 | convolution fusion | flops 471597056 | bytes 5570560 | tf_op jit(solution)/shard_map/dot_general | solution.py:59
  65.4 4.5 %all-to-all-start.1 = ((bf16[8,32,7168]{2,1,0:T(8,128)(2,1)}), bf16[8,32,7168]{2,1,0:T(8,128)(2,1)}, u32[]{:S(2)}, u32[]{:S(2)}) async-start(bf16[8,32,7168]{2,1,0:T(8,128)(2,1)} %bitcast.104), calls=%async_computation.1 | async-start | bytes 7340032 | tf_op jit(solution)/shard_map/all_to_all | solution.py:112
  69.9 1.6 collective-permute-start.1
  71.5 1.3 convert_reduce_fusion
  72.8 5.8 %fusion.143 = (bf16[256,1024]{1,0:T(8,128)(2,1)S(1)}, f32[256,1024]{1,0:T(8,128)S(1)}) fusion(bf16[1024,1024]{1,0:T(8,128)(2,1)} %param.11, s32[]{:T(128)S(6)} %select_n.75, f32[256]{0:T(256)S(1)} %get-tuple-element.44, bf16[1,1024,3584]{2,1,0:T(8,128)(2,1)} %param.13, bf16[256,7296]{1,0:T(8,128)(2,1)} %bitcast.16), kind=kOutput, calls=%fused_computation.79 | convolution fusion | flops 1881145344 | bytes 11273220 | tf_op jit(solution)/shard_map/dot_general | solution.py:46
  78.6 5.9 %fusion.109 = bf16[256,1024]{1,0:T(8,128)(2,1)S(1)} fusion(f32[256,1024]{1,0:T(8,128)S(1)} %get-tuple-element.54, bf16[3584,2048]{1,0:T(8,128)(2,1)} %bitcast.93, bf16[256,7296]{1,0:T(8,128)(2,1)} %bitcast.16, bf16[1024,1024]{1,0:T(8,128)(2,1)} %param.11, s32[]{:T(128)S(6)} %select_n.75), kind=kOutput, calls=%fused_computation.67 | convolution fusion | flops 1881931776 | bytes 11272196 | tf_op jit(solution)/shard_map/dot_general | solution.py:45
  84.6 1.1 pad_maximum_fusion.grad_ref
  85.6 9.4 %shard_map.73 = bf16[256,3584]{1,0:T(8,128)(2,1)} custom-call(bf16[256,2048]{1,0:T(8,128)(2,1)} %pad_maximum_fusion.grad_ref, bf16[3584,2048]{1,0:T(8,128)(2,1)} %bitcast.94), custom_call_target="tpu_custom_call" | custom-call | tf_op jit(solution)/shard_map/pallas_call | solution.py:32
  95.1 19.1 %collective-permute-done.1 = bf16[128,7168]{1,0:T(8,128)(2,1)S(1)} collective-permute-done((bf16[128,7168]{1,0:T(8,128)(2,1)}, bf16[128,7168]{1,0:T(8,128)(2,1)S(1)}, u32[]{:S(2)}, u32[]{:S(2)}) %collective-permute-start.1) | collective-permute-done | bytes 1835040 | tf_op jit(solution)/shard_map/ppermute | solution.py:68
  114.2 1.3 copy-done
  115.5 3.9 %all-to-all-start.3 = ((bf16[8,32,3584]{2,1,0:T(8,128)(2,1)}), bf16[8,32,3584]{2,1,0:T(8,128)(2,1)S(1)}, u32[]{:S(2)}, u32[]{:S(2)}) async-start(bf16[8,32,3584]{2,1,0:T(8,128)(2,1)} %bitcast.105), calls=%async_computation.3 | async-start | bytes 3670016 | tf_op jit(solution)/shard_map/all_to_all | solution.py:112
  119.4 0.4 fusion.173
  119.8 4.4 %convolution_convert_fusion.1 = bf16[256,7168]{1,0:T(8,128)(2,1)} fusion(bf16[128,256]{1,0:T(8,128)(2,1)S(1)} %fusion.173, bf16[128,7168]{1,0:T(8,128)(2,1)} %copy-done), kind=kOutput, calls=%fused_computation.1 | convolution fusion | flops 471597056 | bytes 5570560 | tf_op jit(solution)/shard_map/dot_general | solution.py:59
  124.2 19.0 %all-to-all-done.3 = bf16[8,32,3584]{2,1,0:T(8,128)(2,1)S(1)} async-done(((bf16[8,32,3584]{2,1,0:T(8,128)(2,1)}), bf16[8,32,3584]{2,1,0:T(8,128)(2,1)S(1)}, u32[]{:S(2)}, u32[]{:S(2)}) %all-to-all-start.3) | async-done | bytes 1835040 | tf_op jit(solution)/shard_map/all_to_all | solution.py:112
  143.2 4.5 %all-to-all-start.2 = ((bf16[8,32,7168]{2,1,0:T(8,128)(2,1)}), bf16[8,32,7168]{2,1,0:T(8,128)(2,1)}, u32[]{:S(2)}, u32[]{:S(2)}) async-start(bf16[8,32,7168]{2,1,0:T(8,128)(2,1)} %bitcast.103), calls=%async_computation.2 | async-start | bytes 7340032 | tf_op jit(solution)/shard_map/all_to_all | solution.py:112
  147.8 5.8 %fusion.149 = (bf16[256,1024]{1,0:T(8,128)(2,1)S(1)}, f32[256,1024]{1,0:T(8,128)S(1)}) fusion(bf16[1024,1024]{1,0:T(8,128)(2,1)} %param.11, s32[]{:T(128)S(6)} %select_n.76, f32[256]{0:T(256)S(1)} %get-tuple-element.43, bf16[1,1024,3584]{2,1,0:T(8,128)(2,1)} %param.13, bf16[256,7168]{1,0:T(8,128)(2,1)} %bitcast.20), kind=kOutput, calls=%fused_computation.85 | convolution fusion | flops 1881145344 | bytes 11273220 | tf_op jit(solution)/shard_map/dot_general | solution.py:46
  153.6 5.9 %fusion.114 = bf16[256,1024]{1,0:T(8,128)(2,1)S(1)} fusion(f32[256,1024]{1,0:T(8,128)S(1)} %get-tuple-element.56, bf16[3584,2048]{1,0:T(8,128)(2,1)} %bitcast.95, bf16[256,7168]{1,0:T(8,128)(2,1)} %bitcast.20, bf16[1024,1024]{1,0:T(8,128)(2,1)} %param.11, s32[]{:T(128)S(6)} %select_n.76), kind=kOutput, calls=%fused_computation.68 | convolution fusion | flops 1881931776 | bytes 11272196 | tf_op jit(solution)/shard_map/dot_general | solution.py:45
  159.6 1.1 pad_maximum_fusion.1.grad_ref
  160.7 9.5 %shard_map.74 = bf16[256,3584]{1,0:T(8,128)(2,1)} custom-call(bf16[256,2048]{1,0:T(8,128)(2,1)} %pad_maximum_fusion.1.grad_ref, bf16[3584,2048]{1,0:T(8,128)(2,1)} %bitcast.96), custom_call_target="tpu_custom_call" | custom-call | tf_op jit(solution)/shard_map/pallas_call | solution.py:32
  170.1 0.4 convolution_convert_fusion.7
  170.5 21.6 %collective-permute-done.2 = bf16[128,7168]{1,0:T(8,128)(2,1)} collective-permute-done((bf16[128,7168]{1,0:T(8,128)(2,1)}, bf16[128,7168]{1,0:T(8,128)(2,1)}, u32[]{:S(2)}, u32[]{:S(2)}) %collective-permute-start.2) | collective-permute-done | bytes 1835040 | tf_op jit(solution)/shard_map/ppermute | solution.py:68
  192.2 3.9 %all-to-all-start.5 = ((bf16[8,32,3584]{2,1,0:T(8,128)(2,1)}), bf16[8,32,3584]{2,1,0:T(8,128)(2,1)S(1)}, u32[]{:S(2)}, u32[]{:S(2)}) async-start(bf16[8,32,3584]{2,1,0:T(8,128)(2,1)} %bitcast.25), calls=%async_computation.5 | async-start | bytes 3670016 | tf_op jit(solution)/shard_map/all_to_all | solution.py:112
  196.0 0.4 fusion.170
  196.4 4.4 %convolution_convert_fusion = bf16[256,7168]{1,0:T(8,128)(2,1)} fusion(bf16[128,256]{1,0:T(8,128)(2,1)S(1)} %fusion.170, bf16[128,7168]{1,0:T(8,128)(2,1)} %collective-permute-done.2), kind=kOutput, calls=%fused_computation | convolution fusion | flops 471597056 | bytes 5570560 | tf_op jit(solution)/shard_map/dot_general | solution.py:59
  200.9 19.0 %all-to-all-done.5 = bf16[8,32,3584]{2,1,0:T(8,128)(2,1)S(1)} async-done(((bf16[8,32,3584]{2,1,0:T(8,128)(2,1)}), bf16[8,32,3584]{2,1,0:T(8,128)(2,1)S(1)}, u32[]{:S(2)}, u32[]{:S(2)}) %all-to-all-start.5) | async-done | bytes 1835040 | tf_op jit(solution)/shard_map/all_to_all | solution.py:112
  219.9 4.7 %all-to-all-start.4 = ((bf16[8,32,7168]{2,1,0:T(8,128)(2,1)}), bf16[8,32,7168]{2,1,0:T(8,128)(2,1)}, u32[]{:S(2)}, u32[]{:S(2)}) async-start(bf16[8,32,7168]{2,1,0:T(8,128)(2,1)} %bitcast.102), calls=%async_computation.4 | async-start | bytes 7340032 | tf_op jit(solution)/shard_map/all_to_all | solution.py:112
  224.6 5.8 %fusion.155 = (bf16[256,1024]{1,0:T(8,128)(2,1)S(1)}, f32[256,1024]{1,0:T(8,128)S(1)}) fusion(bf16[1024,1024]{1,0:T(8,128)(2,1)} %param.11, s32[]{:T(128)S(6)} %select_n.77, f32[256]{0:T(256)S(1)} %get-tuple-element.42, bf16[1,1024,3584]{2,1,0:T(8,128)(2,1)} %param.13, bf16[256,7168]{1,0:T(8,128)(2,1)} %bitcast.24), kind=kOutput, calls=%fused_computation.91 | convolution fusion | flops 1881145344 | bytes 11273220 | tf_op jit(solution)/shard_map/dot_general | solution.py:46
  230.4 5.9 %fusion.119 = bf16[256,1024]{1,0:T(8,128)(2,1)S(1)} fusion(f32[256,1024]{1,0:T(8,128)S(1)} %get-tuple-element.58, bf16[3584,2048]{1,0:T(8,128)(2,1)} %bitcast.97, bf16[256,7168]{1,0:T(8,128)(2,1)} %bitcast.24, bf16[1024,1024]{1,0:T(8,128)(2,1)} %param.11, s32[]{:T(128)S(6)} %select_n.77), kind=kOutput, calls=%fused_computation.69 | convolution fusion | flops 1881931776 | bytes 11272196 | tf_op jit(solution)/shard_map/dot_general | solution.py:45
  236.4 1.1 pad_maximum_fusion.2.grad_ref
  237.5 9.5 %shard_map.75 = bf16[256,3584]{1,0:T(8,128)(2,1)} custom-call(bf16[256,2048]{1,0:T(8,128)(2,1)} %pad_maximum_fusion.2.grad_ref, bf16[3584,2048]{1,0:T(8,128)(2,1)} %bitcast.98), custom_call_target="tpu_custom_call" | custom-call | tf_op jit(solution)/shard_map/pallas_call | solution.py:32
  246.9 1.4 convolution_convert_fusion.6
  248.3 19.6 %all-to-all-done.4 = bf16[8,32,7168]{2,1,0:T(8,128)(2,1)} async-done(((bf16[8,32,7168]{2,1,0:T(8,128)(2,1)}), bf16[8,32,7168]{2,1,0:T(8,128)(2,1)}, u32[]{:S(2)}, u32[]{:S(2)}) %all-to-all-start.4) | async-done | bytes 3670048 | tf_op jit(solution)/shard_map/all_to_all | solution.py:112
  267.9 3.6 all-to-all-start.6
  271.5 0.5 collective-permute-start.3
  272.0 5.8 %fusion.161 = (bf16[256,1024]{1,0:T(8,128)(2,1)S(1)}, f32[256,1024]{1,0:T(8,128)S(1)}) fusion(bf16[1024,1024]{1,0:T(8,128)(2,1)} %param.11, s32[]{:T(128)S(6)} %select_n.78, f32[256]{0:T(256)S(1)} %get-tuple-element.41, bf16[1,1024,3584]{2,1,0:T(8,128)(2,1)} %param.13, bf16[256,7168]{1,0:T(8,128)(2,1)} %bitcast.27), kind=kOutput, calls=%fused_computation.97 | convolution fusion | flops 1881145344 | bytes 11273220 | tf_op jit(solution)/shard_map/dot_general | solution.py:46
  277.8 5.9 %fusion.124 = bf16[256,1024]{1,0:T(8,128)(2,1)S(1)} fusion(f32[256,1024]{1,0:T(8,128)S(1)} %get-tuple-element.60, bf16[3584,2048]{1,0:T(8,128)(2,1)} %bitcast.99, bf16[256,7168]{1,0:T(8,128)(2,1)} %bitcast.27, bf16[1024,1024]{1,0:T(8,128)(2,1)} %param.11, s32[]{:T(128)S(6)} %select_n.78), kind=kOutput, calls=%fused_computation.70 | convolution fusion | flops 1881931776 | bytes 11272196 | tf_op jit(solution)/shard_map/dot_general | solution.py:45
  283.8 1.1 pad_maximum_fusion.3.grad_ref
  284.8 9.4 %shard_map.76 = bf16[256,3584]{1,0:T(8,128)(2,1)} custom-call(bf16[256,2048]{1,0:T(8,128)(2,1)} %pad_maximum_fusion.3.grad_ref, bf16[3584,2048]{1,0:T(8,128)(2,1)} %bitcast.100), custom_call_target="tpu_custom_call" | custom-call | tf_op jit(solution)/shard_map/pallas_call | solution.py:32
  294.3 1.0 all-to-all-done.6
  295.2 1.3 convolution_convert_fusion.5
  296.6 3.6 all-to-all-start.7
  300.3 23.7 %all-to-all-done.7 = bf16[8,32,3584]{2,1,0:T(8,128)(2,1)S(1)} async-done(((bf16[8,32,3584]{2,1,0:T(8,128)(2,1)}), bf16[8,32,3584]{2,1,0:T(8,128)(2,1)S(1)}, u32[]{:S(2)}, u32[]{:S(2)}) %all-to-all-start.7) | async-done | bytes 1835040 | tf_op jit(solution)/shard_map/all_to_all | solution.py:112
  323.9 0.4 convolution_convert_fusion.4
  324.4 19.4 %collective-permute-done.4 = bf16[128,3584]{1,0:T(8,128)(2,1)} collective-permute-done((bf16[128,3584]{1,0:T(8,128)(2,1)}, bf16[128,3584]{1,0:T(8,128)(2,1)}, u32[]{:S(2)}, u32[]{:S(2)}) %collective-permute-start.4) | collective-permute-done | bytes 917536 | tf_op jit(solution)/shard_map/ppermute | solution.py:68
  343.7 23.6 %collective-permute-done.5 = bf16[128,3584]{1,0:T(8,128)(2,1)S(1)} collective-permute-done((bf16[128,3584]{1,0:T(8,128)(2,1)S(1)}, bf16[128,3584]{1,0:T(8,128)(2,1)S(1)}, u32[]{:S(2)}, u32[]{:S(2)}) %collective-permute-start.5) | collective-permute-done | bytes 917536 | tf_op jit(solution)/shard_map/ppermute | solution.py:68
  367.3 2.9 add_convert_fusion
  (30 shorter events, 1.4 us)
Async XLA Ops:
  3.5 2.6 copy-start.1
  10.6 50.3 %all-to-all-start = ((bf16[8,32,7296]{2,1,0:T(8,128)(2,1)}), bf16[8,32,7296]{2,1,0:T(8,128)(2,1)}, u32[]{:S(2)}, u32[]{:S(2)}) async-start(bf16[8,32,7296]{2,1,0:T(8,128)(2,1)} %fusion.20), calls=%async_computation | async-start | bytes 7471104 | tf_op jit(solution)/shard_map/all_to_all | solution.py:112
  15.8 45.1 %collective-permute-start = (bf16[128,7168]{1,0:T(8,128)(2,1)S(1)}, bf16[128,7168]{1,0:T(8,128)(2,1)}, u32[]{:S(2)}, u32[]{:S(2)}) collective-permute-start(bf16[128,7168]{1,0:T(8,128)(2,1)S(1)} %constant_dynamic-update-slice_fusion), channel_id=1, source_target_pairs={{0,8},{8,16},{16,24},{24,0},{1,9},{9,17},{17,25},{25,1},{2,10},{10... | collective-permute-start | bytes 5505032 | tf_op jit(solution)/shard_map/ppermute | solution.py:68
  65.4 48.8 %all-to-all-start.1 = ((bf16[8,32,7168]{2,1,0:T(8,128)(2,1)}), bf16[8,32,7168]{2,1,0:T(8,128)(2,1)}, u32[]{:S(2)}, u32[]{:S(2)}) async-start(bf16[8,32,7168]{2,1,0:T(8,128)(2,1)} %bitcast.104), calls=%async_computation.1 | async-start | bytes 7340032 | tf_op jit(solution)/shard_map/all_to_all | solution.py:112
  69.9 44.3 %collective-permute-start.1 = (bf16[128,7168]{1,0:T(8,128)(2,1)}, bf16[128,7168]{1,0:T(8,128)(2,1)S(1)}, u32[]{:S(2)}, u32[]{:S(2)}) collective-permute-start(bf16[128,7168]{1,0:T(8,128)(2,1)} %collective-permute-done), channel_id=1, source_target_pairs={{0,8},{8,16},{16,24},{24,0},{1,9},{9,17},{17,25},{25,1},{2,10},{10... | collective-permute-start | bytes 5505032 | tf_op jit(solution)/shard_map/ppermute | solution.py:68
  114.2 1.3 copy-start
  115.5 27.7 %all-to-all-start.3 = ((bf16[8,32,3584]{2,1,0:T(8,128)(2,1)}), bf16[8,32,3584]{2,1,0:T(8,128)(2,1)S(1)}, u32[]{:S(2)}, u32[]{:S(2)}) async-start(bf16[8,32,3584]{2,1,0:T(8,128)(2,1)} %bitcast.105), calls=%async_computation.3 | async-start | bytes 3670016 | tf_op jit(solution)/shard_map/all_to_all | solution.py:112
  143.2 48.9 %all-to-all-start.2 = ((bf16[8,32,7168]{2,1,0:T(8,128)(2,1)}), bf16[8,32,7168]{2,1,0:T(8,128)(2,1)}, u32[]{:S(2)}, u32[]{:S(2)}) async-start(bf16[8,32,7168]{2,1,0:T(8,128)(2,1)} %bitcast.103), calls=%async_computation.2 | async-start | bytes 7340032 | tf_op jit(solution)/shard_map/all_to_all | solution.py:112
  147.8 44.4 %collective-permute-start.2 = (bf16[128,7168]{1,0:T(8,128)(2,1)}, bf16[128,7168]{1,0:T(8,128)(2,1)}, u32[]{:S(2)}, u32[]{:S(2)}) collective-permute-start(bf16[128,7168]{1,0:T(8,128)(2,1)} %copy-done), channel_id=1, source_target_pairs={{0,8},{8,16},{16,24},{24,0},{1,9},{9,17},{17,25},{25,1},{2,10},{10... | collective-permute-start | bytes 5505032 | tf_op jit(solution)/shard_map/ppermute | solution.py:68
  192.2 27.7 %all-to-all-start.5 = ((bf16[8,32,3584]{2,1,0:T(8,128)(2,1)}), bf16[8,32,3584]{2,1,0:T(8,128)(2,1)S(1)}, u32[]{:S(2)}, u32[]{:S(2)}) async-start(bf16[8,32,3584]{2,1,0:T(8,128)(2,1)} %bitcast.25), calls=%async_computation.5 | async-start | bytes 3670016 | tf_op jit(solution)/shard_map/all_to_all | solution.py:112
  219.9 48.0 %all-to-all-start.4 = ((bf16[8,32,7168]{2,1,0:T(8,128)(2,1)}), bf16[8,32,7168]{2,1,0:T(8,128)(2,1)}, u32[]{:S(2)}, u32[]{:S(2)}) async-start(bf16[8,32,7168]{2,1,0:T(8,128)(2,1)} %bitcast.102), calls=%async_computation.4 | async-start | bytes 7340032 | tf_op jit(solution)/shard_map/all_to_all | solution.py:112
  267.9 27.4 %all-to-all-start.6 = ((bf16[8,32,3584]{2,1,0:T(8,128)(2,1)}), bf16[8,32,3584]{2,1,0:T(8,128)(2,1)S(1)}, u32[]{:S(2)}, u32[]{:S(2)}) async-start(bf16[8,32,3584]{2,1,0:T(8,128)(2,1)} %bitcast.28), calls=%async_computation.6 | async-start | bytes 3670016 | tf_op jit(solution)/shard_map/all_to_all | solution.py:112
  271.5 25.1 %collective-permute-start.3 = (bf16[128,3584]{1,0:T(8,128)(2,1)}, bf16[128,3584]{1,0:T(8,128)(2,1)}, u32[]{:S(2)}, u32[]{:S(2)}) collective-permute-start(bf16[128,3584]{1,0:T(8,128)(2,1)} %convolution_convert_fusion.6), channel_id=1, source_target_pairs={{0,24},{8,0},{16,8},{24,16},{1,25},{9,1},{17,9},{25,17},{2,26},{10... | collective-permute-start | bytes 2752520 | tf_op jit(solution)/shard_map/ppermute | solution.py:68
  296.6 27.4 %all-to-all-start.7 = ((bf16[8,32,3584]{2,1,0:T(8,128)(2,1)}), bf16[8,32,3584]{2,1,0:T(8,128)(2,1)S(1)}, u32[]{:S(2)}, u32[]{:S(2)}) async-start(bf16[8,32,3584]{2,1,0:T(8,128)(2,1)} %bitcast.30), calls=%async_computation.7 | async-start | bytes 3670016 | tf_op jit(solution)/shard_map/all_to_all | solution.py:112
  300.2 43.5 %collective-permute-start.4 = (bf16[128,3584]{1,0:T(8,128)(2,1)}, bf16[128,3584]{1,0:T(8,128)(2,1)}, u32[]{:S(2)}, u32[]{:S(2)}) collective-permute-start(bf16[128,3584]{1,0:T(8,128)(2,1)} %convolution_convert_fusion.5), channel_id=1, source_target_pairs={{0,16},{8,24},{16,0},{24,8},{1,17},{9,25},{17,1},{25,9},{2,18},{10... | collective-permute-start | bytes 2752520 | tf_op jit(solution)/shard_map/ppermute | solution.py:68
  343.7 23.6 %collective-permute-start.5 = (bf16[128,3584]{1,0:T(8,128)(2,1)S(1)}, bf16[128,3584]{1,0:T(8,128)(2,1)S(1)}, u32[]{:S(2)}, u32[]{:S(2)}) collective-permute-start(bf16[128,3584]{1,0:T(8,128)(2,1)S(1)} %convolution_convert_fusion.4), channel_id=1, source_target_pairs={{0,8},{8,16},{16,24},{24,0},{1,9},{9,17},{17,25},{25,1},{2,10},{10... | collective-permute-start | bytes 2752520 | tf_op jit(solution)/shard_map/ppermute | solution.py:68

commit v16 on v13

--- a/solution.py
+++ b/solution.py
@@ -139,14 +139,14 @@
         return shift(node_sum, n_node, -step)
 
     chunks = {0: jnp.concatenate([hidden_in, out_grad], axis=1)}
+    for step in range(1, n_node):
+        chunks[step] = fetch(step, chunks[step - 1])
     received = {}
     contribs = {}
     sums = {}
     homes = {}
     for slot in range(-1, n_node + 2):
         produced = {}
-        if 0 < slot + 2 < n_node:
-            produced["chunk", slot + 2] = fetch(slot + 2, chunks[slot + 1])
         if 0 <= slot + 1 < n_node:
             produced["received", slot + 1] = send(slot + 1, chunks[slot + 1])
         if 0 <= slot < n_node:

time: 370 us -> 372 us (level)
  transfers between devices with their start and end apart: 15 -> 15, of which waited for: 11 -> 9; matrix products, arithmetic and copies ran while one was open for 20% -> 20% of each run, Pallas kernels for 10% -> 10%
where the time goes in v16:
time: 372 us; the launch traced here: 371 us
  waiting for transfers between devices  208 us (56%)
  matrix products  69.3 us (19%)
  starting transfers between devices  41.8 us (11%)
  Pallas kernels  37.9 us (10%)
  other arithmetic  8.88 us (2%)
  local copies, waits for them, and re-layouts  4.54 us (1%)
    all_to_all x8, waiting for transfers between devices, spread(): lax.all_to_all(rows.reshape(n_local, capacity, rows.shape[-1]), 'local',...  123 us
    ppermute x6, waiting for transfers between devices, shift(): lax.ppermute(value, 'node', [(i, (i + step) % n_node) for i in range(n_no...  85.6 us
    pallas_call x4, Pallas kernels, part_matmul(): pl.pallas_call(part_kernel, grid=(width // tile,), in_specs=[pl.BlockSpec...  37.9 us
    all_to_all x8, starting transfers between devices, spread(): lax.all_to_all(rows.reshape(n_local, capacity, rows.shape[-1]), 'local',...  33.2 us
    dot_general x4, matrix products, expert_backward(): jnp.dot(rows_x, weight_in[:, FF:], preferred_element_type=jnp.float32)  23.7 us
    dot_general x4, matrix products, expert_backward(): lax.dot_general(rows_dy, weight_out, (((1,), (1,)), ((), ())), preferred_...  23.3 us
    dot_general x4, matrix products, select_rows(): lax.dot_general(onehot, rows, (((0,), (0,)), ((), ())), preferred_element...  16.4 us
  transfers between devices with their start and end apart: 15, of which 9 were waited for; matrix products, arithmetic and copies ran while one was open for 20% of the time, Pallas kernels for 10%

profile of v16, /device:TPU:0, one launch (start us, length us, event | category | flops | bytes accessed | tf_op | source)
XLA Modules:
  0.0 371.0 jit_solution(3648664942047969767)
XLA Ops:
  0.0 0.9 copy.11
  0.9 0.2 reshape.88
  1.0 0.6 fusion.133
  1.9 0.1 copy.13
  2.1 0.4 fusion.160
  2.5 0.1 stack_reshape.12
  2.6 0.1 copy.14
  2.8 0.4 fusion.162
  3.3 0.1 stack_reshape.13
  3.3 0.1 copy.15
  3.6 0.4 fusion.164
  4.1 0.1 copy.16
  4.3 0.4 fusion.166
  4.8 0.6 copy.12
  5.4 5.2 %all-to-all-start.4 = ((bf16[8,4,32]{2,1,0:T(4,128)(2,1)}), bf16[8,4,32]{2,1,0:T(4,128)(2,1)S(1)}, u32[]{:S(2)}, u32[]{:S(2)}) async-start(bf16[8,4,32]{2,1,0:T(4,128)(2,1)} %copy.12), calls=%async_computation.4 | async-start | bytes 16384 | tf_op jit(solution)/shard_map/all_to_all | solution.py:107
  10.6 0.4 fusion.171
  11.1 1.3 constant_dynamic-update-slice_fusion
  12.4 3.0 convolution_convert_fusion
  15.4 4.5 %all-to-all-start.3 = ((bf16[8,32,7168]{2,1,0:T(8,128)(2,1)}), bf16[8,32,7168]{2,1,0:T(8,128)(2,1)}, u32[]{:S(2)}, u32[]{:S(2)}) async-start(bf16[8,32,7168]{2,1,0:T(8,128)(2,1)} %bitcast.104), calls=%async_computation.3 | async-start | bytes 7340032 | tf_op jit(solution)/shard_map/all_to_all | solution.py:110
  19.9 1.6 collective-permute-start
  21.5 0.4 fusion.170
  21.9 42.4 %collective-permute-done = bf16[128,7168]{1,0:T(8,128)(2,1)} collective-permute-done((bf16[128,7168]{1,0:T(8,128)(2,1)S(1)}, bf16[128,7168]{1,0:T(8,128)(2,1)}, u32[]{:S(2)}, u32[]{:S(2)}) %collective-permute-start) | collective-permute-done | bytes 1835040 | tf_op jit(solution)/shard_map/ppermute | solution.py:68
  64.3 4.4 %convolution_convert_fusion.1 = bf16[256,7168]{1,0:T(8,128)(2,1)} fusion(bf16[128,256]{1,0:T(8,128)(2,1)S(1)} %fusion.170, bf16[128,7168]{1,0:T(8,128)(2,1)} %collective-permute-done), kind=kOutput, calls=%fused_computation.1 | convolution fusion | flops 471597056 | bytes 5570560 | tf_op jit(solution)/shard_map/dot_general | solution.py:59
  68.7 4.5 %all-to-all-start.2 = ((bf16[8,32,7168]{2,1,0:T(8,128)(2,1)}), bf16[8,32,7168]{2,1,0:T(8,128)(2,1)}, u32[]{:S(2)}, u32[]{:S(2)}) async-start(bf16[8,32,7168]{2,1,0:T(8,128)(2,1)} %bitcast.102), calls=%async_computation.2 | async-start | bytes 7340032 | tf_op jit(solution)/shard_map/all_to_all | solution.py:110
  73.4 5.8 %fusion.141 = (bf16[256,1024]{1,0:T(8,128)(2,1)S(1)}, f32[256,1024]{1,0:T(8,128)S(1)}) fusion(bf16[1024,1024]{1,0:T(8,128)(2,1)} %param.11, s32[]{:T(128)S(6)} %select_n.75, f32[256]{0:T(256)S(1)} %reshape.105, bf16[1,1024,3584]{2,1,0:T(8,128)(2,1)} %param.13, bf16[256,7168]{1,0:T(8,128)(2,1)} %bitcast.6), kind=kOutput, calls=%fused_computation.76 | convolution fusion | flops 1881145344 | bytes 11273220 | tf_op jit(solution)/shard_map/dot_general | solution.py:46
  79.2 5.9 %fusion.107 = bf16[256,1024]{1,0:T(8,128)(2,1)S(1)} fusion(f32[256,1024]{1,0:T(8,128)S(1)} %get-tuple-element.46, bf16[3584,2048]{1,0:T(8,128)(2,1)} %bitcast.93, bf16[256,7168]{1,0:T(8,128)(2,1)} %bitcast.6, bf16[1024,1024]{1,0:T(8,128)(2,1)} %param.11, s32[]{:T(128)S(6)} %select_n.75), kind=kOutput, calls=%fused_computation.64 | convolution fusion | flops 1881931776 | bytes 11272196 | tf_op jit(solution)/shard_map/dot_general | solution.py:45
  85.1 1.1 pad_maximum_fusion.grad_ref
  86.2 9.5 %shard_map.73 = bf16[256,3584]{1,0:T(8,128)(2,1)} custom-call(bf16[256,2048]{1,0:T(8,128)(2,1)} %pad_maximum_fusion.grad_ref, bf16[3584,2048]{1,0:T(8,128)(2,1)} %bitcast.94), custom_call_target="tpu_custom_call" | custom-call | tf_op jit(solution)/shard_map/pallas_call | solution.py:32
  95.6 21.1 %all-to-all-done.2 = bf16[8,32,7168]{2,1,0:T(8,128)(2,1)} async-done(((bf16[8,32,7168]{2,1,0:T(8,128)(2,1)}), bf16[8,32,7168]{2,1,0:T(8,128)(2,1)}, u32[]{:S(2)}, u32[]{:S(2)}) %all-to-all-start.2) | async-done | bytes 3670048 | tf_op jit(solution)/shard_map/all_to_all | solution.py:110
  116.7 3.8 %all-to-all-start.5 = ((bf16[8,32,3584]{2,1,0:T(8,128)(2,1)}), bf16[8,32,3584]{2,1,0:T(8,128)(2,1)S(1)}, u32[]{:S(2)}, u32[]{:S(2)}) async-start(bf16[8,32,3584]{2,1,0:T(8,128)(2,1)} %bitcast.105), calls=%async_computation.5 | async-start | bytes 3670016 | tf_op jit(solution)/shard_map/all_to_all | solution.py:110
  120.5 0.4 fusion.169
  120.9 4.5 %convolution_convert_fusion.2 = bf16[256,7168]{1,0:T(8,128)(2,1)} fusion(bf16[128,256]{1,0:T(8,128)(2,1)S(1)} %fusion.169, bf16[128,7168]{1,0:T(8,128)(2,1)} %collective-permute-done.1), kind=kOutput, calls=%fused_computation.2 | convolution fusion | flops 471597056 | bytes 5570560 | tf_op jit(solution)/shard_map/dot_general | solution.py:59
  125.5 18.6 %all-to-all-done.5 = bf16[8,32,3584]{2,1,0:T(8,128)(2,1)S(1)} async-done(((bf16[8,32,3584]{2,1,0:T(8,128)(2,1)}), bf16[8,32,3584]{2,1,0:T(8,128)(2,1)S(1)}, u32[]{:S(2)}, u32[]{:S(2)}) %all-to-all-start.5) | async-done | bytes 1835040 | tf_op jit(solution)/shard_map/all_to_all | solution.py:110
  144.1 4.5 %all-to-all-start.1 = ((bf16[8,32,7168]{2,1,0:T(8,128)(2,1)}), bf16[8,32,7168]{2,1,0:T(8,128)(2,1)}, u32[]{:S(2)}, u32[]{:S(2)}) async-start(bf16[8,32,7168]{2,1,0:T(8,128)(2,1)} %bitcast.103), calls=%async_computation.1 | async-start | bytes 7340032 | tf_op jit(solution)/shard_map/all_to_all | solution.py:110
  148.7 5.8 %fusion.147 = (bf16[256,1024]{1,0:T(8,128)(2,1)S(1)}, f32[256,1024]{1,0:T(8,128)S(1)}) fusion(bf16[1024,1024]{1,0:T(8,128)(2,1)} %param.11, s32[]{:T(128)S(6)} %select_n.76, f32[256]{0:T(256)S(1)} %reshape.106, bf16[1,1024,3584]{2,1,0:T(8,128)(2,1)} %param.13, bf16[256,7168]{1,0:T(8,128)(2,1)} %bitcast.21), kind=kOutput, calls=%fused_computation.82 | convolution fusion | flops 1881145344 | bytes 11273220 | tf_op jit(solution)/shard_map/dot_general | solution.py:46
  154.5 5.9 %fusion.112 = bf16[256,1024]{1,0:T(8,128)(2,1)S(1)} fusion(f32[256,1024]{1,0:T(8,128)S(1)} %get-tuple-element.48, bf16[3584,2048]{1,0:T(8,128)(2,1)} %bitcast.95, bf16[256,7168]{1,0:T(8,128)(2,1)} %bitcast.21, bf16[1024,1024]{1,0:T(8,128)(2,1)} %param.11, s32[]{:T(128)S(6)} %select_n.76), kind=kOutput, calls=%fused_computation.65 | convolution fusion | flops 1881931776 | bytes 11272196 | tf_op jit(solution)/shard_map/dot_general | solution.py:45
  160.5 1.0 pad_maximum_fusion.1.grad_ref
  161.5 9.5 %shard_map.74 = bf16[256,3584]{1,0:T(8,128)(2,1)} custom-call(bf16[256,2048]{1,0:T(8,128)(2,1)} %pad_maximum_fusion.1.grad_ref, bf16[3584,2048]{1,0:T(8,128)(2,1)} %bitcast.96), custom_call_target="tpu_custom_call" | custom-call | tf_op jit(solution)/shard_map/pallas_call | solution.py:32
  171.0 0.4 convolution_convert_fusion.7
  171.4 20.7 %all-to-all-done.1 = bf16[8,32,7168]{2,1,0:T(8,128)(2,1)} async-done(((bf16[8,32,7168]{2,1,0:T(8,128)(2,1)}), bf16[8,32,7168]{2,1,0:T(8,128)(2,1)}, u32[]{:S(2)}, u32[]{:S(2)}) %all-to-all-start.1) | async-done | bytes 3670048 | tf_op jit(solution)/shard_map/all_to_all | solution.py:110
  192.1 3.6 all-to-all-start.6
  195.7 0.4 fusion.168
  196.1 4.5 %convolution_convert_fusion.3 = bf16[256,7168]{1,0:T(8,128)(2,1)} fusion(bf16[128,256]{1,0:T(8,128)(2,1)S(1)} %fusion.168, bf16[128,7168]{1,0:T(8,128)(2,1)} %collective-permute-done.2), kind=kOutput, calls=%fused_computation.3 | convolution fusion | flops 471597056 | bytes 5570560 | tf_op jit(solution)/shard_map/dot_general | solution.py:59
  200.6 18.9 %all-to-all-done.6 = bf16[8,32,3584]{2,1,0:T(8,128)(2,1)S(1)} async-done(((bf16[8,32,3584]{2,1,0:T(8,128)(2,1)}), bf16[8,32,3584]{2,1,0:T(8,128)(2,1)S(1)}, u32[]{:S(2)}, u32[]{:S(2)}) %all-to-all-start.6) | async-done | bytes 1835040 | tf_op jit(solution)/shard_map/all_to_all | solution.py:110
  219.5 4.7 %all-to-all-start = ((bf16[8,32,7168]{2,1,0:T(8,128)(2,1)}), bf16[8,32,7168]{2,1,0:T(8,128)(2,1)}, u32[]{:S(2)}, u32[]{:S(2)}) async-start(bf16[8,32,7168]{2,1,0:T(8,128)(2,1)} %bitcast.101), calls=%async_computation | async-start | bytes 7340032 | tf_op jit(solution)/shard_map/all_to_all | solution.py:110
  224.3 5.8 %fusion.153 = (bf16[256,1024]{1,0:T(8,128)(2,1)S(1)}, f32[256,1024]{1,0:T(8,128)S(1)}) fusion(bf16[1024,1024]{1,0:T(8,128)(2,1)} %param.11, s32[]{:T(128)S(6)} %select_n.77, f32[256]{0:T(256)S(1)} %reshape.107, bf16[1,1024,3584]{2,1,0:T(8,128)(2,1)} %param.13, bf16[256,7168]{1,0:T(8,128)(2,1)} %bitcast.24), kind=kOutput, calls=%fused_computation.88 | convolution fusion | flops 1881145344 | bytes 11273220 | tf_op jit(solution)/shard_map/dot_general | solution.py:46
  230.2 5.9 %fusion.117 = bf16[256,1024]{1,0:T(8,128)(2,1)S(1)} fusion(f32[256,1024]{1,0:T(8,128)S(1)} %get-tuple-element.50, bf16[3584,2048]{1,0:T(8,128)(2,1)} %bitcast.97, bf16[256,7168]{1,0:T(8,128)(2,1)} %bitcast.24, bf16[1024,1024]{1,0:T(8,128)(2,1)} %param.11, s32[]{:T(128)S(6)} %select_n.77), kind=kOutput, calls=%fused_computation.66 | convolution fusion | flops 1881931776 | bytes 11272196 | tf_op jit(solution)/shard_map/dot_general | solution.py:45
  236.1 1.1 pad_maximum_fusion.2.grad_ref
  237.2 9.4 %shard_map.75 = bf16[256,3584]{1,0:T(8,128)(2,1)} custom-call(bf16[256,2048]{1,0:T(8,128)(2,1)} %pad_maximum_fusion.2.grad_ref, bf16[3584,2048]{1,0:T(8,128)(2,1)} %bitcast.98), custom_call_target="tpu_custom_call" | custom-call | tf_op jit(solution)/shard_map/pallas_call | solution.py:32
  246.6 1.4 convolution_convert_fusion.6
  248.0 19.5 %all-to-all-done = bf16[8,32,7168]{2,1,0:T(8,128)(2,1)} async-done(((bf16[8,32,7168]{2,1,0:T(8,128)(2,1)}), bf16[8,32,7168]{2,1,0:T(8,128)(2,1)}, u32[]{:S(2)}, u32[]{:S(2)}) %all-to-all-start) | async-done | bytes 3670048 | tf_op jit(solution)/shard_map/all_to_all | solution.py:110
  267.5 3.6 all-to-all-start.7
  271.1 1.8 collective-permute-start.3
  272.9 5.8 %fusion.159 = (bf16[256,1024]{1,0:T(8,128)(2,1)S(1)}, f32[256,1024]{1,0:T(8,128)S(1)}) fusion(bf16[1024,1024]{1,0:T(8,128)(2,1)} %param.11, s32[]{:T(128)S(6)} %select_n.78, f32[256]{0:T(256)S(1)} %reshape.108, bf16[1,1024,3584]{2,1,0:T(8,128)(2,1)} %param.13, bf16[256,7168]{1,0:T(8,128)(2,1)} %bitcast.27), kind=kOutput, calls=%fused_computation.94 | convolution fusion | flops 1881145344 | bytes 11273220 | tf_op jit(solution)/shard_map/dot_general | solution.py:46
  278.7 5.9 %fusion.122 = bf16[256,1024]{1,0:T(8,128)(2,1)S(1)} fusion(f32[256,1024]{1,0:T(8,128)S(1)} %get-tuple-element.52, bf16[3584,2048]{1,0:T(8,128)(2,1)} %bitcast.99, bf16[256,7168]{1,0:T(8,128)(2,1)} %bitcast.27, bf16[1024,1024]{1,0:T(8,128)(2,1)} %param.11, s32[]{:T(128)S(6)} %select_n.78), kind=kOutput, calls=%fused_computation.67 | convolution fusion | flops 1881931776 | bytes 11272196 | tf_op jit(solution)/shard_map/dot_general | solution.py:45
  284.6 1.0 pad_maximum_fusion.3.grad_ref
  285.7 9.5 %shard_map.76 = bf16[256,3584]{1,0:T(8,128)(2,1)} custom-call(bf16[256,2048]{1,0:T(8,128)(2,1)} %pad_maximum_fusion.3.grad_ref, bf16[3584,2048]{1,0:T(8,128)(2,1)} %bitcast.100), custom_call_target="tpu_custom_call" | custom-call | tf_op jit(solution)/shard_map/pallas_call | solution.py:32
  295.2 1.3 convolution_convert_fusion.5
  296.5 4.1 %all-to-all-start.8 = ((bf16[8,32,3584]{2,1,0:T(8,128)(2,1)}), bf16[8,32,3584]{2,1,0:T(8,128)(2,1)S(1)}, u32[]{:S(2)}, u32[]{:S(2)}) async-start(bf16[8,32,3584]{2,1,0:T(8,128)(2,1)} %bitcast.30), calls=%async_computation.8 | async-start | bytes 3670016 | tf_op jit(solution)/shard_map/all_to_all | solution.py:110
  300.6 23.8 %all-to-all-done.8 = bf16[8,32,3584]{2,1,0:T(8,128)(2,1)S(1)} async-done(((bf16[8,32,3584]{2,1,0:T(8,128)(2,1)}), bf16[8,32,3584]{2,1,0:T(8,128)(2,1)S(1)}, u32[]{:S(2)}, u32[]{:S(2)}) %all-to-all-start.8) | async-done | bytes 1835040 | tf_op jit(solution)/shard_map/all_to_all | solution.py:110
  324.4 0.4 convolution_convert_fusion.4
  324.9 19.1 %collective-permute-done.4 = bf16[128,3584]{1,0:T(8,128)(2,1)} collective-permute-done((bf16[128,3584]{1,0:T(8,128)(2,1)}, bf16[128,3584]{1,0:T(8,128)(2,1)}, u32[]{:S(2)}, u32[]{:S(2)}) %collective-permute-start.4) | collective-permute-done | bytes 917536 | tf_op jit(solution)/shard_map/ppermute | solution.py:68
  343.9 24.1 %collective-permute-done.5 = bf16[128,3584]{1,0:T(8,128)(2,1)S(1)} collective-permute-done((bf16[128,3584]{1,0:T(8,128)(2,1)S(1)}, bf16[128,3584]{1,0:T(8,128)(2,1)S(1)}, u32[]{:S(2)}, u32[]{:S(2)}) %collective-permute-start.5) | collective-permute-done | bytes 917536 | tf_op jit(solution)/shard_map/ppermute | solution.py:68
  368.1 2.9 add_convert_fusion
  (35 shorter events, 1.1 us)
Async XLA Ops:
  0.0 1.9 copy-start.1
  2.1 9.0 %copy-start = (bf16[128,3584]{1,0:T(8,128)(2,1)S(1)}, bf16[128,3584]{1,0:T(8,128)(2,1)}, u32[]{:S(2)}) copy-start(bf16[128,3584]{1,0:T(8,128)(2,1)} %param.7) | copy-start | bytes 2752516
  5.4 9.9 %all-to-all-start.4 = ((bf16[8,4,32]{2,1,0:T(4,128)(2,1)}), bf16[8,4,32]{2,1,0:T(4,128)(2,1)S(1)}, u32[]{:S(2)}, u32[]{:S(2)}) async-start(bf16[8,4,32]{2,1,0:T(4,128)(2,1)} %copy.12), calls=%async_computation.4 | async-start | bytes 16384 | tf_op jit(solution)/shard_map/all_to_all | solution.py:107
  15.4 53.3 %all-to-all-start.3 = ((bf16[8,32,7168]{2,1,0:T(8,128)(2,1)}), bf16[8,32,7168]{2,1,0:T(8,128)(2,1)}, u32[]{:S(2)}, u32[]{:S(2)}) async-start(bf16[8,32,7168]{2,1,0:T(8,128)(2,1)} %bitcast.104), calls=%async_computation.3 | async-start | bytes 7340032 | tf_op jit(solution)/shard_map/all_to_all | solution.py:110
  19.9 44.4 %collective-permute-start = (bf16[128,7168]{1,0:T(8,128)(2,1)S(1)}, bf16[128,7168]{1,0:T(8,128)(2,1)}, u32[]{:S(2)}, u32[]{:S(2)}) collective-permute-start(bf16[128,7168]{1,0:T(8,128)(2,1)S(1)} %constant_dynamic-update-slice_fusion), channel_id=1, source_target_pairs={{0,8},{8,16},{16,24},{24,0},{1,9},{9,17},{17,25},{25,1},{2,10},{10... | collective-permute-start | bytes 5505032 | tf_op jit(solution)/shard_map/ppermute | solution.py:68
  68.7 48.0 %all-to-all-start.2 = ((bf16[8,32,7168]{2,1,0:T(8,128)(2,1)}), bf16[8,32,7168]{2,1,0:T(8,128)(2,1)}, u32[]{:S(2)}, u32[]{:S(2)}) async-start(bf16[8,32,7168]{2,1,0:T(8,128)(2,1)} %bitcast.102), calls=%async_computation.2 | async-start | bytes 7340032 | tf_op jit(solution)/shard_map/all_to_all | solution.py:110
  73.4 47.6 %collective-permute-start.1 = (bf16[128,7168]{1,0:T(8,128)(2,1)}, bf16[128,7168]{1,0:T(8,128)(2,1)}, u32[]{:S(2)}, u32[]{:S(2)}) collective-permute-start(bf16[128,7168]{1,0:T(8,128)(2,1)} %collective-permute-done), channel_id=1, source_target_pairs={{0,8},{8,16},{16,24},{24,0},{1,9},{9,17},{17,25},{25,1},{2,10},{10... | collective-permute-start | bytes 5505032 | tf_op jit(solution)/shard_map/ppermute | solution.py:68
  116.7 27.4 %all-to-all-start.5 = ((bf16[8,32,3584]{2,1,0:T(8,128)(2,1)}), bf16[8,32,3584]{2,1,0:T(8,128)(2,1)S(1)}, u32[]{:S(2)}, u32[]{:S(2)}) async-start(bf16[8,32,3584]{2,1,0:T(8,128)(2,1)} %bitcast.105), calls=%async_computation.5 | async-start | bytes 3670016 | tf_op jit(solution)/shard_map/all_to_all | solution.py:110
  144.1 48.0 %all-to-all-start.1 = ((bf16[8,32,7168]{2,1,0:T(8,128)(2,1)}), bf16[8,32,7168]{2,1,0:T(8,128)(2,1)}, u32[]{:S(2)}, u32[]{:S(2)}) async-start(bf16[8,32,7168]{2,1,0:T(8,128)(2,1)} %bitcast.103), calls=%async_computation.1 | async-start | bytes 7340032 | tf_op jit(solution)/shard_map/all_to_all | solution.py:110
  148.7 47.4 %collective-permute-start.2 = (bf16[128,7168]{1,0:T(8,128)(2,1)}, bf16[128,7168]{1,0:T(8,128)(2,1)}, u32[]{:S(2)}, u32[]{:S(2)}) collective-permute-start(bf16[128,7168]{1,0:T(8,128)(2,1)} %collective-permute-done.1), channel_id=1, source_target_pairs={{0,8},{8,16},{16,24},{24,0},{1,9},{9,17},{17,25},{25,1},{2,10},{10... | collective-permute-start | bytes 5505032 | tf_op jit(solution)/shard_map/ppermute | solution.py:68
  192.1 27.4 %all-to-all-start.6 = ((bf16[8,32,3584]{2,1,0:T(8,128)(2,1)}), bf16[8,32,3584]{2,1,0:T(8,128)(2,1)S(1)}, u32[]{:S(2)}, u32[]{:S(2)}) async-start(bf16[8,32,3584]{2,1,0:T(8,128)(2,1)} %bitcast.25), calls=%async_computation.6 | async-start | bytes 3670016 | tf_op jit(solution)/shard_map/all_to_all | solution.py:110
  219.5 48.0 %all-to-all-start = ((bf16[8,32,7168]{2,1,0:T(8,128)(2,1)}), bf16[8,32,7168]{2,1,0:T(8,128)(2,1)}, u32[]{:S(2)}, u32[]{:S(2)}) async-start(bf16[8,32,7168]{2,1,0:T(8,128)(2,1)} %bitcast.101), calls=%async_computation | async-start | bytes 7340032 | tf_op jit(solution)/shard_map/all_to_all | solution.py:110
  267.5 27.7 %all-to-all-start.7 = ((bf16[8,32,3584]{2,1,0:T(8,128)(2,1)}), bf16[8,32,3584]{2,1,0:T(8,128)(2,1)S(1)}, u32[]{:S(2)}, u32[]{:S(2)}) async-start(bf16[8,32,3584]{2,1,0:T(8,128)(2,1)} %bitcast.28), calls=%async_computation.7 | async-start | bytes 3670016 | tf_op jit(solution)/shard_map/all_to_all | solution.py:110
  271.1 25.5 %collective-permute-start.3 = (bf16[128,3584]{1,0:T(8,128)(2,1)}, bf16[128,3584]{1,0:T(8,128)(2,1)}, u32[]{:S(2)}, u32[]{:S(2)}) collective-permute-start(bf16[128,3584]{1,0:T(8,128)(2,1)} %convolution_convert_fusion.6), channel_id=1, source_target_pairs={{0,24},{8,0},{16,8},{24,16},{1,25},{9,1},{17,9},{25,17},{2,26},{10... | collective-permute-start | bytes 2752520 | tf_op jit(solution)/shard_map/ppermute | solution.py:68
  296.5 27.9 %all-to-all-start.8 = ((bf16[8,32,3584]{2,1,0:T(8,128)(2,1)}), bf16[8,32,3584]{2,1,0:T(8,128)(2,1)S(1)}, u32[]{:S(2)}, u32[]{:S(2)}) async-start(bf16[8,32,3584]{2,1,0:T(8,128)(2,1)} %bitcast.30), calls=%async_computation.8 | async-start | bytes 3670016 | tf_op jit(solution)/shard_map/all_to_all | solution.py:110
  300.6 43.3 %collective-permute-start.4 = (bf16[128,3584]{1,0:T(8,128)(2,1)}, bf16[128,3584]{1,0:T(8,128)(2,1)}, u32[]{:S(2)}, u32[]{:S(2)}) collective-permute-start(bf16[128,3584]{1,0:T(8,128)(2,1)} %convolution_convert_fusion.5), channel_id=1, source_target_pairs={{0,16},{8,24},{16,0},{24,8},{1,17},{9,25},{17,1},{25,9},{2,18},{10... | collective-permute-start | bytes 2752520 | tf_op jit(solution)/shard_map/ppermute | solution.py:68
  343.9 24.1 %collective-permute-start.5 = (bf16[128,3584]{1,0:T(8,128)(2,1)S(1)}, bf16[128,3584]{1,0:T(8,128)(2,1)S(1)}, u32[]{:S(2)}, u32[]{:S(2)}) collective-permute-start(bf16[128,3584]{1,0:T(8,128)(2,1)S(1)} %convolution_convert_fusion.4), channel_id=1, source_target_pairs={{0,8},{8,16},{16,24},{24,0},{1,9},{9,17},{17,25},{25,1},{2,10},{10... | collective-permute-start | bytes 2752520 | tf_op jit(solution)/shard_map/ppermute | solution.py:68

commit v17 on v13

--- a/solution.py
+++ b/solution.py
@@ -152,8 +152,12 @@
         if 0 <= slot < n_node:
             produced["contrib", slot] = compute(slot, received[slot])
         if 0 <= slot - 1 < n_node:
-            produced["sum", slot - 1] = gather_back(slot - 1, contribs[slot - 1])
-        if 0 <= slot - 2 < n_node:
+            node_sum = gather_back(slot - 1, contribs[slot - 1])
+            if slot - 1 == n_node - 2:
+                produced["home", slot - 1] = send_home(slot - 1, node_sum)
+            else:
+                produced["sum", slot - 1] = node_sum
+        if 0 <= slot - 2 < n_node and slot - 2 != n_node - 2:
             produced["home", slot - 2] = send_home(slot - 2, sums[slot - 2])
         keys = list(produced)
         values = lax.optimization_barrier([produced[key] for key in keys])

time: 370 us -> 390 us (1.054)
  blocking collectives: 0 us -> 28.8 us
  waiting for transfers between devices: 205 us -> 198 us
    all_to_all x0 -> x1, blocking collectives: none -> 28.8 us  [spread(): lax.all_to_all(rows.reshape(n_local, capacity, rows.shape[-1]), 'local',...]
    all_to_all x8 -> x7, waiting for transfers between devices: 119 us -> 111 us  [spread(): lax.all_to_all(rows.reshape(n_local, capacity, rows.shape[-1]), 'local',...]
    all_to_all x8 -> x7, starting transfers between devices: 33.9 us -> 30.4 us  [spread(): lax.all_to_all(rows.reshape(n_local, capacity, rows.shape[-1]), 'local',...]
  transfers between devices with their start and end apart: 15 -> 14, of which waited for: 11 -> 10; matrix products, arithmetic and copies ran while one was open for 20% -> 19% of each run, Pallas kernels for 10% -> 10%
where the time goes in v17:
time: 390 us; the launch traced here: 389 us
  waiting for transfers between devices  198 us (51%)
  matrix products  70.3 us (18%)
  starting transfers between devices  38.8 us (10%)
  Pallas kernels  37.8 us (10%)
  blocking collectives  28.8 us (7%)
  other arithmetic  8.6 us (2%)
  local copies, waits for them, and re-layouts  5.86 us (2%)
    all_to_all x7, waiting for transfers between devices, spread(): lax.all_to_all(rows.reshape(n_local, capacity, rows.shape[-1]), 'local',...  111 us
    ppermute x6, waiting for transfers between devices, shift(): lax.ppermute(value, 'node', [(i, (i + step) % n_node) for i in range(n_no...  86.9 us
    pallas_call x4, Pallas kernels, part_matmul(): pl.pallas_call(part_kernel, grid=(width // tile,), in_specs=[pl.BlockSpec...  37.8 us
    all_to_all x7, starting transfers between devices, spread(): lax.all_to_all(rows.reshape(n_local, capacity, rows.shape[-1]), 'local',...  30.4 us
    all_to_all x1, blocking collectives, spread(): lax.all_to_all(rows.reshape(n_local, capacity, rows.shape[-1]), 'local',...  28.8 us
    dot_general x4, matrix products, expert_backward(): lax.dot_general(rows_dy, weight_out, (((1,), (1,)), ((), ())), preferred_...  24.2 us
    dot_general x4, matrix products, expert_backward(): jnp.dot(rows_x, weight_in[:, FF:], preferred_element_type=jnp.float32)  23.7 us
    dot_general x4, matrix products, select_rows(): lax.dot_general(onehot, rows, (((0,), (0,)), ((), ())), preferred_element...  16.5 us
  transfers between devices with their start and end apart: 14, of which 10 were waited for; matrix products, arithmetic and copies ran while one was open for 19% of the time, Pallas kernels for 10%

profile of v17, /device:TPU:0, one launch (start us, length us, event | category | flops | bytes accessed | tf_op | source)
XLA Modules:
  0.0 388.6 jit_solution(5328710333115562288)
XLA Ops:
  0.0 0.9 copy.11
  0.9 0.2 reshape.88
  1.1 0.6 fusion.133
  2.0 0.4 fusion.169
  2.5 1.3 constant_dynamic-update-slice_fusion
  3.7 2.9 convolution_convert_fusion.3
  6.7 5.3 %all-to-all-start = ((bf16[8,32,7168]{2,1,0:T(8,128)(2,1)}), bf16[8,32,7168]{2,1,0:T(8,128)(2,1)}, u32[]{:S(2)}, u32[]{:S(2)}) async-start(bf16[8,32,7168]{2,1,0:T(8,128)(2,1)} %bitcast.101), calls=%async_computation | async-start | bytes 7340032 | tf_op jit(solution)/shard_map/all_to_all | solution.py:110
  12.0 2.4 collective-permute-start
  14.4 0.1 copy.13
  14.5 0.1 copy.16
  14.7 0.1 copy.15
  15.0 0.4 fusion.161
  15.6 0.4 fusion.162
  16.1 0.4 fusion.164
  16.8 0.4 fusion.166
  17.3 0.6 copy.12
  17.9 0.4 fusion.170
  18.3 37.3 %all-to-all-done = bf16[8,32,7168]{2,1,0:T(8,128)(2,1)} async-done(((bf16[8,32,7168]{2,1,0:T(8,128)(2,1)}), bf16[8,32,7168]{2,1,0:T(8,128)(2,1)}, u32[]{:S(2)}, u32[]{:S(2)}) %all-to-all-start) | async-done | bytes 3670048 | tf_op jit(solution)/shard_map/all_to_all | solution.py:110
  55.6 3.3 all-to-all-start.2
  58.9 4.5 %convolution_convert_fusion.2 = bf16[256,7168]{1,0:T(8,128)(2,1)} fusion(bf16[128,256]{1,0:T(8,128)(2,1)S(1)} %fusion.170, bf16[128,7168]{1,0:T(8,128)(2,1)} %collective-permute-done), kind=kOutput, calls=%fused_computation.2 | convolution fusion | flops 471597056 | bytes 5570560 | tf_op jit(solution)/shard_map/dot_general | solution.py:59
  63.4 0.1 all-to-all-done.2
  63.6 4.5 %all-to-all-start.1 = ((bf16[8,32,7168]{2,1,0:T(8,128)(2,1)}), bf16[8,32,7168]{2,1,0:T(8,128)(2,1)}, u32[]{:S(2)}, u32[]{:S(2)}) async-start(bf16[8,32,7168]{2,1,0:T(8,128)(2,1)} %bitcast.102), calls=%async_computation.1 | async-start | bytes 7340032 | tf_op jit(solution)/shard_map/all_to_all | solution.py:110
  68.2 2.3 collective-permute-start.1
  70.5 5.8 %fusion.141 = (bf16[256,1024]{1,0:T(8,128)(2,1)S(1)}, f32[256,1024]{1,0:T(8,128)S(1)}) fusion(bf16[1024,1024]{1,0:T(8,128)(2,1)} %param.11, s32[]{:T(128)S(6)} %select_n.75, f32[256]{0:T(256)S(1)} %reshape.105, bf16[1,1024,3584]{2,1,0:T(8,128)(2,1)} %param.13, bf16[256,7168]{1,0:T(8,128)(2,1)} %bitcast.4), kind=kOutput, calls=%fused_computation.76 | convolution fusion | flops 1881145344 | bytes 11273220 | tf_op jit(solution)/shard_map/dot_general | solution.py:46
  76.3 5.9 %fusion.107 = bf16[256,1024]{1,0:T(8,128)(2,1)S(1)} fusion(f32[256,1024]{1,0:T(8,128)S(1)} %get-tuple-element.50, bf16[3584,2048]{1,0:T(8,128)(2,1)} %bitcast.93, bf16[256,7168]{1,0:T(8,128)(2,1)} %bitcast.4, bf16[1024,1024]{1,0:T(8,128)(2,1)} %param.11, s32[]{:T(128)S(6)} %select_n.75), kind=kOutput, calls=%fused_computation.64 | convolution fusion | flops 1881931776 | bytes 11272196 | tf_op jit(solution)/shard_map/dot_general | solution.py:45
  82.2 1.1 pad_maximum_fusion.grad_ref
  83.3 9.4 %shard_map.73 = bf16[256,3584]{1,0:T(8,128)(2,1)} custom-call(bf16[256,2048]{1,0:T(8,128)(2,1)} %pad_maximum_fusion.grad_ref, bf16[3584,2048]{1,0:T(8,128)(2,1)} %bitcast.94), custom_call_target="tpu_custom_call" | custom-call | tf_op jit(solution)/shard_map/pallas_call | solution.py:32
  92.7 20.5 %collective-permute-done.1 = bf16[128,7168]{1,0:T(8,128)(2,1)S(1)} collective-permute-done((bf16[128,7168]{1,0:T(8,128)(2,1)}, bf16[128,7168]{1,0:T(8,128)(2,1)S(1)}, u32[]{:S(2)}, u32[]{:S(2)}) %collective-permute-start.1) | collective-permute-done | bytes 1835040 | tf_op jit(solution)/shard_map/ppermute | solution.py:68
  113.2 1.2 copy-done
  114.5 3.9 all-to-all-start.4
  118.4 0.4 fusion.171
  118.8 4.5 %convolution_convert_fusion.1 = bf16[256,7168]{1,0:T(8,128)(2,1)} fusion(bf16[128,256]{1,0:T(8,128)(2,1)S(1)} %fusion.171, bf16[128,7168]{1,0:T(8,128)(2,1)} %copy-done), kind=kOutput, calls=%fused_computation.1 | convolution fusion | flops 471597056 | bytes 5570560 | tf_op jit(solution)/shard_map/dot_general | solution.py:59
  123.3 18.9 %all-to-all-done.4 = bf16[8,32,3584]{2,1,0:T(8,128)(2,1)S(1)} async-done(((bf16[8,32,3584]{2,1,0:T(8,128)(2,1)}), bf16[8,32,3584]{2,1,0:T(8,128)(2,1)S(1)}, u32[]{:S(2)}, u32[]{:S(2)}) %all-to-all-start.4) | async-done | bytes 1835040 | tf_op jit(solution)/shard_map/all_to_all | solution.py:110
  142.2 4.5 %all-to-all-start.3 = ((bf16[8,32,7168]{2,1,0:T(8,128)(2,1)}), bf16[8,32,7168]{2,1,0:T(8,128)(2,1)}, u32[]{:S(2)}, u32[]{:S(2)}) async-start(bf16[8,32,7168]{2,1,0:T(8,128)(2,1)} %bitcast.103), calls=%async_computation.3 | async-start | bytes 7340032 | tf_op jit(solution)/shard_map/all_to_all | solution.py:110
  146.8 5.8 %fusion.147 = (bf16[256,1024]{1,0:T(8,128)(2,1)S(1)}, f32[256,1024]{1,0:T(8,128)S(1)}) fusion(bf16[1024,1024]{1,0:T(8,128)(2,1)} %param.11, s32[]{:T(128)S(6)} %select_n.76, f32[256]{0:T(256)S(1)} %reshape.106, bf16[1,1024,3584]{2,1,0:T(8,128)(2,1)} %param.13, bf16[256,7168]{1,0:T(8,128)(2,1)} %bitcast.20), kind=kOutput, calls=%fused_computation.82 | convolution fusion | flops 1881145344 | bytes 11273220 | tf_op jit(solution)/shard_map/dot_general | solution.py:46
  152.6 5.9 %fusion.112 = bf16[256,1024]{1,0:T(8,128)(2,1)S(1)} fusion(f32[256,1024]{1,0:T(8,128)S(1)} %get-tuple-element.52, bf16[3584,2048]{1,0:T(8,128)(2,1)} %bitcast.95, bf16[256,7168]{1,0:T(8,128)(2,1)} %bitcast.20, bf16[1024,1024]{1,0:T(8,128)(2,1)} %param.11, s32[]{:T(128)S(6)} %select_n.76), kind=kOutput, calls=%fused_computation.65 | convolution fusion | flops 1881931776 | bytes 11272196 | tf_op jit(solution)/shard_map/dot_general | solution.py:45
  158.6 1.1 pad_maximum_fusion.1.grad_ref
  159.6 9.4 %shard_map.74 = bf16[256,3584]{1,0:T(8,128)(2,1)} custom-call(bf16[256,2048]{1,0:T(8,128)(2,1)} %pad_maximum_fusion.1.grad_ref, bf16[3584,2048]{1,0:T(8,128)(2,1)} %bitcast.96), custom_call_target="tpu_custom_call" | custom-call | tf_op jit(solution)/shard_map/pallas_call | solution.py:32
  169.1 0.4 convolution_convert_fusion.7
  169.5 21.7 %collective-permute-done.2 = bf16[128,7168]{1,0:T(8,128)(2,1)} collective-permute-done((bf16[128,7168]{1,0:T(8,128)(2,1)}, bf16[128,7168]{1,0:T(8,128)(2,1)}, u32[]{:S(2)}, u32[]{:S(2)}) %collective-permute-start.2) | collective-permute-done | bytes 1835040 | tf_op jit(solution)/shard_map/ppermute | solution.py:68
  191.2 3.9 all-to-all-start.6
  195.1 0.4 fusion.168
  195.5 4.5 %convolution_convert_fusion = bf16[256,7168]{1,0:T(8,128)(2,1)} fusion(bf16[128,256]{1,0:T(8,128)(2,1)S(1)} %fusion.168, bf16[128,7168]{1,0:T(8,128)(2,1)} %collective-permute-done.2), kind=kOutput, calls=%fused_computation | convolution fusion | flops 471597056 | bytes 5570560 | tf_op jit(solution)/shard_map/dot_general | solution.py:59
  200.0 18.9 %all-to-all-done.6 = bf16[8,32,3584]{2,1,0:T(8,128)(2,1)S(1)} async-done(((bf16[8,32,3584]{2,1,0:T(8,128)(2,1)}), bf16[8,32,3584]{2,1,0:T(8,128)(2,1)S(1)}, u32[]{:S(2)}, u32[]{:S(2)}) %all-to-all-start.6) | async-done | bytes 1835040 | tf_op jit(solution)/shard_map/all_to_all | solution.py:110
  218.9 4.7 %all-to-all-start.5 = ((bf16[8,32,7168]{2,1,0:T(8,128)(2,1)}), bf16[8,32,7168]{2,1,0:T(8,128)(2,1)}, u32[]{:S(2)}, u32[]{:S(2)}) async-start(bf16[8,32,7168]{2,1,0:T(8,128)(2,1)} %bitcast.104), calls=%async_computation.5 | async-start | bytes 7340032 | tf_op jit(solution)/shard_map/all_to_all | solution.py:110
  223.7 5.8 %fusion.153 = (bf16[256,1024]{1,0:T(8,128)(2,1)S(1)}, f32[256,1024]{1,0:T(8,128)S(1)}) fusion(bf16[1024,1024]{1,0:T(8,128)(2,1)} %param.11, s32[]{:T(128)S(6)} %select_n.77, f32[256]{0:T(256)S(1)} %reshape.107, bf16[1,1024,3584]{2,1,0:T(8,128)(2,1)} %param.13, bf16[256,7168]{1,0:T(8,128)(2,1)} %bitcast.24), kind=kOutput, calls=%fused_computation.88 | convolution fusion | flops 1881145344 | bytes 11273220 | tf_op jit(solution)/shard_map/dot_general | solution.py:46
  229.5 5.9 %fusion.117 = bf16[256,1024]{1,0:T(8,128)(2,1)S(1)} fusion(f32[256,1024]{1,0:T(8,128)S(1)} %get-tuple-element.54, bf16[3584,2048]{1,0:T(8,128)(2,1)} %bitcast.97, bf16[256,7168]{1,0:T(8,128)(2,1)} %bitcast.24, bf16[1024,1024]{1,0:T(8,128)(2,1)} %param.11, s32[]{:T(128)S(6)} %select_n.77), kind=kOutput, calls=%fused_computation.66 | convolution fusion | flops 1881931776 | bytes 11272196 | tf_op jit(solution)/shard_map/dot_general | solution.py:45
  235.5 1.1 pad_maximum_fusion.2.grad_ref
  236.6 9.5 %shard_map.75 = bf16[256,3584]{1,0:T(8,128)(2,1)} custom-call(bf16[256,2048]{1,0:T(8,128)(2,1)} %pad_maximum_fusion.2.grad_ref, bf16[3584,2048]{1,0:T(8,128)(2,1)} %bitcast.98), custom_call_target="tpu_custom_call" | custom-call | tf_op jit(solution)/shard_map/pallas_call | solution.py:32
  246.0 1.4 convolution_convert_fusion.6
  247.4 19.5 %all-to-all-done.5 = bf16[8,32,7168]{2,1,0:T(8,128)(2,1)} async-done(((bf16[8,32,7168]{2,1,0:T(8,128)(2,1)}), bf16[8,32,7168]{2,1,0:T(8,128)(2,1)}, u32[]{:S(2)}, u32[]{:S(2)}) %all-to-all-start.5) | async-done | bytes 3670048 | tf_op jit(solution)/shard_map/all_to_all | solution.py:110
  266.9 3.6 all-to-all-start.7
  270.6 0.4 collective-permute-start.4
  271.0 6.8 %fusion.159 = (bf16[256,1024]{1,0:T(8,128)(2,1)S(1)}, f32[256,1024]{1,0:T(8,128)}) fusion(bf16[1024,1024]{1,0:T(8,128)(2,1)} %param.11, s32[]{:T(128)S(6)} %select_n.78, f32[256]{0:T(256)S(1)} %reshape.108, bf16[1,1024,3584]{2,1,0:T(8,128)(2,1)} %param.13, bf16[256,7168]{1,0:T(8,128)(2,1)} %bitcast.27), kind=kOutput, calls=%fused_computation.94 | convolution fusion | flops 1881145344 | bytes 11273220 | tf_op jit(solution)/shard_map/dot_general | solution.py:46
  277.8 16.4 %all-to-all-done.7 = bf16[8,32,3584]{2,1,0:T(8,128)(2,1)S(1)} async-done(((bf16[8,32,3584]{2,1,0:T(8,128)(2,1)}), bf16[8,32,3584]{2,1,0:T(8,128)(2,1)S(1)}, u32[]{:S(2)}, u32[]{:S(2)}) %all-to-all-start.7) | async-done | bytes 1835040 | tf_op jit(solution)/shard_map/all_to_all | solution.py:110
  294.3 1.3 convolution_convert_fusion.5
  295.6 5.9 %fusion.122 = bf16[256,1024]{1,0:T(8,128)(2,1)S(1)} fusion(f32[256,1024]{1,0:T(8,128)S(1)} %copy-done.3, bf16[3584,2048]{1,0:T(8,128)(2,1)} %bitcast.99, bf16[256,7168]{1,0:T(8,128)(2,1)} %bitcast.27, bf16[1024,1024]{1,0:T(8,128)(2,1)} %param.11, s32[]{:T(128)S(6)} %select_n.78), kind=kOutput, calls=%fused_computation.67 | convolution fusion | flops 1881931776 | bytes 11272196 | tf_op jit(solution)/shard_map/dot_general | solution.py:45
  301.6 1.1 pad_maximum_fusion.3.grad_ref
  302.6 9.4 %shard_map.76 = bf16[256,3584]{1,0:T(8,128)(2,1)} custom-call(bf16[256,2048]{1,0:T(8,128)(2,1)} %pad_maximum_fusion.3.grad_ref, bf16[3584,2048]{1,0:T(8,128)(2,1)} %bitcast.100), custom_call_target="tpu_custom_call" | custom-call | tf_op jit(solution)/shard_map/pallas_call | solution.py:32
  312.1 21.5 %collective-permute-done.3 = bf16[128,3584]{1,0:T(8,128)(2,1)S(1)} collective-permute-done((bf16[128,3584]{1,0:T(8,128)(2,1)}, bf16[128,3584]{1,0:T(8,128)(2,1)S(1)}, u32[]{:S(2)}, u32[]{:S(2)}) %collective-permute-start.3) | collective-permute-done | bytes 917536 | tf_op jit(solution)/shard_map/ppermute | solution.py:68
  333.6 28.8 %all_to_all.45 = bf16[8,32,3584]{2,1,0:T(8,128)(2,1)S(1)} all-to-all(bf16[8,32,3584]{2,1,0:T(8,128)(2,1)} %bitcast.106), channel_id=1, replica_groups=mesh['node'=4,'local'=8] {'local'}, dimensions={0} | all-to-all | bytes 3670016 | tf_op jit(solution)/shard_map/all_to_all | solution.py:110
  362.3 0.4 convolution_convert_fusion.4
  362.8 23.2 %collective-permute-done.5 = bf16[128,3584]{1,0:T(8,128)(2,1)S(1)} collective-permute-done((bf16[128,3584]{1,0:T(8,128)(2,1)S(1)}, bf16[128,3584]{1,0:T(8,128)(2,1)S(1)}, u32[]{:S(2)}, u32[]{:S(2)}) %collective-permute-start.5) | collective-permute-done | bytes 917536 | tf_op jit(solution)/shard_map/ppermute | solution.py:68
  386.0 2.5 add_convert_fusion
  (38 shorter events, 1.5 us)
Async XLA Ops:
  0.0 2.4 copy-start.1
  6.7 7.7 %copy-start.2 = (s32[4,128,8]{1,2,0:T(8,128)S(1)}, s32[4,128,8]{1,2,0:T(8,128)}, u32[]{:S(2)}) copy-start(s32[4,128,8]{1,2,0:T(8,128)} %param.10) | copy-start | bytes 49156
  6.7 48.9 %all-to-all-start = ((bf16[8,32,7168]{2,1,0:T(8,128)(2,1)}), bf16[8,32,7168]{2,1,0:T(8,128)(2,1)}, u32[]{:S(2)}, u32[]{:S(2)}) async-start(bf16[8,32,7168]{2,1,0:T(8,128)(2,1)} %bitcast.101), calls=%async_computation | async-start | bytes 7340032 | tf_op jit(solution)/shard_map/all_to_all | solution.py:110
  12.0 46.9 %collective-permute-start = (bf16[128,7168]{1,0:T(8,128)(2,1)S(1)}, bf16[128,7168]{1,0:T(8,128)(2,1)}, u32[]{:S(2)}, u32[]{:S(2)}) collective-permute-start(bf16[128,7168]{1,0:T(8,128)(2,1)S(1)} %constant_dynamic-update-slice_fusion), channel_id=1, source_target_pairs={{0,8},{8,16},{16,24},{24,0},{1,9},{9,17},{17,25},{25,1},{2,10},{10... | collective-permute-start | bytes 5505032 | tf_op jit(solution)/shard_map/ppermute | solution.py:68
  55.6 8.0 %all-to-all-start.2 = ((bf16[8,4,32]{2,1,0:T(4,128)(2,1)}), bf16[8,4,32]{2,1,0:T(4,128)(2,1)S(1)}, u32[]{:S(2)}, u32[]{:S(2)}) async-start(bf16[8,4,32]{2,1,0:T(4,128)(2,1)} %copy.12), calls=%async_computation.2 | async-start | bytes 16384 | tf_op jit(solution)/shard_map/all_to_all | solution.py:107
  63.6 49.7 %all-to-all-start.1 = ((bf16[8,32,7168]{2,1,0:T(8,128)(2,1)}), bf16[8,32,7168]{2,1,0:T(8,128)(2,1)}, u32[]{:S(2)}, u32[]{:S(2)}) async-start(bf16[8,32,7168]{2,1,0:T(8,128)(2,1)} %bitcast.102), calls=%async_computation.1 | async-start | bytes 7340032 | tf_op jit(solution)/shard_map/all_to_all | solution.py:110
  68.2 45.0 %collective-permute-start.1 = (bf16[128,7168]{1,0:T(8,128)(2,1)}, bf16[128,7168]{1,0:T(8,128)(2,1)S(1)}, u32[]{:S(2)}, u32[]{:S(2)}) collective-permute-start(bf16[128,7168]{1,0:T(8,128)(2,1)} %collective-permute-done), channel_id=1, source_target_pairs={{0,8},{8,16},{16,24},{24,0},{1,9},{9,17},{17,25},{25,1},{2,10},{10... | collective-permute-start | bytes 5505032 | tf_op jit(solution)/shard_map/ppermute | solution.py:68
  113.2 1.2 copy-start
  114.5 27.7 %all-to-all-start.4 = ((bf16[8,32,3584]{2,1,0:T(8,128)(2,1)}), bf16[8,32,3584]{2,1,0:T(8,128)(2,1)S(1)}, u32[]{:S(2)}, u32[]{:S(2)}) async-start(bf16[8,32,3584]{2,1,0:T(8,128)(2,1)} %bitcast.105), calls=%async_computation.4 | async-start | bytes 3670016 | tf_op jit(solution)/shard_map/all_to_all | solution.py:110
  142.2 49.0 %all-to-all-start.3 = ((bf16[8,32,7168]{2,1,0:T(8,128)(2,1)}), bf16[8,32,7168]{2,1,0:T(8,128)(2,1)}, u32[]{:S(2)}, u32[]{:S(2)}) async-start(bf16[8,32,7168]{2,1,0:T(8,128)(2,1)} %bitcast.103), calls=%async_computation.3 | async-start | bytes 7340032 | tf_op jit(solution)/shard_map/all_to_all | solution.py:110
  146.8 44.4 %collective-permute-start.2 = (bf16[128,7168]{1,0:T(8,128)(2,1)}, bf16[128,7168]{1,0:T(8,128)(2,1)}, u32[]{:S(2)}, u32[]{:S(2)}) collective-permute-start(bf16[128,7168]{1,0:T(8,128)(2,1)} %copy-done), channel_id=1, source_target_pairs={{0,8},{8,16},{16,24},{24,0},{1,9},{9,17},{17,25},{25,1},{2,10},{10... | collective-permute-start | bytes 5505032 | tf_op jit(solution)/shard_map/ppermute | solution.py:68
  191.2 27.7 %all-to-all-start.6 = ((bf16[8,32,3584]{2,1,0:T(8,128)(2,1)}), bf16[8,32,3584]{2,1,0:T(8,128)(2,1)S(1)}, u32[]{:S(2)}, u32[]{:S(2)}) async-start(bf16[8,32,3584]{2,1,0:T(8,128)(2,1)} %bitcast.25), calls=%async_computation.6 | async-start | bytes 3670016 | tf_op jit(solution)/shard_map/all_to_all | solution.py:110
  218.9 48.0 %all-to-all-start.5 = ((bf16[8,32,7168]{2,1,0:T(8,128)(2,1)}), bf16[8,32,7168]{2,1,0:T(8,128)(2,1)}, u32[]{:S(2)}, u32[]{:S(2)}) async-start(bf16[8,32,7168]{2,1,0:T(8,128)(2,1)} %bitcast.104), calls=%async_computation.5 | async-start | bytes 7340032 | tf_op jit(solution)/shard_map/all_to_all | solution.py:110
  266.9 27.4 %all-to-all-start.7 = ((bf16[8,32,3584]{2,1,0:T(8,128)(2,1)}), bf16[8,32,3584]{2,1,0:T(8,128)(2,1)S(1)}, u32[]{:S(2)}, u32[]{:S(2)}) async-start(bf16[8,32,3584]{2,1,0:T(8,128)(2,1)} %bitcast.28), calls=%async_computation.7 | async-start | bytes 3670016 | tf_op jit(solution)/shard_map/all_to_all | solution.py:110
  270.6 41.5 %collective-permute-start.4 = (bf16[128,3584]{1,0:T(8,128)(2,1)}, bf16[128,3584]{1,0:T(8,128)(2,1)}, u32[]{:S(2)}, u32[]{:S(2)}) collective-permute-start(bf16[128,3584]{1,0:T(8,128)(2,1)} %convolution_convert_fusion.6), channel_id=1, source_target_pairs={{0,24},{8,0},{16,8},{24,16},{1,25},{9,1},{17,9},{25,17},{2,26},{10... | collective-permute-start | bytes 2752520 | tf_op jit(solution)/shard_map/ppermute | solution.py:68
  294.3 1.3 copy-start.3
  295.6 37.9 %collective-permute-start.3 = (bf16[128,3584]{1,0:T(8,128)(2,1)}, bf16[128,3584]{1,0:T(8,128)(2,1)S(1)}, u32[]{:S(2)}, u32[]{:S(2)}) collective-permute-start(bf16[128,3584]{1,0:T(8,128)(2,1)} %convolution_convert_fusion.5), channel_id=1, source_target_pairs={{0,16},{8,24},{16,0},{24,8},{1,17},{9,25},{17,1},{25,9},{2,18},{10... | collective-permute-start | bytes 2752520 | tf_op jit(solution)/shard_map/ppermute | solution.py:68
  362.7 23.3 %collective-permute-start.5 = (bf16[128,3584]{1,0:T(8,128)(2,1)S(1)}, bf16[128,3584]{1,0:T(8,128)(2,1)S(1)}, u32[]{:S(2)}, u32[]{:S(2)}) collective-permute-start(bf16[128,3584]{1,0:T(8,128)(2,1)S(1)} %convolution_convert_fusion.4), channel_id=1, source_target_pairs={{0,8},{8,16},{16,24},{24,0},{1,9},{9,17},{17,25},{25,1},{2,10},{10... | collective-permute-start | bytes 2752520 | tf_op jit(solution)/shard_map/ppermute | solution.py:68
